TPU v7x, 256 devices: a whole 4x4x8 slice. The times are simulated.
256 devices in a mesh: ctx: 32 (over y, x, core), head: 8 (over z).
Axes of the slice: x: 4, y: 4, z: 8, core: 2. Of those that a mesh axis runs over, the one named last changes fastest.
Arguments:
- ssm_input: bfloat16 [8192, 8192], P('ctx', 'head'), may hold values from -6 to 6
- gate_input: bfloat16 [8192, 8192], P('ctx', 'head'), may hold values from -6 to 6
- step_raw: float32 [8192, 128], P('ctx', 'head'), may hold values from -4 to 4
- b_matrix: bfloat16 [8192, 1024], P('ctx', 'head'), may hold values from -6 to 6
- c_matrix: bfloat16 [8192, 1024], P('ctx', 'head'), may hold values from -6 to 6
- step_bias: float32 [128], P('head'), may hold values from -6 to -4
- log_rate: float32 [128], P('head')
- skip_gain: float32 [128], P('head'), may hold values from 0.5 to 1.5
- norm_weight: float32 [8192], P('head'), may hold values from 0.5 to 1.5
- doc_resets: int32 [8192], P('ctx'), may hold values from 0 to 1, as said below
- grad_output: bfloat16 [8192, 8192], P('ctx', 'head'), may hold values from -6 to 6
Outputs:
- grad_input: bfloat16 [8192, 8192], P('ctx', 'head')
- grad_gate: bfloat16 [8192, 8192], P('ctx', 'head')
- grad_step: float32 [8192, 128], P('ctx', 'head')
- grad_b_matrix: float32 [8192, 1024], P('ctx', 'head')
- grad_c_matrix: float32 [8192, 1024], P('ctx', 'head')
Inputs may be any that keep to these rules, and one draw needn't show every extreme that they name: `doc_resets`: exactly 4 positions hold 1, all of them among positions 1 to 127; all others hold 0.
All inputs are finite; a program needn't handle non-finite values.
Results may differ from a plain program's by a relative error of at most 0.001.
Values sent between devices are 32-bit elements; how exact they have to be, the bound alone decides.
No kernel may reach another device: no remote copies, remote signals or barrier semaphores. Data moves between devices by JAX's collectives and lax.ppermute only.
A program may use at most 64 MiB of HBM per device.

v0:
```python
import jax
import jax.numpy as jnp
from jax import lax
from jax.sharding import PartitionSpec as P

HEAD_DIM = 64
STATE = 128
SPAN = 256


HIGHEST_PRECISION = lax.Precision.HIGHEST
EPSILON = 1e-05


def carried_in(array, axis, combine, identity):
    size, index = (lax.axis_size(axis), lax.axis_index(axis))
    everything = jax.tree.map(lambda part: lax.all_gather(part, axis), array)
    start = jax.tree.map(
        lambda part, zero: jnp.broadcast_to(jnp.asarray(zero, part.dtype), part.shape),
        array,
        identity,
    )

    def turn(k, before):
        at = size - 1 - k
        reached = at > index
        new = combine(before, jax.tree.map(lambda part: part[at], everything))
        return jax.tree.map(lambda a, b: jnp.where(reached, a, b), new, before)

    return lax.fori_loop(0, size, turn, start)


def span_mix(x_span, dt_span, b_span, c_span, log_cum, segment):
    log_rows = jnp.moveaxis(log_cum, 0, -1)
    spread = log_rows[..., :, None] - log_rows[..., None, :]
    places = jnp.arange(x_span.shape[0], dtype=jnp.int32)
    keep_mask = (
        (places[:, None] >= places[None, :]) & (segment[:, None] == segment[None, :])
    ).astype(jnp.float32)
    masked = jnp.exp(jnp.minimum(spread, 0.0)) * keep_mask
    scores = jnp.einsum("tgn,sgn->gts", c_span, b_span, precision=HIGHEST_PRECISION)
    weights = scores[:, None] * masked * jnp.moveaxis(dt_span, 0, -1)[..., None, :]
    return jnp.einsum("ghts,sghp->tghp", weights, x_span, precision=HIGHEST_PRECISION)


def block_decays(dt_spans, segment, decay_rate):
    log_cum = jnp.cumsum(dt_spans * decay_rate, axis=1)
    closing = segment[:, -1]
    through = jnp.exp(log_cum[:, -1]) * (closing == 0).astype(jnp.float32)[:, None, None]
    return (log_cum, closing, through)


def local_states(x_spans, dt_spans, b_spans, segment, decay_rate):
    log_cum, closing, through = block_decays(dt_spans, segment, decay_rate)
    same_doc = (segment == closing[:, None]).astype(jnp.float32)
    tail_decay = jnp.exp(log_cum[:, -1:] - log_cum) * same_doc[:, :, None, None]
    added_terms = jnp.einsum(
        "kqgh,kqghp,kqgn->kghpn",
        tail_decay * dt_spans,
        x_spans,
        b_spans,
        precision=HIGHEST_PRECISION,
    )

    def advance(carried_pair, item_pair):
        carry_state, product = carried_pair
        decay_now, fresh_state = item_pair
        return (
            (decay_now[..., None, None] * carry_state + fresh_state, product * decay_now),
            carry_state,
        )

    initial = (
        jnp.zeros(added_terms.shape[1:], jnp.float32),
        jnp.ones(through.shape[1:], jnp.float32),
    )
    (final_state, product), starts = lax.scan(advance, initial, (through, added_terms))
    return (starts, final_state, product)


def output_part(x_spans, dt_spans, b_spans, c_spans, segment, decay_rate, starts, entry_state):
    log_cum, closing, through = block_decays(dt_spans, segment, decay_rate)

    def rolling(product, decay_now):
        return (product * decay_now, product)

    _, before = lax.scan(rolling, jnp.ones(through.shape[1:], jnp.float32), through)
    full_start = starts + before[..., None, None] * entry_state[None]
    opened = (segment == 0).astype(jnp.float32)
    entry_decay = jnp.exp(log_cum) * opened[:, :, None, None]
    carried = (
        jnp.einsum("kqgn,kghpn->kqghp", c_spans, full_start, precision=HIGHEST_PRECISION)
        * entry_decay[..., None]
    )
    mix_block = jax.checkpoint(lambda pieces: span_mix(*pieces))
    inner_part = lax.map(mix_block, (x_spans, dt_spans, b_spans, c_spans, log_cum, segment))
    return inner_part + carried


def compose(earlier, later):
    decay_early, sum_early = earlier
    decay_late, sum_late = later
    return (decay_early * decay_late, decay_late[..., None, None] * sum_early + sum_late)


def body(
    ssm_input,
    gate_input,
    step_raw,
    b_matrix,
    c_matrix,
    step_bias,
    log_rate,
    skip_gain,
    norm_weight,
    doc_resets,
    grad_output,
):
    tokens_here = ssm_input.shape[0]
    heads_here = step_raw.shape[1]
    groups_here = b_matrix.shape[1] // STATE
    per_group = heads_here // groups_here
    spans = tokens_here // SPAN
    x_float = ssm_input.astype(jnp.float32)
    gate_float = gate_input.astype(jnp.float32)
    shifted = step_raw + step_bias[None, :]
    step_size = jax.nn.softplus(shifted)
    decay_rate = (-jnp.exp(log_rate)).reshape(groups_here, per_group)
    x_spans = x_float.reshape(spans, SPAN, groups_here, per_group, HEAD_DIM)
    dt_spans = step_size.reshape(spans, SPAN, groups_here, per_group)
    b_spans = b_matrix.astype(jnp.float32).reshape(spans, SPAN, groups_here, STATE)
    c_spans = c_matrix.astype(jnp.float32).reshape(spans, SPAN, groups_here, STATE)
    segment = jnp.cumsum(doc_resets.reshape(spans, SPAN), axis=1, dtype=jnp.int32)

    def states_call(x_value, dt_value, b_value):
        return local_states(x_value, dt_value, b_value, segment, decay_rate)

    (starts, end_local, through_all), states_back = jax.vjp(states_call, x_spans, dt_spans, b_spans)
    identity = (jnp.ones_like(through_all), jnp.zeros_like(end_local))
    decay_table = lax.all_gather(through_all, "ctx", axis=0, tiled=True)
    own_index = lax.axis_index("ctx")
    ctx_count = lax.axis_size("ctx")
    flat_end = end_local.reshape(heads_here, HEAD_DIM, STATE)
    row_ids = jnp.arange(lax.axis_size("ctx") * heads_here, dtype=jnp.int32)
    receiver = row_ids // heads_here
    head_ids = row_ids % heads_here
    devices = jnp.arange(ctx_count, dtype=jnp.int32)
    between = (devices[None, :] > own_index) & (devices[None, :] < receiver[:, None])
    factors = jnp.where(between, decay_table[:, head_ids].T, 1.0)
    weight = jnp.prod(factors, axis=1) * (own_index < receiver).astype(jnp.float32)
    entry_state = lax.psum_scatter(
        weight[:, None, None] * jnp.take(flat_end, head_ids, axis=0),
        "ctx",
        scatter_dimension=0,
        tiled=True,
    ).reshape(end_local.shape)

    def output_call(x_value, dt_value, b_value, c_value, start_value, entry_value):
        return output_part(
            x_value, dt_value, b_value, c_value, segment, decay_rate, start_value, entry_value
        )

    core_part, output_back = jax.vjp(
        output_call, x_spans, dt_spans, b_spans, c_spans, starts, entry_state
    )
    skip_cols = jnp.repeat(skip_gain, HEAD_DIM)[None, :]
    core_out = core_part.reshape(tokens_here, heads_here * HEAD_DIM) + x_float * skip_cols
    gate_sig = jax.nn.sigmoid(gate_float)
    gate_act = gate_float * gate_sig
    gated = core_out * gate_act
    weighted_grad = norm_weight[None, :] * grad_output.astype(jnp.float32)
    norm_width = lax.axis_size("head") * gated.shape[1]
    squares = lax.psum(jnp.sum(gated * gated, axis=1), "head")
    inv_rms = lax.rsqrt(squares / norm_width + EPSILON)
    normed = gated * inv_rms[:, None]
    product = lax.psum(jnp.sum(weighted_grad * normed, axis=1), "head")
    grad_gated = inv_rms[:, None] * (weighted_grad - normed * (product / norm_width)[:, None])
    grad_core = grad_gated * gate_act
    grad_gate = grad_gated * core_out * gate_sig * (1.0 + gate_float * (1.0 - gate_sig))
    first_grads = output_back(grad_core.reshape(core_part.shape))
    _, exit_adjoint = carried_in((through_all, first_grads[5]), "ctx", compose, identity)
    through_grad = jnp.sum(exit_adjoint * entry_state, axis=(2, 3))
    second_grads = states_back((first_grads[4], exit_adjoint, through_grad))
    grad_input = (first_grads[0] + second_grads[0]).reshape(
        tokens_here, heads_here * HEAD_DIM
    ) + grad_core * skip_cols
    grad_step = (first_grads[1] + second_grads[1]).reshape(
        tokens_here, heads_here
    ) * jax.nn.sigmoid(shifted)
    grad_b_matrix = (first_grads[2] + second_grads[2]).reshape(tokens_here, groups_here * STATE)
    grad_c_matrix = first_grads[3].reshape(tokens_here, groups_here * STATE)
    return (
        grad_input.astype(jnp.bfloat16),
        grad_gate.astype(jnp.bfloat16),
        grad_step,
        grad_b_matrix,
        grad_c_matrix,
    )


def solution(mesh):
    return jax.shard_map(
        body,
        mesh=mesh,
        in_specs=(
            P("ctx", "head"),
            P("ctx", "head"),
            P("ctx", "head"),
            P("ctx", "head"),
            P("ctx", "head"),
            P("head"),
            P("head"),
            P("head"),
            P("head"),
            P("ctx"),
            P("ctx", "head"),
        ),
        out_specs=(
            P("ctx", "head"),
            P("ctx", "head"),
            P("ctx", "head"),
            P("ctx", "head"),
            P("ctx", "head"),
        ),
        check_vma=False,
    )
```

profile of v0, /device:TPU:6, one launch (start us, length us, event | category | flops | bytes accessed | tf_op | source)
XLA Modules:
  0.0 403.6 jit_solution(4905228115888977162)
XLA Ops:
  14.6 1.3 copy.242
  15.8 20.9 %all-gather = f32[32,1,1,16]{3,2,1,0:T(1,128)S(1)} all-gather(f32[1,1,1,16]{3,2,1,0:T(1,128)S(1)} %get-tuple-element.418), channel_id=2, replica_groups=mesh['ctx'=32,'head'=8] {'ctx'}, dimensions={0}, use_global_device_ids=true | all-gather | bytes 2112 | tf_op jit(solution)/shard_map/all_gather | solution.py:140
  36.8 1.5 fusion.46
  38.3 7.0 %gather_fusion.1 = f32[512,64,128]{2,1,0:T(8,128)} fusion(f32[16,64,128]{2,1,0:T(8,128)S(1)} %fusion.46, s32[1024]{0:T(1024)S(1)} %pad_clamp_fusion), kind=kCustom, calls=%fused_computation.1 | custom fusion | bytes 33556480 | tf_op jit(solution)/shard_map/jit(_take)/gather | solution.py:152
  45.3 1.0 gather_fusion
  46.6 11.9 %select_multiply_fusion = f32[512,64,128]{2,1,0:T(8,128)} fusion(f32[512,64,128]{2,1,0:T(8,128)} %gather_fusion.1, f32[512]{0:T(512)S(1)} %compare_select_fusion.3, pred[512]{0:T(512)(128)(4,1)S(1)} %compare_and_fusion), kind=kLoop, calls=%fused_computation.5 | loop fusion | flops 8388608 | bytes 33556992 | tf_op jit(solution)/shard_map/mul | solution.py:152
  60.3 123.2 %reduce-scatter.2.cloned.1.call-done = f32[16,64,128]{2,1,0:T(8,128)} async-done(((f32[512,64,128]{2,1,0:T(8,128)}), f32[16,64,128]{2,1,0:T(8,128)}) %reduce-scatter.2.cloned.1.call-update) | async-done | bytes 524304 | tf_op jit(solution)/shard_map/reduce_scatter | solution.py:151
  183.5 1.6 convolution_bitcast_fusion.1
  185.2 3.2 fusion.38
  189.4 17.4 %psum.14 = f32[256]{0:T(256)S(1)} all-reduce(f32[256]{0:T(256)S(1)} %get-tuple-element.406), channel_id=1, replica_groups=mesh['ctx'=32,'head'=8] {'head'}, use_global_device_ids=true, to_apply=%region_7.8 | all-reduce | flops 256 | bytes 2048 | tf_op jit(solution)/shard_map/psum | solution.py:173
  207.1 15.2 %psum.15 = f32[256]{0:T(256)S(1)} all-reduce(f32[256]{0:T(256)S(1)} %multiply_reduce_fusion.1), channel_id=1, replica_groups=mesh['ctx'=32,'head'=8] {'head'}, use_global_device_ids=true, to_apply=%region_9.10 | all-reduce | flops 256 | bytes 2048 | tf_op jit(solution)/shard_map/psum | solution.py:176
  222.3 3.0 fusion.56
  225.3 1.4 fusion.58
  226.8 1.1 convert.11
  228.8 2.0 multiply_reduce_fusion
  230.7 1.5 copy.259
  232.2 1.0 copy.279
  233.2 3.2 convolution_bitcast_fusion.3
  236.4 65.7 %all-gather.5.cloned.1.call-done = f32[512,64,128]{2,1,0:T(8,128)} async-done(((f32[16,64,128]{2,1,0:T(8,128)}), f32[512,64,128]{2,1,0:T(8,128)}) %all-gather.5.cloned.1.call-update) | async-done | bytes 16777232 | tf_op jit(solution)/shard_map/all_gather | solution.py:17
  302.1 59.4 %while.11 = (s32[]{:T(128)}, f32[1,16,64,128]{3,2,1,0:T(8,128)S(1)}, s32[]{:T(128)}, f32[32,1,16]{2,1,0:T(1,128)}, f32[32,1,16,64,128]{4,3,2,1,0:T(8,128)}, /*index=5*/s32[]{:T(128)}, s32[]{:T(128)}, s32[]{:T(128)}, s32[]{:T(128)}) while((s32[]{:T(128)}, f32[1,16,64,128]{3,2,1,0:T(8,128)S(1)}, s32[]{:T(128)}, ...), condition=%wide.region_11.12_spmd.clone, body=%wide.region_10.11_spmd.clone.sunk | while | flops 524296 | bytes 1573223 | solution.py:30
  302.8 1.2 fusion.115
  304.6 1.2 fusion.115
  306.5 1.2 fusion.115
  308.3 1.2 fusion.115
  310.2 1.2 fusion.115
  312.0 1.2 fusion.115
  313.9 1.2 fusion.115
  315.7 1.2 fusion.115
  317.6 1.2 fusion.115
  319.4 1.2 fusion.115
  321.3 1.2 fusion.115
  323.2 1.2 fusion.115
  325.0 1.2 fusion.115
  326.9 1.2 fusion.115
  328.7 1.2 fusion.115
  330.6 1.2 fusion.115
  332.4 1.2 fusion.115
  334.3 1.2 fusion.115
  336.1 1.2 fusion.115
  338.0 1.2 fusion.115
  339.9 1.2 fusion.115
  341.7 1.2 fusion.115
  343.6 1.2 fusion.115
  345.4 1.2 fusion.115
  347.3 1.2 fusion.115
  349.1 1.2 fusion.115
  351.0 1.2 fusion.115
  352.8 1.2 fusion.115
  354.7 1.2 fusion.115
  356.5 1.2 fusion.115
  358.4 1.2 fusion.115
  360.3 1.2 fusion.115
  361.5 1.6 fusion.50
  363.0 1.8 fusion.47
  365.6 8.3 %fusion.77 = (f32[16,256]{1,0:T(8,128)S(1)}, f32[16,256]{1,0:T(8,128)S(1)}, f32[16,256]{1,0:T(8,128)}, f32[256,256]{1,0:T(8,128)S(1)}) fusion(f32[16,256]{1,0:T(8,128)S(1)} %bitcast.277, f32[256,256]{1,0:T(8,128)S(1)} %fusion.81, f32[16,256]{1,0:T(8,128)S(1)} %bitcast.279, f32[256,256]{1,0:T(8,128)S(1)} %fusion.85, f32[256,1,16,64]{0,3,2,1:T(8,128)S(1)} %copy-done.8, ...), kind=kOutput, calls=%fused_computation.95 | convolution fusion | flops 825151488 | bytes 2965504 | tf_op jit(solution)/shard_map/transpose(jvp())/while/body/eval_jaxpr/checkpoint/ghts,sghp->tghp/dot_general | solution.py:43
  375.0 1.4 pad_add_fusion.1
  377.4 2.5 reduce-window.36
  380.1 2.7 reduce-window.34
  382.9 1.9 convolution_add_fusion
  384.8 1.2 fusion.49
  388.0 1.1 fusion.83
  389.2 1.4 bitcast_multiply_fusion.1
  390.6 4.8 %fusion.41 = f32[256,16,64]{0,2,1:T(8,128)S(1)} fusion(f32[16,256]{1,0:T(8,128)} %bitcast.280, f32[256,256]{1,0:T(8,128)} %copy-done.13, f32[16,256]{1,0:T(8,128)} %bitcast.276, f32[256,256]{1,0:T(8,128)} %copy-done.14, f32[256,1,16,64]{0,3,2,1:T(8,128)S(1)} %bitcast.251, f32[256,16,64]{0,2,1:T(8,128)S(1)} %copy-done.9, f32[256,16]{0,1:T(8,128)S(1)} %bitcast.264), kind=kOutput, calls=%fused_computation.47 | convolution fusion | flops 811073536 | bytes 3719168 | tf_op jit(solution)/shard_map/transpose(jvp())/while/body/eval_jaxpr/checkpoint/ghts,sghp->tghp/dot_general | solution.py:43
  395.7 1.0 copy.278
  (179 shorter events, 36.4 us)
Async XLA Ops:
  7.2 176.4 %reduce-scatter.2.cloned.1.call-start = ((), (), s32[]{:S(2)}) async-start(), calls=%async_computation.1 | async-start | bytes 17301504 | tf_op jit(solution)/shard_map/reduce_scatter | solution.py:151
  7.9 0.8 copy-start.32
  10.9 3.1 copy-start.30
  10.9 49.1 %copy-start.21 = (s32[256]{0:T(256)}, s32[256]{0:T(256)S(1)}, u32[]{:S(2)}) copy-start(s32[256]{0:T(256)S(1)} %get-tuple-element.298) | copy-start | bytes 3076
  14.0 31.3 %copy-start.29 = (f32[16]{0:T(128)}, f32[16]{0:T(128)S(1)}, u32[]{:S(2)}) copy-start(f32[16]{0:T(128)S(1)} %get-tuple-element.419) | copy-start | bytes 196
  14.1 1.7 copy-start.27
  36.7 8.5 %copy-start.20 = (f32[32,1,1,16]{3,2,1,0:T(1,128)}, f32[32,1,1,16]{3,2,1,0:T(1,128)S(1)}, u32[]{:S(2)}) copy-start(f32[32,1,1,16]{3,2,1,0:T(1,128)S(1)} %all-gather) | copy-start | bytes 6148
  58.5 0.7 copy-start.33
  58.5 1.1 copy-start.10
  58.5 1.3 copy-start.11
  58.5 1.6 copy-start.5
  58.5 1.6 copy-start.6
  58.5 243.5 %all-gather.5.cloned.1.call-start = ((), (), s32[]{:S(2)}) async-start(), calls=%async_computation.2 | async-start | bytes 17301504 | tf_op jit(solution)/shard_map/all_gather | solution.py:17
  58.6 129.8 %copy-start.24 = (f32[1,256,1,16]{1,3,2,0:T(8,128)}, f32[1,256,1,16]{1,3,2,0:T(8,128)S(1)}, u32[]{:S(2)}) copy-start(f32[1,256,1,16]{1,3,2,0:T(8,128)S(1)} %copy.248) | copy-start | bytes 49156
  59.1 166.2 %copy-start.15 = (f32[1,256,1,16]{1,3,2,0:T(8,128)}, f32[1,256,1,16]{1,3,2,0:T(8,128)S(1)}, u32[]{:S(2)}) copy-start(f32[1,256,1,16]{1,3,2,0:T(8,128)S(1)} %copy.254) | copy-start | bytes 49156
  59.5 162.8 %copy-start.18 = (f32[1024]{0:T(1024)}, f32[1024]{0:T(1024)S(1)}, u32[]{:S(2)}) copy-start(f32[1024]{0:T(1024)S(1)} %mul.544) | copy-start | bytes 12292
  59.7 128.7 %copy-start.1 = (bf16[256,1024]{0,1:T(8,128)(2,1)}, bf16[256,1024]{0,1:T(8,128)(2,1)S(1)}, u32[]{:S(2)}) copy-start(bf16[256,1024]{0,1:T(8,128)(2,1)S(1)} %copy.255) | copy-start | bytes 1572868
  185.2 3.7 copy-start.3
  185.2 21.7 %copy-start.23 = (f32[1024]{0:T(1024)S(1)}, f32[1024]{0:T(1024)}, u32[]{:S(2)}) copy-start(f32[1024]{0:T(1024)} %param.21) | copy-start | bytes 12292
  188.4 1.0 copy-start.2
  225.3 6.9 %copy-start.4 = (bf16[256,1024]{0,1:T(8,128)(2,1)S(1)}, bf16[256,1024]{0,1:T(8,128)(2,1)}, u32[]{:S(2)}) copy-start(bf16[256,1024]{0,1:T(8,128)(2,1)} %get-tuple-element.412) | copy-start | bytes 1572868
  225.3 7.9 %copy-start = (f32[16,64,128]{2,1,0:T(8,128)S(1)}, f32[16,64,128]{2,1,0:T(8,128)}, u32[]{:S(2)}) copy-start(f32[16,64,128]{2,1,0:T(8,128)} %reduce-scatter.2.cloned.1.call-done) | copy-start | bytes 1572868
  236.4 125.1 %copy-start.7 = (bf16[256,128]{1,0:T(8,128)(2,1)S(1)}, bf16[256,128]{1,0:T(8,128)(2,1)}, u32[]{:S(2)}) copy-start(bf16[256,128]{1,0:T(8,128)(2,1)} %param.16) | copy-start | bytes 196612
  302.1 62.8 %copy-start.17 = (f32[256,16]{0,1:T(8,128)S(1)}, f32[256,16]{0,1:T(8,128)}, u32[]{:S(2)}) copy-start(f32[256,16]{0,1:T(8,128)} %param.15) | copy-start | bytes 49156
  302.1 62.8 %copy-start.28 = (f32[256]{0:T(256)S(1)}, f32[256]{0:T(256)}, u32[]{:S(2)}) copy-start(f32[256]{0:T(256)} %copy-done.27) | copy-start | bytes 3076
  302.1 62.8 %copy-start.31 = (f32[16]{0:T(128)S(1)}, f32[16]{0:T(128)}, u32[]{:S(2)}) copy-start(f32[16]{0:T(128)} %param.18) | copy-start | bytes 196
  302.1 62.9 %copy-start.22 = (s32[256]{0:T(256)S(1)}, s32[256]{0:T(256)}, u32[]{:S(2)}) copy-start(s32[256]{0:T(256)} %copy-done.21) | copy-start | bytes 3076
  361.4 4.1 %copy-start.8 = (f32[256,1,16,64]{0,3,2,1:T(8,128)S(1)}, f32[256,1,16,64]{0,3,2,1:T(8,128)}, u32[]{:S(2)}) copy-start(f32[256,1,16,64]{0,3,2,1:T(8,128)} %convert.11) | copy-start | bytes 3145732
  361.4 4.1 %copy-start.25 = (f32[1,256,1,16]{1,3,2,0:T(8,128)S(1)}, f32[1,256,1,16]{1,3,2,0:T(8,128)}, u32[]{:S(2)}) copy-start(f32[1,256,1,16]{1,3,2,0:T(8,128)} %copy-done.24) | copy-start | bytes 49156
  363.0 2.5 copy-start.16
  365.0 8.9 %copy-start.26 = (f32[256,1,16]{0,2,1:T(8,128)}, f32[256,1,16]{0,2,1:T(8,128)S(1)}, u32[]{:S(2)}) copy-start(f32[256,1,16]{0,2,1:T(8,128)S(1)} %get-tuple-element.299) | copy-start | bytes 49156
  365.1 8.8 %copy-start.13 = (f32[256,256]{1,0:T(8,128)}, f32[256,256]{1,0:T(8,128)S(1)}, u32[]{:S(2)}) copy-start(f32[256,256]{1,0:T(8,128)S(1)} %fusion.81) | copy-start | bytes 786436
  365.5 8.4 %copy-start.14 = (f32[256,256]{1,0:T(8,128)}, f32[256,256]{1,0:T(8,128)S(1)}, u32[]{:S(2)}) copy-start(f32[256,256]{1,0:T(8,128)S(1)} %fusion.85) | copy-start | bytes 786436
  365.6 9.4 %copy-start.12 = (f32[1,256,1,16]{3,2,1,0:T(1,128)S(1)}, f32[1,256,1,16]{3,2,1,0:T(1,128)}, u32[]{:S(2)}) copy-start(f32[1,256,1,16]{3,2,1,0:T(1,128)} %copy.259) | copy-start | bytes 49156
  375.0 15.7 %copy-start.9 = (f32[256,16,64]{0,2,1:T(8,128)S(1)}, f32[256,16,64]{0,2,1:T(8,128)}, u32[]{:S(2)}) copy-start(f32[256,16,64]{0,2,1:T(8,128)} %get-tuple-element.426) | copy-start | bytes 3145732
  388.0 7.5 %copy-start.19 = (f32[1024]{0:T(1024)S(1)}, f32[1024]{0:T(1024)}, u32[]{:S(2)}) copy-start(f32[1024]{0:T(1024)} %copy-done.18) | copy-start | bytes 12292
Sparse Core Ops, SparseCore 0:
  58.6 124.8 reduce-scatter.1
  226.9 75.1 all-gather.4
where the time goes:
time: 408 us; the launch traced here: 404 us
  waiting for transfers between devices  189 us (46%)
  other arithmetic  72.1 us (18%)
  blocking collectives  53.5 us (13%)
  local copies, waits for them, and re-layouts  40.9 us (10%)
  matrix products  31.2 us (8%)
  between operations  15.9 us (4%)
    reduce_scatter x1, waiting for transfers between devices, body(): lax.psum_scatter(weight[:, None, None] * jnp.take(flat_end, head_ids, axi...  123 us
    all_gather x1, waiting for transfers between devices, carried_in(): everything = jax.tree.map(lambda part: lax.all_gather(part, axis), array)  65.7 us
    select_n x32, other arithmetic, turn(): return jax.tree.map(lambda a, b: jnp.where(reached, a, b), new, before)  37.4 us
    mul x32, local copies, waits for them, and re-layouts, compose(): decay_late[..., None, None] * sum_early + sum_late  21.1 us
    all_gather x1, blocking collectives, body(): decay_table = lax.all_gather(through_all, 'ctx', axis=0, tiled=True)  20.9 us
    psum x1, blocking collectives, body(): squares = lax.psum(jnp.sum(gated * gated, axis=1), 'head')  17.4 us
    dot_general x3, matrix products, span_mix(): jnp.einsum('ghts,sghp->tghp', weights, x_span, precision=HIGHEST_PRECISION)  16.4 us
    psum x1, blocking collectives, body(): product = lax.psum(jnp.sum(weighted_grad * normed, axis=1), 'head')  15.2 us
  transfers between devices with their start and end apart: 2, of which 2 were waited for; matrix products, arithmetic and copies ran while one was open for 3% of the time, Pallas kernels for 0%

commit v1 on v0

--- a/solution.py
+++ b/solution.py
@@ -12,22 +12,24 @@
 EPSILON = 1e-05
 
 
-def carried_in(array, axis, combine, identity):
-    size, index = (lax.axis_size(axis), lax.axis_index(axis))
-    everything = jax.tree.map(lambda part: lax.all_gather(part, axis), array)
-    start = jax.tree.map(
-        lambda part, zero: jnp.broadcast_to(jnp.asarray(zero, part.dtype), part.shape),
-        array,
-        identity,
-    )
-
-    def turn(k, before):
-        at = size - 1 - k
-        reached = at > index
-        new = combine(before, jax.tree.map(lambda part: part[at], everything))
-        return jax.tree.map(lambda a, b: jnp.where(reached, a, b), new, before)
-
-    return lax.fori_loop(0, size, turn, start)
+def exclusive_scan(gain, value, axis, forward):
+    size = lax.axis_size(axis)
+    total = jnp.zeros_like(value)
+    total_gain = jnp.ones_like(gain)
+    distance = 1
+    while distance < size:
+        if forward:
+            pairs = [(i, i + distance) for i in range(size - distance)]
+        else:
+            pairs = [(i + distance, i) for i in range(size - distance)]
+        gain_in, value_in = lax.ppermute((gain, value), axis, pairs)
+        total = total + total_gain[..., None, None] * value_in
+        distance *= 2
+        if distance < size:
+            total_gain = total_gain * gain_in
+            value = value + gain[..., None, None] * value_in
+            gain = gain * gain_in
+    return total
 
 
 def span_mix(x_span, dt_span, b_span, c_span, log_cum, segment):
@@ -95,12 +97,6 @@
     mix_block = jax.checkpoint(lambda pieces: span_mix(*pieces))
     inner_part = lax.map(mix_block, (x_spans, dt_spans, b_spans, c_spans, log_cum, segment))
     return inner_part + carried
-
-
-def compose(earlier, later):
-    decay_early, sum_early = earlier
-    decay_late, sum_late = later
-    return (decay_early * decay_late, decay_late[..., None, None] * sum_early + sum_late)
 
 
 def body(
@@ -136,24 +132,7 @@
         return local_states(x_value, dt_value, b_value, segment, decay_rate)
 
     (starts, end_local, through_all), states_back = jax.vjp(states_call, x_spans, dt_spans, b_spans)
-    identity = (jnp.ones_like(through_all), jnp.zeros_like(end_local))
-    decay_table = lax.all_gather(through_all, "ctx", axis=0, tiled=True)
-    own_index = lax.axis_index("ctx")
-    ctx_count = lax.axis_size("ctx")
-    flat_end = end_local.reshape(heads_here, HEAD_DIM, STATE)
-    row_ids = jnp.arange(lax.axis_size("ctx") * heads_here, dtype=jnp.int32)
-    receiver = row_ids // heads_here
-    head_ids = row_ids % heads_here
-    devices = jnp.arange(ctx_count, dtype=jnp.int32)
-    between = (devices[None, :] > own_index) & (devices[None, :] < receiver[:, None])
-    factors = jnp.where(between, decay_table[:, head_ids].T, 1.0)
-    weight = jnp.prod(factors, axis=1) * (own_index < receiver).astype(jnp.float32)
-    entry_state = lax.psum_scatter(
-        weight[:, None, None] * jnp.take(flat_end, head_ids, axis=0),
-        "ctx",
-        scatter_dimension=0,
-        tiled=True,
-    ).reshape(end_local.shape)
+    entry_state = exclusive_scan(through_all, end_local, "ctx", True)
 
     def output_call(x_value, dt_value, b_value, c_value, start_value, entry_value):
         return output_part(
@@ -170,15 +149,18 @@
     gated = core_out * gate_act
     weighted_grad = norm_weight[None, :] * grad_output.astype(jnp.float32)
     norm_width = lax.axis_size("head") * gated.shape[1]
-    squares = lax.psum(jnp.sum(gated * gated, axis=1), "head")
-    inv_rms = lax.rsqrt(squares / norm_width + EPSILON)
+    sums = lax.psum(
+        jnp.stack([jnp.sum(gated * gated, axis=1), jnp.sum(weighted_grad * gated, axis=1)]),
+        "head",
+    )
+    inv_rms = lax.rsqrt(sums[0] / norm_width + EPSILON)
     normed = gated * inv_rms[:, None]
-    product = lax.psum(jnp.sum(weighted_grad * normed, axis=1), "head")
+    product = sums[1] * inv_rms
     grad_gated = inv_rms[:, None] * (weighted_grad - normed * (product / norm_width)[:, None])
     grad_core = grad_gated * gate_act
     grad_gate = grad_gated * core_out * gate_sig * (1.0 + gate_float * (1.0 - gate_sig))
     first_grads = output_back(grad_core.reshape(core_part.shape))
-    _, exit_adjoint = carried_in((through_all, first_grads[5]), "ctx", compose, identity)
+    exit_adjoint = exclusive_scan(through_all, first_grads[5], "ctx", False)
     through_grad = jnp.sum(exit_adjoint * entry_state, axis=(2, 3))
     second_grads = states_back((first_grads[4], exit_adjoint, through_grad))
     grad_input = (first_grads[0] + second_grads[0]).reshape(

time: 408 us -> 212 us (0.52)
  waiting for transfers between devices: 189 us -> 75.1 us
  starting transfers between devices: 0.08 us -> 53.7 us
  other arithmetic: 72.1 us -> 23.1 us
  blocking collectives: 53.5 us -> 20 us
  local copies, waits for them, and re-layouts: 40.9 us -> 8.88 us
  between operations: 15.9 us -> 2.92 us
  matrix products: 31.2 us -> 26.9 us
    reduce_scatter x1 -> x0, waiting for transfers between devices: 123 us -> none  [body(): lax.psum_scatter(weight[:, None, None] * jnp.take(flat_end, head_ids, axi...]
    ppermute x0 -> x18, waiting for transfers between devices: none -> 75.1 us  [exclusive_scan(): gain_in, value_in = lax.ppermute((gain, value), axis, pairs)]
    all_gather x1 -> x0, waiting for transfers between devices: 65.7 us -> none  [carried_in(): everything = jax.tree.map(lambda part: lax.all_gather(part, axis), array)]
    ppermute x0 -> x18, starting transfers between devices: none -> 53.7 us  [exclusive_scan(): gain_in, value_in = lax.ppermute((gain, value), axis, pairs)]
    select_n x34 -> x0, other arithmetic: 37.4 us -> none  [the longest x32 37.4 us: turn(): return jax.tree.map(lambda a, b: jnp.where(reached, a, b), new, before)]
    mul x35 -> x1, local copies, waits for them, and re-layouts: 21.4 us -> 0.09 us  [block_decays(): jnp.exp(log_cum[:, -1]) * (closing == 0).astype(jnp.float32)[:, None, None]]
    all_gather x1 -> x0, blocking collectives: 20.9 us -> none  [body(): decay_table = lax.all_gather(through_all, 'ctx', axis=0, tiled=True)]
    psum x2 -> x1, blocking collectives: 32.6 us -> 20 us  [body(): lax.psum(jnp.stack([jnp.sum(gated * gated, axis=1), jnp.sum(weighted_grad...]
  transfers between devices with their start and end apart: 2 -> 18, of which waited for: 2 -> 14; matrix products, arithmetic and copies ran while one was open for 3% -> 8% of each run, Pallas kernels for 0% -> 0%
where the time goes in v1:
time: 212 us; the launch traced here: 211 us
  waiting for transfers between devices  75.1 us (35%)
  starting transfers between devices  53.7 us (25%)
  matrix products  26.9 us (13%)
  other arithmetic  23.1 us (11%)
  blocking collectives  20 us (9%)
  local copies, waits for them, and re-layouts  8.88 us (4%)
  between operations  2.92 us (1%)
    ppermute x18, waiting for transfers between devices, exclusive_scan(): gain_in, value_in = lax.ppermute((gain, value), axis, pairs)  75.1 us
    ppermute x18, starting transfers between devices, exclusive_scan(): gain_in, value_in = lax.ppermute((gain, value), axis, pairs)  53.7 us
    psum x1, blocking collectives, body(): lax.psum(jnp.stack([jnp.sum(gated * gated, axis=1), jnp.sum(weighted_grad...  20 us
    dot_general x3, matrix products, span_mix(): jnp.einsum('ghts,sghp->tghp', weights, x_span, precision=HIGHEST_PRECISION)  15.4 us
    another operation x10, other arithmetic  7.91 us
    unnamed x113, local copies, waits for them, and re-layouts  6.2 us
    dot_general x3, matrix products, local_states(): jnp.einsum('kqgh,kqghp,kqgn->kghpn', tail_decay * dt_spans, x_spans, b_sp...  4.68 us
  transfers between devices with their start and end apart: 18, of which 14 were waited for; matrix products, arithmetic and copies ran while one was open for 8% of the time, Pallas kernels for 0%

profile of v1, /device:TPU:6, one launch (start us, length us, event | category | flops | bytes accessed | tf_op | source)
XLA Modules:
  0.0 210.6 jit_solution(7453100632198190240)
XLA Ops:
  0.6 0.7 exponential_negate_fusion
  1.3 0.8 fusion.109
  2.9 1.0 reduce-window.30
  7.2 0.8 multiply_reduce_fusion.5
  8.0 0.8 fusion.93
  8.8 1.2 copy.79
  10.1 0.7 fusion.40
  10.8 1.9 collective-permute-start
  12.7 8.6 %collective-permute-done = f32[1,16,64,128]{3,2,1,0:T(8,128)S(1)} collective-permute-done((f32[1,16,64,128]{3,2,1,0:T(8,128)S(1)}, f32[1,16,64,128]{3,2,1,0:T(8,128)S(1)}, u32[]{:S(2)}, u32[]{:S(2)}) %collective-permute-start) | collective-permute-done | bytes 524320 | tf_op jit(solution)/shard_map/ppermute | solution.py:25
  21.4 5.5 %collective-permute-start.2 = (f32[1,16,64,128]{3,2,1,0:T(8,128)S(1)}, f32[1,16,64,128]{3,2,1,0:T(8,128)S(1)}, u32[]{:S(2)}, u32[]{:S(2)}) collective-permute-start(f32[1,16,64,128]{3,2,1,0:T(8,128)S(1)} %multiply_add_fusion.11), channel_id=1, source_target_pairs={{0,16},{8,24},{16,32},{24,40},{32,48},{40,56},{48,64},{56,72},{64,... | collective-permute-start | bytes 1572872 | tf_op jit(solution)/shard_map/ppermute | solution.py:25
  26.9 1.9 collective-permute-start.10
  28.9 2.4 %collective-permute-start.1 = (f32[1,16]{1,0:T(1,128)S(1)}, f32[1,16]{1,0:T(1,128)S(1)}, u32[]{:S(2)}, u32[]{:S(2)}) collective-permute-start(f32[1,16]{1,0:T(1,128)S(1)} %bitcast.326), channel_id=1, source_target_pairs={{0,8},{8,16},{16,24},{24,32},{32,40},{40,48},{48,56},{56,64},{64,7... | collective-permute-start | bytes 200 | tf_op jit(solution)/shard_map/ppermute | solution.py:25
  31.3 3.1 %collective-permute-done.1 = f32[1,16]{1,0:T(1,128)S(1)} collective-permute-done((f32[1,16]{1,0:T(1,128)S(1)}, f32[1,16]{1,0:T(1,128)S(1)}, u32[]{:S(2)}, u32[]{:S(2)}) %collective-permute-start.1) | collective-permute-done | bytes 96 | tf_op jit(solution)/shard_map/ppermute | solution.py:25
  34.4 1.8 collective-permute-done.2
  36.4 4.3 %collective-permute-start.4 = (f32[1,16,64,128]{3,2,1,0:T(8,128)S(1)}, f32[1,16,64,128]{3,2,1,0:T(8,128)S(1)}, u32[]{:S(2)}, u32[]{:S(2)}) collective-permute-start(f32[1,16,64,128]{3,2,1,0:T(8,128)S(1)} %multiply_add_fusion.10), channel_id=1, source_target_pairs={{0,32},{8,40},{16,48},{24,56},{32,64},{40,72},{48,80},{56,88},{64,... | collective-permute-start | bytes 1572872 | tf_op jit(solution)/shard_map/ppermute | solution.py:25
  40.7 3.7 %collective-permute-start.3 = (f32[1,16]{1,0:T(1,128)S(1)}, f32[1,16]{1,0:T(1,128)S(1)}, u32[]{:S(2)}, u32[]{:S(2)}) collective-permute-start(f32[1,16]{1,0:T(1,128)S(1)} %get-tuple-element.225), channel_id=1, source_target_pairs={{0,16},{8,24},{16,32},{24,40},{32,48},{40,56},{48,64},{56,72},{64,... | collective-permute-start | bytes 200 | tf_op jit(solution)/shard_map/ppermute | solution.py:25
  44.5 6.3 %collective-permute-done.3 = f32[1,16]{1,0:T(1,128)S(1)} collective-permute-done((f32[1,16]{1,0:T(1,128)S(1)}, f32[1,16]{1,0:T(1,128)S(1)}, u32[]{:S(2)}, u32[]{:S(2)}) %collective-permute-start.3) | collective-permute-done | bytes 96 | tf_op jit(solution)/shard_map/ppermute | solution.py:25
  50.7 1.2 collective-permute-done.4
  52.0 3.6 %collective-permute-start.6 = (f32[1,16,64,128]{3,2,1,0:T(8,128)S(1)}, f32[1,16,64,128]{3,2,1,0:T(8,128)S(1)}, u32[]{:S(2)}, u32[]{:S(2)}) collective-permute-start(f32[1,16,64,128]{3,2,1,0:T(8,128)S(1)} %multiply_add_fusion.9), channel_id=1, source_target_pairs={{0,64},{8,72},{16,80},{24,88},{32,96},{40,104},{48,112},{56,120},{... | collective-permute-start | bytes 1572872 | tf_op jit(solution)/shard_map/ppermute | solution.py:25
  55.7 4.6 %collective-permute-start.5 = (f32[1,16]{1,0:T(1,128)S(1)}, f32[1,16]{1,0:T(1,128)S(1)}, u32[]{:S(2)}, u32[]{:S(2)}) collective-permute-start(f32[1,16]{1,0:T(1,128)S(1)} %mul.703), channel_id=1, source_target_pairs={{0,32},{8,40},{16,48},{24,56},{32,64},{40,72},{48,80},{56,88},{64,... | collective-permute-start | bytes 200 | tf_op jit(solution)/shard_map/ppermute | solution.py:25
  60.3 2.4 %collective-permute-done.5 = f32[1,16]{1,0:T(1,128)S(1)} collective-permute-done((f32[1,16]{1,0:T(1,128)S(1)}, f32[1,16]{1,0:T(1,128)S(1)}, u32[]{:S(2)}, u32[]{:S(2)}) %collective-permute-start.5) | collective-permute-done | bytes 96 | tf_op jit(solution)/shard_map/ppermute | solution.py:25
  62.7 1.7 collective-permute-done.6
  64.4 1.0 multiply_add_fusion.8
  65.4 6.0 %collective-permute-start.8 = (f32[1,16,64,128]{3,2,1,0:T(8,128)}, f32[1,16,64,128]{3,2,1,0:T(8,128)}, u32[]{:S(2)}, u32[]{:S(2)}) collective-permute-start(f32[1,16,64,128]{3,2,1,0:T(8,128)} %multiply_add_fusion.8), channel_id=1, source_target_pairs={{0,128},{8,136},{16,144},{24,152},{32,160},{40,168},{48,176},{56,1... | collective-permute-start | bytes 1572872 | tf_op jit(solution)/shard_map/ppermute | solution.py:25
  71.4 0.8 fusion.75
  72.6 0.9 fusion.112
  73.5 1.6 collective-permute-start.7
  75.3 3.2 %collective-permute-done.7 = f32[1,16]{1,0:T(1,128)S(1)} collective-permute-done((f32[1,16]{1,0:T(1,128)S(1)}, f32[1,16]{1,0:T(1,128)S(1)}, u32[]{:S(2)}, u32[]{:S(2)}) %collective-permute-start.7) | collective-permute-done | bytes 96 | tf_op jit(solution)/shard_map/ppermute | solution.py:25
  78.6 1.6 multiply_add_fusion.7
  80.8 1.0 copy-done.1
  81.7 3.2 %multiply_add_fusion.1 = f32[1,256,1,16,64]{1,4,3,2,0:T(8,128)S(1)} fusion(f32[1,256,1,16,64]{1,4,3,2,0:T(8,128)S(1)} %convolution_bitcast_fusion.1, f32[256,16]{0,1:T(8,128)S(1)} %get-tuple-element.203, bf16[256,16,64]{0,2,1:T(8,128)(2,1)S(1)} %bitcast.296, f32[16,256]{1,0:T(8,128)S(1)} %get-tuple-element.213, f32[256,256]{1,0:T(8,128)S(1)} %copy-done.28, ...), kind=kOutput, calls=%fused_computation.75 | convolution fusion | flops 811073536 | bytes 3194880 | tf_op jit(solution)/shard_map/jvp()/while/body/eval_jaxpr/ghts,sghp->tghp/dot_general | solution.py:45
  85.0 1.6 multiply_reduce_fusion.2
  86.6 20.0 %psum.7 = f32[2,256]{1,0:T(2,128)S(1)} all-reduce(f32[2,256]{1,0:T(2,128)S(1)} %pad_maximum_fusion), channel_id=1, replica_groups=mesh['ctx'=32,'head'=8] {'head'}, use_global_device_ids=true, to_apply=%region_6.7 | all-reduce | flops 512 | bytes 4096 | tf_op jit(solution)/shard_map/psum | solution.py:152
  106.6 3.1 %fusion.51 = (bf16[256,1024]{0,1:T(8,128)(2,1)}, f32[256,1024]{0,1:T(8,128)S(1)}) fusion(bf16[256,1024]{0,1:T(8,128)(2,1)S(1)} %copy.85, f32[1024]{0:T(1024)S(1)} %mul.725, bf16[256,1024]{0,1:T(8,128)(2,1)S(1)} %copy.79, f32[1,256,1,16,64]{1,4,3,2,0:T(8,128)} %copy-done, f32[256]{0:T(256)S(1)} %multiply_multiply_fusion, f32[256,1024]{0,1:T(8,128)} %get-tuple-element.202, ...), kind=kLoop, calls=%fused_computation.59 | loop fusion | flops 5767168 | bytes 5253120 | tf_op jit(solution)/shard_map/convert_element_type | solution.py:176
  109.8 0.6 convolution_bitcast_fusion.2
  110.4 1.9 collective-permute-start.9
  112.3 2.7 %collective-permute-start.12 = (f32[1,16]{1,0:T(1,128)S(1)}, f32[1,16]{1,0:T(1,128)S(1)}, u32[]{:S(2)}, u32[]{:S(2)}) collective-permute-start(f32[1,16]{1,0:T(1,128)S(1)} %get-tuple-element.224), channel_id=1, source_target_pairs={{16,0},{24,8},{32,16},{40,24},{48,32},{56,40},{64,48},{72,56},{80,... | collective-permute-start | bytes 200 | tf_op jit(solution)/shard_map/ppermute | solution.py:25
  115.1 4.0 %collective-permute-done.9 = f32[1,16,64,128]{3,2,1,0:T(8,128)S(1)} collective-permute-done((f32[1,16,64,128]{3,2,1,0:T(8,128)S(1)}, f32[1,16,64,128]{3,2,1,0:T(8,128)S(1)}, u32[]{:S(2)}, u32[]{:S(2)}) %collective-permute-start.9) | collective-permute-done | bytes 524320 | tf_op jit(solution)/shard_map/ppermute | solution.py:25
  119.1 2.7 %collective-permute-start.11 = (f32[1,16,64,128]{3,2,1,0:T(8,128)S(1)}, f32[1,16,64,128]{3,2,1,0:T(8,128)S(1)}, u32[]{:S(2)}, u32[]{:S(2)}) collective-permute-start(f32[1,16,64,128]{3,2,1,0:T(8,128)S(1)} %multiply_add_fusion.6), channel_id=1, source_target_pairs={{16,0},{24,8},{32,16},{40,24},{48,32},{56,40},{64,48},{72,56},{80,... | collective-permute-start | bytes 1572872 | tf_op jit(solution)/shard_map/ppermute | solution.py:25
  121.9 2.7 %collective-permute-start.14 = (f32[1,16]{1,0:T(1,128)S(1)}, f32[1,16]{1,0:T(1,128)S(1)}, u32[]{:S(2)}, u32[]{:S(2)}) collective-permute-start(f32[1,16]{1,0:T(1,128)S(1)} %mul.761), channel_id=1, source_target_pairs={{32,0},{40,8},{48,16},{56,24},{64,32},{72,40},{80,48},{88,56},{96,... | collective-permute-start | bytes 200 | tf_op jit(solution)/shard_map/ppermute | solution.py:25
  124.6 11.3 %collective-permute-done.14 = f32[1,16]{1,0:T(1,128)S(1)} collective-permute-done((f32[1,16]{1,0:T(1,128)S(1)}, f32[1,16]{1,0:T(1,128)S(1)}, u32[]{:S(2)}, u32[]{:S(2)}) %collective-permute-start.14) | collective-permute-done | bytes 96 | tf_op jit(solution)/shard_map/ppermute | solution.py:25
  135.9 1.3 collective-permute-start.16
  137.3 4.0 %collective-permute-done.16 = f32[1,16]{1,0:T(1,128)S(1)} collective-permute-done((f32[1,16]{1,0:T(1,128)S(1)}, f32[1,16]{1,0:T(1,128)S(1)}, u32[]{:S(2)}, u32[]{:S(2)}) %collective-permute-start.16) | collective-permute-done | bytes 96 | tf_op jit(solution)/shard_map/ppermute | solution.py:25
  141.5 0.7 copy-done.10
  142.2 3.9 %collective-permute-start.13 = (f32[1,16,64,128]{3,2,1,0:T(8,128)S(1)}, f32[1,16,64,128]{3,2,1,0:T(8,128)S(1)}, u32[]{:S(2)}, u32[]{:S(2)}) collective-permute-start(f32[1,16,64,128]{3,2,1,0:T(8,128)S(1)} %multiply_add_fusion.5), channel_id=1, source_target_pairs={{32,0},{40,8},{48,16},{56,24},{64,32},{72,40},{80,48},{88,56},{96,... | collective-permute-start | bytes 1572872 | tf_op jit(solution)/shard_map/ppermute | solution.py:25
  146.9 13.5 %collective-permute-done.13 = f32[1,16,64,128]{3,2,1,0:T(8,128)S(1)} collective-permute-done((f32[1,16,64,128]{3,2,1,0:T(8,128)S(1)}, f32[1,16,64,128]{3,2,1,0:T(8,128)S(1)}, u32[]{:S(2)}, u32[]{:S(2)}) %collective-permute-start.13) | collective-permute-done | bytes 524320 | tf_op jit(solution)/shard_map/ppermute | solution.py:25
  160.5 0.7 copy-done.12
  161.1 1.5 collective-permute-start.15
  162.6 8.4 %fusion.72 = (f32[16,256]{1,0:T(8,128)}, f32[16,256]{1,0:T(8,128)}, f32[16,256]{1,0:T(8,128)}, f32[256,256]{1,0:T(8,128)S(1)}) fusion(f32[16,256]{1,0:T(8,128)S(1)} %bitcast.301, f32[256,256]{1,0:T(8,128)S(1)} %fusion.76, f32[16,256]{1,0:T(8,128)S(1)} %bitcast.309, f32[256,256]{1,0:T(8,128)S(1)} %fusion.79, f32[256,1,16,64]{0,3,2,1:T(8,128)S(1)} %convert.9, ...), kind=kOutput, calls=%fused_computation.101 | convolution fusion | flops 825151488 | bytes 2965504 | tf_op jit(solution)/shard_map/transpose(jvp())/while/body/eval_jaxpr/checkpoint/ghts,sghp->tghp/dot_general | solution.py:45
  171.0 5.0 %collective-permute-done.15 = f32[1,16,64,128]{3,2,1,0:T(8,128)S(1)} collective-permute-done((f32[1,16,64,128]{3,2,1,0:T(8,128)S(1)}, f32[1,16,64,128]{3,2,1,0:T(8,128)S(1)}, u32[]{:S(2)}, u32[]{:S(2)}) %collective-permute-start.15) | collective-permute-done | bytes 524320 | tf_op jit(solution)/shard_map/ppermute | solution.py:25
  176.0 0.9 multiply_add_fusion.3
  176.9 1.3 collective-permute-start.17
  178.8 1.0 copy.99
  179.8 1.3 fusion.77
  181.2 2.5 %fusion.42 = f32[256,128]{1,0:T(8,128)} fusion(f32[256,128]{1,0:T(8,128)S(1)} %fusion.77, f32[1,256,1,16,64]{1,4,3,2,0:T(8,128)S(1)} %bitcast.293, f32[1,16,64,128]{3,2,1,0:T(8,128)S(1)} %multiply_add_fusion.7, f32[256,16]{0,1:T(8,128)S(1)} %copy-done.30), kind=kOutput, calls=%fused_computation.50 | convolution fusion | flops 402948096 | bytes 1851392 | tf_op jit(solution)/shard_map/transpose(jvp(kqgn,kghpn->kqghp))/dot_general | solution.py:94
  183.7 9.0 %collective-permute-done.17 = f32[1,16,64,128]{3,2,1,0:T(8,128)} collective-permute-done((f32[1,16,64,128]{3,2,1,0:T(8,128)}, f32[1,16,64,128]{3,2,1,0:T(8,128)}, u32[]{:S(2)}, u32[]{:S(2)}) %collective-permute-start.17) | collective-permute-done | bytes 524320 | tf_op jit(solution)/shard_map/ppermute | solution.py:25
  192.7 1.5 multiply_reduce_fusion.3
  194.5 1.6 fusion.45
  196.5 2.7 %reduce-window.36 = f32[1,16,1,2,128]{4,1,2,3,0:T(8,128)S(1)} reduce-window(f32[1,16,1,2,128]{4,1,2,3,0:T(8,128)S(1)} %copy_bitcast_fusion, f32[]{:T(128)} %constant.120.clone.1), window={size=1x1x1x1x128 pad=0_0x0_0x0_0x0_0x0_127}, to_apply=%region_16.17 | reduce-window | flops 520192 | bytes 32772 | tf_op jit(solution)/shard_map/reduce-window.6
  199.3 2.5 %reduce-window.34 = f32[1,16,1,2,128]{4,1,2,3,0:T(8,128)S(1)} reduce-window(f32[1,16,1,2,128]{4,1,2,3,0:T(8,128)S(1)} %bitcast.307, f32[]{:T(128)} %constant.120.clone.1), window={size=1x1x1x1x128 pad=0_0x0_0x0_0x0_0x0_127}, to_apply=%region_11.12 | reduce-window | flops 520192 | bytes 32772 | tf_op jit(solution)/shard_map/reduce-window.4
  201.9 2.5 %fusion.44 = f32[256,128]{1,0:T(8,128)} fusion(f32[1,256,1,128]{3,1,2,0:T(8,128)S(1)} %convolution_bitcast_fusion.3, bf16[256,16,64]{0,2,1:T(8,128)(2,1)S(1)} %bitcast.298, f32[1,16,64,128]{3,2,1,0:T(8,128)S(1)} %get-tuple-element.201, f32[256,16]{0,1:T(8,128)S(1)} %copy-done.32), kind=kOutput, calls=%fused_computation.52 | convolution fusion | flops 403210240 | bytes 1327104 | tf_op jit(solution)/shard_map/transpose(jvp(kqgh,kqghp,kqgn->kghpn))/dot_general | solution.py:59
  204.4 3.8 %multiply_add_fusion = f32[256,16,64]{0,2,1:T(8,128)S(1)} fusion(f32[256,16,64]{0,2,1:T(8,128)S(1)} %copy-done.18, f32[256,16]{0,1:T(8,128)S(1)} %copy-done.32, f32[16,256]{1,0:T(8,128)S(1)} %bitcast.310, f32[256,256]{1,0:T(8,128)S(1)} %copy-done.25, f32[16,256]{1,0:T(8,128)S(1)} %bitcast.303, f32[256,256]{1,0:T(8,128)S(1)} %copy-done.27, ...), kind=kOutput, calls=%fused_computation.70 | convolution fusion | flops 811073536 | bytes 3719168 | tf_op jit(solution)/shard_map/transpose(jvp())/while/body/eval_jaxpr/checkpoint/ghts,sghp->tghp/dot_general | solution.py:45
  208.4 1.0 copy.98
  209.9 0.7 fusion.91
  (178 shorter events, 7.5 us)
Async XLA Ops:
  0.6 9.4 %copy-start.17 = (bf16[256,128]{1,0:T(8,128)(2,1)S(1)}, bf16[256,128]{1,0:T(8,128)(2,1)}, u32[]{:S(2)}) copy-start(bf16[256,128]{1,0:T(8,128)(2,1)} %param.14) | copy-start | bytes 196612
  2.2 160.5 %copy-start.42 = (f32[256,1,16]{0,2,1:T(8,128)}, f32[256,1,16]{0,2,1:T(8,128)S(1)}, u32[]{:S(2)}) copy-start(f32[256,1,16]{0,2,1:T(8,128)S(1)} %get-tuple-element.122) | copy-start | bytes 49156
  4.9 5.8 %copy-start.46 = (f32[256]{0:T(256)}, f32[256]{0:T(256)S(1)}, u32[]{:S(2)}) copy-start(f32[256]{0:T(256)S(1)} %get-tuple-element.205) | copy-start | bytes 3076
  7.2 102.6 %copy-start.29 = (f32[256,16]{0,1:T(8,128)}, f32[256,16]{0,1:T(8,128)S(1)}, u32[]{:S(2)}) copy-start(f32[256,16]{0,1:T(8,128)S(1)} %get-tuple-element.203) | copy-start | bytes 49156
  8.0 2.8 %copy-start.44 = (f32[16]{0:T(128)}, f32[16]{0:T(128)S(1)}, u32[]{:S(2)}) copy-start(f32[16]{0:T(128)S(1)} %get-tuple-element.188) | copy-start | bytes 196
  8.0 2.8 %copy-start.37 = (f32[256]{0:T(256)}, f32[256]{0:T(256)S(1)}, u32[]{:S(2)}) copy-start(f32[256]{0:T(256)S(1)} %compare_convert_fusion.1) | copy-start | bytes 3076
  8.8 2.0 copy-start.31
  10.8 10.5 %collective-permute-start = (f32[1,16,64,128]{3,2,1,0:T(8,128)S(1)}, f32[1,16,64,128]{3,2,1,0:T(8,128)S(1)}, u32[]{:S(2)}, u32[]{:S(2)}) collective-permute-start(f32[1,16,64,128]{3,2,1,0:T(8,128)S(1)} %fusion.40), channel_id=1, source_target_pairs={{0,8},{8,16},{16,24},{24,32},{32,40},{40,48},{48,56},{56,64},{64,7... | collective-permute-start | bytes 1572872 | tf_op jit(solution)/shard_map/ppermute | solution.py:25
  21.3 15.1 %copy-start.4 = (f32[1,16,64,128]{3,2,1,0:T(8,128)}, f32[1,16,64,128]{3,2,1,0:T(8,128)S(1)}, u32[]{:S(2)}) copy-start(f32[1,16,64,128]{3,2,1,0:T(8,128)S(1)} %collective-permute-done) | copy-start | bytes 1572868
  21.4 14.9 %collective-permute-start.2 = (f32[1,16,64,128]{3,2,1,0:T(8,128)S(1)}, f32[1,16,64,128]{3,2,1,0:T(8,128)S(1)}, u32[]{:S(2)}, u32[]{:S(2)}) collective-permute-start(f32[1,16,64,128]{3,2,1,0:T(8,128)S(1)} %multiply_add_fusion.11), channel_id=1, source_target_pairs={{0,16},{8,24},{16,32},{24,40},{32,48},{40,56},{48,64},{56,72},{64,... | collective-permute-start | bytes 1572872 | tf_op jit(solution)/shard_map/ppermute | solution.py:25
  26.9 4.3 %collective-permute-start.10 = (f32[1,16]{1,0:T(1,128)S(1)}, f32[1,16]{1,0:T(1,128)S(1)}, u32[]{:S(2)}, u32[]{:S(2)}) collective-permute-start(f32[1,16]{1,0:T(1,128)S(1)} %bitcast.325), channel_id=1, source_target_pairs={{8,0},{16,8},{24,16},{32,24},{40,32},{48,40},{56,48},{64,56},{72,6... | collective-permute-start | bytes 200 | tf_op jit(solution)/shard_map/ppermute | solution.py:25
  28.9 5.6 %collective-permute-start.1 = (f32[1,16]{1,0:T(1,128)S(1)}, f32[1,16]{1,0:T(1,128)S(1)}, u32[]{:S(2)}, u32[]{:S(2)}) collective-permute-start(f32[1,16]{1,0:T(1,128)S(1)} %bitcast.326), channel_id=1, source_target_pairs={{0,8},{8,16},{16,24},{24,32},{32,40},{40,48},{48,56},{56,64},{64,7... | collective-permute-start | bytes 200 | tf_op jit(solution)/shard_map/ppermute | solution.py:25
  31.3 110.1 %copy-start.49 = (f32[1,16]{1,0:T(1,128)}, f32[1,16]{1,0:T(1,128)S(1)}, u32[]{:S(2)}) copy-start(f32[1,16]{1,0:T(1,128)S(1)} %collective-permute-done.10) | copy-start | bytes 196
  36.3 15.7 %copy-start.6 = (f32[1,16,64,128]{3,2,1,0:T(8,128)}, f32[1,16,64,128]{3,2,1,0:T(8,128)S(1)}, u32[]{:S(2)}) copy-start(f32[1,16,64,128]{3,2,1,0:T(8,128)S(1)} %collective-permute-done.2) | copy-start | bytes 1572868
  36.4 15.5 %collective-permute-start.4 = (f32[1,16,64,128]{3,2,1,0:T(8,128)S(1)}, f32[1,16,64,128]{3,2,1,0:T(8,128)S(1)}, u32[]{:S(2)}, u32[]{:S(2)}) collective-permute-start(f32[1,16,64,128]{3,2,1,0:T(8,128)S(1)} %multiply_add_fusion.10), channel_id=1, source_target_pairs={{0,32},{8,40},{16,48},{24,56},{32,64},{40,72},{48,80},{56,88},{64,... | collective-permute-start | bytes 1572872 | tf_op jit(solution)/shard_map/ppermute | solution.py:25
  40.7 10.0 %collective-permute-start.3 = (f32[1,16]{1,0:T(1,128)S(1)}, f32[1,16]{1,0:T(1,128)S(1)}, u32[]{:S(2)}, u32[]{:S(2)}) collective-permute-start(f32[1,16]{1,0:T(1,128)S(1)} %get-tuple-element.225), channel_id=1, source_target_pairs={{0,16},{8,24},{16,32},{24,40},{32,48},{40,56},{48,64},{56,72},{64,... | collective-permute-start | bytes 200 | tf_op jit(solution)/shard_map/ppermute | solution.py:25
  51.9 13.5 %copy-start.8 = (f32[1,16,64,128]{3,2,1,0:T(8,128)}, f32[1,16,64,128]{3,2,1,0:T(8,128)S(1)}, u32[]{:S(2)}) copy-start(f32[1,16,64,128]{3,2,1,0:T(8,128)S(1)} %collective-permute-done.4) | copy-start | bytes 1572868
  52.0 20.2 %copy-start.53 = (f32[16]{0:T(128)S(1)}, f32[16]{0:T(128)}, u32[]{:S(2)}) copy-start(f32[16]{0:T(128)} %param.18) | copy-start | bytes 196
  52.0 20.3 %copy-start.20 = (bf16[256,1024]{1,0:T(8,128)(2,1)S(1)}, bf16[256,1024]{1,0:T(8,128)(2,1)}, u32[]{:S(2)}) copy-start(bf16[256,1024]{1,0:T(8,128)(2,1)} %param.12) | copy-start | bytes 1572868
  52.0 12.4 %collective-permute-start.6 = (f32[1,16,64,128]{3,2,1,0:T(8,128)S(1)}, f32[1,16,64,128]{3,2,1,0:T(8,128)S(1)}, u32[]{:S(2)}, u32[]{:S(2)}) collective-permute-start(f32[1,16,64,128]{3,2,1,0:T(8,128)S(1)} %multiply_add_fusion.9), channel_id=1, source_target_pairs={{0,64},{8,72},{16,80},{24,88},{32,96},{40,104},{48,112},{56,120},{... | collective-permute-start | bytes 1572872 | tf_op jit(solution)/shard_map/ppermute | solution.py:25
  55.7 7.0 %collective-permute-start.5 = (f32[1,16]{1,0:T(1,128)S(1)}, f32[1,16]{1,0:T(1,128)S(1)}, u32[]{:S(2)}, u32[]{:S(2)}) collective-permute-start(f32[1,16]{1,0:T(1,128)S(1)} %mul.703), channel_id=1, source_target_pairs={{0,32},{8,40},{16,48},{24,56},{32,64},{40,72},{48,80},{56,88},{64,... | collective-permute-start | bytes 200 | tf_op jit(solution)/shard_map/ppermute | solution.py:25
  64.4 7.0 %copy-start.9 = (f32[1,16,64,128]{3,2,1,0:T(8,128)}, f32[1,16,64,128]{3,2,1,0:T(8,128)S(1)}, u32[]{:S(2)}) copy-start(f32[1,16,64,128]{3,2,1,0:T(8,128)S(1)} %collective-permute-done.6) | copy-start | bytes 1572868
  65.4 7.2 %copy-start.16 = (bf16[256,128]{1,0:T(8,128)(2,1)S(1)}, bf16[256,128]{1,0:T(8,128)(2,1)}, u32[]{:S(2)}) copy-start(bf16[256,128]{1,0:T(8,128)(2,1)} %param.15) | copy-start | bytes 196612
  65.4 13.2 %collective-permute-start.8 = (f32[1,16,64,128]{3,2,1,0:T(8,128)}, f32[1,16,64,128]{3,2,1,0:T(8,128)}, u32[]{:S(2)}, u32[]{:S(2)}) collective-permute-start(f32[1,16,64,128]{3,2,1,0:T(8,128)} %multiply_add_fusion.8), channel_id=1, source_target_pairs={{0,128},{8,136},{16,144},{24,152},{32,160},{40,168},{48,176},{56,1... | collective-permute-start | bytes 1572872 | tf_op jit(solution)/shard_map/ppermute | solution.py:25
  71.4 3.7 %copy-start.21 = (bf16[256,1024]{1,0:T(8,128)(2,1)S(1)}, bf16[256,1024]{1,0:T(8,128)(2,1)}, u32[]{:S(2)}) copy-start(bf16[256,1024]{1,0:T(8,128)(2,1)} %param.21) | copy-start | bytes 1572868
  72.4 34.3 %copy-start.33 = (f32[1024]{0:T(1024)}, f32[1024]{0:T(1024)S(1)}, u32[]{:S(2)}) copy-start(f32[1024]{0:T(1024)S(1)} %mul.725) | copy-start | bytes 12292
  72.4 6.2 %copy-start.5 = (f32[1,16,64,128]{3,2,1,0:T(8,128)S(1)}, f32[1,16,64,128]{3,2,1,0:T(8,128)}, u32[]{:S(2)}) copy-start(f32[1,16,64,128]{3,2,1,0:T(8,128)} %copy-done.4) | copy-start | bytes 1572868
  72.4 6.2 %copy-start.7 = (f32[1,16,64,128]{3,2,1,0:T(8,128)S(1)}, f32[1,16,64,128]{3,2,1,0:T(8,128)}, u32[]{:S(2)}) copy-start(f32[1,16,64,128]{3,2,1,0:T(8,128)} %copy-done.6) | copy-start | bytes 1572868
  73.5 5.1 %collective-permute-start.7 = (f32[1,16]{1,0:T(1,128)S(1)}, f32[1,16]{1,0:T(1,128)S(1)}, u32[]{:S(2)}, u32[]{:S(2)}) collective-permute-start(f32[1,16]{1,0:T(1,128)S(1)} %mul.711), channel_id=1, source_target_pairs={{0,64},{8,72},{16,80},{24,88},{32,96},{40,104},{48,112},{56,120},{... | collective-permute-start | bytes 200 | tf_op jit(solution)/shard_map/ppermute | solution.py:25
  81.7 3.3 %copy-start.36 = (f32[1024]{0:T(1024)S(1)}, f32[1024]{0:T(1024)}, u32[]{:S(2)}) copy-start(f32[1024]{0:T(1024)} %param.19) | copy-start | bytes 12292
  85.0 1.6 copy-start
  110.4 8.6 %collective-permute-start.9 = (f32[1,16,64,128]{3,2,1,0:T(8,128)S(1)}, f32[1,16,64,128]{3,2,1,0:T(8,128)S(1)}, u32[]{:S(2)}, u32[]{:S(2)}) collective-permute-start(f32[1,16,64,128]{3,2,1,0:T(8,128)S(1)} %convolution_bitcast_fusion.2), channel_id=1, source_target_pairs={{8,0},{16,8},{24,16},{32,24},{40,32},{48,40},{56,48},{64,56},{72,6... | collective-permute-start | bytes 1572872 | tf_op jit(solution)/shard_map/ppermute | solution.py:25
  112.3 9.5 %collective-permute-start.12 = (f32[1,16]{1,0:T(1,128)S(1)}, f32[1,16]{1,0:T(1,128)S(1)}, u32[]{:S(2)}, u32[]{:S(2)}) collective-permute-start(f32[1,16]{1,0:T(1,128)S(1)} %get-tuple-element.224), channel_id=1, source_target_pairs={{16,0},{24,8},{32,16},{40,24},{48,32},{56,40},{64,48},{72,56},{80,... | collective-permute-start | bytes 200 | tf_op jit(solution)/shard_map/ppermute | solution.py:25
  119.1 22.3 %collective-permute-start.11 = (f32[1,16,64,128]{3,2,1,0:T(8,128)S(1)}, f32[1,16,64,128]{3,2,1,0:T(8,128)S(1)}, u32[]{:S(2)}, u32[]{:S(2)}) collective-permute-start(f32[1,16,64,128]{3,2,1,0:T(8,128)S(1)} %multiply_add_fusion.6), channel_id=1, source_target_pairs={{16,0},{24,8},{32,16},{40,24},{48,32},{56,40},{64,48},{72,56},{80,... | collective-permute-start | bytes 1572872 | tf_op jit(solution)/shard_map/ppermute | solution.py:25
  121.9 14.0 %collective-permute-start.14 = (f32[1,16]{1,0:T(1,128)S(1)}, f32[1,16]{1,0:T(1,128)S(1)}, u32[]{:S(2)}, u32[]{:S(2)}) collective-permute-start(f32[1,16]{1,0:T(1,128)S(1)} %mul.761), channel_id=1, source_target_pairs={{32,0},{40,8},{48,16},{56,24},{64,32},{72,40},{80,48},{88,56},{96,... | collective-permute-start | bytes 200 | tf_op jit(solution)/shard_map/ppermute | solution.py:25
  135.9 5.5 %collective-permute-start.16 = (f32[1,16]{1,0:T(1,128)S(1)}, f32[1,16]{1,0:T(1,128)S(1)}, u32[]{:S(2)}, u32[]{:S(2)}) collective-permute-start(f32[1,16]{1,0:T(1,128)S(1)} %mul.769), channel_id=1, source_target_pairs={{64,0},{72,8},{80,16},{88,24},{96,32},{104,40},{112,48},{120,56},{... | collective-permute-start | bytes 200 | tf_op jit(solution)/shard_map/ppermute | solution.py:25
  137.3 8.8 %copy-start.2 = (f32[1,256,1,16,64]{1,4,3,2,0:T(8,128)S(1)}, f32[1,256,1,16,64]{1,4,3,2,0:T(8,128)}, u32[]{:S(2)}) copy-start(f32[1,256,1,16,64]{1,4,3,2,0:T(8,128)} %copy-done.1) | copy-start | bytes 3145732
  142.2 18.1 %collective-permute-start.13 = (f32[1,16,64,128]{3,2,1,0:T(8,128)S(1)}, f32[1,16,64,128]{3,2,1,0:T(8,128)S(1)}, u32[]{:S(2)}, u32[]{:S(2)}) collective-permute-start(f32[1,16,64,128]{3,2,1,0:T(8,128)S(1)} %multiply_add_fusion.5), channel_id=1, source_target_pairs={{32,0},{40,8},{48,16},{56,24},{64,32},{72,40},{80,48},{88,56},{96,... | collective-permute-start | bytes 1572872 | tf_op jit(solution)/shard_map/ppermute | solution.py:25
  146.5 16.2 %copy-start.24 = (f32[256,256]{1,0:T(8,128)}, f32[256,256]{1,0:T(8,128)S(1)}, u32[]{:S(2)}) copy-start(f32[256,256]{1,0:T(8,128)S(1)} %fusion.76) | copy-start | bytes 786436
  146.9 24.1 %copy-start.26 = (f32[256,256]{1,0:T(8,128)}, f32[256,256]{1,0:T(8,128)S(1)}, u32[]{:S(2)}) copy-start(f32[256,256]{1,0:T(8,128)S(1)} %fusion.79) | copy-start | bytes 786436
  161.1 14.8 %collective-permute-start.15 = (f32[1,16,64,128]{3,2,1,0:T(8,128)S(1)}, f32[1,16,64,128]{3,2,1,0:T(8,128)S(1)}, u32[]{:S(2)}, u32[]{:S(2)}) collective-permute-start(f32[1,16,64,128]{3,2,1,0:T(8,128)S(1)} %multiply_add_fusion.4), channel_id=1, source_target_pairs={{64,0},{72,8},{80,16},{88,24},{96,32},{104,40},{112,48},{120,56},{... | collective-permute-start | bytes 1572872 | tf_op jit(solution)/shard_map/ppermute | solution.py:25
  171.0 7.8 %copy-start.19 = (f32[256,256]{1,0:T(8,128)}, f32[256,256]{1,0:T(8,128)S(1)}, u32[]{:S(2)}) copy-start(f32[256,256]{1,0:T(8,128)S(1)} %get-tuple-element.182) | copy-start | bytes 786436
  176.0 2.8 %copy-start.14 = (f32[1,16,64,128]{3,2,1,0:T(8,128)}, f32[1,16,64,128]{3,2,1,0:T(8,128)S(1)}, u32[]{:S(2)}) copy-start(f32[1,16,64,128]{3,2,1,0:T(8,128)S(1)} %collective-permute-done.15) | copy-start | bytes 1572868
  176.0 2.8 %copy-start.3 = (bf16[256,1024]{0,1:T(8,128)(2,1)S(1)}, bf16[256,1024]{0,1:T(8,128)(2,1)}, u32[]{:S(2)}) copy-start(bf16[256,1024]{0,1:T(8,128)(2,1)} %get-tuple-element.209) | copy-start | bytes 1572868
  176.9 15.8 %collective-permute-start.17 = (f32[1,16,64,128]{3,2,1,0:T(8,128)}, f32[1,16,64,128]{3,2,1,0:T(8,128)}, u32[]{:S(2)}, u32[]{:S(2)}) collective-permute-start(f32[1,16,64,128]{3,2,1,0:T(8,128)} %multiply_add_fusion.3), channel_id=1, source_target_pairs={{128,0},{136,8},{144,16},{152,24},{160,32},{168,40},{176,48},{184,... | collective-permute-start | bytes 1572872 | tf_op jit(solution)/shard_map/ppermute | solution.py:25
  178.2 3.0 %copy-start.30 = (f32[256,16]{0,1:T(8,128)S(1)}, f32[256,16]{0,1:T(8,128)}, u32[]{:S(2)}) copy-start(f32[256,16]{0,1:T(8,128)} %copy-done.29) | copy-start | bytes 49156
  181.2 11.5 %copy-start.11 = (f32[1,16,64,128]{3,2,1,0:T(8,128)S(1)}, f32[1,16,64,128]{3,2,1,0:T(8,128)}, u32[]{:S(2)}) copy-start(f32[1,16,64,128]{3,2,1,0:T(8,128)} %copy-done.10) | copy-start | bytes 1572868
  181.2 11.5 %copy-start.13 = (f32[1,16,64,128]{3,2,1,0:T(8,128)S(1)}, f32[1,16,64,128]{3,2,1,0:T(8,128)}, u32[]{:S(2)}) copy-start(f32[1,16,64,128]{3,2,1,0:T(8,128)} %copy-done.12) | copy-start | bytes 1572868
  181.2 11.5 %copy-start.15 = (f32[1,16,64,128]{3,2,1,0:T(8,128)S(1)}, f32[1,16,64,128]{3,2,1,0:T(8,128)}, u32[]{:S(2)}) copy-start(f32[1,16,64,128]{3,2,1,0:T(8,128)} %copy-done.14) | copy-start | bytes 1572868
  181.2 11.5 %copy-start.50 = (f32[1,16]{1,0:T(1,128)S(1)}, f32[1,16]{1,0:T(1,128)}, u32[]{:S(2)}) copy-start(f32[1,16]{1,0:T(1,128)} %copy-done.49) | copy-start | bytes 196
  194.4 1.6 copy-start.22
  194.4 1.7 copy-start.35
  194.4 1.7 copy-start.38
  194.5 1.7 copy-start.40
  194.5 1.7 copy-start.41
  194.5 1.7 copy-start.45
  194.5 1.7 copy-start.47
  194.5 1.7 copy-start.48
  194.5 7.4 %copy-start.32 = (f32[256,16]{0,1:T(8,128)S(1)}, f32[256,16]{0,1:T(8,128)}, u32[]{:S(2)}) copy-start(f32[256,16]{0,1:T(8,128)} %copy-done.31) | copy-start | bytes 49156
  196.1 8.3 %copy-start.25 = (f32[256,256]{1,0:T(8,128)S(1)}, f32[256,256]{1,0:T(8,128)}, u32[]{:S(2)}) copy-start(f32[256,256]{1,0:T(8,128)} %copy-done.24) | copy-start | bytes 786436
  196.1 8.3 %copy-start.27 = (f32[256,256]{1,0:T(8,128)S(1)}, f32[256,256]{1,0:T(8,128)}, u32[]{:S(2)}) copy-start(f32[256,256]{1,0:T(8,128)} %copy-done.26) | copy-start | bytes 786436
  196.1 8.3 %copy-start.43 = (f32[256,1,16]{0,2,1:T(8,128)S(1)}, f32[256,1,16]{0,2,1:T(8,128)}, u32[]{:S(2)}) copy-start(f32[256,1,16]{0,2,1:T(8,128)} %copy-done.42) | copy-start | bytes 49156
  201.8 2.6 %copy-start.18 = (f32[256,16,64]{0,2,1:T(8,128)S(1)}, f32[256,16,64]{0,2,1:T(8,128)}, u32[]{:S(2)}) copy-start(f32[256,16,64]{0,2,1:T(8,128)} %get-tuple-element.227) | copy-start | bytes 3145732
  204.4 3.8 %copy-start.34 = (f32[1024]{0:T(1024)S(1)}, f32[1024]{0:T(1024)}, u32[]{:S(2)}) copy-start(f32[1024]{0:T(1024)} %copy-done.33) | copy-start | bytes 12292
  (8 other events, 10.2 us)

commit v2 on v1

--- a/solution.py
+++ b/solution.py
@@ -10,6 +10,21 @@
 
 HIGHEST_PRECISION = lax.Precision.HIGHEST
 EPSILON = 1e-05
+
+
+def pack_pair(gain, value):
+    rows = value.reshape(-1, value.shape[-1])
+    pad = jnp.zeros((8, value.shape[-1]), value.dtype)
+    pad = pad.at[0, : gain.size].set(gain.reshape(-1))
+    return jnp.concatenate([rows, pad], axis=0)
+
+
+def unpack_pair(packed, gain, value):
+    rows = value.size // value.shape[-1]
+    return (
+        packed[rows, : gain.size].reshape(gain.shape),
+        packed[:rows].reshape(value.shape),
+    )
 
 
 def exclusive_scan(gain, value, axis, forward):
@@ -22,7 +37,8 @@
             pairs = [(i, i + distance) for i in range(size - distance)]
         else:
             pairs = [(i + distance, i) for i in range(size - distance)]
-        gain_in, value_in = lax.ppermute((gain, value), axis, pairs)
+        moved = lax.ppermute(pack_pair(gain, value), axis, pairs)
+        gain_in, value_in = unpack_pair(moved, gain, value)
         total = total + total_gain[..., None, None] * value_in
         distance *= 2
         if distance < size:
@@ -30,6 +46,16 @@
             value = value + gain[..., None, None] * value_in
             gain = gain * gain_in
     return total
+
+
+def butterfly_sum(value, axis):
+    size = lax.axis_size(axis)
+    step = 1
+    while step < size:
+        pairs = [(i, i ^ step) for i in range(size)]
+        value = value + lax.ppermute(value, axis, pairs)
+        step *= 2
+    return value
 
 
 def span_mix(x_span, dt_span, b_span, c_span, log_cum, segment):
@@ -149,7 +175,7 @@
     gated = core_out * gate_act
     weighted_grad = norm_weight[None, :] * grad_output.astype(jnp.float32)
     norm_width = lax.axis_size("head") * gated.shape[1]
-    sums = lax.psum(
+    sums = butterfly_sum(
         jnp.stack([jnp.sum(gated * gated, axis=1), jnp.sum(weighted_grad * gated, axis=1)]),
         "head",
     )

time: 212 us -> 227 us (1.071)
  blocking collectives: 20 us -> 0 us
  waiting for transfers between devices: 75.1 us -> 94.2 us
  other arithmetic: 23.1 us -> 38.5 us
  starting transfers between devices: 53.7 us -> 43.1 us
  local copies, waits for them, and re-layouts: 8.88 us -> 16 us
  matrix products: 26.9 us -> 30.7 us
    psum x1 -> x0, blocking collectives: 20 us -> none  [body(): lax.psum(jnp.stack([jnp.sum(gated * gated, axis=1), jnp.sum(weighted_grad...]
    ppermute x18 -> x13, waiting for transfers between devices: 75.1 us -> 94.2 us  [the longest x10 89.4 us: exclusive_scan(): moved = lax.ppermute(pack_pair(gain, value), axis, pairs)]
    ppermute x18 -> x13, starting transfers between devices: 53.7 us -> 43.1 us  [the longest x10 30.9 us: exclusive_scan(): moved = lax.ppermute(pack_pair(gain, value), axis, pairs)]
    concatenate x0 -> x10, other arithmetic: none -> 5.31 us  [pack_pair(): return jnp.concatenate([rows, pad], axis=0)]
    unnamed x113 -> x119, local copies, waits for them, and re-layouts: 6.2 us -> 11.4 us
    add x8, other arithmetic: 2.55 us -> 6.33 us  [exclusive_scan(): value = value + gain[..., None, None] * value_in]
  transfers between devices with their start and end apart: 18 -> 13, of which waited for: 14 -> 13; matrix products, arithmetic and copies ran while one was open for 8% -> 10% of each run, Pallas kernels for 0% -> 0%
where the time goes in v2:
time: 227 us; the launch traced here: 225 us
  waiting for transfers between devices  94.2 us (41%)
  starting transfers between devices  43.1 us (19%)
  other arithmetic  38.5 us (17%)
  matrix products  30.7 us (14%)
  local copies, waits for them, and re-layouts  16 us (7%)
  between operations  2.91 us (1%)
    ppermute x10, waiting for transfers between devices, exclusive_scan(): moved = lax.ppermute(pack_pair(gain, value), axis, pairs)  89.4 us
    ppermute x10, starting transfers between devices, exclusive_scan(): moved = lax.ppermute(pack_pair(gain, value), axis, pairs)  30.9 us
    dot_general x3, matrix products, span_mix(): jnp.einsum('ghts,sghp->tghp', weights, x_span, precision=HIGHEST_PRECISION)  16.5 us
    ppermute x3, starting transfers between devices, butterfly_sum(): value = value + lax.ppermute(value, axis, pairs)  12.2 us
    unnamed x119, local copies, waits for them, and re-layouts  11.4 us
    another operation x10, other arithmetic  7.72 us
    dot_general x3, matrix products, local_states(): jnp.einsum('kqgh,kqghp,kqgn->kghpn', tail_decay * dt_spans, x_spans, b_sp...  6.94 us
    add x8, other arithmetic, exclusive_scan(): value = value + gain[..., None, None] * value_in  6.33 us
  transfers between devices with their start and end apart: 13, of which 13 were waited for; matrix products, arithmetic and copies ran while one was open for 10% of the time, Pallas kernels for 0%

profile of v2, /device:TPU:6, one launch (start us, length us, event | category | flops | bytes accessed | tf_op | source)
XLA Modules:
  0.0 225.4 jit_solution(6709399124379600674)
XLA Ops:
  1.3 1.4 fusion.105
  3.5 1.0 reduce-window.30
  8.6 0.8 fusion.91
  9.4 1.2 copy.100
  11.4 1.9 collective-permute-start
  13.3 8.6 %collective-permute-done = f32[1032,128]{1,0:T(8,128)S(1)} collective-permute-done((f32[1032,128]{1,0:T(8,128)S(1)}, f32[1032,128]{1,0:T(8,128)S(1)}, u32[]{:S(2)}, u32[]{:S(2)}) %collective-permute-start) | collective-permute-done | bytes 528416 | tf_op jit(solution)/shard_map/ppermute | solution.py:40
  22.2 5.5 %collective-permute-start.1 = (f32[1032,128]{1,0:T(8,128)S(1)}, f32[1032,128]{1,0:T(8,128)S(1)}, u32[]{:S(2)}, u32[]{:S(2)}) collective-permute-start(f32[1032,128]{1,0:T(8,128)S(1)} %select_maximum_fusion.7), channel_id=1, source_target_pairs={{0,16},{8,24},{16,32},{24,40},{32,48},{40,56},{48,64},{56,72},{64,... | collective-permute-start | bytes 1585160 | tf_op jit(solution)/shard_map/ppermute | solution.py:40
  27.7 9.4 %collective-permute-done.1 = f32[1032,128]{1,0:T(8,128)S(1)} collective-permute-done((f32[1032,128]{1,0:T(8,128)S(1)}, f32[1032,128]{1,0:T(8,128)S(1)}, u32[]{:S(2)}, u32[]{:S(2)}) %collective-permute-start.1) | collective-permute-done | bytes 528416 | tf_op jit(solution)/shard_map/ppermute | solution.py:40
  37.3 4.3 %collective-permute-start.2 = (f32[1032,128]{1,0:T(8,128)S(1)}, f32[1032,128]{1,0:T(8,128)S(1)}, u32[]{:S(2)}, u32[]{:S(2)}) collective-permute-start(f32[1032,128]{1,0:T(8,128)S(1)} %select_maximum_fusion.6), channel_id=1, source_target_pairs={{0,32},{8,40},{16,48},{24,56},{32,64},{40,72},{48,80},{56,88},{64,... | collective-permute-start | bytes 1585160 | tf_op jit(solution)/shard_map/ppermute | solution.py:40
  41.6 11.2 %collective-permute-done.2 = f32[1032,128]{1,0:T(8,128)S(1)} collective-permute-done((f32[1032,128]{1,0:T(8,128)S(1)}, f32[1032,128]{1,0:T(8,128)S(1)}, u32[]{:S(2)}, u32[]{:S(2)}) %collective-permute-start.2) | collective-permute-done | bytes 528416 | tf_op jit(solution)/shard_map/ppermute | solution.py:40
  53.1 3.5 %collective-permute-start.3 = (f32[1032,128]{1,0:T(8,128)S(1)}, f32[1032,128]{1,0:T(8,128)S(1)}, u32[]{:S(2)}, u32[]{:S(2)}) collective-permute-start(f32[1032,128]{1,0:T(8,128)S(1)} %select_maximum_fusion.5), channel_id=1, source_target_pairs={{0,64},{8,72},{16,80},{24,88},{32,96},{40,104},{48,112},{56,120},{... | collective-permute-start | bytes 1585160 | tf_op jit(solution)/shard_map/ppermute | solution.py:40
  56.6 8.8 %collective-permute-done.3 = f32[1032,128]{1,0:T(8,128)S(1)} collective-permute-done((f32[1032,128]{1,0:T(8,128)S(1)}, f32[1032,128]{1,0:T(8,128)S(1)}, u32[]{:S(2)}, u32[]{:S(2)}) %collective-permute-start.3) | collective-permute-done | bytes 528416 | tf_op jit(solution)/shard_map/ppermute | solution.py:40
  66.2 0.8 select_maximum_fusion.4
  67.1 5.9 %collective-permute-start.4 = (f32[1032,128]{1,0:T(8,128)}, f32[1032,128]{1,0:T(8,128)}, u32[]{:S(2)}, u32[]{:S(2)}) collective-permute-start(f32[1032,128]{1,0:T(8,128)} %select_maximum_fusion.4), channel_id=1, source_target_pairs={{0,128},{8,136},{16,144},{24,152},{32,160},{40,168},{48,176},{56,1... | collective-permute-start | bytes 1585160 | tf_op jit(solution)/shard_map/ppermute | solution.py:40
  73.1 1.3 copy.106
  74.4 1.2 copy.107
  75.7 0.9 fusion.75
  77.3 2.9 %collective-permute-done.4 = f32[1032,128]{1,0:T(8,128)} collective-permute-done((f32[1032,128]{1,0:T(8,128)}, f32[1032,128]{1,0:T(8,128)}, u32[]{:S(2)}, u32[]{:S(2)}) %collective-permute-start.4) | collective-permute-done | bytes 528416 | tf_op jit(solution)/shard_map/ppermute | solution.py:40
  80.2 2.0 fusion.66
  83.6 1.0 copy-done.12
  84.6 3.3 %fusion.37 = f32[1,256,1,16,64]{1,4,3,2,0:T(8,128)S(1)} fusion(bf16[256,16,64]{0,2,1:T(8,128)(2,1)S(1)} %bitcast.289, f32[16,256]{1,0:T(8,128)S(1)} %get-tuple-element.342, f32[256,256]{1,0:T(8,128)S(1)} %copy-done.28, f32[16,256]{1,0:T(8,128)S(1)} %bitcast.310, f32[256,256]{1,0:T(8,128)S(1)} %fusion.111, ...), kind=kOutput, calls=%fused_computation.40 | convolution fusion | flops 811073536 | bytes 3194880 | tf_op jit(solution)/shard_map/jvp()/while/body/eval_jaxpr/ghts,sghp->tghp/dot_general | solution.py:71
  88.8 1.9 collective-permute-start.5
  90.8 1.7 collective-permute-done.5
  92.4 3.4 %collective-permute-start.6 = (f32[2,256]{1,0:T(2,128)S(1)}, f32[2,256]{1,0:T(2,128)S(1)}, u32[]{:S(2)}, u32[]{:S(2)}) collective-permute-start(f32[2,256]{1,0:T(2,128)S(1)} %fusion.104), channel_id=1, source_target_pairs={{0,2},{1,3},{2,0},{3,1},{4,6},{5,7},{6,4},{7,5},{8,10},{9,11},{10,... | collective-permute-start | bytes 6152 | tf_op jit(solution)/shard_map/ppermute | solution.py:56
  95.8 1.6 collective-permute-done.6
  97.4 6.9 %collective-permute-start.7 = (f32[2,256]{1,0:T(2,128)S(1)}, f32[2,256]{1,0:T(2,128)S(1)}, u32[]{:S(2)}, u32[]{:S(2)}) collective-permute-start(f32[2,256]{1,0:T(2,128)S(1)} %fusion.124), channel_id=1, source_target_pairs={{0,4},{1,5},{2,6},{3,7},{4,0},{5,1},{6,2},{7,3},{8,12},{9,13},{10,... | collective-permute-start | bytes 6152 | tf_op jit(solution)/shard_map/ppermute | solution.py:56
  104.3 1.6 collective-permute-done.7
  105.9 1.6 broadcast_multiply_fusion
  108.1 0.9 fusion.64
  109.0 1.9 collective-permute-start.8
  111.1 6.9 %collective-permute-done.8 = f32[1032,128]{1,0:T(8,128)} collective-permute-done((f32[1032,128]{1,0:T(8,128)}, f32[1032,128]{1,0:T(8,128)}, u32[]{:S(2)}, u32[]{:S(2)}) %collective-permute-start.8) | collective-permute-done | bytes 528416 | tf_op jit(solution)/shard_map/ppermute | solution.py:40
  118.7 1.4 multiply_add_fusion.3
  120.1 0.9 select_maximum_fusion.3
  121.0 2.7 %collective-permute-start.9 = (f32[1032,128]{1,0:T(8,128)}, f32[1032,128]{1,0:T(8,128)}, u32[]{:S(2)}, u32[]{:S(2)}) collective-permute-start(f32[1032,128]{1,0:T(8,128)} %select_maximum_fusion.3), channel_id=1, source_target_pairs={{16,0},{24,8},{32,16},{40,24},{48,32},{56,40},{64,48},{72,56},{80,... | collective-permute-start | bytes 1585160 | tf_op jit(solution)/shard_map/ppermute | solution.py:40
  123.7 1.1 convert.9
  125.0 13.8 %collective-permute-done.9 = f32[1032,128]{1,0:T(8,128)} collective-permute-done((f32[1032,128]{1,0:T(8,128)}, f32[1032,128]{1,0:T(8,128)}, u32[]{:S(2)}, u32[]{:S(2)}) %collective-permute-start.9) | collective-permute-done | bytes 528416 | tf_op jit(solution)/shard_map/ppermute | solution.py:40
  139.5 1.5 multiply_add_fusion.2
  141.0 0.9 select_maximum_fusion.2
  141.9 2.5 %collective-permute-start.10 = (f32[1032,128]{1,0:T(8,128)}, f32[1032,128]{1,0:T(8,128)}, u32[]{:S(2)}, u32[]{:S(2)}) collective-permute-start(f32[1032,128]{1,0:T(8,128)} %select_maximum_fusion.2), channel_id=1, source_target_pairs={{32,0},{40,8},{48,16},{56,24},{64,32},{72,40},{80,48},{88,56},{96,... | collective-permute-start | bytes 1585160 | tf_op jit(solution)/shard_map/ppermute | solution.py:40
  144.4 2.5 %convolution_bitcast_fusion.3 = f32[256,128]{1,0:T(8,128)} fusion(f32[16,64,128]{2,1,0:T(8,128)S(1)} %bitcast.297, f32[1,256,1,16,64]{1,4,3,2,0:T(8,128)S(1)} %copy-done.1), kind=kOutput, calls=%fused_computation.50 | convolution fusion | flops 402653184 | bytes 1703936 | tf_op jit(solution)/shard_map/transpose(jvp(kqgn,kghpn->kqghp))/dot_general | solution.py:120
  146.9 0.8 fusion.76
  147.7 1.1 fusion.78
  149.0 10.3 %collective-permute-done.10 = f32[1032,128]{1,0:T(8,128)} collective-permute-done((f32[1032,128]{1,0:T(8,128)}, f32[1032,128]{1,0:T(8,128)}, u32[]{:S(2)}, u32[]{:S(2)}) %collective-permute-start.10) | collective-permute-done | bytes 528416 | tf_op jit(solution)/shard_map/ppermute | solution.py:40
  160.0 1.5 multiply_add_fusion.1
  161.5 0.8 copy-done.6
  162.3 0.8 select_maximum_fusion.1
  163.1 1.3 collective-permute-start.11
  164.5 8.4 %fusion.72 = (f32[16,256]{1,0:T(8,128)}, f32[16,256]{1,0:T(8,128)}, f32[16,256]{1,0:T(8,128)S(1)}, f32[256,256]{1,0:T(8,128)}) fusion(f32[16,256]{1,0:T(8,128)S(1)} %bitcast.311, f32[256,256]{1,0:T(8,128)S(1)} %copy-done.25, f32[16,256]{1,0:T(8,128)S(1)} %bitcast.328, f32[256,256]{1,0:T(8,128)S(1)} %copy-done.27, f32[256,1,16,64]{0,3,2,1:T(8,128)S(1)} %copy-done.19, ...), kind=kOutput, calls=%fused_computation.105 | convolution fusion | flops 825151488 | bytes 2965504 | tf_op jit(solution)/shard_map/transpose(jvp())/while/body/eval_jaxpr/checkpoint/ghts,sghp->tghp/dot_general | solution.py:71
  173.0 6.0 %collective-permute-done.11 = f32[1032,128]{1,0:T(8,128)} collective-permute-done((f32[1032,128]{1,0:T(8,128)}, f32[1032,128]{1,0:T(8,128)}, u32[]{:S(2)}, u32[]{:S(2)}) %collective-permute-start.11) | collective-permute-done | bytes 528416 | tf_op jit(solution)/shard_map/ppermute | solution.py:40
  179.7 1.4 multiply_add_fusion
  181.2 0.8 select_maximum_fusion
  182.0 1.3 collective-permute-start.12
  183.3 1.2 convolution_bitcast_fusion.2
  185.5 1.0 convolution_add_fusion
  187.1 11.5 %collective-permute-done.12 = f32[1032,128]{1,0:T(8,128)} collective-permute-done((f32[1032,128]{1,0:T(8,128)}, f32[1032,128]{1,0:T(8,128)}, u32[]{:S(2)}, u32[]{:S(2)}) %collective-permute-start.12) | collective-permute-done | bytes 528416 | tf_op jit(solution)/shard_map/ppermute | solution.py:40
  198.5 3.1 %multiply_reduce_fusion.3 = (f32[1024]{0:T(1024)S(1)}, f32[1024]{0:T(1024)S(1)}, f32[1024,128]{1,0:T(8,128)}) fusion(f32[1024,128]{1,0:T(8,128)} %copy-done.4, f32[1032,128]{1,0:T(8,128)} %collective-permute-done.12, f32[1024]{0:T(1024)S(1)} %mul.971, f32[1032,128]{1,0:T(8,128)} %collective-permute-done.11, f32[1024]{0:T(1024)S(1)} %mul.959, ...), kind=kLoop, calls=%fused_computation.89 | loop fusion | flops 1570816 | bytes 3694592 | tf_op jit(solution)/shard_map/transpose(jvp())/while/body/eval_jaxpr/reduce_sum | solution.py:97
  202.3 2.7 %fusion.49 = (f32[256,16]{0,1:T(8,128)S(1)}, f32[256,16,64]{0,2,1:T(8,128)}) fusion(bf16[256,1024]{0,1:T(8,128)(2,1)S(1)} %copy.100, f32[16,64,128]{2,1,0:T(8,128)} %bitcast.298, bf16[256,128]{1,0:T(8,128)(2,1)S(1)} %copy-done.18), kind=kOutput, calls=%fused_computation.53 | convolution fusion | flops 403435520 | bytes 2179072 | tf_op jit(solution)/shard_map/transpose(jvp(kqgh,kqghp,kqgn->kghpn))/dot_general | solution.py:85
  205.4 2.5 %reduce-window.36 = f32[1,16,1,2,128]{4,1,2,3,0:T(8,128)S(1)} reduce-window(f32[1,16,1,2,128]{4,1,2,3,0:T(8,128)S(1)} %copy_bitcast_fusion, f32[]{:T(128)} %constant.304.clone.1), window={size=1x1x1x1x128 pad=0_0x0_0x0_0x0_0x0_127}, to_apply=%region_17.18 | reduce-window | flops 520192 | bytes 32772 | tf_op jit(solution)/shard_map/reduce-window.6
  208.0 2.5 %reduce-window.34 = f32[1,16,1,2,128]{4,1,2,3,0:T(8,128)S(1)} reduce-window(f32[1,16,1,2,128]{4,1,2,3,0:T(8,128)S(1)} %bitcast.317, f32[]{:T(128)} %constant.304.clone.1), window={size=1x1x1x1x128 pad=0_0x0_0x0_0x0_0x0_127}, to_apply=%region_10.11 | reduce-window | flops 520192 | bytes 32772 | tf_op jit(solution)/shard_map/reduce-window.4
  210.6 3.6 %fusion.48 = f32[256,128]{1,0:T(8,128)} fusion(f32[1,256,1,128]{3,1,2,0:T(8,128)S(1)} %copy-done.23, f32[16,64,128]{2,1,0:T(8,128)} %bitcast.299, bf16[256,16,64]{0,2,1:T(8,128)(2,1)S(1)} %bitcast.291, f32[256,16]{0,1:T(8,128)S(1)} %copy-done.30), kind=kOutput, calls=%fused_computation.52 | convolution fusion | flops 403210240 | bytes 1327104 | tf_op jit(solution)/shard_map/transpose(jvp(kqgh,kqghp,kqgn->kghpn))/dot_general | solution.py:85
  214.3 4.9 %fusion.40 = f32[256,16,64]{0,2,1:T(8,128)S(1)} fusion(f32[16,256]{1,0:T(8,128)S(1)} %bitcast.329, f32[256,256]{1,0:T(8,128)S(1)} %copy-done.26, f32[16,256]{1,0:T(8,128)S(1)} %bitcast.313, f32[256,256]{1,0:T(8,128)} %fusion.78, f32[256,1,16,64]{0,3,2,1:T(8,128)S(1)} %bitcast.294, f32[256,16,64]{0,2,1:T(8,128)S(1)} %copy-done.20, f32[256,16]{0,1:T(8,128)S(1)} %copy-done.30), kind=kOutput, calls=%fused_computation.41 | convolution fusion | flops 811073536 | bytes 3719168 | tf_op jit(solution)/shard_map/transpose(jvp())/while/body/eval_jaxpr/checkpoint/ghts,sghp->tghp/dot_general | solution.py:71
  219.2 1.9 fusion.55
  221.1 2.1 copy.120
  223.7 1.0 copy.119
  (219 shorter events, 17.3 us)
Async XLA Ops:
  0.6 10.0 %copy-start.18 = (bf16[256,128]{1,0:T(8,128)(2,1)S(1)}, bf16[256,128]{1,0:T(8,128)(2,1)}, u32[]{:S(2)}) copy-start(bf16[256,128]{1,0:T(8,128)(2,1)} %param.34) | copy-start | bytes 196612
  1.3 4.1 %copy-start.53 = (f32[16]{0:T(128)}, f32[16]{0:T(128)S(1)}, u32[]{:S(2)}) copy-start(f32[16]{0:T(128)S(1)} %exponential_negate_fusion) | copy-start | bytes 196
  5.5 5.8 %copy-start.48 = (f32[256]{0:T(256)}, f32[256]{0:T(256)S(1)}, u32[]{:S(2)}) copy-start(f32[256]{0:T(256)S(1)} %get-tuple-element.328) | copy-start | bytes 3076
  5.5 70.2 %copy-start.35 = (s32[256]{0:T(256)}, s32[256]{0:T(256)S(1)}, u32[]{:S(2)}) copy-start(s32[256]{0:T(256)S(1)} %get-tuple-element.282) | copy-start | bytes 3076
  8.5 2.8 %copy-start.46 = (f32[16]{0:T(128)}, f32[16]{0:T(128)S(1)}, u32[]{:S(2)}) copy-start(f32[16]{0:T(128)S(1)} %get-tuple-element.318) | copy-start | bytes 196
  8.5 2.8 %copy-start.38 = (f32[256]{0:T(256)}, f32[256]{0:T(256)S(1)}, u32[]{:S(2)}) copy-start(f32[256]{0:T(256)S(1)} %compare_convert_fusion.1) | copy-start | bytes 3076
  9.4 2.0 copy-start.29
  11.4 10.5 %collective-permute-start = (f32[1032,128]{1,0:T(8,128)S(1)}, f32[1032,128]{1,0:T(8,128)S(1)}, u32[]{:S(2)}, u32[]{:S(2)}) collective-permute-start(f32[1032,128]{1,0:T(8,128)S(1)} %fusion.63), channel_id=1, source_target_pairs={{0,8},{8,16},{16,24},{24,32},{32,40},{40,48},{48,56},{56,64},{64,7... | collective-permute-start | bytes 1585160 | tf_op jit(solution)/shard_map/ppermute | solution.py:40
  22.2 14.9 %collective-permute-start.1 = (f32[1032,128]{1,0:T(8,128)S(1)}, f32[1032,128]{1,0:T(8,128)S(1)}, u32[]{:S(2)}, u32[]{:S(2)}) collective-permute-start(f32[1032,128]{1,0:T(8,128)S(1)} %select_maximum_fusion.7), channel_id=1, source_target_pairs={{0,16},{8,24},{16,32},{24,40},{32,48},{40,56},{48,64},{56,72},{64,... | collective-permute-start | bytes 1585160 | tf_op jit(solution)/shard_map/ppermute | solution.py:40
  37.3 15.6 %collective-permute-start.2 = (f32[1032,128]{1,0:T(8,128)S(1)}, f32[1032,128]{1,0:T(8,128)S(1)}, u32[]{:S(2)}, u32[]{:S(2)}) collective-permute-start(f32[1032,128]{1,0:T(8,128)S(1)} %select_maximum_fusion.6), channel_id=1, source_target_pairs={{0,32},{8,40},{16,48},{24,56},{32,64},{40,72},{48,80},{56,88},{64,... | collective-permute-start | bytes 1585160 | tf_op jit(solution)/shard_map/ppermute | solution.py:40
  52.9 12.7 %copy-start.15 = (f32[1032,128]{1,0:T(8,128)}, f32[1032,128]{1,0:T(8,128)S(1)}, u32[]{:S(2)}) copy-start(f32[1032,128]{1,0:T(8,128)S(1)} %collective-permute-done.2) | copy-start | bytes 1585156
  53.1 12.3 %collective-permute-start.3 = (f32[1032,128]{1,0:T(8,128)S(1)}, f32[1032,128]{1,0:T(8,128)S(1)}, u32[]{:S(2)}, u32[]{:S(2)}) collective-permute-start(f32[1032,128]{1,0:T(8,128)S(1)} %select_maximum_fusion.5), channel_id=1, source_target_pairs={{0,64},{8,72},{16,80},{24,88},{32,96},{40,104},{48,112},{56,120},{... | collective-permute-start | bytes 1585160 | tf_op jit(solution)/shard_map/ppermute | solution.py:40
  65.5 7.5 %copy-start.56 = (f32[16]{0:T(128)S(1)}, f32[16]{0:T(128)}, u32[]{:S(2)}) copy-start(f32[16]{0:T(128)} %param.38) | copy-start | bytes 196
  67.1 13.1 %collective-permute-start.4 = (f32[1032,128]{1,0:T(8,128)}, f32[1032,128]{1,0:T(8,128)}, u32[]{:S(2)}, u32[]{:S(2)}) collective-permute-start(f32[1032,128]{1,0:T(8,128)} %select_maximum_fusion.4), channel_id=1, source_target_pairs={{0,128},{8,136},{16,144},{24,152},{32,160},{40,168},{48,176},{56,1... | collective-permute-start | bytes 1585160 | tf_op jit(solution)/shard_map/ppermute | solution.py:40
  73.1 14.7 %copy-start.33 = (f32[1024]{0:T(1024)}, f32[1024]{0:T(1024)S(1)}, u32[]{:S(2)}) copy-start(f32[1024]{0:T(1024)S(1)} %mul.910) | copy-start | bytes 12292
  73.1 3.4 %copy-start.17 = (bf16[256,128]{1,0:T(8,128)(2,1)S(1)}, bf16[256,128]{1,0:T(8,128)(2,1)}, u32[]{:S(2)}) copy-start(bf16[256,128]{1,0:T(8,128)(2,1)} %param.35) | copy-start | bytes 196612
  75.7 12.2 %copy-start.2 = (bf16[256,1024]{0,1:T(8,128)(2,1)}, bf16[256,1024]{0,1:T(8,128)(2,1)S(1)}, u32[]{:S(2)}) copy-start(bf16[256,1024]{0,1:T(8,128)(2,1)S(1)} %copy.107) | copy-start | bytes 1572868
  82.2 2.4 %copy-start.28 = (f32[256,256]{1,0:T(8,128)S(1)}, f32[256,256]{1,0:T(8,128)}, u32[]{:S(2)}) copy-start(f32[256,256]{1,0:T(8,128)} %fusion.75) | copy-start | bytes 786436
  84.6 3.3 %copy-start.31 = (f32[1024]{0:T(1024)S(1)}, f32[1024]{0:T(1024)}, u32[]{:S(2)}) copy-start(f32[1024]{0:T(1024)} %param.39) | copy-start | bytes 12292
  88.8 3.6 %collective-permute-start.5 = (f32[2,256]{1,0:T(2,128)S(1)}, f32[2,256]{1,0:T(2,128)S(1)}, u32[]{:S(2)}, u32[]{:S(2)}) collective-permute-start(f32[2,256]{1,0:T(2,128)S(1)} %pad_maximum_fusion), channel_id=1, source_target_pairs={{0,1},{1,0},{2,3},{3,2},{4,5},{5,4},{6,7},{7,6},{8,9},{9,8},{10,11... | collective-permute-start | bytes 6152 | tf_op jit(solution)/shard_map/ppermute | solution.py:56
  92.4 4.9 %collective-permute-start.6 = (f32[2,256]{1,0:T(2,128)S(1)}, f32[2,256]{1,0:T(2,128)S(1)}, u32[]{:S(2)}, u32[]{:S(2)}) collective-permute-start(f32[2,256]{1,0:T(2,128)S(1)} %fusion.104), channel_id=1, source_target_pairs={{0,2},{1,3},{2,0},{3,1},{4,6},{5,7},{6,4},{7,5},{8,10},{9,11},{10,... | collective-permute-start | bytes 6152 | tf_op jit(solution)/shard_map/ppermute | solution.py:56
  97.4 8.5 %collective-permute-start.7 = (f32[2,256]{1,0:T(2,128)S(1)}, f32[2,256]{1,0:T(2,128)S(1)}, u32[]{:S(2)}, u32[]{:S(2)}) collective-permute-start(f32[2,256]{1,0:T(2,128)S(1)} %fusion.124), channel_id=1, source_target_pairs={{0,4},{1,5},{2,6},{3,7},{4,0},{5,1},{6,2},{7,3},{8,12},{9,13},{10,... | collective-permute-start | bytes 6152 | tf_op jit(solution)/shard_map/ppermute | solution.py:56
  105.9 1.6 copy-start.40
  105.9 1.6 copy-start.50
  107.5 1.5 copy-start
  108.1 2.8 %copy-start.9 = (f32[1024,128]{1,0:T(8,128)}, f32[1024,128]{1,0:T(8,128)S(1)}, u32[]{:S(2)}) copy-start(f32[1024,128]{1,0:T(8,128)S(1)} %fusion.112) | copy-start | bytes 1572868
  109.0 9.0 %collective-permute-start.8 = (f32[1032,128]{1,0:T(8,128)}, f32[1032,128]{1,0:T(8,128)}, u32[]{:S(2)}, u32[]{:S(2)}) collective-permute-start(f32[1032,128]{1,0:T(8,128)} %fusion.64), channel_id=1, source_target_pairs={{8,0},{16,8},{24,16},{32,24},{40,32},{48,40},{56,48},{64,56},{72,6... | collective-permute-start | bytes 1585160 | tf_op jit(solution)/shard_map/ppermute | solution.py:40
  118.7 6.2 %copy-start.55 = (f32[1,16]{1,0:T(1,128)}, f32[1,16]{1,0:T(1,128)S(1)}, u32[]{:S(2)}) copy-start(f32[1,16]{1,0:T(1,128)S(1)} %slice_multiply_fusion.13) | copy-start | bytes 196
  120.1 4.7 %copy-start.8 = (f32[1024,128]{1,0:T(8,128)}, f32[1024,128]{1,0:T(8,128)S(1)}, u32[]{:S(2)}) copy-start(f32[1024,128]{1,0:T(8,128)S(1)} %multiply_add_fusion.3) | copy-start | bytes 1572868
  121.0 17.8 %collective-permute-start.9 = (f32[1032,128]{1,0:T(8,128)}, f32[1032,128]{1,0:T(8,128)}, u32[]{:S(2)}, u32[]{:S(2)}) collective-permute-start(f32[1032,128]{1,0:T(8,128)} %select_maximum_fusion.3), channel_id=1, source_target_pairs={{16,0},{24,8},{32,16},{40,24},{48,32},{56,40},{64,48},{72,56},{80,... | collective-permute-start | bytes 1585160 | tf_op jit(solution)/shard_map/ppermute | solution.py:40
  139.5 4.9 %copy-start.1 = (f32[1,256,1,16,64]{1,4,3,2,0:T(8,128)S(1)}, f32[1,256,1,16,64]{1,4,3,2,0:T(8,128)}, u32[]{:S(2)}) copy-start(f32[1,256,1,16,64]{1,4,3,2,0:T(8,128)} %copy-done) | copy-start | bytes 3145732
  139.5 4.9 %copy-start.5 = (f32[1024,128]{1,0:T(8,128)S(1)}, f32[1024,128]{1,0:T(8,128)}, u32[]{:S(2)}) copy-start(f32[1024,128]{1,0:T(8,128)} %copy-done.4) | copy-start | bytes 1572868
  141.0 5.9 %copy-start.7 = (f32[1024,128]{1,0:T(8,128)}, f32[1024,128]{1,0:T(8,128)S(1)}, u32[]{:S(2)}) copy-start(f32[1024,128]{1,0:T(8,128)S(1)} %multiply_add_fusion.2) | copy-start | bytes 1572868
  141.9 5.0 %copy-start.36 = (s32[256]{0:T(256)S(1)}, s32[256]{0:T(256)}, u32[]{:S(2)}) copy-start(s32[256]{0:T(256)} %copy-done.35) | copy-start | bytes 3076
  141.9 17.4 %collective-permute-start.10 = (f32[1032,128]{1,0:T(8,128)}, f32[1032,128]{1,0:T(8,128)}, u32[]{:S(2)}, u32[]{:S(2)}) collective-permute-start(f32[1032,128]{1,0:T(8,128)} %select_maximum_fusion.2), channel_id=1, source_target_pairs={{32,0},{40,8},{48,16},{56,24},{64,32},{72,40},{80,48},{88,56},{96,... | collective-permute-start | bytes 1585160 | tf_op jit(solution)/shard_map/ppermute | solution.py:40
  160.0 4.5 %copy-start.19 = (f32[256,1,16,64]{0,3,2,1:T(8,128)S(1)}, f32[256,1,16,64]{0,3,2,1:T(8,128)}, u32[]{:S(2)}) copy-start(f32[256,1,16,64]{0,3,2,1:T(8,128)} %convert.9) | copy-start | bytes 3145732
  160.0 4.5 %copy-start.25 = (f32[256,256]{1,0:T(8,128)S(1)}, f32[256,256]{1,0:T(8,128)}, u32[]{:S(2)}) copy-start(f32[256,256]{1,0:T(8,128)} %fusion.76) | copy-start | bytes 786436
  160.0 4.5 %copy-start.27 = (f32[256,256]{1,0:T(8,128)S(1)}, f32[256,256]{1,0:T(8,128)}, u32[]{:S(2)}) copy-start(f32[256,256]{1,0:T(8,128)} %fusion.78) | copy-start | bytes 786436
  160.0 4.5 %copy-start.44 = (f32[256,1,16]{0,2,1:T(8,128)S(1)}, f32[256,1,16]{0,2,1:T(8,128)}, u32[]{:S(2)}) copy-start(f32[256,1,16]{0,2,1:T(8,128)} %get-tuple-element.283) | copy-start | bytes 49156
  163.1 15.9 %collective-permute-start.11 = (f32[1032,128]{1,0:T(8,128)}, f32[1032,128]{1,0:T(8,128)}, u32[]{:S(2)}, u32[]{:S(2)}) collective-permute-start(f32[1032,128]{1,0:T(8,128)} %select_maximum_fusion.1), channel_id=1, source_target_pairs={{64,0},{72,8},{80,16},{88,24},{96,32},{104,40},{112,48},{120,56},{... | collective-permute-start | bytes 1585160 | tf_op jit(solution)/shard_map/ppermute | solution.py:40
  179.7 3.6 %copy-start.21 = (f32[256,256]{1,0:T(8,128)S(1)}, f32[256,256]{1,0:T(8,128)}, u32[]{:S(2)}) copy-start(f32[256,256]{1,0:T(8,128)} %get-tuple-element.313) | copy-start | bytes 786436
  181.2 3.4 %copy-start.13 = (f32[1,256,1,16,64]{1,4,3,2,0:T(8,128)S(1)}, f32[1,256,1,16,64]{1,4,3,2,0:T(8,128)}, u32[]{:S(2)}) copy-start(f32[1,256,1,16,64]{1,4,3,2,0:T(8,128)} %copy-done.12) | copy-start | bytes 3145732
  182.0 16.5 %collective-permute-start.12 = (f32[1032,128]{1,0:T(8,128)}, f32[1032,128]{1,0:T(8,128)}, u32[]{:S(2)}, u32[]{:S(2)}) collective-permute-start(f32[1032,128]{1,0:T(8,128)} %select_maximum_fusion), channel_id=1, source_target_pairs={{128,0},{136,8},{144,16},{152,24},{160,32},{168,40},{176,48},{184,... | collective-permute-start | bytes 1585160 | tf_op jit(solution)/shard_map/ppermute | solution.py:40
  202.2 2.8 %copy-start.24 = (f32[256,16]{0,1:T(8,128)S(1)}, f32[256,16]{0,1:T(8,128)}, u32[]{:S(2)}) copy-start(f32[256,16]{0,1:T(8,128)} %param.33) | copy-start | bytes 49156
  202.2 2.8 %copy-start.37 = (f32[1,1,1,16]{1,3,2,0:T(8,128)S(1)}, f32[1,1,1,16]{1,3,2,0:T(8,128)}, u32[]{:S(2)}) copy-start(f32[1,1,1,16]{1,3,2,0:T(8,128)} %get-tuple-element.346) | copy-start | bytes 196
  202.2 2.8 %copy-start.39 = (f32[256]{0:T(256)S(1)}, f32[256]{0:T(256)}, u32[]{:S(2)}) copy-start(f32[256]{0:T(256)} %copy-done.38) | copy-start | bytes 3076
  202.2 2.8 %copy-start.42 = (f32[16,256]{1,0:T(8,128)S(1)}, f32[16,256]{1,0:T(8,128)}, u32[]{:S(2)}) copy-start(f32[16,256]{1,0:T(8,128)} %get-tuple-element.310) | copy-start | bytes 49156
  202.2 2.8 %copy-start.43 = (f32[16,256]{1,0:T(8,128)S(1)}, f32[16,256]{1,0:T(8,128)}, u32[]{:S(2)}) copy-start(f32[16,256]{1,0:T(8,128)} %get-tuple-element.311) | copy-start | bytes 49156
  202.2 2.8 %copy-start.47 = (f32[16]{0:T(128)S(1)}, f32[16]{0:T(128)}, u32[]{:S(2)}) copy-start(f32[16]{0:T(128)} %copy-done.46) | copy-start | bytes 196
  202.2 2.8 %copy-start.49 = (f32[256]{0:T(256)S(1)}, f32[256]{0:T(256)}, u32[]{:S(2)}) copy-start(f32[256]{0:T(256)} %copy-done.48) | copy-start | bytes 3076
  202.2 2.8 %copy-start.52 = (f32[16]{0:T(128)S(1)}, f32[16]{0:T(128)}, u32[]{:S(2)}) copy-start(f32[16]{0:T(128)} %param.36) | copy-start | bytes 196
  202.2 8.4 %copy-start.23 = (f32[1,256,1,128]{3,1,2,0:T(8,128)S(1)}, f32[1,256,1,128]{3,1,2,0:T(8,128)}, u32[]{:S(2)}) copy-start(f32[1,256,1,128]{3,1,2,0:T(8,128)} %convolution_bitcast_fusion.2) | copy-start | bytes 393220
  202.3 8.4 %copy-start.30 = (f32[256,16]{0,1:T(8,128)S(1)}, f32[256,16]{0,1:T(8,128)}, u32[]{:S(2)}) copy-start(f32[256,16]{0,1:T(8,128)} %copy-done.29) | copy-start | bytes 49156
  205.0 9.3 %copy-start.45 = (f32[256,1,16]{0,2,1:T(8,128)S(1)}, f32[256,1,16]{0,2,1:T(8,128)}, u32[]{:S(2)}) copy-start(f32[256,1,16]{0,2,1:T(8,128)} %get-tuple-element.283) | copy-start | bytes 49156
  210.5 3.7 %copy-start.20 = (f32[256,16,64]{0,2,1:T(8,128)S(1)}, f32[256,16,64]{0,2,1:T(8,128)}, u32[]{:S(2)}) copy-start(f32[256,16,64]{0,2,1:T(8,128)} %get-tuple-element.352) | copy-start | bytes 3145732
  210.5 3.7 %copy-start.26 = (f32[256,256]{1,0:T(8,128)S(1)}, f32[256,256]{1,0:T(8,128)}, u32[]{:S(2)}) copy-start(f32[256,256]{1,0:T(8,128)} %fusion.76) | copy-start | bytes 786436
  214.2 4.9 %copy-start.3 = (bf16[256,1024]{0,1:T(8,128)(2,1)S(1)}, bf16[256,1024]{0,1:T(8,128)(2,1)}, u32[]{:S(2)}) copy-start(bf16[256,1024]{0,1:T(8,128)(2,1)} %copy-done.2) | copy-start | bytes 1572868
  214.3 4.9 %copy-start.11 = (f32[1,256,1,16,64]{1,4,3,2,0:T(8,128)S(1)}, f32[1,256,1,16,64]{1,4,3,2,0:T(8,128)}, u32[]{:S(2)}) copy-start(f32[1,256,1,16,64]{1,4,3,2,0:T(8,128)} %copy-done.10) | copy-start | bytes 3145732
  214.3 4.9 %copy-start.32 = (f32[1024]{0:T(1024)S(1)}, f32[1024]{0:T(1024)}, u32[]{:S(2)}) copy-start(f32[1024]{0:T(1024)} %param.39) | copy-start | bytes 12292
  214.3 4.9 %copy-start.34 = (f32[1024]{0:T(1024)S(1)}, f32[1024]{0:T(1024)}, u32[]{:S(2)}) copy-start(f32[1024]{0:T(1024)} %copy-done.33) | copy-start | bytes 12292
  214.3 4.9 %copy-start.41 = (f32[1,256]{1,0:T(1,128)S(1)}, f32[1,256]{1,0:T(1,128)}, u32[]{:S(2)}) copy-start(f32[1,256]{1,0:T(1,128)} %copy-done.40) | copy-start | bytes 3076
  214.3 4.9 %copy-start.51 = (f32[256]{0:T(256)S(1)}, f32[256]{0:T(256)}, u32[]{:S(2)}) copy-start(f32[256]{0:T(256)} %copy-done.50) | copy-start | bytes 3076
  221.1 2.6 %copy-start.14 = (bf16[256,1024]{0,1:T(8,128)(2,1)S(1)}, bf16[256,1024]{0,1:T(8,128)(2,1)}, u32[]{:S(2)}) copy-start(bf16[256,1024]{0,1:T(8,128)(2,1)} %get-tuple-element.348) | copy-start | bytes 1572868
  221.1 3.6 %copy-start.54 = (f32[16]{0:T(128)S(1)}, f32[16]{0:T(128)}, u32[]{:S(2)}) copy-start(f32[16]{0:T(128)} %copy-done.53) | copy-start | bytes 196
  (6 other events, 5.3 us)

commit v3 on v1

--- a/solution.py
+++ b/solution.py
@@ -12,24 +12,71 @@
 EPSILON = 1e-05
 
 
-def exclusive_scan(gain, value, axis, forward):
-    size = lax.axis_size(axis)
+def exclusive_scan(gain, value, move, count):
     total = jnp.zeros_like(value)
     total_gain = jnp.ones_like(gain)
     distance = 1
-    while distance < size:
-        if forward:
-            pairs = [(i, i + distance) for i in range(size - distance)]
-        else:
-            pairs = [(i + distance, i) for i in range(size - distance)]
-        gain_in, value_in = lax.ppermute((gain, value), axis, pairs)
+    while distance < count:
+        gain_in, value_in = move((gain, value), distance)
         total = total + total_gain[..., None, None] * value_in
         distance *= 2
-        if distance < size:
+        if distance < count:
             total_gain = total_gain * gain_in
             value = value + gain[..., None, None] * value_in
             gain = gain * gain_in
     return total
+
+
+def chip_scan(gain, value, axis, forward):
+    size = lax.axis_size(axis)
+    index = lax.axis_index(axis)
+    place = index if forward else size - 1 - index
+    second = place % 2
+    is_second = second == 1
+    half = value.shape[1] // 2
+
+    def device(p):
+        return p if forward else size - 1 - p
+
+    def move(tree, pairs):
+        return lax.ppermute(tree, axis, [(device(a), device(b)) for a, b in pairs])
+
+    def pick(array, which):
+        return lax.dynamic_slice_in_dim(array, which * half, half, axis=1)
+
+    partners = [(p, p ^ 1) for p in range(size)]
+    own_gain, own_value = pick(gain, second), pick(value, second)
+    got_gain, got_value = move((pick(gain, 1 - second), pick(value, 1 - second)), partners)
+    first_gain = jnp.where(is_second, got_gain, own_gain)
+    first_value = jnp.where(is_second, got_value, own_value)
+    second_gain = jnp.where(is_second, own_gain, got_gain)
+    second_value = jnp.where(is_second, own_value, got_value)
+    chip_value = second_gain[..., None, None] * first_value + second_value
+    chip_gain = first_gain * second_gain
+
+    def chip_move(tree, distance):
+        step = 2 * distance
+        return move(tree, [(p, p + step) for p in range(size - step)])
+
+    prefix = exclusive_scan(chip_gain, chip_value, chip_move, size // 2)
+    after_first = first_value + first_gain[..., None, None] * prefix
+    own_entry = jnp.where(is_second, after_first, prefix)
+    got_entry = move(jnp.where(is_second, prefix, after_first), partners)
+    return jnp.where(
+        is_second,
+        jnp.concatenate([got_entry, own_entry], axis=1),
+        jnp.concatenate([own_entry, got_entry], axis=1),
+    )
+
+
+def butterfly_sum(value, axis):
+    size = lax.axis_size(axis)
+    step = 1
+    while step < size:
+        pairs = [(i, i ^ step) for i in range(size)]
+        value = value + lax.ppermute(value, axis, pairs)
+        step *= 2
+    return value
 
 
 def span_mix(x_span, dt_span, b_span, c_span, log_cum, segment):
@@ -132,7 +179,7 @@
         return local_states(x_value, dt_value, b_value, segment, decay_rate)
 
     (starts, end_local, through_all), states_back = jax.vjp(states_call, x_spans, dt_spans, b_spans)
-    entry_state = exclusive_scan(through_all, end_local, "ctx", True)
+    entry_state = chip_scan(through_all, end_local, "ctx", True)
 
     def output_call(x_value, dt_value, b_value, c_value, start_value, entry_value):
         return output_part(
@@ -149,7 +196,7 @@
     gated = core_out * gate_act
     weighted_grad = norm_weight[None, :] * grad_output.astype(jnp.float32)
     norm_width = lax.axis_size("head") * gated.shape[1]
-    sums = lax.psum(
+    sums = butterfly_sum(
         jnp.stack([jnp.sum(gated * gated, axis=1), jnp.sum(weighted_grad * gated, axis=1)]),
         "head",
     )
@@ -160,7 +207,7 @@
     grad_core = grad_gated * gate_act
     grad_gate = grad_gated * core_out * gate_sig * (1.0 + gate_float * (1.0 - gate_sig))
     first_grads = output_back(grad_core.reshape(core_part.shape))
-    exit_adjoint = exclusive_scan(through_all, first_grads[5], "ctx", False)
+    exit_adjoint = chip_scan(through_all, first_grads[5], "ctx", False)
     through_grad = jnp.sum(exit_adjoint * entry_state, axis=(2, 3))
     second_grads = states_back((first_grads[4], exit_adjoint, through_grad))
     grad_input = (first_grads[0] + second_grads[0]).reshape(

time: 212 us -> 174 us (0.82)
  waiting for transfers between devices: 75.1 us -> 53.3 us
  blocking collectives: 20 us -> 0 us
  matrix products: 26.9 us -> 29.7 us
    ppermute x18 -> x23, waiting for transfers between devices: 75.1 us -> 53.3 us  [the longest x20 48.5 us: move(): return lax.ppermute(tree, axis, [(device(a), device(b)) for a, b in pairs])]
    psum x1 -> x0, blocking collectives: 20 us -> none  [body(): lax.psum(jnp.stack([jnp.sum(gated * gated, axis=1), jnp.sum(weighted_grad...]
    select_n x0 -> x4, other arithmetic: none -> 2.96 us  [the longest x2 1.81 us: chip_scan(): own_entry = jnp.where(is_second, after_first, prefix)]
    ppermute x18 -> x23, starting transfers between devices: 53.7 us -> 52.3 us  [the longest x20 40 us: move(): return lax.ppermute(tree, axis, [(device(a), device(b)) for a, b in pairs])]
    unnamed x113 -> x93, local copies, waits for them, and re-layouts: 6.2 us -> 6.94 us
  transfers between devices with their start and end apart: 18 -> 23, of which waited for: 14 -> 14; matrix products, arithmetic and copies ran while one was open for 8% -> 15% of each run, Pallas kernels for 0% -> 0%
where the time goes in v3:
time: 174 us; the launch traced here: 172 us
  waiting for transfers between devices  53.3 us (31%)
  starting transfers between devices  52.3 us (30%)
  matrix products  29.7 us (17%)
  other arithmetic  22.3 us (13%)
  local copies, waits for them, and re-layouts  11 us (6%)
  between operations  2.92 us (2%)
    ppermute x20, waiting for transfers between devices, move(): return lax.ppermute(tree, axis, [(device(a), device(b)) for a, b in pairs])  48.5 us
    ppermute x20, starting transfers between devices, move(): return lax.ppermute(tree, axis, [(device(a), device(b)) for a, b in pairs])  40 us
    dot_general x3, matrix products, span_mix(): jnp.einsum('ghts,sghp->tghp', weights, x_span, precision=HIGHEST_PRECISION)  16.4 us
    ppermute x3, starting transfers between devices, butterfly_sum(): value = value + lax.ppermute(value, axis, pairs)  12.3 us
    another operation x10, other arithmetic  7.73 us
    unnamed x93, local copies, waits for them, and re-layouts  6.94 us
    dot_general x3, matrix products, local_states(): jnp.einsum('kqgh,kqghp,kqgn->kghpn', tail_decay * dt_spans, x_spans, b_sp...  6.77 us
    ppermute x3, waiting for transfers between devices, butterfly_sum(): value = value + lax.ppermute(value, axis, pairs)  4.8 us
  transfers between devices with their start and end apart: 23, of which 14 were waited for; matrix products, arithmetic and copies ran while one was open for 15% of the time, Pallas kernels for 0%

profile of v3, /device:TPU:6, one launch (start us, length us, event | category | flops | bytes accessed | tf_op | source)
XLA Modules:
  0.0 171.6 jit_solution(17843173875594263411)
XLA Ops:
  0.7 0.7 exponential_negate_fusion
  1.3 1.4 fusion.126
  3.5 1.0 reduce-window.30
  8.4 0.8 fusion.109
  9.2 0.8 fusion.105
  10.0 1.2 copy.79
  11.3 0.7 fusion.45
  12.2 0.7 dynamic-slice_reduce_fusion.1
  13.4 0.8 collective-permute-done
  14.3 3.4 %collective-permute-start.2 = (f32[1,8,64,128]{3,2,1,0:T(8,128)S(1)}, f32[1,8,64,128]{3,2,1,0:T(8,128)S(1)}, u32[]{:S(2)}, u32[]{:S(2)}) collective-permute-start(f32[1,8,64,128]{3,2,1,0:T(8,128)S(1)} %fusion.77), channel_id=1, source_target_pairs={{0,16},{8,24},{16,32},{24,40},{32,48},{40,56},{48,64},{56,72},{64,... | collective-permute-start | bytes 786440 | tf_op jit(solution)/shard_map/ppermute | solution.py:42
  17.7 7.0 %collective-permute-done.2 = f32[1,8,64,128]{3,2,1,0:T(8,128)S(1)} collective-permute-done((f32[1,8,64,128]{3,2,1,0:T(8,128)S(1)}, f32[1,8,64,128]{3,2,1,0:T(8,128)S(1)}, u32[]{:S(2)}, u32[]{:S(2)}) %collective-permute-start.2) | collective-permute-done | bytes 262176 | tf_op jit(solution)/shard_map/ppermute | solution.py:42
  24.8 4.3 %collective-permute-start.4 = (f32[1,8,64,128]{3,2,1,0:T(8,128)S(1)}, f32[1,8,64,128]{3,2,1,0:T(8,128)S(1)}, u32[]{:S(2)}, u32[]{:S(2)}) collective-permute-start(f32[1,8,64,128]{3,2,1,0:T(8,128)S(1)} %multiply_add_fusion.9), channel_id=1, source_target_pairs={{0,32},{8,40},{16,48},{24,56},{32,64},{40,72},{48,80},{56,88},{64,... | collective-permute-start | bytes 786440 | tf_op jit(solution)/shard_map/ppermute | solution.py:42
  29.2 4.0 %collective-permute-start.3 = (f32[1,8]{1,0:T(1,128)S(1)}, f32[1,8]{1,0:T(1,128)S(1)}, u32[]{:S(2)}, u32[]{:S(2)}) collective-permute-start(f32[1,8]{1,0:T(1,128)S(1)} %get-tuple-element.230), channel_id=1, source_target_pairs={{0,16},{8,24},{16,32},{24,40},{32,48},{40,56},{48,64},{56,72},{64,... | collective-permute-start | bytes 104 | tf_op jit(solution)/shard_map/ppermute | solution.py:42
  33.2 3.7 %collective-permute-done.3 = f32[1,8]{1,0:T(1,128)S(1)} collective-permute-done((f32[1,8]{1,0:T(1,128)S(1)}, f32[1,8]{1,0:T(1,128)S(1)}, u32[]{:S(2)}, u32[]{:S(2)}) %collective-permute-start.3) | collective-permute-done | bytes 64 | tf_op jit(solution)/shard_map/ppermute | solution.py:42
  37.0 3.5 %collective-permute-start.6 = (f32[1,8,64,128]{3,2,1,0:T(8,128)S(1)}, f32[1,8,64,128]{3,2,1,0:T(8,128)S(1)}, u32[]{:S(2)}, u32[]{:S(2)}) collective-permute-start(f32[1,8,64,128]{3,2,1,0:T(8,128)S(1)} %multiply_add_fusion.8), channel_id=1, source_target_pairs={{0,64},{8,72},{16,80},{24,88},{32,96},{40,104},{48,112},{56,120},{... | collective-permute-start | bytes 786440 | tf_op jit(solution)/shard_map/ppermute | solution.py:42
  40.5 4.3 %collective-permute-start.5 = (f32[1,8]{1,0:T(1,128)S(1)}, f32[1,8]{1,0:T(1,128)S(1)}, u32[]{:S(2)}, u32[]{:S(2)}) collective-permute-start(f32[1,8]{1,0:T(1,128)S(1)} %mul.725), channel_id=1, source_target_pairs={{0,32},{8,40},{16,48},{24,56},{32,64},{40,72},{48,80},{56,88},{64,... | collective-permute-start | bytes 104 | tf_op jit(solution)/shard_map/ppermute | solution.py:42
  44.7 2.7 %collective-permute-done.5 = f32[1,8]{1,0:T(1,128)S(1)} collective-permute-done((f32[1,8]{1,0:T(1,128)S(1)}, f32[1,8]{1,0:T(1,128)S(1)}, u32[]{:S(2)}, u32[]{:S(2)}) %collective-permute-start.5) | collective-permute-done | bytes 64 | tf_op jit(solution)/shard_map/ppermute | solution.py:42
  47.5 3.9 %collective-permute-start.8 = (f32[1,8,64,128]{3,2,1,0:T(8,128)S(1)}, f32[1,8,64,128]{3,2,1,0:T(8,128)S(1)}, u32[]{:S(2)}, u32[]{:S(2)}) collective-permute-start(f32[1,8,64,128]{3,2,1,0:T(8,128)S(1)} %multiply_add_fusion.7), channel_id=1, source_target_pairs={{0,128},{8,136},{16,144},{24,152},{32,160},{40,168},{48,176},{56,1... | collective-permute-start | bytes 786440 | tf_op jit(solution)/shard_map/ppermute | solution.py:42
  51.4 0.9 fusion.130
  52.3 1.3 collective-permute-start.7
  53.6 1.7 collective-permute-done.7
  55.6 0.8 fusion.84
  56.5 0.7 mul.749
  57.2 1.2 copy.85
  58.4 1.2 copy.86
  59.7 0.7 fusion.80
  61.1 1.0 copy-done
  62.1 3.3 %fusion.37 = f32[1,256,1,16,64]{1,4,3,2,0:T(8,128)S(1)} fusion(bf16[256,16,64]{0,2,1:T(8,128)(2,1)S(1)} %bitcast.331, f32[16,256]{1,0:T(8,128)S(1)} %copy-done.32, f32[256,256]{1,0:T(8,128)S(1)} %copy-done.12, f32[16,256]{1,0:T(8,128)S(1)} %bitcast.341, f32[256,256]{1,0:T(8,128)S(1)} %copy-done.7, f32[1,256,1,16,64]{1,4,3,2,0:T(8,128)S(1)} %convolution_bitcast_fusion.1, ...), kind=kOutput, calls=%fused_computation.40 | convolution fusion | flops 811073536 | bytes 3194880 | tf_op jit(solution)/shard_map/jvp()/while/body/eval_jaxpr/ghts,sghp->tghp/dot_general | solution.py:92
  66.0 2.0 %collective-permute-start.10 = (f32[2,256]{1,0:T(2,128)S(1)}, f32[2,256]{1,0:T(2,128)S(1)}, u32[]{:S(2)}, u32[]{:S(2)}) collective-permute-start(f32[2,256]{1,0:T(2,128)S(1)} %pad_maximum_fusion), channel_id=1, source_target_pairs={{0,1},{1,0},{2,3},{3,2},{4,5},{5,4},{6,7},{7,6},{8,9},{9,8},{10,11... | collective-permute-start | bytes 6152 | tf_op jit(solution)/shard_map/ppermute | solution.py:77
  68.0 1.7 collective-permute-done.10
  69.7 3.4 %collective-permute-start.11 = (f32[2,256]{1,0:T(2,128)S(1)}, f32[2,256]{1,0:T(2,128)S(1)}, u32[]{:S(2)}, u32[]{:S(2)}) collective-permute-start(f32[2,256]{1,0:T(2,128)S(1)} %fusion.125), channel_id=1, source_target_pairs={{0,2},{1,3},{2,0},{3,1},{4,6},{5,7},{6,4},{7,5},{8,10},{9,11},{10,... | collective-permute-start | bytes 6152 | tf_op jit(solution)/shard_map/ppermute | solution.py:77
  73.0 1.6 collective-permute-done.11
  74.6 6.9 %collective-permute-start.12 = (f32[2,256]{1,0:T(2,128)S(1)}, f32[2,256]{1,0:T(2,128)S(1)}, u32[]{:S(2)}, u32[]{:S(2)}) collective-permute-start(f32[2,256]{1,0:T(2,128)S(1)} %fusion.136), channel_id=1, source_target_pairs={{0,4},{1,5},{2,6},{3,7},{4,0},{5,1},{6,2},{7,3},{8,12},{9,13},{10,... | collective-permute-start | bytes 6152 | tf_op jit(solution)/shard_map/ppermute | solution.py:77
  81.6 1.6 collective-permute-done.12
  83.1 1.6 fusion.55
  86.2 0.8 collective-permute-done.14
  87.2 2.7 %collective-permute-start.15 = (f32[1,8,64,128]{3,2,1,0:T(8,128)S(1)}, f32[1,8,64,128]{3,2,1,0:T(8,128)S(1)}, u32[]{:S(2)}, u32[]{:S(2)}) collective-permute-start(f32[1,8,64,128]{3,2,1,0:T(8,128)S(1)} %fusion.76), channel_id=1, source_target_pairs={{248,232},{240,224},{232,216},{224,208},{216,200},{208,192},{200,1... | collective-permute-start | bytes 786440 | tf_op jit(solution)/shard_map/ppermute | solution.py:42
  90.0 4.2 %collective-permute-start.16 = (f32[1,8]{1,0:T(1,128)S(1)}, f32[1,8]{1,0:T(1,128)S(1)}, u32[]{:S(2)}, u32[]{:S(2)}) collective-permute-start(f32[1,8]{1,0:T(1,128)S(1)} %get-tuple-element.225), channel_id=1, source_target_pairs={{248,232},{240,224},{232,216},{224,208},{216,200},{208,192},{200,1... | collective-permute-start | bytes 104 | tf_op jit(solution)/shard_map/ppermute | solution.py:42
  94.3 7.8 %collective-permute-done.16 = f32[1,8]{1,0:T(1,128)S(1)} collective-permute-done((f32[1,8]{1,0:T(1,128)S(1)}, f32[1,8]{1,0:T(1,128)S(1)}, u32[]{:S(2)}, u32[]{:S(2)}) %collective-permute-start.16) | collective-permute-done | bytes 64 | tf_op jit(solution)/shard_map/ppermute | solution.py:42
  102.0 1.9 %collective-permute-start.18 = (f32[1,8]{1,0:T(1,128)S(1)}, f32[1,8]{1,0:T(1,128)S(1)}, u32[]{:S(2)}, u32[]{:S(2)}) collective-permute-start(f32[1,8]{1,0:T(1,128)S(1)} %mul.785), channel_id=1, source_target_pairs={{248,216},{240,208},{232,200},{224,192},{216,184},{208,176},{200,1... | collective-permute-start | bytes 104 | tf_op jit(solution)/shard_map/ppermute | solution.py:42
  104.0 5.9 %collective-permute-done.18 = f32[1,8]{1,0:T(1,128)S(1)} collective-permute-done((f32[1,8]{1,0:T(1,128)S(1)}, f32[1,8]{1,0:T(1,128)S(1)}, u32[]{:S(2)}, u32[]{:S(2)}) %collective-permute-start.18) | collective-permute-done | bytes 64 | tf_op jit(solution)/shard_map/ppermute | solution.py:42
  109.9 1.3 collective-permute-start.20
  111.2 4.2 %collective-permute-done.20 = f32[1,8]{1,0:T(1,128)S(1)} collective-permute-done((f32[1,8]{1,0:T(1,128)S(1)}, f32[1,8]{1,0:T(1,128)S(1)}, u32[]{:S(2)}, u32[]{:S(2)}) %collective-permute-start.20) | collective-permute-done | bytes 64 | tf_op jit(solution)/shard_map/ppermute | solution.py:42
  115.5 1.9 %collective-permute-start.17 = (f32[1,8,64,128]{3,2,1,0:T(8,128)S(1)}, f32[1,8,64,128]{3,2,1,0:T(8,128)S(1)}, u32[]{:S(2)}, u32[]{:S(2)}) collective-permute-start(f32[1,8,64,128]{3,2,1,0:T(8,128)S(1)} %multiply_add_fusion.4), channel_id=1, source_target_pairs={{248,216},{240,208},{232,200},{224,192},{216,184},{208,176},{200,1... | collective-permute-start | bytes 786440 | tf_op jit(solution)/shard_map/ppermute | solution.py:42
  117.9 8.2 %collective-permute-done.17 = f32[1,8,64,128]{3,2,1,0:T(8,128)S(1)} collective-permute-done((f32[1,8,64,128]{3,2,1,0:T(8,128)S(1)}, f32[1,8,64,128]{3,2,1,0:T(8,128)S(1)}, u32[]{:S(2)}, u32[]{:S(2)}) %collective-permute-start.17) | collective-permute-done | bytes 262176 | tf_op jit(solution)/shard_map/ppermute | solution.py:42
  126.2 1.3 collective-permute-start.19
  127.5 8.2 %fusion.75 = (f32[16,256]{1,0:T(8,128)}, f32[16,256]{1,0:T(8,128)}, f32[16,256]{1,0:T(8,128)}, f32[256,256]{1,0:T(8,128)S(1)}) fusion(f32[16,256]{1,0:T(8,128)S(1)} %bitcast.342, f32[256,256]{1,0:T(8,128)S(1)} %fusion.85, f32[16,256]{1,0:T(8,128)S(1)} %bitcast.356, f32[256,256]{1,0:T(8,128)S(1)} %fusion.91, f32[256,1,16,64]{0,3,2,1:T(8,128)S(1)} %convert.9, ...), kind=kOutput, calls=%fused_computation.91 | convolution fusion | flops 825151488 | bytes 2965504 | tf_op jit(solution)/shard_map/transpose(jvp())/while/body/eval_jaxpr/checkpoint/ghts,sghp->tghp/dot_general | solution.py:92
  135.7 0.8 multiply_reduce_fusion
  136.7 1.3 collective-permute-start.21
  138.0 1.8 %convolution_bitcast_fusion.3 = f32[256,128]{1,0:T(8,128)S(1)} fusion(f32[1,256,1,16,64]{1,4,3,2,0:T(8,128)S(1)} %bitcast.328, f32[256,16]{0,1:T(8,128)S(1)} %copy-done.14, f32[8,64,128]{2,1,0:T(8,128)S(1)} %bitcast.335, f32[8,64,128]{2,1,0:T(8,128)S(1)} %bitcast.339, pred[]{:T(512)S(6)} %eq.98), kind=kOutput, calls=%fused_computation.50 | convolution fusion | flops 403308544 | bytes 1720321 | tf_op jit(solution)/shard_map/transpose(jvp(kqgn,kghpn->kqghp))/dot_general | solution.py:141
  139.8 1.0 convolution_add_fusion
  140.8 5.6 %collective-permute-done.21 = f32[1,8,64,128]{3,2,1,0:T(8,128)S(1)} collective-permute-done((f32[1,8,64,128]{3,2,1,0:T(8,128)S(1)}, f32[1,8,64,128]{3,2,1,0:T(8,128)S(1)}, u32[]{:S(2)}, u32[]{:S(2)}) %collective-permute-start.21) | collective-permute-done | bytes 262176 | tf_op jit(solution)/shard_map/ppermute | solution.py:42
  146.4 1.0 fusion.79
  147.4 1.3 convolution_bitcast_fusion.2
  148.7 1.0 copy.99
  149.7 1.1 fusion.78
  150.9 2.6 %fusion.49 = (f32[256,16]{0,1:T(8,128)S(1)}, f32[256,16,64]{0,2,1:T(8,128)}) fusion(bf16[256,1024]{0,1:T(8,128)(2,1)S(1)} %copy.79, bf16[256,128]{1,0:T(8,128)(2,1)S(1)} %copy-done.5, f32[8,64,128]{2,1,0:T(8,128)S(1)} %bitcast.336, f32[8,64,128]{2,1,0:T(8,128)} %bitcast.80, pred[]{:T(512)S(6)} %eq.108), kind=kOutput, calls=%fused_computation.53 | convolution fusion | flops 403828736 | bytes 2179073 | tf_op jit(solution)/shard_map/transpose(jvp(kqgh,kqghp,kqgn->kghpn))/dot_general | solution.py:106
  153.9 1.3 multiply_reduce_fusion.3
  155.4 2.5 %reduce-window.36 = f32[1,16,1,2,128]{4,1,2,3,0:T(8,128)S(1)} reduce-window(f32[1,16,1,2,128]{4,1,2,3,0:T(8,128)S(1)} %copy_bitcast_fusion, f32[]{:T(128)} %constant.154.clone.1), window={size=1x1x1x1x128 pad=0_0x0_0x0_0x0_0x0_127}, to_apply=%region_15.16 | reduce-window | flops 520192 | bytes 32772 | tf_op jit(solution)/shard_map/reduce-window.6
  158.0 2.5 %reduce-window.34 = f32[1,16,1,2,128]{4,1,2,3,0:T(8,128)S(1)} reduce-window(f32[1,16,1,2,128]{4,1,2,3,0:T(8,128)S(1)} %bitcast.348, f32[]{:T(128)} %constant.154.clone.1), window={size=1x1x1x1x128 pad=0_0x0_0x0_0x0_0x0_127}, to_apply=%region_10.11 | reduce-window | flops 520192 | bytes 32772 | tf_op jit(solution)/shard_map/reduce-window.4
  160.7 3.5 %fusion.48 = f32[256,128]{1,0:T(8,128)} fusion(f32[1,256,1,128]{3,1,2,0:T(8,128)S(1)} %copy-done.15, bf16[256,16,64]{0,2,1:T(8,128)(2,1)S(1)} %bitcast.333, f32[256,16]{0,1:T(8,128)S(1)} %copy-done.19, f32[8,64,128]{2,1,0:T(8,128)S(1)} %bitcast.337, f32[8,64,128]{2,1,0:T(8,128)} %bitcast.80, pred[]{:T(512)S(6)} %eq.108), kind=kOutput, calls=%fused_computation.52 | convolution fusion | flops 403603456 | bytes 1327105 | tf_op jit(solution)/shard_map/transpose(jvp(kqgh,kqghp,kqgn->kghpn))/dot_general | solution.py:106
  164.7 5.0 %fusion.40 = f32[256,16,64]{0,2,1:T(8,128)S(1)} fusion(f32[16,256]{1,0:T(8,128)S(1)} %bitcast.357, f32[256,256]{1,0:T(8,128)S(1)} %copy-done.9, f32[16,256]{1,0:T(8,128)S(1)} %bitcast.344, f32[256,256]{1,0:T(8,128)S(1)} %copy-done.11, f32[256,1,16,64]{0,3,2,1:T(8,128)S(1)} %bitcast.329, f32[256,16,64]{0,2,1:T(8,128)} %get-tuple-element.234, ...), kind=kOutput, calls=%fused_computation.41 | convolution fusion | flops 811073536 | bytes 3719168 | tf_op jit(solution)/shard_map/transpose(jvp())/while/body/eval_jaxpr/checkpoint/ghts,sghp->tghp/dot_general | solution.py:92
  169.9 1.0 copy.98
  170.9 0.7 fusion.103
  (177 shorter events, 9.8 us)
Async XLA Ops:
  0.6 10.7 %copy-start.4 = (bf16[256,128]{1,0:T(8,128)(2,1)S(1)}, bf16[256,128]{1,0:T(8,128)(2,1)}, u32[]{:S(2)}) copy-start(bf16[256,128]{1,0:T(8,128)(2,1)} %param.14) | copy-start | bytes 196612
  1.3 1.4 copy-start.40
  5.0 6.3 %copy-start.33 = (f32[256]{0:T(256)}, f32[256]{0:T(256)S(1)}, u32[]{:S(2)}) copy-start(f32[256]{0:T(256)S(1)} %get-tuple-element.208) | copy-start | bytes 3076
  5.0 50.6 %copy-start.21 = (s32[256]{0:T(256)}, s32[256]{0:T(256)S(1)}, u32[]{:S(2)}) copy-start(s32[256]{0:T(256)S(1)} %get-tuple-element.121) | copy-start | bytes 3076
  9.2 2.1 %copy-start.36 = (f32[16]{0:T(128)}, f32[16]{0:T(128)S(1)}, u32[]{:S(2)}) copy-start(f32[16]{0:T(128)S(1)} %get-tuple-element.219) | copy-start | bytes 196
  9.2 2.1 %copy-start.25 = (f32[256]{0:T(256)}, f32[256]{0:T(256)S(1)}, u32[]{:S(2)}) copy-start(f32[256]{0:T(256)S(1)} %compare_convert_fusion.1) | copy-start | bytes 3076
  10.0 1.3 copy-start.18
  12.0 2.2 %collective-permute-start.1 = (f32[1,8,64,128]{3,2,1,0:T(8,128)S(1)}, f32[1,8,64,128]{3,2,1,0:T(8,128)S(1)}, u32[]{:S(2)}, u32[]{:S(2)}) collective-permute-start(f32[1,8,64,128]{3,2,1,0:T(8,128)S(1)} %dynamic-slice_bitcast_fusion.1), channel_id=1, source_target_pairs={{0,8},{8,0},{16,24},{24,16},{32,40},{40,32},{48,56},{56,48},{64,72... | collective-permute-start | bytes 786440 | tf_op jit(solution)/shard_map/ppermute | solution.py:42
  12.9 1.3 collective-permute-start
  14.2 41.1 %copy-start.39 = (f32[8]{0:T(128)}, f32[8]{0:T(128)S(1)}, u32[]{:S(2)}) copy-start(f32[8]{0:T(128)S(1)} %get-tuple-element.231) | copy-start | bytes 100
  14.3 10.4 %collective-permute-start.2 = (f32[1,8,64,128]{3,2,1,0:T(8,128)S(1)}, f32[1,8,64,128]{3,2,1,0:T(8,128)S(1)}, u32[]{:S(2)}, u32[]{:S(2)}) collective-permute-start(f32[1,8,64,128]{3,2,1,0:T(8,128)S(1)} %fusion.77), channel_id=1, source_target_pairs={{0,16},{8,24},{16,32},{24,40},{32,48},{40,56},{48,64},{56,72},{64,... | collective-permute-start | bytes 786440 | tf_op jit(solution)/shard_map/ppermute | solution.py:42
  24.7 26.7 %copy-start.3 = (bf16[256,128]{1,0:T(8,128)(2,1)S(1)}, bf16[256,128]{1,0:T(8,128)(2,1)}, u32[]{:S(2)}) copy-start(bf16[256,128]{1,0:T(8,128)(2,1)} %param.15) | copy-start | bytes 196612
  24.8 12.0 %collective-permute-start.4 = (f32[1,8,64,128]{3,2,1,0:T(8,128)S(1)}, f32[1,8,64,128]{3,2,1,0:T(8,128)S(1)}, u32[]{:S(2)}, u32[]{:S(2)}) collective-permute-start(f32[1,8,64,128]{3,2,1,0:T(8,128)S(1)} %multiply_add_fusion.9), channel_id=1, source_target_pairs={{0,32},{8,40},{16,48},{24,56},{32,64},{40,72},{48,80},{56,88},{64,... | collective-permute-start | bytes 786440 | tf_op jit(solution)/shard_map/ppermute | solution.py:42
  29.2 7.7 %collective-permute-start.3 = (f32[1,8]{1,0:T(1,128)S(1)}, f32[1,8]{1,0:T(1,128)S(1)}, u32[]{:S(2)}, u32[]{:S(2)}) collective-permute-start(f32[1,8]{1,0:T(1,128)S(1)} %get-tuple-element.230), channel_id=1, source_target_pairs={{0,16},{8,24},{16,32},{24,40},{32,48},{40,56},{48,64},{56,72},{64,... | collective-permute-start | bytes 104 | tf_op jit(solution)/shard_map/ppermute | solution.py:42
  37.0 10.5 %collective-permute-start.6 = (f32[1,8,64,128]{3,2,1,0:T(8,128)S(1)}, f32[1,8,64,128]{3,2,1,0:T(8,128)S(1)}, u32[]{:S(2)}, u32[]{:S(2)}) collective-permute-start(f32[1,8,64,128]{3,2,1,0:T(8,128)S(1)} %multiply_add_fusion.8), channel_id=1, source_target_pairs={{0,64},{8,72},{16,80},{24,88},{32,96},{40,104},{48,112},{56,120},{... | collective-permute-start | bytes 786440 | tf_op jit(solution)/shard_map/ppermute | solution.py:42
  40.5 7.0 %collective-permute-start.5 = (f32[1,8]{1,0:T(1,128)S(1)}, f32[1,8]{1,0:T(1,128)S(1)}, u32[]{:S(2)}, u32[]{:S(2)}) collective-permute-start(f32[1,8]{1,0:T(1,128)S(1)} %mul.725), channel_id=1, source_target_pairs={{0,32},{8,40},{16,48},{24,56},{32,64},{40,72},{48,80},{56,88},{64,... | collective-permute-start | bytes 104 | tf_op jit(solution)/shard_map/ppermute | solution.py:42
  47.5 7.8 %collective-permute-start.8 = (f32[1,8,64,128]{3,2,1,0:T(8,128)S(1)}, f32[1,8,64,128]{3,2,1,0:T(8,128)S(1)}, u32[]{:S(2)}, u32[]{:S(2)}) collective-permute-start(f32[1,8,64,128]{3,2,1,0:T(8,128)S(1)} %multiply_add_fusion.7), channel_id=1, source_target_pairs={{0,128},{8,136},{16,144},{24,152},{32,160},{40,168},{48,176},{56,1... | collective-permute-start | bytes 786440 | tf_op jit(solution)/shard_map/ppermute | solution.py:42
  52.3 3.0 %collective-permute-start.7 = (f32[1,8]{1,0:T(1,128)S(1)}, f32[1,8]{1,0:T(1,128)S(1)}, u32[]{:S(2)}, u32[]{:S(2)}) collective-permute-start(f32[1,8]{1,0:T(1,128)S(1)} %mul.733), channel_id=1, source_target_pairs={{0,64},{8,72},{16,80},{24,88},{32,96},{40,104},{48,112},{56,120},{... | collective-permute-start | bytes 104 | tf_op jit(solution)/shard_map/ppermute | solution.py:42
  55.3 1.1 copy-start.43
  55.5 4.9 %collective-permute-start.9 = (f32[1,8,64,128]{3,2,1,0:T(8,128)S(1)}, f32[1,8,64,128]{3,2,1,0:T(8,128)S(1)}, u32[]{:S(2)}, u32[]{:S(2)}) collective-permute-start(f32[1,8,64,128]{3,2,1,0:T(8,128)S(1)} %get-tuple-element.210), channel_id=1, source_target_pairs={{0,8},{8,0},{16,24},{24,16},{32,40},{40,32},{48,56},{56,48},{64,72... | collective-permute-start | bytes 786440 | tf_op jit(solution)/shard_map/ppermute | solution.py:42
  60.4 1.7 copy-start.7
  60.4 1.7 copy-start.12
  60.4 1.6 copy-start.13
  60.4 1.6 copy-start.32
  62.1 3.3 %copy-start.16 = (f32[1024]{0:T(1024)S(1)}, f32[1024]{0:T(1024)}, u32[]{:S(2)}) copy-start(f32[1024]{0:T(1024)} %mul.749) | copy-start | bytes 12292
  62.1 3.3 %copy-start.24 = (f32[1024]{0:T(1024)S(1)}, f32[1024]{0:T(1024)}, u32[]{:S(2)}) copy-start(f32[1024]{0:T(1024)} %param.19) | copy-start | bytes 12292
  66.0 3.7 %collective-permute-start.10 = (f32[2,256]{1,0:T(2,128)S(1)}, f32[2,256]{1,0:T(2,128)S(1)}, u32[]{:S(2)}, u32[]{:S(2)}) collective-permute-start(f32[2,256]{1,0:T(2,128)S(1)} %pad_maximum_fusion), channel_id=1, source_target_pairs={{0,1},{1,0},{2,3},{3,2},{4,5},{5,4},{6,7},{7,6},{8,9},{9,8},{10,11... | collective-permute-start | bytes 6152 | tf_op jit(solution)/shard_map/ppermute | solution.py:77
  69.7 4.9 %collective-permute-start.11 = (f32[2,256]{1,0:T(2,128)S(1)}, f32[2,256]{1,0:T(2,128)S(1)}, u32[]{:S(2)}, u32[]{:S(2)}) collective-permute-start(f32[2,256]{1,0:T(2,128)S(1)} %fusion.125), channel_id=1, source_target_pairs={{0,2},{1,3},{2,0},{3,1},{4,6},{5,7},{6,4},{7,5},{8,10},{9,11},{10,... | collective-permute-start | bytes 6152 | tf_op jit(solution)/shard_map/ppermute | solution.py:77
  74.6 8.5 %collective-permute-start.12 = (f32[2,256]{1,0:T(2,128)S(1)}, f32[2,256]{1,0:T(2,128)S(1)}, u32[]{:S(2)}, u32[]{:S(2)}) collective-permute-start(f32[2,256]{1,0:T(2,128)S(1)} %fusion.136), channel_id=1, source_target_pairs={{0,4},{1,5},{2,6},{3,7},{4,0},{5,1},{6,2},{7,3},{8,12},{9,13},{10,... | collective-permute-start | bytes 6152 | tf_op jit(solution)/shard_map/ppermute | solution.py:77
  81.6 4.0 %collective-permute-start.13 = (f32[1,8]{1,0:T(1,128)}, f32[1,8]{1,0:T(1,128)}, u32[]{:S(2)}, u32[]{:S(2)}) collective-permute-start(f32[1,8]{1,0:T(1,128)} %bitcast.140), channel_id=1, source_target_pairs={{248,240},{240,248},{232,224},{224,232},{216,208},{208,216},{200,1... | collective-permute-start | bytes 104 | tf_op jit(solution)/shard_map/ppermute | solution.py:42
  85.4 1.6 collective-permute-start.14
  86.2 60.2 %copy-start.38 = (f32[8]{0:T(128)}, f32[8]{0:T(128)S(1)}, u32[]{:S(2)}) copy-start(f32[8]{0:T(128)S(1)} %get-tuple-element.226) | copy-start | bytes 100
  87.2 28.2 %collective-permute-start.15 = (f32[1,8,64,128]{3,2,1,0:T(8,128)S(1)}, f32[1,8,64,128]{3,2,1,0:T(8,128)S(1)}, u32[]{:S(2)}, u32[]{:S(2)}) collective-permute-start(f32[1,8,64,128]{3,2,1,0:T(8,128)S(1)} %fusion.76), channel_id=1, source_target_pairs={{248,232},{240,224},{232,216},{224,208},{216,200},{208,192},{200,1... | collective-permute-start | bytes 786440 | tf_op jit(solution)/shard_map/ppermute | solution.py:42
  89.9 27.5 %copy-start.22 = (s32[256]{0:T(256)S(1)}, s32[256]{0:T(256)}, u32[]{:S(2)}) copy-start(s32[256]{0:T(256)} %copy-done.21) | copy-start | bytes 3076
  90.0 12.0 %collective-permute-start.16 = (f32[1,8]{1,0:T(1,128)S(1)}, f32[1,8]{1,0:T(1,128)S(1)}, u32[]{:S(2)}, u32[]{:S(2)}) collective-permute-start(f32[1,8]{1,0:T(1,128)S(1)} %get-tuple-element.225), channel_id=1, source_target_pairs={{248,232},{240,224},{232,216},{224,208},{216,200},{208,192},{200,1... | collective-permute-start | bytes 104 | tf_op jit(solution)/shard_map/ppermute | solution.py:42
  102.0 7.9 %collective-permute-start.18 = (f32[1,8]{1,0:T(1,128)S(1)}, f32[1,8]{1,0:T(1,128)S(1)}, u32[]{:S(2)}, u32[]{:S(2)}) collective-permute-start(f32[1,8]{1,0:T(1,128)S(1)} %mul.785), channel_id=1, source_target_pairs={{248,216},{240,208},{232,200},{224,192},{216,184},{208,176},{200,1... | collective-permute-start | bytes 104 | tf_op jit(solution)/shard_map/ppermute | solution.py:42
  109.9 5.5 %collective-permute-start.20 = (f32[1,8]{1,0:T(1,128)S(1)}, f32[1,8]{1,0:T(1,128)S(1)}, u32[]{:S(2)}, u32[]{:S(2)}) collective-permute-start(f32[1,8]{1,0:T(1,128)S(1)} %mul.793), channel_id=1, source_target_pairs={{248,184},{240,176},{232,168},{224,160},{216,152},{208,144},{200,1... | collective-permute-start | bytes 104 | tf_op jit(solution)/shard_map/ppermute | solution.py:42
  115.4 12.2 %copy-start.30 = (f32[256,1,16]{0,2,1:T(8,128)S(1)}, f32[256,1,16]{0,2,1:T(8,128)}, u32[]{:S(2)}) copy-start(f32[256,1,16]{0,2,1:T(8,128)} %get-tuple-element.122) | copy-start | bytes 49156
  115.5 10.7 %collective-permute-start.17 = (f32[1,8,64,128]{3,2,1,0:T(8,128)S(1)}, f32[1,8,64,128]{3,2,1,0:T(8,128)S(1)}, u32[]{:S(2)}, u32[]{:S(2)}) collective-permute-start(f32[1,8,64,128]{3,2,1,0:T(8,128)S(1)} %multiply_add_fusion.4), channel_id=1, source_target_pairs={{248,216},{240,208},{232,200},{224,192},{216,184},{208,176},{200,1... | collective-permute-start | bytes 786440 | tf_op jit(solution)/shard_map/ppermute | solution.py:42
  117.5 18.2 %copy-start.8 = (f32[256,256]{1,0:T(8,128)}, f32[256,256]{1,0:T(8,128)S(1)}, u32[]{:S(2)}) copy-start(f32[256,256]{1,0:T(8,128)S(1)} %fusion.85) | copy-start | bytes 786436
  117.9 17.8 %copy-start.10 = (f32[256,256]{1,0:T(8,128)}, f32[256,256]{1,0:T(8,128)S(1)}, u32[]{:S(2)}) copy-start(f32[256,256]{1,0:T(8,128)S(1)} %fusion.91) | copy-start | bytes 786436
  126.2 10.3 %collective-permute-start.19 = (f32[1,8,64,128]{3,2,1,0:T(8,128)S(1)}, f32[1,8,64,128]{3,2,1,0:T(8,128)S(1)}, u32[]{:S(2)}, u32[]{:S(2)}) collective-permute-start(f32[1,8,64,128]{3,2,1,0:T(8,128)S(1)} %multiply_add_fusion.3), channel_id=1, source_target_pairs={{248,184},{240,176},{232,168},{224,160},{216,152},{208,144},{200,1... | collective-permute-start | bytes 786440 | tf_op jit(solution)/shard_map/ppermute | solution.py:42
  127.5 8.2 %copy-start.1 = (f32[1,256,1,16,64]{1,4,3,2,0:T(8,128)S(1)}, f32[1,256,1,16,64]{1,4,3,2,0:T(8,128)}, u32[]{:S(2)}) copy-start(f32[1,256,1,16,64]{1,4,3,2,0:T(8,128)} %copy-done) | copy-start | bytes 3145732
  135.7 2.2 %copy-start.14 = (f32[256,16]{0,1:T(8,128)S(1)}, f32[256,16]{0,1:T(8,128)}, u32[]{:S(2)}) copy-start(f32[256,16]{0,1:T(8,128)} %get-tuple-element.206) | copy-start | bytes 49156
  136.7 9.8 %collective-permute-start.21 = (f32[1,8,64,128]{3,2,1,0:T(8,128)S(1)}, f32[1,8,64,128]{3,2,1,0:T(8,128)S(1)}, u32[]{:S(2)}, u32[]{:S(2)}) collective-permute-start(f32[1,8,64,128]{3,2,1,0:T(8,128)S(1)} %multiply_add_fusion.2), channel_id=1, source_target_pairs={{248,120},{240,112},{232,104},{224,96},{216,88},{208,80},{200,72},... | collective-permute-start | bytes 786440 | tf_op jit(solution)/shard_map/ppermute | solution.py:42
  146.4 2.2 %copy-start.2 = (bf16[256,1024]{0,1:T(8,128)(2,1)S(1)}, bf16[256,1024]{0,1:T(8,128)(2,1)}, u32[]{:S(2)}) copy-start(bf16[256,1024]{0,1:T(8,128)(2,1)} %get-tuple-element.212) | copy-start | bytes 1572868
  147.4 3.4 %collective-permute-start.22 = (f32[1,8,64,128]{3,2,1,0:T(8,128)}, f32[1,8,64,128]{3,2,1,0:T(8,128)}, u32[]{:S(2)}, u32[]{:S(2)}) collective-permute-start(f32[1,8,64,128]{3,2,1,0:T(8,128)} %get-tuple-element.203), channel_id=1, source_target_pairs={{248,240},{240,248},{232,224},{224,232},{216,208},{208,216},{200,1... | collective-permute-start | bytes 786440 | tf_op jit(solution)/shard_map/ppermute | solution.py:42
  149.7 1.1 copy-start.5
  150.8 2.7 %copy-start.6 = (f32[256,16]{0,1:T(8,128)S(1)}, f32[256,16]{0,1:T(8,128)}, u32[]{:S(2)}) copy-start(f32[256,16]{0,1:T(8,128)} %param.13) | copy-start | bytes 49156
  150.8 2.7 %copy-start.20 = (f32[256,16]{0,1:T(8,128)S(1)}, f32[256,16]{0,1:T(8,128)}, u32[]{:S(2)}) copy-start(f32[256,16]{0,1:T(8,128)} %multiply_reduce_fusion) | copy-start | bytes 49156
  150.8 2.7 %copy-start.23 = (f32[1,1,1,16]{1,3,2,0:T(8,128)S(1)}, f32[1,1,1,16]{1,3,2,0:T(8,128)}, u32[]{:S(2)}) copy-start(f32[1,1,1,16]{1,3,2,0:T(8,128)} %get-tuple-element.218) | copy-start | bytes 196
  150.8 2.7 %copy-start.26 = (f32[256]{0:T(256)S(1)}, f32[256]{0:T(256)}, u32[]{:S(2)}) copy-start(f32[256]{0:T(256)} %copy-done.25) | copy-start | bytes 3076
  150.8 2.7 %copy-start.28 = (f32[16,256]{1,0:T(8,128)S(1)}, f32[16,256]{1,0:T(8,128)}, u32[]{:S(2)}) copy-start(f32[16,256]{1,0:T(8,128)} %get-tuple-element.169) | copy-start | bytes 49156
  150.8 2.7 %copy-start.29 = (f32[16,256]{1,0:T(8,128)S(1)}, f32[16,256]{1,0:T(8,128)}, u32[]{:S(2)}) copy-start(f32[16,256]{1,0:T(8,128)} %get-tuple-element.180) | copy-start | bytes 49156
  150.8 2.7 %copy-start.34 = (f32[256]{0:T(256)S(1)}, f32[256]{0:T(256)}, u32[]{:S(2)}) copy-start(f32[256]{0:T(256)} %copy-done.33) | copy-start | bytes 3076
  150.9 2.7 %copy-start.35 = (f32[16]{0:T(128)S(1)}, f32[16]{0:T(128)}, u32[]{:S(2)}) copy-start(f32[16]{0:T(128)} %param.16) | copy-start | bytes 196
  150.9 2.7 %copy-start.37 = (f32[16]{0:T(128)S(1)}, f32[16]{0:T(128)}, u32[]{:S(2)}) copy-start(f32[16]{0:T(128)} %copy-done.36) | copy-start | bytes 196
  153.5 7.1 %copy-start.15 = (f32[1,256,1,128]{3,1,2,0:T(8,128)S(1)}, f32[1,256,1,128]{3,1,2,0:T(8,128)}, u32[]{:S(2)}) copy-start(f32[1,256,1,128]{3,1,2,0:T(8,128)} %convolution_bitcast_fusion.2) | copy-start | bytes 393220
  153.5 7.2 %copy-start.19 = (f32[256,16]{0,1:T(8,128)S(1)}, f32[256,16]{0,1:T(8,128)}, u32[]{:S(2)}) copy-start(f32[256,16]{0,1:T(8,128)} %copy-done.18) | copy-start | bytes 49156
  158.0 6.6 %copy-start.9 = (f32[256,256]{1,0:T(8,128)S(1)}, f32[256,256]{1,0:T(8,128)}, u32[]{:S(2)}) copy-start(f32[256,256]{1,0:T(8,128)} %copy-done.8) | copy-start | bytes 786436
  158.0 6.7 %copy-start.11 = (f32[256,256]{1,0:T(8,128)S(1)}, f32[256,256]{1,0:T(8,128)}, u32[]{:S(2)}) copy-start(f32[256,256]{1,0:T(8,128)} %copy-done.10) | copy-start | bytes 786436
  158.0 6.7 %copy-start.31 = (f32[256,1,16]{0,2,1:T(8,128)S(1)}, f32[256,1,16]{0,2,1:T(8,128)}, u32[]{:S(2)}) copy-start(f32[256,1,16]{0,2,1:T(8,128)} %get-tuple-element.122) | copy-start | bytes 49156
  164.7 5.0 %copy-start.17 = (f32[1024]{0:T(1024)S(1)}, f32[1024]{0:T(1024)}, u32[]{:S(2)}) copy-start(f32[1024]{0:T(1024)} %mul.749) | copy-start | bytes 12292
  169.9 1.0 copy-start.27
  (3 other events, 2.8 us)

commit v4 on v3

--- a/solution.py
+++ b/solution.py
@@ -69,14 +69,10 @@
     )
 
 
-def butterfly_sum(value, axis):
+def head_sum(value, axis):
     size = lax.axis_size(axis)
-    step = 1
-    while step < size:
-        pairs = [(i, i ^ step) for i in range(size)]
-        value = value + lax.ppermute(value, axis, pairs)
-        step *= 2
-    return value
+    spread = jnp.broadcast_to(value[None], (size,) + value.shape)
+    return jnp.sum(lax.all_to_all(spread, axis, 0, 0), axis=0)
 
 
 def span_mix(x_span, dt_span, b_span, c_span, log_cum, segment):
@@ -196,7 +192,7 @@
     gated = core_out * gate_act
     weighted_grad = norm_weight[None, :] * grad_output.astype(jnp.float32)
     norm_width = lax.axis_size("head") * gated.shape[1]
-    sums = butterfly_sum(
+    sums = head_sum(
         jnp.stack([jnp.sum(gated * gated, axis=1), jnp.sum(weighted_grad * gated, axis=1)]),
         "head",
     )

time: 174 us -> 176 us (1.011)
  starting transfers between devices: 52.3 us -> 48.7 us
  waiting for transfers between devices: 53.3 us -> 56.2 us
  other arithmetic: 22.3 us -> 24.8 us
    ppermute x3 -> x0, starting transfers between devices: 12.3 us -> none  [butterfly_sum(): value = value + lax.ppermute(value, axis, pairs)]
    all_to_all x0 -> x1, starting transfers between devices: none -> 8.46 us  [head_sum(): return jnp.sum(lax.all_to_all(spread, axis, 0, 0), axis=0)]
    all_to_all x0 -> x1, waiting for transfers between devices: none -> 7.76 us  [head_sum(): return jnp.sum(lax.all_to_all(spread, axis, 0, 0), axis=0)]
    ppermute x3 -> x0, waiting for transfers between devices: 4.8 us -> none  [butterfly_sum(): value = value + lax.ppermute(value, axis, pairs)]
    unnamed x93 -> x105, local copies, waits for them, and re-layouts: 6.94 us -> 6.25 us
  transfers between devices with their start and end apart: 23 -> 21, of which waited for: 14 -> 12; matrix products, arithmetic and copies ran while one was open for 15% -> 15% of each run, Pallas kernels for 0% -> 0%
where the time goes in v4:
time: 176 us; the launch traced here: 173 us
  waiting for transfers between devices  56.2 us (32%)
  starting transfers between devices  48.7 us (28%)
  matrix products  29.3 us (17%)
  other arithmetic  24.8 us (14%)
  local copies, waits for them, and re-layouts  10.9 us (6%)
  between operations  2.98 us (2%)
    ppermute x20, waiting for transfers between devices, move(): return lax.ppermute(tree, axis, [(device(a), device(b)) for a, b in pairs])  48.4 us
    ppermute x20, starting transfers between devices, move(): return lax.ppermute(tree, axis, [(device(a), device(b)) for a, b in pairs])  40.2 us
    dot_general x3, matrix products, span_mix(): jnp.einsum('ghts,sghp->tghp', weights, x_span, precision=HIGHEST_PRECISION)  15.9 us
    all_to_all x1, starting transfers between devices, head_sum(): return jnp.sum(lax.all_to_all(spread, axis, 0, 0), axis=0)  8.46 us
    all_to_all x1, waiting for transfers between devices, head_sum(): return jnp.sum(lax.all_to_all(spread, axis, 0, 0), axis=0)  7.76 us
    another operation x10, other arithmetic  7.72 us
    dot_general x3, matrix products, local_states(): jnp.einsum('kqgh,kqghp,kqgn->kghpn', tail_decay * dt_spans, x_spans, b_sp...  6.79 us
    unnamed x105, local copies, waits for them, and re-layouts  6.25 us
  transfers between devices with their start and end apart: 21, of which 12 were waited for; matrix products, arithmetic and copies ran while one was open for 15% of the time, Pallas kernels for 0%

profile of v4, /device:TPU:6, one launch (start us, length us, event | category | flops | bytes accessed | tf_op | source)
XLA Modules:
  0.0 172.8 jit_solution(3428633882798449353)
XLA Ops:
  0.7 0.7 exponential_negate_fusion
  1.3 1.4 fusion.125
  3.5 1.0 reduce-window.30
  7.7 0.6 multiply_bitcast_fusion
  8.4 0.8 fusion.109
  9.2 0.8 fusion.105
  10.0 1.2 copy.122
  11.3 0.7 fusion.45
  12.2 0.7 dynamic-slice_reduce_fusion.1
  13.3 0.8 collective-permute-done
  14.2 3.4 %collective-permute-start.2 = (f32[1,8,64,128]{3,2,1,0:T(8,128)S(1)}, f32[1,8,64,128]{3,2,1,0:T(8,128)S(1)}, u32[]{:S(2)}, u32[]{:S(2)}) collective-permute-start(f32[1,8,64,128]{3,2,1,0:T(8,128)S(1)} %fusion.77), channel_id=1, source_target_pairs={{0,16},{8,24},{16,32},{24,40},{32,48},{40,56},{48,64},{56,72},{64,... | collective-permute-start | bytes 786440 | tf_op jit(solution)/shard_map/ppermute | solution.py:42
  17.6 7.0 %collective-permute-done.2 = f32[1,8,64,128]{3,2,1,0:T(8,128)S(1)} collective-permute-done((f32[1,8,64,128]{3,2,1,0:T(8,128)S(1)}, f32[1,8,64,128]{3,2,1,0:T(8,128)S(1)}, u32[]{:S(2)}, u32[]{:S(2)}) %collective-permute-start.2) | collective-permute-done | bytes 262176 | tf_op jit(solution)/shard_map/ppermute | solution.py:42
  24.8 4.3 %collective-permute-start.4 = (f32[1,8,64,128]{3,2,1,0:T(8,128)S(1)}, f32[1,8,64,128]{3,2,1,0:T(8,128)S(1)}, u32[]{:S(2)}, u32[]{:S(2)}) collective-permute-start(f32[1,8,64,128]{3,2,1,0:T(8,128)S(1)} %multiply_add_fusion.9), channel_id=1, source_target_pairs={{0,32},{8,40},{16,48},{24,56},{32,64},{40,72},{48,80},{56,88},{64,... | collective-permute-start | bytes 786440 | tf_op jit(solution)/shard_map/ppermute | solution.py:42
  29.1 4.0 %collective-permute-start.3 = (f32[1,8]{1,0:T(1,128)S(1)}, f32[1,8]{1,0:T(1,128)S(1)}, u32[]{:S(2)}, u32[]{:S(2)}) collective-permute-start(f32[1,8]{1,0:T(1,128)S(1)} %get-tuple-element.240), channel_id=1, source_target_pairs={{0,16},{8,24},{16,32},{24,40},{32,48},{40,56},{48,64},{56,72},{64,... | collective-permute-start | bytes 104 | tf_op jit(solution)/shard_map/ppermute | solution.py:42
  33.1 3.7 %collective-permute-done.3 = f32[1,8]{1,0:T(1,128)S(1)} collective-permute-done((f32[1,8]{1,0:T(1,128)S(1)}, f32[1,8]{1,0:T(1,128)S(1)}, u32[]{:S(2)}, u32[]{:S(2)}) %collective-permute-start.3) | collective-permute-done | bytes 64 | tf_op jit(solution)/shard_map/ppermute | solution.py:42
  36.9 3.5 %collective-permute-start.6 = (f32[1,8,64,128]{3,2,1,0:T(8,128)S(1)}, f32[1,8,64,128]{3,2,1,0:T(8,128)S(1)}, u32[]{:S(2)}, u32[]{:S(2)}) collective-permute-start(f32[1,8,64,128]{3,2,1,0:T(8,128)S(1)} %multiply_add_fusion.8), channel_id=1, source_target_pairs={{0,64},{8,72},{16,80},{24,88},{32,96},{40,104},{48,112},{56,120},{... | collective-permute-start | bytes 786440 | tf_op jit(solution)/shard_map/ppermute | solution.py:42
  40.4 4.3 %collective-permute-start.5 = (f32[1,8]{1,0:T(1,128)S(1)}, f32[1,8]{1,0:T(1,128)S(1)}, u32[]{:S(2)}, u32[]{:S(2)}) collective-permute-start(f32[1,8]{1,0:T(1,128)S(1)} %mul.725), channel_id=1, source_target_pairs={{0,32},{8,40},{16,48},{24,56},{32,64},{40,72},{48,80},{56,88},{64,... | collective-permute-start | bytes 104 | tf_op jit(solution)/shard_map/ppermute | solution.py:42
  44.7 2.7 %collective-permute-done.5 = f32[1,8]{1,0:T(1,128)S(1)} collective-permute-done((f32[1,8]{1,0:T(1,128)S(1)}, f32[1,8]{1,0:T(1,128)S(1)}, u32[]{:S(2)}, u32[]{:S(2)}) %collective-permute-start.5) | collective-permute-done | bytes 64 | tf_op jit(solution)/shard_map/ppermute | solution.py:42
  47.5 3.9 %collective-permute-start.8 = (f32[1,8,64,128]{3,2,1,0:T(8,128)S(1)}, f32[1,8,64,128]{3,2,1,0:T(8,128)S(1)}, u32[]{:S(2)}, u32[]{:S(2)}) collective-permute-start(f32[1,8,64,128]{3,2,1,0:T(8,128)S(1)} %multiply_add_fusion.7), channel_id=1, source_target_pairs={{0,128},{8,136},{16,144},{24,152},{32,160},{40,168},{48,176},{56,1... | collective-permute-start | bytes 786440 | tf_op jit(solution)/shard_map/ppermute | solution.py:42
  51.4 0.9 fusion.129
  52.3 1.3 collective-permute-start.7
  53.6 1.7 collective-permute-done.7
  56.0 0.8 fusion.84
  56.8 0.7 mul.749
  57.7 1.2 copy.129
  58.9 0.7 fusion.80
  60.4 1.0 copy-done.1
  61.3 3.2 %fusion.37 = f32[1,256,1,16,64]{1,4,3,2,0:T(8,128)S(1)} fusion(bf16[256,16,64]{0,2,1:T(8,128)(2,1)S(1)} %bitcast.331, f32[16,256]{1,0:T(8,128)S(1)} %copy-done.36, f32[256,256]{1,0:T(8,128)S(1)} %copy-done.15, f32[16,256]{1,0:T(8,128)S(1)} %bitcast.341, f32[256,256]{1,0:T(8,128)S(1)} %copy-done.10, ...), kind=kOutput, calls=%fused_computation.40 | convolution fusion | flops 811073536 | bytes 3194880 | tf_op jit(solution)/shard_map/jvp()/while/body/eval_jaxpr/ghts,sghp->tghp/dot_general | solution.py:88
  64.6 1.6 multiply_reduce_fusion.2
  66.2 0.6 broadcast_in_dim.96
  66.9 8.5 %all-to-all-start = ((f32[8,2,256]{2,1,0:T(2,128)}), f32[8,2,256]{2,1,0:T(2,128)S(1)}, u32[]{:S(2)}, u32[]{:S(2)}) async-start(f32[8,2,256]{2,1,0:T(2,128)} %broadcast_in_dim.96), calls=%async_computation | async-start | bytes 32768 | tf_op jit(solution)/shard_map/all_to_all | solution.py:75
  75.3 7.8 %all-to-all-done = f32[8,2,256]{2,1,0:T(2,128)S(1)} async-done(((f32[8,2,256]{2,1,0:T(2,128)}), f32[8,2,256]{2,1,0:T(2,128)S(1)}, u32[]{:S(2)}, u32[]{:S(2)}) %all-to-all-start) | async-done | bytes 16416 | tf_op jit(solution)/shard_map/all_to_all | solution.py:75
  83.1 3.1 %fusion.55 = (bf16[256,1024]{0,1:T(8,128)(2,1)}, f32[256,1024]{0,1:T(8,128)S(1)}) fusion(bf16[256,1024]{0,1:T(8,128)(2,1)S(1)} %copy.128, f32[1024]{0:T(1024)S(1)} %copy-done.19, bf16[256,1024]{0,1:T(8,128)(2,1)S(1)} %copy.122, f32[1,256,1,16,64]{1,4,3,2,0:T(8,128)} %copy-done, f32[256]{0:T(256)S(1)} %multiply_multiply_fusion, ...), kind=kLoop, calls=%fused_computation.59 | loop fusion | flops 5767168 | bytes 5253120 | tf_op jit(solution)/shard_map/convert_element_type | solution.py:219
  86.3 0.6 fusion.57
  87.3 0.7 fusion.122
  87.9 0.8 collective-permute-done.11
  88.8 2.8 %collective-permute-start.12 = (f32[1,8,64,128]{3,2,1,0:T(8,128)S(1)}, f32[1,8,64,128]{3,2,1,0:T(8,128)S(1)}, u32[]{:S(2)}, u32[]{:S(2)}) collective-permute-start(f32[1,8,64,128]{3,2,1,0:T(8,128)S(1)} %fusion.76), channel_id=1, source_target_pairs={{248,232},{240,224},{232,216},{224,208},{216,200},{208,192},{200,1... | collective-permute-start | bytes 786440 | tf_op jit(solution)/shard_map/ppermute | solution.py:42
  91.8 4.2 %collective-permute-start.13 = (f32[1,8]{1,0:T(1,128)S(1)}, f32[1,8]{1,0:T(1,128)S(1)}, u32[]{:S(2)}, u32[]{:S(2)}) collective-permute-start(f32[1,8]{1,0:T(1,128)S(1)} %get-tuple-element.235), channel_id=1, source_target_pairs={{248,232},{240,224},{232,216},{224,208},{216,200},{208,192},{200,1... | collective-permute-start | bytes 104 | tf_op jit(solution)/shard_map/ppermute | solution.py:42
  96.0 7.7 %collective-permute-done.13 = f32[1,8]{1,0:T(1,128)S(1)} collective-permute-done((f32[1,8]{1,0:T(1,128)S(1)}, f32[1,8]{1,0:T(1,128)S(1)}, u32[]{:S(2)}, u32[]{:S(2)}) %collective-permute-start.13) | collective-permute-done | bytes 64 | tf_op jit(solution)/shard_map/ppermute | solution.py:42
  103.7 1.9 %collective-permute-start.15 = (f32[1,8]{1,0:T(1,128)S(1)}, f32[1,8]{1,0:T(1,128)S(1)}, u32[]{:S(2)}, u32[]{:S(2)}) collective-permute-start(f32[1,8]{1,0:T(1,128)S(1)} %mul.785), channel_id=1, source_target_pairs={{248,216},{240,208},{232,200},{224,192},{216,184},{208,176},{200,1... | collective-permute-start | bytes 104 | tf_op jit(solution)/shard_map/ppermute | solution.py:42
  105.7 5.9 %collective-permute-done.15 = f32[1,8]{1,0:T(1,128)S(1)} collective-permute-done((f32[1,8]{1,0:T(1,128)S(1)}, f32[1,8]{1,0:T(1,128)S(1)}, u32[]{:S(2)}, u32[]{:S(2)}) %collective-permute-start.15) | collective-permute-done | bytes 64 | tf_op jit(solution)/shard_map/ppermute | solution.py:42
  111.6 1.3 collective-permute-start.17
  112.9 4.2 %collective-permute-done.17 = f32[1,8]{1,0:T(1,128)S(1)} collective-permute-done((f32[1,8]{1,0:T(1,128)S(1)}, f32[1,8]{1,0:T(1,128)S(1)}, u32[]{:S(2)}, u32[]{:S(2)}) %collective-permute-start.17) | collective-permute-done | bytes 64 | tf_op jit(solution)/shard_map/ppermute | solution.py:42
  117.2 1.9 %collective-permute-start.14 = (f32[1,8,64,128]{3,2,1,0:T(8,128)S(1)}, f32[1,8,64,128]{3,2,1,0:T(8,128)S(1)}, u32[]{:S(2)}, u32[]{:S(2)}) collective-permute-start(f32[1,8,64,128]{3,2,1,0:T(8,128)S(1)} %multiply_add_fusion.4), channel_id=1, source_target_pairs={{248,216},{240,208},{232,200},{224,192},{216,184},{208,176},{200,1... | collective-permute-start | bytes 786440 | tf_op jit(solution)/shard_map/ppermute | solution.py:42
  119.6 8.2 %collective-permute-done.14 = f32[1,8,64,128]{3,2,1,0:T(8,128)S(1)} collective-permute-done((f32[1,8,64,128]{3,2,1,0:T(8,128)S(1)}, f32[1,8,64,128]{3,2,1,0:T(8,128)S(1)}, u32[]{:S(2)}, u32[]{:S(2)}) %collective-permute-start.14) | collective-permute-done | bytes 262176 | tf_op jit(solution)/shard_map/ppermute | solution.py:42
  127.9 1.3 collective-permute-start.16
  129.2 8.2 %fusion.75 = (f32[16,256]{1,0:T(8,128)}, f32[16,256]{1,0:T(8,128)}, f32[16,256]{1,0:T(8,128)}, f32[256,256]{1,0:T(8,128)S(1)}) fusion(f32[16,256]{1,0:T(8,128)S(1)} %bitcast.342, f32[256,256]{1,0:T(8,128)S(1)} %fusion.85, f32[16,256]{1,0:T(8,128)S(1)} %bitcast.351, f32[256,256]{1,0:T(8,128)S(1)} %fusion.91, f32[256,1,16,64]{0,3,2,1:T(8,128)S(1)} %convert.9, ...), kind=kOutput, calls=%fused_computation.91 | convolution fusion | flops 825151488 | bytes 2965504 | tf_op jit(solution)/shard_map/transpose(jvp())/while/body/eval_jaxpr/checkpoint/ghts,sghp->tghp/dot_general | solution.py:88
  137.4 0.8 multiply_reduce_fusion
  138.3 1.3 collective-permute-start.18
  139.7 1.8 %convolution_bitcast_fusion.3 = f32[256,128]{1,0:T(8,128)S(1)} fusion(f32[1,256,1,16,64]{1,4,3,2,0:T(8,128)S(1)} %bitcast.328, f32[256,16]{0,1:T(8,128)S(1)} %copy-done.18, f32[8,64,128]{2,1,0:T(8,128)S(1)} %bitcast.335, f32[8,64,128]{2,1,0:T(8,128)S(1)} %bitcast.339, pred[]{:T(512)S(6)} %eq.98), kind=kOutput, calls=%fused_computation.50 | convolution fusion | flops 403308544 | bytes 1720321 | tf_op jit(solution)/shard_map/transpose(jvp(kqgn,kghpn->kqghp))/dot_general | solution.py:137
  141.5 1.0 convolution_add_fusion
  142.5 5.6 %collective-permute-done.18 = f32[1,8,64,128]{3,2,1,0:T(8,128)S(1)} collective-permute-done((f32[1,8,64,128]{3,2,1,0:T(8,128)S(1)}, f32[1,8,64,128]{3,2,1,0:T(8,128)S(1)}, u32[]{:S(2)}, u32[]{:S(2)}) %collective-permute-start.18) | collective-permute-done | bytes 262176 | tf_op jit(solution)/shard_map/ppermute | solution.py:42
  148.1 1.0 fusion.79
  149.1 1.3 convolution_bitcast_fusion.2
  150.3 1.0 copy.143
  151.3 1.1 fusion.78
  152.5 2.6 %fusion.49 = (f32[256,16]{0,1:T(8,128)S(1)}, f32[256,16,64]{0,2,1:T(8,128)}) fusion(bf16[256,1024]{0,1:T(8,128)(2,1)S(1)} %copy.122, bf16[256,128]{1,0:T(8,128)(2,1)S(1)} %copy-done.7, f32[8,64,128]{2,1,0:T(8,128)S(1)} %bitcast.336, f32[8,64,128]{2,1,0:T(8,128)} %bitcast.80, pred[]{:T(512)S(6)} %eq.108), kind=kOutput, calls=%fused_computation.53 | convolution fusion | flops 403828736 | bytes 2179073 | tf_op jit(solution)/shard_map/transpose(jvp(kqgh,kqghp,kqgn->kghpn))/dot_general | solution.py:102
  155.5 1.3 multiply_reduce_fusion.3
  157.1 2.5 %reduce-window.36 = f32[1,16,1,2,128]{4,1,2,3,0:T(8,128)S(1)} reduce-window(f32[1,16,1,2,128]{4,1,2,3,0:T(8,128)S(1)} %copy_bitcast_fusion, f32[]{:T(128)} %constant.154.clone.1), window={size=1x1x1x1x128 pad=0_0x0_0x0_0x0_0x0_127}, to_apply=%region_16.17 | reduce-window | flops 520192 | bytes 32772 | tf_op jit(solution)/shard_map/reduce-window.6
  159.7 2.5 %reduce-window.34 = f32[1,16,1,2,128]{4,1,2,3,0:T(8,128)S(1)} reduce-window(f32[1,16,1,2,128]{4,1,2,3,0:T(8,128)S(1)} %bitcast.348, f32[]{:T(128)} %constant.154.clone.1), window={size=1x1x1x1x128 pad=0_0x0_0x0_0x0_0x0_127}, to_apply=%region_11.12 | reduce-window | flops 520192 | bytes 32772 | tf_op jit(solution)/shard_map/reduce-window.4
  162.3 3.5 %fusion.48 = f32[256,128]{1,0:T(8,128)} fusion(f32[1,256,1,128]{3,1,2,0:T(8,128)} %convolution_bitcast_fusion.2, bf16[256,16,64]{0,2,1:T(8,128)(2,1)S(1)} %bitcast.333, f32[256,16]{0,1:T(8,128)S(1)} %copy-done.22, f32[8,64,128]{2,1,0:T(8,128)S(1)} %bitcast.337, f32[8,64,128]{2,1,0:T(8,128)} %bitcast.80, pred[]{:T(512)S(6)} %eq.108), kind=kOutput, calls=%fused_computation.52 | convolution fusion | flops 403603456 | bytes 1327105 | tf_op jit(solution)/shard_map/transpose(jvp(kqgh,kqghp,kqgn->kghpn))/dot_general | solution.py:102
  166.3 4.5 %fusion.40 = f32[256,16,64]{0,2,1:T(8,128)S(1)} fusion(f32[16,256]{1,0:T(8,128)} %bitcast.350, f32[256,256]{1,0:T(8,128)S(1)} %copy-done.12, f32[16,256]{1,0:T(8,128)S(1)} %bitcast.344, f32[256,256]{1,0:T(8,128)S(1)} %copy-done.14, f32[256,1,16,64]{0,3,2,1:T(8,128)S(1)} %bitcast.329, f32[256,16,64]{0,2,1:T(8,128)S(1)} %copy-done.4, f32[256,16]{0,1:T(8,128)S(1)} %copy-done.22), kind=kOutput, calls=%fused_computation.41 | convolution fusion | flops 811073536 | bytes 3719168 | tf_op jit(solution)/shard_map/transpose(jvp())/while/body/eval_jaxpr/checkpoint/ghts,sghp->tghp/dot_general | solution.py:88
  171.1 1.0 copy.142
  172.1 0.7 fusion.103
  (184 shorter events, 8.1 us)
Async XLA Ops:
  0.6 10.6 %copy-start.6 = (bf16[256,128]{1,0:T(8,128)(2,1)S(1)}, bf16[256,128]{1,0:T(8,128)(2,1)}, u32[]{:S(2)}) copy-start(bf16[256,128]{1,0:T(8,128)(2,1)} %param.14) | copy-start | bytes 196612
  1.3 7.8 %copy-start.46 = (f32[16]{0:T(128)}, f32[16]{0:T(128)S(1)}, u32[]{:S(2)}) copy-start(f32[16]{0:T(128)S(1)} %exponential_negate_fusion) | copy-start | bytes 196
  5.0 7.0 %copy-start.24 = (s32[256]{0:T(256)}, s32[256]{0:T(256)S(1)}, u32[]{:S(2)}) copy-start(s32[256]{0:T(256)S(1)} %get-tuple-element.121) | copy-start | bytes 3076
  5.0 7.0 %copy-start.37 = (f32[256]{0:T(256)}, f32[256]{0:T(256)S(1)}, u32[]{:S(2)}) copy-start(f32[256]{0:T(256)S(1)} %get-tuple-element.218) | copy-start | bytes 3076
  9.1 2.8 %copy-start.41 = (f32[16]{0:T(128)}, f32[16]{0:T(128)S(1)}, u32[]{:S(2)}) copy-start(f32[16]{0:T(128)S(1)} %get-tuple-element.229) | copy-start | bytes 196
  9.2 2.8 %copy-start.29 = (f32[256]{0:T(256)}, f32[256]{0:T(256)S(1)}, u32[]{:S(2)}) copy-start(f32[256]{0:T(256)S(1)} %compare_convert_fusion.1) | copy-start | bytes 3076
  10.0 2.0 %copy-start.21 = (f32[256,16]{0,1:T(8,128)}, f32[256,16]{0,1:T(8,128)S(1)}, u32[]{:S(2)}) copy-start(f32[256,16]{0,1:T(8,128)S(1)} %fusion.105) | copy-start | bytes 49156
  12.0 2.1 %collective-permute-start.1 = (f32[1,8,64,128]{3,2,1,0:T(8,128)S(1)}, f32[1,8,64,128]{3,2,1,0:T(8,128)S(1)}, u32[]{:S(2)}, u32[]{:S(2)}) collective-permute-start(f32[1,8,64,128]{3,2,1,0:T(8,128)S(1)} %dynamic-slice_bitcast_fusion.1), channel_id=1, source_target_pairs={{0,8},{8,0},{16,24},{24,16},{32,40},{40,32},{48,56},{56,48},{64,72... | collective-permute-start | bytes 786440 | tf_op jit(solution)/shard_map/ppermute | solution.py:42
  12.8 1.3 collective-permute-start
  14.1 41.1 %copy-start.45 = (f32[8]{0:T(128)}, f32[8]{0:T(128)S(1)}, u32[]{:S(2)}) copy-start(f32[8]{0:T(128)S(1)} %get-tuple-element.241) | copy-start | bytes 100
  14.2 10.4 %collective-permute-start.2 = (f32[1,8,64,128]{3,2,1,0:T(8,128)S(1)}, f32[1,8,64,128]{3,2,1,0:T(8,128)S(1)}, u32[]{:S(2)}, u32[]{:S(2)}) collective-permute-start(f32[1,8,64,128]{3,2,1,0:T(8,128)S(1)} %fusion.77), channel_id=1, source_target_pairs={{0,16},{8,24},{16,32},{24,40},{32,48},{40,56},{48,64},{56,72},{64,... | collective-permute-start | bytes 786440 | tf_op jit(solution)/shard_map/ppermute | solution.py:42
  24.7 26.7 %copy-start.5 = (bf16[256,128]{1,0:T(8,128)(2,1)S(1)}, bf16[256,128]{1,0:T(8,128)(2,1)}, u32[]{:S(2)}) copy-start(bf16[256,128]{1,0:T(8,128)(2,1)} %param.15) | copy-start | bytes 196612
  24.8 12.0 %collective-permute-start.4 = (f32[1,8,64,128]{3,2,1,0:T(8,128)S(1)}, f32[1,8,64,128]{3,2,1,0:T(8,128)S(1)}, u32[]{:S(2)}, u32[]{:S(2)}) collective-permute-start(f32[1,8,64,128]{3,2,1,0:T(8,128)S(1)} %multiply_add_fusion.9), channel_id=1, source_target_pairs={{0,32},{8,40},{16,48},{24,56},{32,64},{40,72},{48,80},{56,88},{64,... | collective-permute-start | bytes 786440 | tf_op jit(solution)/shard_map/ppermute | solution.py:42
  29.1 7.7 %collective-permute-start.3 = (f32[1,8]{1,0:T(1,128)S(1)}, f32[1,8]{1,0:T(1,128)S(1)}, u32[]{:S(2)}, u32[]{:S(2)}) collective-permute-start(f32[1,8]{1,0:T(1,128)S(1)} %get-tuple-element.240), channel_id=1, source_target_pairs={{0,16},{8,24},{16,32},{24,40},{32,48},{40,56},{48,64},{56,72},{64,... | collective-permute-start | bytes 104 | tf_op jit(solution)/shard_map/ppermute | solution.py:42
  36.9 10.5 %collective-permute-start.6 = (f32[1,8,64,128]{3,2,1,0:T(8,128)S(1)}, f32[1,8,64,128]{3,2,1,0:T(8,128)S(1)}, u32[]{:S(2)}, u32[]{:S(2)}) collective-permute-start(f32[1,8,64,128]{3,2,1,0:T(8,128)S(1)} %multiply_add_fusion.8), channel_id=1, source_target_pairs={{0,64},{8,72},{16,80},{24,88},{32,96},{40,104},{48,112},{56,120},{... | collective-permute-start | bytes 786440 | tf_op jit(solution)/shard_map/ppermute | solution.py:42
  40.4 7.0 %collective-permute-start.5 = (f32[1,8]{1,0:T(1,128)S(1)}, f32[1,8]{1,0:T(1,128)S(1)}, u32[]{:S(2)}, u32[]{:S(2)}) collective-permute-start(f32[1,8]{1,0:T(1,128)S(1)} %mul.725), channel_id=1, source_target_pairs={{0,32},{8,40},{16,48},{24,56},{32,64},{40,72},{48,80},{56,88},{64,... | collective-permute-start | bytes 104 | tf_op jit(solution)/shard_map/ppermute | solution.py:42
  47.5 7.8 %collective-permute-start.8 = (f32[1,8,64,128]{3,2,1,0:T(8,128)S(1)}, f32[1,8,64,128]{3,2,1,0:T(8,128)S(1)}, u32[]{:S(2)}, u32[]{:S(2)}) collective-permute-start(f32[1,8,64,128]{3,2,1,0:T(8,128)S(1)} %multiply_add_fusion.7), channel_id=1, source_target_pairs={{0,128},{8,136},{16,144},{24,152},{32,160},{40,168},{48,176},{56,1... | collective-permute-start | bytes 786440 | tf_op jit(solution)/shard_map/ppermute | solution.py:42
  52.3 3.0 %collective-permute-start.7 = (f32[1,8]{1,0:T(1,128)S(1)}, f32[1,8]{1,0:T(1,128)S(1)}, u32[]{:S(2)}, u32[]{:S(2)}) collective-permute-start(f32[1,8]{1,0:T(1,128)S(1)} %mul.733), channel_id=1, source_target_pairs={{0,64},{8,72},{16,80},{24,88},{32,96},{40,104},{48,112},{56,120},{... | collective-permute-start | bytes 104 | tf_op jit(solution)/shard_map/ppermute | solution.py:42
  55.3 1.5 copy-start.49
  55.3 2.2 %copy-start.8 = (bf16[256,1024]{1,0:T(8,128)(2,1)S(1)}, bf16[256,1024]{1,0:T(8,128)(2,1)}, u32[]{:S(2)}) copy-start(bf16[256,1024]{1,0:T(8,128)(2,1)} %param.12) | copy-start | bytes 1572868
  55.5 4.3 %collective-permute-start.9 = (f32[1,8,64,128]{3,2,1,0:T(8,128)S(1)}, f32[1,8,64,128]{3,2,1,0:T(8,128)S(1)}, u32[]{:S(2)}, u32[]{:S(2)}) collective-permute-start(f32[1,8,64,128]{3,2,1,0:T(8,128)S(1)} %get-tuple-element.220), channel_id=1, source_target_pairs={{0,8},{8,0},{16,24},{24,16},{32,40},{40,32},{48,56},{56,48},{64,72... | collective-permute-start | bytes 786440 | tf_op jit(solution)/shard_map/ppermute | solution.py:42
  59.7 1.6 copy-start.10
  59.7 1.6 copy-start.15
  59.7 1.6 copy-start.16
  59.7 1.6 copy-start.36
  61.3 3.3 %copy-start.19 = (f32[1024]{0:T(1024)S(1)}, f32[1024]{0:T(1024)}, u32[]{:S(2)}) copy-start(f32[1024]{0:T(1024)} %mul.749) | copy-start | bytes 12292
  61.3 3.3 %copy-start.28 = (f32[1024]{0:T(1024)S(1)}, f32[1024]{0:T(1024)}, u32[]{:S(2)}) copy-start(f32[1024]{0:T(1024)} %param.19) | copy-start | bytes 12292
  64.6 1.6 copy-start
  66.9 16.2 %all-to-all-start = ((f32[8,2,256]{2,1,0:T(2,128)}), f32[8,2,256]{2,1,0:T(2,128)S(1)}, u32[]{:S(2)}, u32[]{:S(2)}) async-start(f32[8,2,256]{2,1,0:T(2,128)} %broadcast_in_dim.96), calls=%async_computation | async-start | bytes 32768 | tf_op jit(solution)/shard_map/all_to_all | solution.py:75
  75.3 11.9 %collective-permute-start.10 = (f32[1,8]{1,0:T(1,128)}, f32[1,8]{1,0:T(1,128)}, u32[]{:S(2)}, u32[]{:S(2)}) collective-permute-start(f32[1,8]{1,0:T(1,128)} %bitcast.140), channel_id=1, source_target_pairs={{248,240},{240,248},{232,224},{224,232},{216,208},{208,216},{200,1... | collective-permute-start | bytes 104 | tf_op jit(solution)/shard_map/ppermute | solution.py:42
  83.1 3.1 %copy-start.17 = (f32[256,16]{0,1:T(8,128)S(1)}, f32[256,16]{0,1:T(8,128)}, u32[]{:S(2)}) copy-start(f32[256,16]{0,1:T(8,128)} %get-tuple-element.216) | copy-start | bytes 49156
  87.0 1.8 %collective-permute-start.11 = (f32[1,8,64,128]{3,2,1,0:T(8,128)S(1)}, f32[1,8,64,128]{3,2,1,0:T(8,128)S(1)}, u32[]{:S(2)}, u32[]{:S(2)}) collective-permute-start(f32[1,8,64,128]{3,2,1,0:T(8,128)S(1)} %dynamic-slice_bitcast_fusion), channel_id=1, source_target_pairs={{248,240},{240,248},{232,224},{224,232},{216,208},{208,216},{200,1... | collective-permute-start | bytes 786440 | tf_op jit(solution)/shard_map/ppermute | solution.py:42
  87.9 60.2 %copy-start.44 = (f32[8]{0:T(128)}, f32[8]{0:T(128)S(1)}, u32[]{:S(2)}) copy-start(f32[8]{0:T(128)S(1)} %get-tuple-element.236) | copy-start | bytes 100
  88.8 28.2 %collective-permute-start.12 = (f32[1,8,64,128]{3,2,1,0:T(8,128)S(1)}, f32[1,8,64,128]{3,2,1,0:T(8,128)S(1)}, u32[]{:S(2)}, u32[]{:S(2)}) collective-permute-start(f32[1,8,64,128]{3,2,1,0:T(8,128)S(1)} %fusion.76), channel_id=1, source_target_pairs={{248,232},{240,224},{232,216},{224,208},{216,200},{208,192},{200,1... | collective-permute-start | bytes 786440 | tf_op jit(solution)/shard_map/ppermute | solution.py:42
  91.6 27.5 %copy-start.26 = (s32[256]{0:T(256)S(1)}, s32[256]{0:T(256)}, u32[]{:S(2)}) copy-start(s32[256]{0:T(256)} %copy-done.24) | copy-start | bytes 3076
  91.8 12.0 %collective-permute-start.13 = (f32[1,8]{1,0:T(1,128)S(1)}, f32[1,8]{1,0:T(1,128)S(1)}, u32[]{:S(2)}, u32[]{:S(2)}) collective-permute-start(f32[1,8]{1,0:T(1,128)S(1)} %get-tuple-element.235), channel_id=1, source_target_pairs={{248,232},{240,224},{232,216},{224,208},{216,200},{208,192},{200,1... | collective-permute-start | bytes 104 | tf_op jit(solution)/shard_map/ppermute | solution.py:42
  103.7 7.9 %collective-permute-start.15 = (f32[1,8]{1,0:T(1,128)S(1)}, f32[1,8]{1,0:T(1,128)S(1)}, u32[]{:S(2)}, u32[]{:S(2)}) collective-permute-start(f32[1,8]{1,0:T(1,128)S(1)} %mul.785), channel_id=1, source_target_pairs={{248,216},{240,208},{232,200},{224,192},{216,184},{208,176},{200,1... | collective-permute-start | bytes 104 | tf_op jit(solution)/shard_map/ppermute | solution.py:42
  111.6 5.5 %collective-permute-start.17 = (f32[1,8]{1,0:T(1,128)S(1)}, f32[1,8]{1,0:T(1,128)S(1)}, u32[]{:S(2)}, u32[]{:S(2)}) collective-permute-start(f32[1,8]{1,0:T(1,128)S(1)} %mul.793), channel_id=1, source_target_pairs={{248,184},{240,176},{232,168},{224,160},{216,152},{208,144},{200,1... | collective-permute-start | bytes 104 | tf_op jit(solution)/shard_map/ppermute | solution.py:42
  117.1 12.2 %copy-start.35 = (f32[256,1,16]{0,2,1:T(8,128)S(1)}, f32[256,1,16]{0,2,1:T(8,128)}, u32[]{:S(2)}) copy-start(f32[256,1,16]{0,2,1:T(8,128)} %get-tuple-element.122) | copy-start | bytes 49156
  117.2 10.7 %collective-permute-start.14 = (f32[1,8,64,128]{3,2,1,0:T(8,128)S(1)}, f32[1,8,64,128]{3,2,1,0:T(8,128)S(1)}, u32[]{:S(2)}, u32[]{:S(2)}) collective-permute-start(f32[1,8,64,128]{3,2,1,0:T(8,128)S(1)} %multiply_add_fusion.4), channel_id=1, source_target_pairs={{248,216},{240,208},{232,200},{224,192},{216,184},{208,176},{200,1... | collective-permute-start | bytes 786440 | tf_op jit(solution)/shard_map/ppermute | solution.py:42
  119.2 18.2 %copy-start.11 = (f32[256,256]{1,0:T(8,128)}, f32[256,256]{1,0:T(8,128)S(1)}, u32[]{:S(2)}) copy-start(f32[256,256]{1,0:T(8,128)S(1)} %fusion.85) | copy-start | bytes 786436
  119.6 17.8 %copy-start.13 = (f32[256,256]{1,0:T(8,128)}, f32[256,256]{1,0:T(8,128)S(1)}, u32[]{:S(2)}) copy-start(f32[256,256]{1,0:T(8,128)S(1)} %fusion.91) | copy-start | bytes 786436
  127.9 10.3 %collective-permute-start.16 = (f32[1,8,64,128]{3,2,1,0:T(8,128)S(1)}, f32[1,8,64,128]{3,2,1,0:T(8,128)S(1)}, u32[]{:S(2)}, u32[]{:S(2)}) collective-permute-start(f32[1,8,64,128]{3,2,1,0:T(8,128)S(1)} %multiply_add_fusion.3), channel_id=1, source_target_pairs={{248,184},{240,176},{232,168},{224,160},{216,152},{208,144},{200,1... | collective-permute-start | bytes 786440 | tf_op jit(solution)/shard_map/ppermute | solution.py:42
  129.2 8.2 %copy-start.2 = (f32[1,256,1,16,64]{1,4,3,2,0:T(8,128)S(1)}, f32[1,256,1,16,64]{1,4,3,2,0:T(8,128)}, u32[]{:S(2)}) copy-start(f32[1,256,1,16,64]{1,4,3,2,0:T(8,128)} %copy-done.1) | copy-start | bytes 3145732
  137.4 2.2 %copy-start.18 = (f32[256,16]{0,1:T(8,128)S(1)}, f32[256,16]{0,1:T(8,128)}, u32[]{:S(2)}) copy-start(f32[256,16]{0,1:T(8,128)} %get-tuple-element.216) | copy-start | bytes 49156
  138.3 9.8 %collective-permute-start.18 = (f32[1,8,64,128]{3,2,1,0:T(8,128)S(1)}, f32[1,8,64,128]{3,2,1,0:T(8,128)S(1)}, u32[]{:S(2)}, u32[]{:S(2)}) collective-permute-start(f32[1,8,64,128]{3,2,1,0:T(8,128)S(1)} %multiply_add_fusion.2), channel_id=1, source_target_pairs={{248,120},{240,112},{232,104},{224,96},{216,88},{208,80},{200,72},... | collective-permute-start | bytes 786440 | tf_op jit(solution)/shard_map/ppermute | solution.py:42
  148.1 2.2 %copy-start.3 = (bf16[256,1024]{0,1:T(8,128)(2,1)S(1)}, bf16[256,1024]{0,1:T(8,128)(2,1)}, u32[]{:S(2)}) copy-start(bf16[256,1024]{0,1:T(8,128)(2,1)} %get-tuple-element.222) | copy-start | bytes 1572868
  149.1 3.4 %collective-permute-start.19 = (f32[1,8,64,128]{3,2,1,0:T(8,128)}, f32[1,8,64,128]{3,2,1,0:T(8,128)}, u32[]{:S(2)}, u32[]{:S(2)}) collective-permute-start(f32[1,8,64,128]{3,2,1,0:T(8,128)} %get-tuple-element.213), channel_id=1, source_target_pairs={{248,240},{240,248},{232,224},{224,232},{216,208},{208,216},{200,1... | collective-permute-start | bytes 786440 | tf_op jit(solution)/shard_map/ppermute | solution.py:42
  151.3 1.1 copy-start.7
  152.5 2.7 %copy-start.9 = (f32[256,16]{0,1:T(8,128)S(1)}, f32[256,16]{0,1:T(8,128)}, u32[]{:S(2)}) copy-start(f32[256,16]{0,1:T(8,128)} %param.13) | copy-start | bytes 49156
  152.5 2.7 %copy-start.23 = (f32[256,16]{0,1:T(8,128)S(1)}, f32[256,16]{0,1:T(8,128)}, u32[]{:S(2)}) copy-start(f32[256,16]{0,1:T(8,128)} %multiply_reduce_fusion) | copy-start | bytes 49156
  152.5 2.7 %copy-start.27 = (f32[1,1,1,16]{1,3,2,0:T(8,128)S(1)}, f32[1,1,1,16]{1,3,2,0:T(8,128)}, u32[]{:S(2)}) copy-start(f32[1,1,1,16]{1,3,2,0:T(8,128)} %get-tuple-element.228) | copy-start | bytes 196
  152.5 2.7 %copy-start.30 = (f32[256]{0:T(256)S(1)}, f32[256]{0:T(256)}, u32[]{:S(2)}) copy-start(f32[256]{0:T(256)} %copy-done.29) | copy-start | bytes 3076
  152.5 2.7 %copy-start.33 = (f32[16,256]{1,0:T(8,128)S(1)}, f32[16,256]{1,0:T(8,128)}, u32[]{:S(2)}) copy-start(f32[16,256]{1,0:T(8,128)} %get-tuple-element.189) | copy-start | bytes 49156
  152.5 2.7 %copy-start.34 = (f32[16,256]{1,0:T(8,128)S(1)}, f32[16,256]{1,0:T(8,128)}, u32[]{:S(2)}) copy-start(f32[16,256]{1,0:T(8,128)} %get-tuple-element.200) | copy-start | bytes 49156
  152.5 2.7 %copy-start.38 = (f32[256]{0:T(256)S(1)}, f32[256]{0:T(256)}, u32[]{:S(2)}) copy-start(f32[256]{0:T(256)} %copy-done.37) | copy-start | bytes 3076
  152.5 2.7 %copy-start.39 = (f32[16]{0:T(128)S(1)}, f32[16]{0:T(128)}, u32[]{:S(2)}) copy-start(f32[16]{0:T(128)} %param.16) | copy-start | bytes 196
  152.5 2.7 %copy-start.42 = (f32[16]{0:T(128)S(1)}, f32[16]{0:T(128)}, u32[]{:S(2)}) copy-start(f32[16]{0:T(128)} %copy-done.41) | copy-start | bytes 196
  155.1 7.1 %copy-start.22 = (f32[256,16]{0,1:T(8,128)S(1)}, f32[256,16]{0,1:T(8,128)}, u32[]{:S(2)}) copy-start(f32[256,16]{0,1:T(8,128)} %copy-done.21) | copy-start | bytes 49156
  159.6 6.7 %copy-start.4 = (f32[256,16,64]{0,2,1:T(8,128)S(1)}, f32[256,16,64]{0,2,1:T(8,128)}, u32[]{:S(2)}) copy-start(f32[256,16,64]{0,2,1:T(8,128)} %get-tuple-element.244) | copy-start | bytes 3145732
  159.6 6.7 %copy-start.12 = (f32[256,256]{1,0:T(8,128)S(1)}, f32[256,256]{1,0:T(8,128)}, u32[]{:S(2)}) copy-start(f32[256,256]{1,0:T(8,128)} %copy-done.11) | copy-start | bytes 786436
  159.6 6.7 %copy-start.14 = (f32[256,256]{1,0:T(8,128)S(1)}, f32[256,256]{1,0:T(8,128)}, u32[]{:S(2)}) copy-start(f32[256,256]{1,0:T(8,128)} %copy-done.13) | copy-start | bytes 786436
  166.3 4.5 %copy-start.20 = (f32[1024]{0:T(1024)S(1)}, f32[1024]{0:T(1024)}, u32[]{:S(2)}) copy-start(f32[1024]{0:T(1024)} %mul.749) | copy-start | bytes 12292
  171.1 1.1 copy-start.31
  (7 other events, 6.8 us)

commit v5 on v4

--- a/solution.py
+++ b/solution.py
@@ -12,53 +12,58 @@
 EPSILON = 1e-05
 
 
-def exclusive_scan(gain, value, move, count):
+def exclusive_scan(value, window, move, count):
     total = jnp.zeros_like(value)
-    total_gain = jnp.ones_like(gain)
     distance = 1
     while distance < count:
-        gain_in, value_in = move((gain, value), distance)
-        total = total + total_gain[..., None, None] * value_in
+        value_in = move(value, distance)
+        total = total + window(1 - distance, -1)[..., None, None] * value_in
+        if 2 * distance < count:
+            value = value + window(1 - distance, 0)[..., None, None] * value_in
         distance *= 2
-        if distance < count:
-            total_gain = total_gain * gain_in
-            value = value + gain[..., None, None] * value_in
-            gain = gain * gain_in
     return total
 
 
-def chip_scan(gain, value, axis, forward):
+def chip_scan(table, value, axis, forward):
     size = lax.axis_size(axis)
     index = lax.axis_index(axis)
     place = index if forward else size - 1 - index
     second = place % 2
     is_second = second == 1
+    chip = place // 2
     half = value.shape[1] // 2
 
     def device(p):
         return p if forward else size - 1 - p
 
-    def move(tree, pairs):
-        return lax.ppermute(tree, axis, [(device(a), device(b)) for a, b in pairs])
-
-    def pick(array, which):
-        return lax.dynamic_slice_in_dim(array, which * half, half, axis=1)
+    def move(array, pairs):
+        return lax.ppermute(array, axis, [(device(a), device(b)) for a, b in pairs])
+
+    def pick(array, which, axis_at):
+        return lax.dynamic_slice_in_dim(array, which * half, half, axis=axis_at)
+
+    ordered = table if forward else table[::-1]
+    gains = pick(ordered, second, 2).reshape((size // 2, 2) + ordered.shape[1:2] + (half,))
+    first_gain = gains[chip, 0]
+    chip_gains = gains[:, 0] * gains[:, 1]
+    chips = jnp.arange(size // 2, dtype=jnp.int32)
+
+    def window(low, high):
+        inside = (chips >= chip + low) & (chips <= chip + high)
+        return jnp.prod(jnp.where(inside[:, None, None], chip_gains, 1.0), axis=0)
 
     partners = [(p, p ^ 1) for p in range(size)]
-    own_gain, own_value = pick(gain, second), pick(value, second)
-    got_gain, got_value = move((pick(gain, 1 - second), pick(value, 1 - second)), partners)
-    first_gain = jnp.where(is_second, got_gain, own_gain)
+    own_value = pick(value, second, 1)
+    got_value = move(pick(value, 1 - second, 1), partners)
     first_value = jnp.where(is_second, got_value, own_value)
-    second_gain = jnp.where(is_second, own_gain, got_gain)
     second_value = jnp.where(is_second, own_value, got_value)
-    chip_value = second_gain[..., None, None] * first_value + second_value
-    chip_gain = first_gain * second_gain
-
-    def chip_move(tree, distance):
+    chip_value = gains[chip, 1][..., None, None] * first_value + second_value
+
+    def chip_move(array, distance):
         step = 2 * distance
-        return move(tree, [(p, p + step) for p in range(size - step)])
-
-    prefix = exclusive_scan(chip_gain, chip_value, chip_move, size // 2)
+        return move(array, [(p, p + step) for p in range(size - step)])
+
+    prefix = exclusive_scan(chip_value, window, chip_move, size // 2)
     after_first = first_value + first_gain[..., None, None] * prefix
     own_entry = jnp.where(is_second, after_first, prefix)
     got_entry = move(jnp.where(is_second, prefix, after_first), partners)
@@ -175,7 +180,8 @@
         return local_states(x_value, dt_value, b_value, segment, decay_rate)
 
     (starts, end_local, through_all), states_back = jax.vjp(states_call, x_spans, dt_spans, b_spans)
-    entry_state = chip_scan(through_all, end_local, "ctx", True)
+    decay_table = lax.all_gather(through_all, "ctx")
+    entry_state = chip_scan(decay_table, end_local, "ctx", True)
 
     def output_call(x_value, dt_value, b_value, c_value, start_value, entry_value):
         return output_part(
@@ -203,7 +209,7 @@
     grad_core = grad_gated * gate_act
     grad_gate = grad_gated * core_out * gate_sig * (1.0 + gate_float * (1.0 - gate_sig))
     first_grads = output_back(grad_core.reshape(core_part.shape))
-    exit_adjoint = chip_scan(through_all, first_grads[5], "ctx", False)
+    exit_adjoint = chip_scan(decay_table, first_grads[5], "ctx", False)
     through_grad = jnp.sum(exit_adjoint * entry_state, axis=(2, 3))
     second_grads = states_back((first_grads[4], exit_adjoint, through_grad))
     grad_input = (first_grads[0] + second_grads[0]).reshape(

time: 176 us -> 204 us (1.16)
  blocking collectives: 0 us -> 20.9 us
  starting transfers between devices: 48.7 us -> 35.2 us
  local copies, waits for them, and re-layouts: 10.9 us -> 19.8 us
  waiting for transfers between devices: 56.2 us -> 62 us
  other arithmetic: 24.8 us -> 30 us
    all_gather x0 -> x1, blocking collectives: none -> 20.9 us  [body(): decay_table = lax.all_gather(through_all, 'ctx')]
    ppermute x20 -> x12, starting transfers between devices: 40.2 us -> 26.8 us  [move(): return lax.ppermute(array, axis, [(device(a), device(b)) for a, b in pairs])]
    ppermute x20 -> x12, waiting for transfers between devices: 48.4 us -> 54.4 us  [move(): return lax.ppermute(array, axis, [(device(a), device(b)) for a, b in pairs])]
    select_n x2, other arithmetic: 1.13 us -> 3.8 us  [chip_scan(): got_entry = move(jnp.where(is_second, prefix, after_first), partners)]
    unnamed x105 -> x99, local copies, waits for them, and re-layouts: 6.25 us -> 8.78 us
    reduce_sum x0 -> x4, local copies, waits for them, and re-layouts: none -> 2.49 us  [the longest x2 1.63 us: span_mix(): spread = log_rows[..., :, None] - log_rows[..., None, :]]
    another operation x22 -> x21, local copies, waits for them, and re-layouts: 1.05 us -> 3.46 us
    mul x1 -> x7, local copies, waits for them, and re-layouts: 0.09 us -> 2.39 us  [the longest x1 0.98 us: output_part(): jnp.einsum('kqgn,kghpn->kqghp', c_spans, full_start, precision=HIGHEST_PR...]
  transfers between devices with their start and end apart: 21 -> 13, of which waited for: 12 -> 10; matrix products, arithmetic and copies ran while one was open for 15% -> 7% of each run, Pallas kernels for 0% -> 0%
where the time goes in v5:
time: 204 us; the launch traced here: 202 us
  waiting for transfers between devices  62 us (30%)
  starting transfers between devices  35.2 us (17%)
  matrix products  31.2 us (15%)
  other arithmetic  30 us (15%)
  blocking collectives  20.9 us (10%)
  local copies, waits for them, and re-layouts  19.8 us (10%)
  between operations  2.83 us (1%)
    ppermute x12, waiting for transfers between devices, move(): return lax.ppermute(array, axis, [(device(a), device(b)) for a, b in pairs])  54.4 us
    ppermute x12, starting transfers between devices, move(): return lax.ppermute(array, axis, [(device(a), device(b)) for a, b in pairs])  26.8 us
    all_gather x1, blocking collectives, body(): decay_table = lax.all_gather(through_all, 'ctx')  20.9 us
    dot_general x3, matrix products, span_mix(): jnp.einsum('ghts,sghp->tghp', weights, x_span, precision=HIGHEST_PRECISION)  17.9 us
    unnamed x99, local copies, waits for them, and re-layouts  8.78 us
    all_to_all x1, starting transfers between devices, head_sum(): return jnp.sum(lax.all_to_all(spread, axis, 0, 0), axis=0)  8.46 us
    all_to_all x1, waiting for transfers between devices, head_sum(): return jnp.sum(lax.all_to_all(spread, axis, 0, 0), axis=0)  7.68 us
    another operation x9, other arithmetic  6.92 us
  transfers between devices with their start and end apart: 13, of which 10 were waited for; matrix products, arithmetic and copies ran while one was open for 7% of the time, Pallas kernels for 0%

profile of v5, /device:TPU:6, one launch (start us, length us, event | category | flops | bytes accessed | tf_op | source)
XLA Modules:
  0.0 202.0 jit_solution(3865728406094622996)
XLA Ops:
  0.7 0.7 exponential_negate_fusion
  1.3 0.8 copy.203
  2.1 0.7 fusion.128
  3.7 1.0 reduce-window.30
  7.9 1.0 exponential_multiply_fusion
  10.3 0.7 fusion.45
  11.1 20.9 %all-gather = f32[32,1,1,16]{3,2,1,0:T(1,128)S(1)} all-gather(f32[1,1,1,16]{3,2,1,0:T(1,128)S(1)} %get-tuple-element.252), channel_id=2, replica_groups=mesh['ctx'=32,'head'=8] {'ctx'}, dimensions={0}, use_global_device_ids=true | all-gather | bytes 2112 | tf_op jit(solution)/shard_map/all_gather | solution.py:183
  32.3 4.0 %collective-permute-start.1 = (f32[1,8,64,128]{3,2,1,0:T(8,128)S(1)}, f32[1,8,64,128]{3,2,1,0:T(8,128)S(1)}, u32[]{:S(2)}, u32[]{:S(2)}) collective-permute-start(f32[1,8,64,128]{3,2,1,0:T(8,128)S(1)} %fusion.77), channel_id=1, source_target_pairs={{0,16},{8,24},{16,32},{24,40},{32,48},{40,56},{48,64},{56,72},{64,... | collective-permute-start | bytes 786440 | tf_op jit(solution)/shard_map/ppermute | solution.py:40
  36.5 6.2 %collective-permute-done.1 = f32[1,8,64,128]{3,2,1,0:T(8,128)S(1)} collective-permute-done((f32[1,8,64,128]{3,2,1,0:T(8,128)S(1)}, f32[1,8,64,128]{3,2,1,0:T(8,128)S(1)}, u32[]{:S(2)}, u32[]{:S(2)}) %collective-permute-start.1) | collective-permute-done | bytes 262176 | tf_op jit(solution)/shard_map/ppermute | solution.py:40
  42.8 4.7 %collective-permute-start.2 = (f32[1,8,64,128]{3,2,1,0:T(8,128)S(1)}, f32[1,8,64,128]{3,2,1,0:T(8,128)S(1)}, u32[]{:S(2)}, u32[]{:S(2)}) collective-permute-start(f32[1,8,64,128]{3,2,1,0:T(8,128)S(1)} %multiply_add_fusion.9), channel_id=1, source_target_pairs={{0,32},{8,40},{16,48},{24,56},{32,64},{40,72},{48,80},{56,88},{64,... | collective-permute-start | bytes 786440 | tf_op jit(solution)/shard_map/ppermute | solution.py:40
  47.5 6.6 %collective-permute-done.2 = f32[1,8,64,128]{3,2,1,0:T(8,128)S(1)} collective-permute-done((f32[1,8,64,128]{3,2,1,0:T(8,128)S(1)}, f32[1,8,64,128]{3,2,1,0:T(8,128)S(1)}, u32[]{:S(2)}, u32[]{:S(2)}) %collective-permute-start.2) | collective-permute-done | bytes 262176 | tf_op jit(solution)/shard_map/ppermute | solution.py:40
  54.2 3.0 %collective-permute-start.3 = (f32[1,8,64,128]{3,2,1,0:T(8,128)S(1)}, f32[1,8,64,128]{3,2,1,0:T(8,128)S(1)}, u32[]{:S(2)}, u32[]{:S(2)}) collective-permute-start(f32[1,8,64,128]{3,2,1,0:T(8,128)S(1)} %multiply_add_fusion.8), channel_id=1, source_target_pairs={{0,64},{8,72},{16,80},{24,88},{32,96},{40,104},{48,112},{56,120},{... | collective-permute-start | bytes 786440 | tf_op jit(solution)/shard_map/ppermute | solution.py:40
  57.3 0.8 fusion.84
  58.1 3.4 %collective-permute-done.3 = f32[1,8,64,128]{3,2,1,0:T(8,128)S(1)} collective-permute-done((f32[1,8,64,128]{3,2,1,0:T(8,128)S(1)}, f32[1,8,64,128]{3,2,1,0:T(8,128)S(1)}, u32[]{:S(2)}, u32[]{:S(2)}) %collective-permute-start.3) | collective-permute-done | bytes 262176 | tf_op jit(solution)/shard_map/ppermute | solution.py:40
  61.5 5.7 %collective-permute-start.4 = (f32[1,8,64,128]{3,2,1,0:T(8,128)S(1)}, f32[1,8,64,128]{3,2,1,0:T(8,128)S(1)}, u32[]{:S(2)}, u32[]{:S(2)}) collective-permute-start(f32[1,8,64,128]{3,2,1,0:T(8,128)S(1)} %multiply_add_fusion.7), channel_id=1, source_target_pairs={{0,128},{8,136},{16,144},{24,152},{32,160},{40,168},{48,176},{56,1... | collective-permute-start | bytes 786440 | tf_op jit(solution)/shard_map/ppermute | solution.py:40
  67.3 0.9 fusion.133
  68.2 2.9 %collective-permute-done.4 = f32[1,8,64,128]{3,2,1,0:T(8,128)S(1)} collective-permute-done((f32[1,8,64,128]{3,2,1,0:T(8,128)S(1)}, f32[1,8,64,128]{3,2,1,0:T(8,128)S(1)}, u32[]{:S(2)}, u32[]{:S(2)}) %collective-permute-start.4) | collective-permute-done | bytes 262176 | tf_op jit(solution)/shard_map/ppermute | solution.py:40
  71.1 0.7 copy-done.13
  71.8 1.9 fusion.81
  74.4 1.0 copy.215
  75.7 1.2 copy.217
  77.7 1.0 copy-done.1
  78.7 3.2 %fusion.37 = f32[1,256,1,16,64]{1,4,3,2,0:T(8,128)S(1)} fusion(bf16[256,16,64]{0,2,1:T(8,128)(2,1)S(1)} %bitcast.318, f32[16,256]{1,0:T(8,128)S(1)} %copy.209, f32[256,256]{1,0:T(8,128)S(1)} %copy-done.15, f32[16,256]{1,0:T(8,128)S(1)} %copy.207, f32[256,256]{1,0:T(8,128)S(1)} %copy-done.14, f32[1,256,1,16,64]{1,4,3,2,0:T(8,128)S(1)} %convolution_bitcast_fusion.1, ...), kind=kOutput, calls=%fused_computation.40 | convolution fusion | flops 811073536 | bytes 3194880 | tf_op jit(solution)/shard_map/jvp()/while/body/eval_jaxpr/ghts,sghp->tghp/dot_general | solution.py:93
  82.0 1.6 multiply_reduce_fusion.2
  83.6 0.6 broadcast_in_dim.247
  84.2 8.5 %all-to-all-start = ((f32[8,2,256]{2,1,0:T(2,128)}), f32[8,2,256]{2,1,0:T(2,128)S(1)}, u32[]{:S(2)}, u32[]{:S(2)}) async-start(f32[8,2,256]{2,1,0:T(2,128)} %broadcast_in_dim.247), calls=%async_computation | async-start | bytes 32768 | tf_op jit(solution)/shard_map/all_to_all | solution.py:80
  92.7 7.7 %all-to-all-done = f32[8,2,256]{2,1,0:T(2,128)S(1)} async-done(((f32[8,2,256]{2,1,0:T(2,128)}), f32[8,2,256]{2,1,0:T(2,128)S(1)}, u32[]{:S(2)}, u32[]{:S(2)}) %all-to-all-start) | async-done | bytes 16416 | tf_op jit(solution)/shard_map/all_to_all | solution.py:80
  100.5 3.1 %fusion.55 = (bf16[256,1024]{0,1:T(8,128)(2,1)}, f32[256,1024]{0,1:T(8,128)S(1)}) fusion(bf16[256,1024]{0,1:T(8,128)(2,1)S(1)} %copy.216, f32[1024]{0:T(1024)S(1)} %mul.782, bf16[256,1024]{0,1:T(8,128)(2,1)S(1)} %copy.202, f32[1,256,1,16,64]{1,4,3,2,0:T(8,128)} %copy-done, f32[256]{0:T(256)S(1)} %multiply_multiply_fusion.1, ...), kind=kLoop, calls=%fused_computation.59 | loop fusion | flops 5767168 | bytes 5253120 | tf_op jit(solution)/shard_map/convert_element_type | solution.py:225
  103.6 0.6 fusion.57
  105.1 1.0 collective-permute-done.6
  106.1 0.8 fusion.76
  106.9 3.3 %collective-permute-start.7 = (f32[1,8,64,128]{3,2,1,0:T(8,128)}, f32[1,8,64,128]{3,2,1,0:T(8,128)}, u32[]{:S(2)}, u32[]{:S(2)}) collective-permute-start(f32[1,8,64,128]{3,2,1,0:T(8,128)} %fusion.76), channel_id=1, source_target_pairs={{248,232},{240,224},{232,216},{224,208},{216,200},{208,192},{200,1... | collective-permute-start | bytes 786440 | tf_op jit(solution)/shard_map/ppermute | solution.py:40
  110.5 9.3 %collective-permute-done.7 = f32[1,8,64,128]{3,2,1,0:T(8,128)} collective-permute-done((f32[1,8,64,128]{3,2,1,0:T(8,128)}, f32[1,8,64,128]{3,2,1,0:T(8,128)}, u32[]{:S(2)}, u32[]{:S(2)}) %collective-permute-start.7) | collective-permute-done | bytes 262176 | tf_op jit(solution)/shard_map/ppermute | solution.py:40
  119.8 1.1 multiply_add_fusion.4
  121.0 3.0 %collective-permute-start.8 = (f32[1,8,64,128]{3,2,1,0:T(8,128)S(1)}, f32[1,8,64,128]{3,2,1,0:T(8,128)S(1)}, u32[]{:S(2)}, u32[]{:S(2)}) collective-permute-start(f32[1,8,64,128]{3,2,1,0:T(8,128)S(1)} %multiply_add_fusion.4), channel_id=1, source_target_pairs={{248,216},{240,208},{232,200},{224,192},{216,184},{208,176},{200,1... | collective-permute-start | bytes 786440 | tf_op jit(solution)/shard_map/ppermute | solution.py:40
  124.0 9.2 %collective-permute-done.8 = f32[1,8,64,128]{3,2,1,0:T(8,128)S(1)} collective-permute-done((f32[1,8,64,128]{3,2,1,0:T(8,128)S(1)}, f32[1,8,64,128]{3,2,1,0:T(8,128)S(1)}, u32[]{:S(2)}, u32[]{:S(2)}) %collective-permute-start.8) | collective-permute-done | bytes 262176 | tf_op jit(solution)/shard_map/ppermute | solution.py:40
  133.3 1.3 collective-permute-start.9
  134.6 9.4 %collective-permute-done.9 = f32[1,8,64,128]{3,2,1,0:T(8,128)S(1)} collective-permute-done((f32[1,8,64,128]{3,2,1,0:T(8,128)S(1)}, f32[1,8,64,128]{3,2,1,0:T(8,128)S(1)}, u32[]{:S(2)}, u32[]{:S(2)}) %collective-permute-start.9) | collective-permute-done | bytes 262176 | tf_op jit(solution)/shard_map/ppermute | solution.py:40
  144.1 1.4 collective-permute-start.10
  145.6 0.7 bitcast_convert_fusion
  146.2 1.1 convert.9
  147.5 6.5 %collective-permute-done.10 = f32[1,8,64,128]{3,2,1,0:T(8,128)S(1)} collective-permute-done((f32[1,8,64,128]{3,2,1,0:T(8,128)S(1)}, f32[1,8,64,128]{3,2,1,0:T(8,128)S(1)}, u32[]{:S(2)}, u32[]{:S(2)}) %collective-permute-start.10) | collective-permute-done | bytes 262176 | tf_op jit(solution)/shard_map/ppermute | solution.py:40
  154.0 1.9 fusion.79
  156.0 2.5 %convolution_bitcast_fusion.3 = f32[256,128]{1,0:T(8,128)} fusion(f32[1,256,1,16,64]{1,4,3,2,0:T(8,128)S(1)} %bitcast.314, f32[256,16]{0,1:T(8,128)S(1)} %copy.215, f32[8,64,128]{2,1,0:T(8,128)S(1)} %bitcast.327, f32[8,64,128]{2,1,0:T(8,128)S(1)} %bitcast.331, pred[]{:T(512)S(6)} %eq.98), kind=kOutput, calls=%fused_computation.50 | convolution fusion | flops 403308544 | bytes 1720321 | tf_op jit(solution)/shard_map/transpose(jvp(kqgn,kghpn->kqghp))/dot_general | solution.py:142
  158.4 2.0 %copy.239 = bf16[256,1024]{1,0:T(8,128)(2,1)} copy(bf16[256,1024]{0,1:T(8,128)(2,1)} %get-tuple-element.242) | data formatting | bytes 1048576
  160.5 0.8 copy.228
  161.2 1.1 fusion.78
  162.3 2.6 %fusion.49 = (f32[256,16]{0,1:T(8,128)S(1)}, f32[256,16,64]{0,2,1:T(8,128)}) fusion(bf16[256,1024]{0,1:T(8,128)(2,1)S(1)} %copy.202, bf16[256,128]{1,0:T(8,128)(2,1)} %param.14, f32[8,64,128]{2,1,0:T(8,128)S(1)} %bitcast.328, f32[8,64,128]{2,1,0:T(8,128)} %bitcast.77, pred[]{:T(512)S(6)} %eq.108), kind=kOutput, calls=%fused_computation.53 | convolution fusion | flops 403828736 | bytes 2179073 | tf_op jit(solution)/shard_map/transpose(jvp(kqgh,kqghp,kqgn->kghpn))/dot_general | solution.py:107
  165.0 0.8 multiply_multiply_fusion
  165.9 0.7 copy.221
  167.1 9.3 %fusion.75 = (f32[16,256]{1,0:T(8,128)}, f32[16,256]{1,0:T(8,128)}, f32[16,256]{1,0:T(8,128)}, f32[256,256]{1,0:T(8,128)S(1)}) fusion(f32[16,256]{1,0:T(8,128)S(1)} %copy.219, f32[256,256]{1,0:T(8,128)S(1)} %fusion.85, f32[16,256]{1,0:T(8,128)} %copy.221, f32[256,256]{1,0:T(8,128)S(1)} %fusion.92, f32[256,1,16,64]{0,3,2,1:T(8,128)} %convert.9, ...), kind=kOutput, calls=%fused_computation.91 | convolution fusion | flops 825151488 | bytes 2965504 | tf_op jit(solution)/shard_map/transpose(jvp())/while/body/eval_jaxpr/checkpoint/ghts,sghp->tghp/dot_general | solution.py:93
  176.3 0.8 copy.226
  177.2 0.8 copy.227
  178.0 1.3 multiply_reduce_fusion.3
  179.4 1.2 fusion.130
  180.7 2.5 %reduce-window.36 = f32[1,16,1,2,128]{4,1,2,3,0:T(8,128)S(1)} reduce-window(f32[1,16,1,2,128]{4,1,2,3,0:T(8,128)S(1)} %copy.234, f32[]{:T(128)} %constant.167.clone.1), window={size=1x1x1x1x128 pad=0_0x0_0x0_0x0_0x0_127}, to_apply=%region_30.31 | reduce-window | flops 520192 | bytes 32772 | tf_op jit(solution)/shard_map/reduce-window.6
  183.2 0.7 slice_reduce_fusion
  184.6 2.5 %reduce-window.34 = f32[1,16,1,2,128]{4,1,2,3,0:T(8,128)S(1)} reduce-window(f32[1,16,1,2,128]{4,1,2,3,0:T(8,128)S(1)} %copy.229, f32[]{:T(128)} %constant.167.clone.1), window={size=1x1x1x1x128 pad=0_0x0_0x0_0x0_0x0_127}, to_apply=%region_25.26 | reduce-window | flops 520192 | bytes 32772 | tf_op jit(solution)/shard_map/reduce-window.4
  187.1 0.7 slice_reduce_fusion.1
  188.4 5.4 %fusion.40 = f32[256,16,64]{0,2,1:T(8,128)S(1)} fusion(f32[16,256]{1,0:T(8,128)} %copy.221, f32[256,256]{1,0:T(8,128)S(1)} %copy-done.17, f32[16,256]{1,0:T(8,128)} %copy-done.29, f32[256,256]{1,0:T(8,128)} %copy-done.18, f32[256,1,16,64]{0,3,2,1:T(8,128)S(1)} %bitcast.316, f32[256,16,64]{0,2,1:T(8,128)} %get-tuple-element.260, f32[256,16]{0,1:T(8,128)S(1)} %copy-done.22), kind=kOutput, calls=%fused_computation.41 | convolution fusion | flops 811073536 | bytes 3719168 | tf_op jit(solution)/shard_map/transpose(jvp())/while/body/eval_jaxpr/checkpoint/ghts,sghp->tghp/dot_general | solution.py:93
  194.7 1.0 convolution_add_fusion
  195.7 3.5 %fusion.48 = f32[256,128]{1,0:T(8,128)} fusion(f32[1,256,1,128]{3,1,2,0:T(8,128)S(1)} %convolution_bitcast_fusion.2, bf16[256,16,64]{0,2,1:T(8,128)(2,1)S(1)} %bitcast.320, f32[256,16]{0,1:T(8,128)S(1)} %copy-done.22, f32[8,64,128]{2,1,0:T(8,128)S(1)} %bitcast.329, f32[8,64,128]{2,1,0:T(8,128)} %bitcast.77, pred[]{:T(512)S(6)} %eq.108), kind=kOutput, calls=%fused_computation.52 | convolution fusion | flops 403603456 | bytes 1327105 | tf_op jit(solution)/shard_map/transpose(jvp(kqgh,kqghp,kqgn->kghpn))/dot_general | solution.py:107
  199.3 1.0 copy.238
  201.3 0.7 copy.240
  (185 shorter events, 12.5 us)
Async XLA Ops:
  0.6 8.9 %copy-start.34 = (f32[16]{0:T(128)S(1)}, f32[16]{0:T(128)}, u32[]{:S(2)}) copy-start(f32[16]{0:T(128)} %param.16) | copy-start | bytes 196
  1.3 1.6 copy-start.42
  2.9 6.8 %copy-start.9 = (bf16[256,1024]{1,0:T(8,128)(2,1)S(1)}, bf16[256,1024]{1,0:T(8,128)(2,1)}, u32[]{:S(2)}) copy-start(bf16[256,1024]{1,0:T(8,128)(2,1)} %param.11) | copy-start | bytes 1572868
  5.7 3.9 %copy-start.33 = (f32[256]{0:T(256)}, f32[256]{0:T(256)S(1)}, u32[]{:S(2)}) copy-start(f32[256]{0:T(256)S(1)} %get-tuple-element.238) | copy-start | bytes 3076
  5.7 51.5 %copy-start.25 = (s32[256]{0:T(256)}, s32[256]{0:T(256)S(1)}, u32[]{:S(2)}) copy-start(s32[256]{0:T(256)S(1)} %get-tuple-element.121) | copy-start | bytes 3076
  8.8 1.4 copy-start.6
  8.9 0.6 copy-start.37
  8.9 0.6 copy-start.30
  9.7 0.6 copy-start.21
  11.0 21.2 %collective-permute-start = (f32[1,8,64,128]{3,2,1,0:T(8,128)S(1)}, f32[1,8,64,128]{3,2,1,0:T(8,128)S(1)}, u32[]{:S(2)}, u32[]{:S(2)}) collective-permute-start(f32[1,8,64,128]{3,2,1,0:T(8,128)S(1)} %dynamic-slice_bitcast_fusion.1), channel_id=1, source_target_pairs={{0,8},{8,0},{16,24},{24,16},{32,40},{40,32},{48,56},{56,48},{64,72... | collective-permute-start | bytes 786440 | tf_op jit(solution)/shard_map/ppermute | solution.py:40
  32.3 10.5 %collective-permute-start.1 = (f32[1,8,64,128]{3,2,1,0:T(8,128)S(1)}, f32[1,8,64,128]{3,2,1,0:T(8,128)S(1)}, u32[]{:S(2)}, u32[]{:S(2)}) collective-permute-start(f32[1,8,64,128]{3,2,1,0:T(8,128)S(1)} %fusion.77), channel_id=1, source_target_pairs={{0,16},{8,24},{16,32},{24,40},{32,48},{40,56},{48,64},{56,72},{64,... | collective-permute-start | bytes 786440 | tf_op jit(solution)/shard_map/ppermute | solution.py:40
  42.8 24.5 %copy-start.4 = (bf16[256,128]{1,0:T(8,128)(2,1)S(1)}, bf16[256,128]{1,0:T(8,128)(2,1)}, u32[]{:S(2)}) copy-start(bf16[256,128]{1,0:T(8,128)(2,1)} %param.15) | copy-start | bytes 196612
  42.8 11.2 %collective-permute-start.2 = (f32[1,8,64,128]{3,2,1,0:T(8,128)S(1)}, f32[1,8,64,128]{3,2,1,0:T(8,128)S(1)}, u32[]{:S(2)}, u32[]{:S(2)}) collective-permute-start(f32[1,8,64,128]{3,2,1,0:T(8,128)S(1)} %multiply_add_fusion.9), channel_id=1, source_target_pairs={{0,32},{8,40},{16,48},{24,56},{32,64},{40,72},{48,80},{56,88},{64,... | collective-permute-start | bytes 786440 | tf_op jit(solution)/shard_map/ppermute | solution.py:40
  54.2 7.3 %collective-permute-start.3 = (f32[1,8,64,128]{3,2,1,0:T(8,128)S(1)}, f32[1,8,64,128]{3,2,1,0:T(8,128)S(1)}, u32[]{:S(2)}, u32[]{:S(2)}) collective-permute-start(f32[1,8,64,128]{3,2,1,0:T(8,128)S(1)} %multiply_add_fusion.8), channel_id=1, source_target_pairs={{0,64},{8,72},{16,80},{24,88},{32,96},{40,104},{48,112},{56,120},{... | collective-permute-start | bytes 786440 | tf_op jit(solution)/shard_map/ppermute | solution.py:40
  61.5 9.6 %collective-permute-start.4 = (f32[1,8,64,128]{3,2,1,0:T(8,128)S(1)}, f32[1,8,64,128]{3,2,1,0:T(8,128)S(1)}, u32[]{:S(2)}, u32[]{:S(2)}) collective-permute-start(f32[1,8,64,128]{3,2,1,0:T(8,128)S(1)} %multiply_add_fusion.7), channel_id=1, source_target_pairs={{0,128},{8,136},{16,144},{24,152},{32,160},{40,168},{48,176},{56,1... | collective-permute-start | bytes 786440 | tf_op jit(solution)/shard_map/ppermute | solution.py:40
  71.1 0.7 copy-start.13
  71.8 2.4 %copy-start.45 = (f32[16]{0:T(128)S(1)}, f32[16]{0:T(128)}, u32[]{:S(2)}) copy-start(f32[16]{0:T(128)} %param.18) | copy-start | bytes 196
  71.8 3.7 %copy-start.10 = (bf16[256,1024]{1,0:T(8,128)(2,1)S(1)}, bf16[256,1024]{1,0:T(8,128)(2,1)}, u32[]{:S(2)}) copy-start(bf16[256,1024]{1,0:T(8,128)(2,1)} %param.12) | copy-start | bytes 1572868
  73.7 3.4 %collective-permute-start.5 = (f32[1,8,64,128]{3,2,1,0:T(8,128)}, f32[1,8,64,128]{3,2,1,0:T(8,128)S(1)}, u32[]{:S(2)}, u32[]{:S(2)}) collective-permute-start(f32[1,8,64,128]{3,2,1,0:T(8,128)} %get-tuple-element.240), channel_id=1, source_target_pairs={{0,8},{8,0},{16,24},{24,16},{32,40},{40,32},{48,56},{56,48},{64,72... | collective-permute-start | bytes 786440 | tf_op jit(solution)/shard_map/ppermute | solution.py:40
  74.4 26.1 %copy-start.19 = (f32[1024]{0:T(1024)}, f32[1024]{0:T(1024)S(1)}, u32[]{:S(2)}) copy-start(f32[1024]{0:T(1024)S(1)} %mul.782) | copy-start | bytes 12292
  77.1 1.6 copy-start.14
  77.1 1.6 copy-start.15
  77.7 1.0 copy-start.1
  78.7 3.3 %copy-start.27 = (f32[1024]{0:T(1024)S(1)}, f32[1024]{0:T(1024)}, u32[]{:S(2)}) copy-start(f32[1024]{0:T(1024)} %param.19) | copy-start | bytes 12292
  82.0 1.6 copy-start
  84.2 16.2 %all-to-all-start = ((f32[8,2,256]{2,1,0:T(2,128)}), f32[8,2,256]{2,1,0:T(2,128)S(1)}, u32[]{:S(2)}, u32[]{:S(2)}) async-start(f32[8,2,256]{2,1,0:T(2,128)} %broadcast_in_dim.247), calls=%async_computation | async-start | bytes 32768 | tf_op jit(solution)/shard_map/all_to_all | solution.py:80
  104.2 6.1 %copy-start.44 = (pred[16]{0:T(512)(128)(4,1)S(1)}, pred[16]{0:T(512)(128)(4,1)}, u32[]{:S(2)}) copy-start(pred[16]{0:T(512)(128)(4,1)} %get-tuple-element.264) | copy-start | bytes 52
  104.3 1.8 collective-permute-start.6
  106.1 28.5 %copy-start.7 = (bf16[256,128]{1,0:T(8,128)(2,1)S(1)}, bf16[256,128]{1,0:T(8,128)(2,1)}, u32[]{:S(2)}) copy-start(bf16[256,128]{1,0:T(8,128)(2,1)} %param.14) | copy-start | bytes 196612
  106.9 13.0 %collective-permute-start.7 = (f32[1,8,64,128]{3,2,1,0:T(8,128)}, f32[1,8,64,128]{3,2,1,0:T(8,128)}, u32[]{:S(2)}, u32[]{:S(2)}) collective-permute-start(f32[1,8,64,128]{3,2,1,0:T(8,128)} %fusion.76), channel_id=1, source_target_pairs={{248,232},{240,224},{232,216},{224,208},{216,200},{208,192},{200,1... | collective-permute-start | bytes 786440 | tf_op jit(solution)/shard_map/ppermute | solution.py:40
  121.0 24.6 %copy-start.5 = (bf16[256,128]{1,0:T(8,128)(2,1)S(1)}, bf16[256,128]{1,0:T(8,128)(2,1)}, u32[]{:S(2)}) copy-start(bf16[256,128]{1,0:T(8,128)(2,1)} %param.15) | copy-start | bytes 196612
  121.0 12.2 %collective-permute-start.8 = (f32[1,8,64,128]{3,2,1,0:T(8,128)S(1)}, f32[1,8,64,128]{3,2,1,0:T(8,128)S(1)}, u32[]{:S(2)}, u32[]{:S(2)}) collective-permute-start(f32[1,8,64,128]{3,2,1,0:T(8,128)S(1)} %multiply_add_fusion.4), channel_id=1, source_target_pairs={{248,216},{240,208},{232,200},{224,192},{216,184},{208,176},{200,1... | collective-permute-start | bytes 786440 | tf_op jit(solution)/shard_map/ppermute | solution.py:40
  133.3 10.7 %collective-permute-start.9 = (f32[1,8,64,128]{3,2,1,0:T(8,128)S(1)}, f32[1,8,64,128]{3,2,1,0:T(8,128)S(1)}, u32[]{:S(2)}, u32[]{:S(2)}) collective-permute-start(f32[1,8,64,128]{3,2,1,0:T(8,128)S(1)} %multiply_add_fusion.3), channel_id=1, source_target_pairs={{248,184},{240,176},{232,168},{224,160},{216,152},{208,144},{200,1... | collective-permute-start | bytes 786440 | tf_op jit(solution)/shard_map/ppermute | solution.py:40
  144.1 3.3 %copy-start.2 = (f32[1,256,1,16,64]{1,4,3,2,0:T(8,128)S(1)}, f32[1,256,1,16,64]{1,4,3,2,0:T(8,128)}, u32[]{:S(2)}) copy-start(f32[1,256,1,16,64]{1,4,3,2,0:T(8,128)} %copy-done.1) | copy-start | bytes 3145732
  144.1 9.9 %collective-permute-start.10 = (f32[1,8,64,128]{3,2,1,0:T(8,128)S(1)}, f32[1,8,64,128]{3,2,1,0:T(8,128)S(1)}, u32[]{:S(2)}, u32[]{:S(2)}) collective-permute-start(f32[1,8,64,128]{3,2,1,0:T(8,128)S(1)} %multiply_add_fusion.2), channel_id=1, source_target_pairs={{248,120},{240,112},{232,104},{224,96},{216,88},{208,80},{200,72},... | collective-permute-start | bytes 786440 | tf_op jit(solution)/shard_map/ppermute | solution.py:40
  147.4 6.7 %copy-start.39 = (f32[8]{0:T(128)S(1)}, f32[8]{0:T(128)}, u32[]{:S(2)}) copy-start(f32[8]{0:T(128)} %get-tuple-element.254) | copy-start | bytes 100
  156.0 6.3 %collective-permute-start.11 = (f32[1,8,64,128]{3,2,1,0:T(8,128)}, f32[1,8,64,128]{3,2,1,0:T(8,128)}, u32[]{:S(2)}, u32[]{:S(2)}) collective-permute-start(f32[1,8,64,128]{3,2,1,0:T(8,128)} %get-tuple-element.233), channel_id=1, source_target_pairs={{248,240},{240,248},{232,224},{224,232},{216,208},{208,216},{200,1... | collective-permute-start | bytes 786440 | tf_op jit(solution)/shard_map/ppermute | solution.py:40
  162.3 2.7 %copy-start.31 = (f32[256]{0:T(256)S(1)}, f32[256]{0:T(256)}, u32[]{:S(2)}) copy-start(f32[256]{0:T(256)} %copy-done.30) | copy-start | bytes 3076
  162.3 2.7 %copy-start.35 = (f32[16]{0:T(128)S(1)}, f32[16]{0:T(128)}, u32[]{:S(2)}) copy-start(f32[16]{0:T(128)} %param.16) | copy-start | bytes 196
  162.3 4.2 %copy-start.26 = (s32[256]{0:T(256)S(1)}, s32[256]{0:T(256)}, u32[]{:S(2)}) copy-start(s32[256]{0:T(256)} %copy-done.25) | copy-start | bytes 3076
  164.9 1.7 copy-start.3
  165.9 10.5 %copy-start.29 = (f32[16,256]{1,0:T(8,128)}, f32[16,256]{1,0:T(8,128)S(1)}, u32[]{:S(2)}) copy-start(f32[16,256]{1,0:T(8,128)S(1)} %copy.219) | copy-start | bytes 49156
  166.7 9.7 %copy-start.16 = (f32[256,256]{1,0:T(8,128)}, f32[256,256]{1,0:T(8,128)S(1)}, u32[]{:S(2)}) copy-start(f32[256,256]{1,0:T(8,128)S(1)} %fusion.85) | copy-start | bytes 786436
  167.1 9.3 %copy-start.18 = (f32[256,256]{1,0:T(8,128)}, f32[256,256]{1,0:T(8,128)S(1)}, u32[]{:S(2)}) copy-start(f32[256,256]{1,0:T(8,128)S(1)} %fusion.92) | copy-start | bytes 786436
  178.0 1.4 copy-start.11
  178.0 1.4 copy-start.12
  179.3 9.1 %copy-start.17 = (f32[256,256]{1,0:T(8,128)S(1)}, f32[256,256]{1,0:T(8,128)}, u32[]{:S(2)}) copy-start(f32[256,256]{1,0:T(8,128)} %copy-done.16) | copy-start | bytes 786436
  179.3 9.1 %copy-start.22 = (f32[256,16]{0,1:T(8,128)S(1)}, f32[256,16]{0,1:T(8,128)}, u32[]{:S(2)}) copy-start(f32[256,16]{0,1:T(8,128)} %copy-done.21) | copy-start | bytes 49156
  188.4 5.4 %copy-start.20 = (f32[1024]{0:T(1024)S(1)}, f32[1024]{0:T(1024)}, u32[]{:S(2)}) copy-start(f32[1024]{0:T(1024)} %copy-done.19) | copy-start | bytes 12292
  193.8 0.9 copy-start.8
  195.7 4.5 %copy-start.40 = (f32[16,2]{0,1:T(2,128)S(1)}, f32[16,2]{0,1:T(2,128)}, u32[]{:S(2)}) copy-start(f32[16,2]{0,1:T(2,128)} %slice_reduce_fusion) | copy-start | bytes 388
  195.7 4.6 %copy-start.41 = (f32[16,2]{0,1:T(2,128)S(1)}, f32[16,2]{0,1:T(2,128)}, u32[]{:S(2)}) copy-start(f32[16,2]{0,1:T(2,128)} %slice_reduce_fusion.1) | copy-start | bytes 388
  195.7 4.6 %copy-start.24 = (f32[1,16,1,2,128]{4,3,2,1,0:T(2,128)S(1)}, f32[1,16,1,2,128]{4,3,2,1,0:T(2,128)}, u32[]{:S(2)}) copy-start(f32[1,16,1,2,128]{4,3,2,1,0:T(2,128)} %copy.230) | copy-start | bytes 49156
  199.2 1.2 copy-start.23
  199.2 1.3 copy-start.28
  199.3 1.5 copy-start.32
  199.3 1.5 copy-start.38
  199.3 1.5 copy-start.43
  200.3 1.0 copy-start.36

commit v6 on v4

--- a/solution.py
+++ b/solution.py
@@ -73,6 +73,22 @@
     size = lax.axis_size(axis)
     spread = jnp.broadcast_to(value[None], (size,) + value.shape)
     return jnp.sum(lax.all_to_all(spread, axis, 0, 0), axis=0)
+
+
+def split_scan(gain, value, axis, forward, pieces):
+    width = value.shape[1] // pieces
+    return jnp.concatenate(
+        [
+            chip_scan(
+                gain[:, k * width : (k + 1) * width],
+                value[:, k * width : (k + 1) * width],
+                axis,
+                forward,
+            )
+            for k in range(pieces)
+        ],
+        axis=1,
+    )
 
 
 def span_mix(x_span, dt_span, b_span, c_span, log_cum, segment):
@@ -175,7 +191,7 @@
         return local_states(x_value, dt_value, b_value, segment, decay_rate)
 
     (starts, end_local, through_all), states_back = jax.vjp(states_call, x_spans, dt_spans, b_spans)
-    entry_state = chip_scan(through_all, end_local, "ctx", True)
+    entry_state = split_scan(through_all, end_local, "ctx", True, 2)
 
     def output_call(x_value, dt_value, b_value, c_value, start_value, entry_value):
         return output_part(
@@ -203,7 +219,7 @@
     grad_core = grad_gated * gate_act
     grad_gate = grad_gated * core_out * gate_sig * (1.0 + gate_float * (1.0 - gate_sig))
     first_grads = output_back(grad_core.reshape(core_part.shape))
-    exit_adjoint = chip_scan(through_all, first_grads[5], "ctx", False)
+    exit_adjoint = split_scan(through_all, first_grads[5], "ctx", False, 2)
     through_grad = jnp.sum(exit_adjoint * entry_state, axis=(2, 3))
     second_grads = states_back((first_grads[4], exit_adjoint, through_grad))
     grad_input = (first_grads[0] + second_grads[0]).reshape(

time: 176 us -> 207 us (1.18)
  starting transfers between devices: 48.7 us -> 101 us
  waiting for transfers between devices: 56.2 us -> 31.6 us
  other arithmetic: 24.8 us -> 28 us
    ppermute x20 -> x40, starting transfers between devices: 40.2 us -> 92.9 us  [move(): return lax.ppermute(tree, axis, [(device(a), device(b)) for a, b in pairs])]
    ppermute x20 -> x40, waiting for transfers between devices: 48.4 us -> 25.4 us  [move(): return lax.ppermute(tree, axis, [(device(a), device(b)) for a, b in pairs])]
    dot_general x3, matrix products: 6.79 us -> 4.07 us  [local_states(): jnp.einsum('kqgh,kqghp,kqgn->kghpn', tail_decay * dt_spans, x_spans, b_sp...]
    unnamed x105 -> x155, local copies, waits for them, and re-layouts: 6.25 us -> 6.56 us
  transfers between devices with their start and end apart: 21 -> 41, of which waited for: 12 -> 15; matrix products, arithmetic and copies ran while one was open for 15% -> 13% of each run, Pallas kernels for 0% -> 0%
where the time goes in v6:
time: 207 us; the launch traced here: 205 us
  starting transfers between devices  101 us (49%)
  waiting for transfers between devices  31.6 us (15%)
  matrix products  28.3 us (14%)
  other arithmetic  28 us (14%)
  local copies, waits for them, and re-layouts  12.4 us (6%)
  between operations  3.45 us (2%)
    ppermute x40, starting transfers between devices, move(): return lax.ppermute(tree, axis, [(device(a), device(b)) for a, b in pairs])  92.9 us
    ppermute x40, waiting for transfers between devices, move(): return lax.ppermute(tree, axis, [(device(a), device(b)) for a, b in pairs])  25.4 us
    dot_general x3, matrix products, span_mix(): jnp.einsum('ghts,sghp->tghp', weights, x_span, precision=HIGHEST_PRECISION)  17 us
    all_to_all x1, starting transfers between devices, head_sum(): return jnp.sum(lax.all_to_all(spread, axis, 0, 0), axis=0)  8.47 us
    another operation x10, other arithmetic  7.73 us
    unnamed x155, local copies, waits for them, and re-layouts  6.56 us
    all_to_all x1, waiting for transfers between devices, head_sum(): return jnp.sum(lax.all_to_all(spread, axis, 0, 0), axis=0)  6.27 us
  transfers between devices with their start and end apart: 41, of which 15 were waited for; matrix products, arithmetic and copies ran while one was open for 13% of the time, Pallas kernels for 0%

profile of v6, /device:TPU:6, one launch (start us, length us, event | category | flops | bytes accessed | tf_op | source)
XLA Modules:
  0.0 205.3 jit_solution(11811836352079599565)
XLA Ops:
  1.3 1.4 fusion.119
  3.6 1.0 reduce-window.30
  9.8 0.8 fusion.106
  10.7 1.2 copy.122
  14.5 0.8 fusion.81
  15.3 0.9 fusion.130
  17.4 1.1 convert.9
  18.6 1.2 fusion.122
  19.9 1.3 fusion.123
  21.6 2.7 %collective-permute-start.23 = (f32[1,4]{1,0:T(1,128)S(1)}, f32[1,4]{1,0:T(1,128)S(1)}, u32[]{:S(2)}, u32[]{:S(2)}) collective-permute-start(f32[1,4]{1,0:T(1,128)S(1)} %get-tuple-element.213), channel_id=1, source_target_pairs={{248,232},{240,224},{232,216},{224,208},{216,200},{208,192},{200,1... | collective-permute-start | bytes 56 | tf_op jit(solution)/shard_map/ppermute | solution.py:42
  24.3 2.4 %collective-permute-start.33 = (f32[1,4]{1,0:T(1,128)S(1)}, f32[1,4]{1,0:T(1,128)S(1)}, u32[]{:S(2)}, u32[]{:S(2)}) collective-permute-start(f32[1,4]{1,0:T(1,128)S(1)} %get-tuple-element.218), channel_id=1, source_target_pairs={{248,232},{240,224},{232,216},{224,208},{216,200},{208,192},{200,1... | collective-permute-start | bytes 56 | tf_op jit(solution)/shard_map/ppermute | solution.py:42
  26.9 5.5 %collective-permute-start.3 = (f32[1,4]{1,0:T(1,128)S(1)}, f32[1,4]{1,0:T(1,128)S(1)}, u32[]{:S(2)}, u32[]{:S(2)}) collective-permute-start(f32[1,4]{1,0:T(1,128)S(1)} %get-tuple-element.228), channel_id=1, source_target_pairs={{0,16},{8,24},{16,32},{24,40},{32,48},{40,56},{48,64},{56,72},{64,... | collective-permute-start | bytes 56 | tf_op jit(solution)/shard_map/ppermute | solution.py:42
  32.5 3.1 %collective-permute-start.13 = (f32[1,4]{1,0:T(1,128)S(1)}, f32[1,4]{1,0:T(1,128)S(1)}, u32[]{:S(2)}, u32[]{:S(2)}) collective-permute-start(f32[1,4]{1,0:T(1,128)S(1)} %get-tuple-element.233), channel_id=1, source_target_pairs={{0,16},{8,24},{16,32},{24,40},{32,48},{40,56},{48,64},{56,72},{64,... | collective-permute-start | bytes 56 | tf_op jit(solution)/shard_map/ppermute | solution.py:42
  35.6 1.9 collective-permute-start.25
  37.6 1.9 collective-permute-start.35
  39.5 6.3 %collective-permute-start.5 = (f32[1,4]{1,0:T(1,128)S(1)}, f32[1,4]{1,0:T(1,128)S(1)}, u32[]{:S(2)}, u32[]{:S(2)}) collective-permute-start(f32[1,4]{1,0:T(1,128)S(1)} %mul.931), channel_id=1, source_target_pairs={{0,32},{8,40},{16,48},{24,56},{32,64},{40,72},{48,80},{56,88},{64,... | collective-permute-start | bytes 56 | tf_op jit(solution)/shard_map/ppermute | solution.py:42
  45.9 5.4 %collective-permute-start.15 = (f32[1,4]{1,0:T(1,128)S(1)}, f32[1,4]{1,0:T(1,128)S(1)}, u32[]{:S(2)}, u32[]{:S(2)}) collective-permute-start(f32[1,4]{1,0:T(1,128)S(1)} %mul.960), channel_id=1, source_target_pairs={{0,32},{8,40},{16,48},{24,56},{32,64},{40,72},{48,80},{56,88},{64,... | collective-permute-start | bytes 56 | tf_op jit(solution)/shard_map/ppermute | solution.py:42
  51.3 1.3 collective-permute-start.27
  52.7 1.3 collective-permute-start.37
  54.0 5.2 %collective-permute-start.7 = (f32[1,4]{1,0:T(1,128)S(1)}, f32[1,4]{1,0:T(1,128)S(1)}, u32[]{:S(2)}, u32[]{:S(2)}) collective-permute-start(f32[1,4]{1,0:T(1,128)S(1)} %mul.939), channel_id=1, source_target_pairs={{0,64},{8,72},{16,80},{24,88},{32,96},{40,104},{48,112},{56,120},{... | collective-permute-start | bytes 56 | tf_op jit(solution)/shard_map/ppermute | solution.py:42
  59.2 3.9 %collective-permute-start.17 = (f32[1,4]{1,0:T(1,128)S(1)}, f32[1,4]{1,0:T(1,128)S(1)}, u32[]{:S(2)}, u32[]{:S(2)}) collective-permute-start(f32[1,4]{1,0:T(1,128)S(1)} %mul.968), channel_id=1, source_target_pairs={{0,64},{8,72},{16,80},{24,88},{32,96},{40,104},{48,112},{56,120},{... | collective-permute-start | bytes 56 | tf_op jit(solution)/shard_map/ppermute | solution.py:42
  64.5 3.7 %collective-permute-start.2 = (f32[1,4,64,128]{3,2,1,0:T(8,128)S(1)}, f32[1,4,64,128]{3,2,1,0:T(8,128)S(1)}, u32[]{:S(2)}, u32[]{:S(2)}) collective-permute-start(f32[1,4,64,128]{3,2,1,0:T(8,128)S(1)} %select_add_fusion.3), channel_id=1, source_target_pairs={{0,16},{8,24},{16,32},{24,40},{32,48},{40,56},{48,64},{56,72},{64,... | collective-permute-start | bytes 393224 | tf_op jit(solution)/shard_map/ppermute | solution.py:42
  68.3 2.5 %collective-permute-start.12 = (f32[1,4,64,128]{3,2,1,0:T(8,128)S(1)}, f32[1,4,64,128]{3,2,1,0:T(8,128)S(1)}, u32[]{:S(2)}, u32[]{:S(2)}) collective-permute-start(f32[1,4,64,128]{3,2,1,0:T(8,128)S(1)} %select_add_fusion.2), channel_id=1, source_target_pairs={{0,16},{8,24},{16,32},{24,40},{32,48},{40,56},{48,64},{56,72},{64,... | collective-permute-start | bytes 393224 | tf_op jit(solution)/shard_map/ppermute | solution.py:42
  71.5 4.8 %collective-permute-start.4 = (f32[1,4,64,128]{3,2,1,0:T(8,128)S(1)}, f32[1,4,64,128]{3,2,1,0:T(8,128)S(1)}, u32[]{:S(2)}, u32[]{:S(2)}) collective-permute-start(f32[1,4,64,128]{3,2,1,0:T(8,128)S(1)} %multiply_add_fusion.19), channel_id=1, source_target_pairs={{0,32},{8,40},{16,48},{24,56},{32,64},{40,72},{48,80},{56,88},{64,... | collective-permute-start | bytes 393224 | tf_op jit(solution)/shard_map/ppermute | solution.py:42
  76.5 4.2 %collective-permute-start.14 = (f32[1,4,64,128]{3,2,1,0:T(8,128)S(1)}, f32[1,4,64,128]{3,2,1,0:T(8,128)S(1)}, u32[]{:S(2)}, u32[]{:S(2)}) collective-permute-start(f32[1,4,64,128]{3,2,1,0:T(8,128)S(1)} %multiply_add_fusion.14), channel_id=1, source_target_pairs={{0,32},{8,40},{16,48},{24,56},{32,64},{40,72},{48,80},{56,88},{64,... | collective-permute-start | bytes 393224 | tf_op jit(solution)/shard_map/ppermute | solution.py:42
  80.8 3.5 %collective-permute-start.6 = (f32[1,4,64,128]{3,2,1,0:T(8,128)S(1)}, f32[1,4,64,128]{3,2,1,0:T(8,128)S(1)}, u32[]{:S(2)}, u32[]{:S(2)}) collective-permute-start(f32[1,4,64,128]{3,2,1,0:T(8,128)S(1)} %multiply_add_fusion.18), channel_id=1, source_target_pairs={{0,64},{8,72},{16,80},{24,88},{32,96},{40,104},{48,112},{56,120},{... | collective-permute-start | bytes 393224 | tf_op jit(solution)/shard_map/ppermute | solution.py:42
  84.9 3.5 %collective-permute-start.16 = (f32[1,4,64,128]{3,2,1,0:T(8,128)S(1)}, f32[1,4,64,128]{3,2,1,0:T(8,128)S(1)}, u32[]{:S(2)}, u32[]{:S(2)}) collective-permute-start(f32[1,4,64,128]{3,2,1,0:T(8,128)S(1)} %multiply_add_fusion.13), channel_id=1, source_target_pairs={{0,64},{8,72},{16,80},{24,88},{32,96},{40,104},{48,112},{56,120},{... | collective-permute-start | bytes 393224 | tf_op jit(solution)/shard_map/ppermute | solution.py:42
  88.5 5.3 %collective-permute-start.8 = (f32[1,4,64,128]{3,2,1,0:T(8,128)S(1)}, f32[1,4,64,128]{3,2,1,0:T(8,128)S(1)}, u32[]{:S(2)}, u32[]{:S(2)}) collective-permute-start(f32[1,4,64,128]{3,2,1,0:T(8,128)S(1)} %multiply_add_fusion.17), channel_id=1, source_target_pairs={{0,128},{8,136},{16,144},{24,152},{32,160},{40,168},{48,176},{56,1... | collective-permute-start | bytes 393224 | tf_op jit(solution)/shard_map/ppermute | solution.py:42
  93.9 3.6 %collective-permute-start.18 = (f32[1,4,64,128]{3,2,1,0:T(8,128)S(1)}, f32[1,4,64,128]{3,2,1,0:T(8,128)S(1)}, u32[]{:S(2)}, u32[]{:S(2)}) collective-permute-start(f32[1,4,64,128]{3,2,1,0:T(8,128)S(1)} %multiply_add_fusion.12), channel_id=1, source_target_pairs={{0,128},{8,136},{16,144},{24,152},{32,160},{40,168},{48,176},{56,1... | collective-permute-start | bytes 393224 | tf_op jit(solution)/shard_map/ppermute | solution.py:42
  97.7 2.3 %collective-permute-done.18 = f32[1,4,64,128]{3,2,1,0:T(8,128)S(1)} collective-permute-done((f32[1,4,64,128]{3,2,1,0:T(8,128)S(1)}, f32[1,4,64,128]{3,2,1,0:T(8,128)S(1)}, u32[]{:S(2)}, u32[]{:S(2)}) %collective-permute-start.18) | collective-permute-done | bytes 131104 | tf_op jit(solution)/shard_map/ppermute | solution.py:42
  102.4 1.0 copy-done.1
  103.4 3.2 %fusion.37 = f32[1,256,1,16,64]{1,4,3,2,0:T(8,128)S(1)} fusion(bf16[256,16,64]{0,2,1:T(8,128)(2,1)S(1)} %bitcast.325, f32[16,256]{1,0:T(8,128)S(1)} %copy-done.36, f32[256,256]{1,0:T(8,128)S(1)} %copy-done.18, f32[16,256]{1,0:T(8,128)S(1)} %bitcast.336, f32[256,256]{1,0:T(8,128)S(1)} %copy-done.17, ...), kind=kOutput, calls=%fused_computation.40 | convolution fusion | flops 811073536 | bytes 3194880 | tf_op jit(solution)/shard_map/jvp()/while/body/eval_jaxpr/ghts,sghp->tghp/dot_general | solution.py:104
  106.7 1.6 multiply_reduce_fusion.2
  108.9 8.5 %all-to-all-start = ((f32[8,2,256]{2,1,0:T(2,128)}), f32[8,2,256]{2,1,0:T(2,128)S(1)}, u32[]{:S(2)}, u32[]{:S(2)}) async-start(f32[8,2,256]{2,1,0:T(2,128)} %broadcast_in_dim.97), calls=%async_computation | async-start | bytes 32768 | tf_op jit(solution)/shard_map/all_to_all | solution.py:75
  118.9 6.3 %all-to-all-done = f32[8,2,256]{2,1,0:T(2,128)S(1)} async-done(((f32[8,2,256]{2,1,0:T(2,128)}), f32[8,2,256]{2,1,0:T(2,128)S(1)}, u32[]{:S(2)}, u32[]{:S(2)}) %all-to-all-start) | async-done | bytes 16416 | tf_op jit(solution)/shard_map/all_to_all | solution.py:75
  125.2 3.1 %fusion.56 = (bf16[256,1024]{0,1:T(8,128)(2,1)}, f32[256,1024]{0,1:T(8,128)S(1)}) fusion(bf16[256,1024]{0,1:T(8,128)(2,1)S(1)} %copy.128, f32[1024]{0:T(1024)} %mul.985, bf16[256,1024]{0,1:T(8,128)(2,1)S(1)} %copy.122, f32[1,256,1,16,64]{1,4,3,2,0:T(8,128)} %copy-done, f32[256]{0:T(256)S(1)} %multiply_multiply_fusion, f32[256,1024]{0,1:T(8,128)} %get-tuple-element.221, ...), kind=kLoop, calls=%fused_computation.61 | loop fusion | flops 5767168 | bytes 5253120 | tf_op jit(solution)/shard_map/convert_element_type | solution.py:235
  128.4 2.5 %convolution_bitcast_fusion.4 = f32[256,128]{1,0:T(8,128)} fusion(f32[1,256,1,16,64]{1,4,3,2,0:T(8,128)S(1)} %bitcast.318, f32[256,16]{0,1:T(8,128)S(1)} %copy-done.23, f32[1,8,64,128]{3,2,1,0:T(8,128)S(1)} %maximum_select_fusion.1, f32[1,8,64,128]{3,2,1,0:T(8,128)S(1)} %maximum_select_fusion), kind=kOutput, calls=%fused_computation.52 | convolution fusion | flops 403046400 | bytes 1720320 | tf_op jit(solution)/shard_map/transpose(jvp(kqgn,kghpn->kqghp))/dot_general | solution.py:153
  131.5 0.8 fusion.82
  133.6 1.0 copy.143
  135.1 9.0 %fusion.74 = (f32[16,256]{1,0:T(8,128)S(1)}, f32[16,256]{1,0:T(8,128)S(1)}, f32[16,256]{1,0:T(8,128)}, f32[256,256]{1,0:T(8,128)S(1)}) fusion(f32[16,256]{1,0:T(8,128)S(1)} %bitcast.337, f32[256,256]{1,0:T(8,128)} %fusion.82, f32[16,256]{1,0:T(8,128)S(1)} %bitcast.345, f32[256,256]{1,0:T(8,128)S(1)} %fusion.84, f32[256,1,16,64]{0,3,2,1:T(8,128)} %convert.9, ...), kind=kOutput, calls=%fused_computation.91 | convolution fusion | flops 825151488 | bytes 2965504 | tf_op jit(solution)/shard_map/transpose(jvp())/while/body/eval_jaxpr/checkpoint/ghts,sghp->tghp/dot_general | solution.py:104
  144.0 1.0 convolution_add_fusion
  145.8 3.5 %collective-permute-start.22 = (f32[1,4,64,128]{3,2,1,0:T(8,128)S(1)}, f32[1,4,64,128]{3,2,1,0:T(8,128)S(1)}, u32[]{:S(2)}, u32[]{:S(2)}) collective-permute-start(f32[1,4,64,128]{3,2,1,0:T(8,128)S(1)} %select_add_fusion.1), channel_id=1, source_target_pairs={{248,232},{240,224},{232,216},{224,208},{216,200},{208,192},{200,1... | collective-permute-start | bytes 393224 | tf_op jit(solution)/shard_map/ppermute | solution.py:42
  149.4 3.4 %collective-permute-start.32 = (f32[1,4,64,128]{3,2,1,0:T(8,128)S(1)}, f32[1,4,64,128]{3,2,1,0:T(8,128)S(1)}, u32[]{:S(2)}, u32[]{:S(2)}) collective-permute-start(f32[1,4,64,128]{3,2,1,0:T(8,128)S(1)} %select_add_fusion), channel_id=1, source_target_pairs={{248,232},{240,224},{232,216},{224,208},{216,200},{208,192},{200,1... | collective-permute-start | bytes 393224 | tf_op jit(solution)/shard_map/ppermute | solution.py:42
  152.8 2.4 %collective-permute-done.22 = f32[1,4,64,128]{3,2,1,0:T(8,128)S(1)} collective-permute-done((f32[1,4,64,128]{3,2,1,0:T(8,128)S(1)}, f32[1,4,64,128]{3,2,1,0:T(8,128)S(1)}, u32[]{:S(2)}, u32[]{:S(2)}) %collective-permute-start.22) | collective-permute-done | bytes 131104 | tf_op jit(solution)/shard_map/ppermute | solution.py:42
  155.3 3.7 %collective-permute-start.24 = (f32[1,4,64,128]{3,2,1,0:T(8,128)S(1)}, f32[1,4,64,128]{3,2,1,0:T(8,128)S(1)}, u32[]{:S(2)}, u32[]{:S(2)}) collective-permute-start(f32[1,4,64,128]{3,2,1,0:T(8,128)S(1)} %multiply_add_fusion.9), channel_id=1, source_target_pairs={{248,216},{240,208},{232,200},{224,192},{216,184},{208,176},{200,1... | collective-permute-start | bytes 393224 | tf_op jit(solution)/shard_map/ppermute | solution.py:42
  159.2 1.9 collective-permute-start.34
  161.1 3.7 %collective-permute-done.24 = f32[1,4,64,128]{3,2,1,0:T(8,128)S(1)} collective-permute-done((f32[1,4,64,128]{3,2,1,0:T(8,128)S(1)}, f32[1,4,64,128]{3,2,1,0:T(8,128)S(1)}, u32[]{:S(2)}, u32[]{:S(2)}) %collective-permute-start.24) | collective-permute-done | bytes 131104 | tf_op jit(solution)/shard_map/ppermute | solution.py:42
  164.8 1.3 collective-permute-start.26
  166.1 2.4 %collective-permute-done.34 = f32[1,4,64,128]{3,2,1,0:T(8,128)S(1)} collective-permute-done((f32[1,4,64,128]{3,2,1,0:T(8,128)S(1)}, f32[1,4,64,128]{3,2,1,0:T(8,128)S(1)}, u32[]{:S(2)}, u32[]{:S(2)}) %collective-permute-start.34) | collective-permute-done | bytes 131104 | tf_op jit(solution)/shard_map/ppermute | solution.py:42
  168.6 1.3 collective-permute-start.36
  169.9 3.3 %collective-permute-done.26 = f32[1,4,64,128]{3,2,1,0:T(8,128)S(1)} collective-permute-done((f32[1,4,64,128]{3,2,1,0:T(8,128)S(1)}, f32[1,4,64,128]{3,2,1,0:T(8,128)S(1)}, u32[]{:S(2)}, u32[]{:S(2)}) %collective-permute-start.26) | collective-permute-done | bytes 131104 | tf_op jit(solution)/shard_map/ppermute | solution.py:42
  173.3 1.3 collective-permute-start.28
  174.6 0.9 collective-permute-done.36
  175.6 1.3 collective-permute-start.38
  176.9 5.6 %collective-permute-done.28 = f32[1,4,64,128]{3,2,1,0:T(8,128)S(1)} collective-permute-done((f32[1,4,64,128]{3,2,1,0:T(8,128)S(1)}, f32[1,4,64,128]{3,2,1,0:T(8,128)S(1)}, u32[]{:S(2)}, u32[]{:S(2)}) %collective-permute-start.28) | collective-permute-done | bytes 131104 | tf_op jit(solution)/shard_map/ppermute | solution.py:42
  182.8 1.9 collective-permute-done.38
  185.4 1.1 collective-permute-done.39
  186.5 1.8 fusion.47
  188.4 1.6 fusion.50
  191.5 2.5 %reduce-window.36 = f32[1,16,1,2,128]{4,1,2,3,0:T(8,128)S(1)} reduce-window(f32[1,16,1,2,128]{4,1,2,3,0:T(8,128)S(1)} %copy_bitcast_fusion, f32[]{:T(128)} %constant.146.clone.1), window={size=1x1x1x1x128 pad=0_0x0_0x0_0x0_0x0_127}, to_apply=%region_16.17 | reduce-window | flops 520192 | bytes 32772 | tf_op jit(solution)/shard_map/reduce-window.6
  194.1 2.5 %reduce-window.34 = f32[1,16,1,2,128]{4,1,2,3,0:T(8,128)S(1)} reduce-window(f32[1,16,1,2,128]{4,1,2,3,0:T(8,128)S(1)} %bitcast.343, f32[]{:T(128)} %constant.146.clone.1), window={size=1x1x1x1x128 pad=0_0x0_0x0_0x0_0x0_127}, to_apply=%region_11.12 | reduce-window | flops 520192 | bytes 32772 | tf_op jit(solution)/shard_map/reduce-window.4
  196.7 1.3 fusion.49
  198.5 4.8 %fusion.40 = f32[256,16,64]{0,2,1:T(8,128)S(1)} fusion(f32[16,256]{1,0:T(8,128)S(1)} %bitcast.346, f32[256,256]{1,0:T(8,128)} %fusion.82, f32[16,256]{1,0:T(8,128)S(1)} %bitcast.339, f32[256,256]{1,0:T(8,128)} %copy-done.19, f32[256,1,16,64]{0,3,2,1:T(8,128)S(1)} %bitcast.322, f32[256,16,64]{0,2,1:T(8,128)S(1)} %copy-done.6, f32[256,16]{0,1:T(8,128)S(1)} %copy-done.21), kind=kOutput, calls=%fused_computation.41 | convolution fusion | flops 811073536 | bytes 3719168 | tf_op jit(solution)/shard_map/transpose(jvp())/while/body/eval_jaxpr/checkpoint/ghts,sghp->tghp/dot_general | solution.py:104
  203.5 1.0 copy.142
  (307 shorter events, 25.3 us)
Async XLA Ops:
  0.6 11.3 %copy-start.8 = (bf16[256,128]{1,0:T(8,128)(2,1)S(1)}, bf16[256,128]{1,0:T(8,128)(2,1)}, u32[]{:S(2)}) copy-start(bf16[256,128]{1,0:T(8,128)(2,1)} %param.14) | copy-start | bytes 196612
  9.8 8.8 %collective-permute-start.20 = (f32[1,4]{1,0:T(1,128)}, f32[1,4]{1,0:T(1,128)}, u32[]{:S(2)}, u32[]{:S(2)}) collective-permute-start(f32[1,4]{1,0:T(1,128)} %constant_dynamic-slice_fusion.4), channel_id=1, source_target_pairs={{248,240},{240,248},{232,224},{224,232},{216,208},{208,216},{200,1... | collective-permute-start | bytes 56 | tf_op jit(solution)/shard_map/ppermute | solution.py:42
  12.7 51.7 %collective-permute-start.1 = (f32[1,4,64,128]{3,2,1,0:T(8,128)S(1)}, f32[1,4,64,128]{3,2,1,0:T(8,128)S(1)}, u32[]{:S(2)}, u32[]{:S(2)}) collective-permute-start(f32[1,4,64,128]{3,2,1,0:T(8,128)S(1)} %constant_dynamic-slice_fusion.9), channel_id=1, source_target_pairs={{0,8},{8,0},{16,24},{24,16},{32,40},{40,32},{48,56},{56,48},{64,72... | collective-permute-start | bytes 393224 | tf_op jit(solution)/shard_map/ppermute | solution.py:42
  13.9 6.0 %collective-permute-start.30 = (f32[1,4]{1,0:T(1,128)}, f32[1,4]{1,0:T(1,128)}, u32[]{:S(2)}, u32[]{:S(2)}) collective-permute-start(f32[1,4]{1,0:T(1,128)} %constant_dynamic-slice_fusion.1), channel_id=1, source_target_pairs={{248,240},{240,248},{232,224},{224,232},{216,208},{208,216},{200,1... | collective-permute-start | bytes 56 | tf_op jit(solution)/shard_map/ppermute | solution.py:42
  13.9 54.3 %collective-permute-start.11 = (f32[1,4,64,128]{3,2,1,0:T(8,128)S(1)}, f32[1,4,64,128]{3,2,1,0:T(8,128)S(1)}, u32[]{:S(2)}, u32[]{:S(2)}) collective-permute-start(f32[1,4,64,128]{3,2,1,0:T(8,128)S(1)} %constant_dynamic-slice_fusion.6), channel_id=1, source_target_pairs={{0,8},{8,0},{16,24},{24,16},{32,40},{40,32},{48,56},{56,48},{64,72... | collective-permute-start | bytes 393224 | tf_op jit(solution)/shard_map/ppermute | solution.py:42
  19.8 51.6 %copy-start.60 = (f32[1,4]{1,0:T(1,128)}, f32[1,4]{1,0:T(1,128)S(1)}, u32[]{:S(2)}) copy-start(f32[1,4]{1,0:T(1,128)S(1)} %get-tuple-element.213) | copy-start | bytes 52
  19.8 4.5 %collective-permute-start = (f32[1,4]{1,0:T(1,128)S(1)}, f32[1,4]{1,0:T(1,128)S(1)}, u32[]{:S(2)}, u32[]{:S(2)}) collective-permute-start(f32[1,4]{1,0:T(1,128)S(1)} %get-tuple-element.257), channel_id=1, source_target_pairs={{0,8},{8,0},{16,24},{24,16},{32,40},{40,32},{48,56},{56,48},{64,72... | collective-permute-start | bytes 56 | tf_op jit(solution)/shard_map/ppermute | solution.py:42
  21.1 50.2 %copy-start.62 = (f32[1,4]{1,0:T(1,128)}, f32[1,4]{1,0:T(1,128)S(1)}, u32[]{:S(2)}) copy-start(f32[1,4]{1,0:T(1,128)S(1)} %get-tuple-element.218) | copy-start | bytes 52
  21.1 5.7 %collective-permute-start.10 = (f32[1,4]{1,0:T(1,128)S(1)}, f32[1,4]{1,0:T(1,128)S(1)}, u32[]{:S(2)}, u32[]{:S(2)}) collective-permute-start(f32[1,4]{1,0:T(1,128)S(1)} %get-tuple-element.258), channel_id=1, source_target_pairs={{0,8},{8,0},{16,24},{24,16},{32,40},{40,32},{48,56},{56,48},{64,72... | collective-permute-start | bytes 56 | tf_op jit(solution)/shard_map/ppermute | solution.py:42
  21.6 10.9 %collective-permute-start.23 = (f32[1,4]{1,0:T(1,128)S(1)}, f32[1,4]{1,0:T(1,128)S(1)}, u32[]{:S(2)}, u32[]{:S(2)}) collective-permute-start(f32[1,4]{1,0:T(1,128)S(1)} %get-tuple-element.213), channel_id=1, source_target_pairs={{248,232},{240,224},{232,216},{224,208},{216,200},{208,192},{200,1... | collective-permute-start | bytes 56 | tf_op jit(solution)/shard_map/ppermute | solution.py:42
  24.3 11.3 %collective-permute-start.33 = (f32[1,4]{1,0:T(1,128)S(1)}, f32[1,4]{1,0:T(1,128)S(1)}, u32[]{:S(2)}, u32[]{:S(2)}) collective-permute-start(f32[1,4]{1,0:T(1,128)S(1)} %get-tuple-element.218), channel_id=1, source_target_pairs={{248,232},{240,224},{232,216},{224,208},{216,200},{208,192},{200,1... | collective-permute-start | bytes 56 | tf_op jit(solution)/shard_map/ppermute | solution.py:42
  26.9 10.7 %collective-permute-start.3 = (f32[1,4]{1,0:T(1,128)S(1)}, f32[1,4]{1,0:T(1,128)S(1)}, u32[]{:S(2)}, u32[]{:S(2)}) collective-permute-start(f32[1,4]{1,0:T(1,128)S(1)} %get-tuple-element.228), channel_id=1, source_target_pairs={{0,16},{8,24},{16,32},{24,40},{32,48},{40,56},{48,64},{56,72},{64,... | collective-permute-start | bytes 56 | tf_op jit(solution)/shard_map/ppermute | solution.py:42
  32.5 38.9 %copy-start.52 = (f32[1,4]{1,0:T(1,128)}, f32[1,4]{1,0:T(1,128)S(1)}, u32[]{:S(2)}) copy-start(f32[1,4]{1,0:T(1,128)S(1)} %collective-permute-done.23) | copy-start | bytes 52
  32.5 7.0 %collective-permute-start.13 = (f32[1,4]{1,0:T(1,128)S(1)}, f32[1,4]{1,0:T(1,128)S(1)}, u32[]{:S(2)}, u32[]{:S(2)}) collective-permute-start(f32[1,4]{1,0:T(1,128)S(1)} %get-tuple-element.233), channel_id=1, source_target_pairs={{0,16},{8,24},{16,32},{24,40},{32,48},{40,56},{48,64},{56,72},{64,... | collective-permute-start | bytes 56 | tf_op jit(solution)/shard_map/ppermute | solution.py:42
  35.6 40.8 %copy-start.68 = (f32[1,4]{1,0:T(1,128)}, f32[1,4]{1,0:T(1,128)S(1)}, u32[]{:S(2)}) copy-start(f32[1,4]{1,0:T(1,128)S(1)} %mul.1021) | copy-start | bytes 52
  35.6 35.8 %copy-start.50 = (f32[1,4]{1,0:T(1,128)}, f32[1,4]{1,0:T(1,128)S(1)}, u32[]{:S(2)}) copy-start(f32[1,4]{1,0:T(1,128)S(1)} %collective-permute-done.33) | copy-start | bytes 52
  35.6 10.3 %collective-permute-start.25 = (f32[1,4]{1,0:T(1,128)S(1)}, f32[1,4]{1,0:T(1,128)S(1)}, u32[]{:S(2)}, u32[]{:S(2)}) collective-permute-start(f32[1,4]{1,0:T(1,128)S(1)} %mul.1021), channel_id=1, source_target_pairs={{248,216},{240,208},{232,200},{224,192},{216,184},{208,176},{200,1... | collective-permute-start | bytes 56 | tf_op jit(solution)/shard_map/ppermute | solution.py:42
  37.5 33.8 %copy-start.66 = (f32[1,4]{1,0:T(1,128)}, f32[1,4]{1,0:T(1,128)S(1)}, u32[]{:S(2)}) copy-start(f32[1,4]{1,0:T(1,128)S(1)} %mul.1050) | copy-start | bytes 52
  37.6 13.8 %collective-permute-start.35 = (f32[1,4]{1,0:T(1,128)S(1)}, f32[1,4]{1,0:T(1,128)S(1)}, u32[]{:S(2)}, u32[]{:S(2)}) collective-permute-start(f32[1,4]{1,0:T(1,128)S(1)} %mul.1050), channel_id=1, source_target_pairs={{248,216},{240,208},{232,200},{224,192},{216,184},{208,176},{200,1... | collective-permute-start | bytes 56 | tf_op jit(solution)/shard_map/ppermute | solution.py:42
  39.5 13.1 %collective-permute-start.5 = (f32[1,4]{1,0:T(1,128)S(1)}, f32[1,4]{1,0:T(1,128)S(1)}, u32[]{:S(2)}, u32[]{:S(2)}) collective-permute-start(f32[1,4]{1,0:T(1,128)S(1)} %mul.931), channel_id=1, source_target_pairs={{0,32},{8,40},{16,48},{24,56},{32,64},{40,72},{48,80},{56,88},{64,... | collective-permute-start | bytes 56 | tf_op jit(solution)/shard_map/ppermute | solution.py:42
  45.9 8.1 %collective-permute-start.15 = (f32[1,4]{1,0:T(1,128)S(1)}, f32[1,4]{1,0:T(1,128)S(1)}, u32[]{:S(2)}, u32[]{:S(2)}) collective-permute-start(f32[1,4]{1,0:T(1,128)S(1)} %mul.960), channel_id=1, source_target_pairs={{0,32},{8,40},{16,48},{24,56},{32,64},{40,72},{48,80},{56,88},{64,... | collective-permute-start | bytes 56 | tf_op jit(solution)/shard_map/ppermute | solution.py:42
  51.3 25.1 %copy-start.72 = (f32[1,4]{1,0:T(1,128)}, f32[1,4]{1,0:T(1,128)S(1)}, u32[]{:S(2)}) copy-start(f32[1,4]{1,0:T(1,128)S(1)} %mul.1029) | copy-start | bytes 52
  51.3 7.9 %collective-permute-start.27 = (f32[1,4]{1,0:T(1,128)S(1)}, f32[1,4]{1,0:T(1,128)S(1)}, u32[]{:S(2)}, u32[]{:S(2)}) collective-permute-start(f32[1,4]{1,0:T(1,128)S(1)} %mul.1029), channel_id=1, source_target_pairs={{248,184},{240,176},{232,168},{224,160},{216,152},{208,144},{200,1... | collective-permute-start | bytes 56 | tf_op jit(solution)/shard_map/ppermute | solution.py:42
  52.7 23.7 %copy-start.70 = (f32[1,4]{1,0:T(1,128)}, f32[1,4]{1,0:T(1,128)S(1)}, u32[]{:S(2)}) copy-start(f32[1,4]{1,0:T(1,128)S(1)} %mul.1058) | copy-start | bytes 52
  52.7 11.0 %collective-permute-start.37 = (f32[1,4]{1,0:T(1,128)S(1)}, f32[1,4]{1,0:T(1,128)S(1)}, u32[]{:S(2)}, u32[]{:S(2)}) collective-permute-start(f32[1,4]{1,0:T(1,128)S(1)} %mul.1058), channel_id=1, source_target_pairs={{248,184},{240,176},{232,168},{224,160},{216,152},{208,144},{200,1... | collective-permute-start | bytes 56 | tf_op jit(solution)/shard_map/ppermute | solution.py:42
  54.0 10.2 %collective-permute-start.7 = (f32[1,4]{1,0:T(1,128)S(1)}, f32[1,4]{1,0:T(1,128)S(1)}, u32[]{:S(2)}, u32[]{:S(2)}) collective-permute-start(f32[1,4]{1,0:T(1,128)S(1)} %mul.939), channel_id=1, source_target_pairs={{0,64},{8,72},{16,80},{24,88},{32,96},{40,104},{48,112},{56,120},{... | collective-permute-start | bytes 56 | tf_op jit(solution)/shard_map/ppermute | solution.py:42
  59.2 5.2 %collective-permute-start.17 = (f32[1,4]{1,0:T(1,128)S(1)}, f32[1,4]{1,0:T(1,128)S(1)}, u32[]{:S(2)}, u32[]{:S(2)}) collective-permute-start(f32[1,4]{1,0:T(1,128)S(1)} %mul.968), channel_id=1, source_target_pairs={{0,64},{8,72},{16,80},{24,88},{32,96},{40,104},{48,112},{56,120},{... | collective-permute-start | bytes 56 | tf_op jit(solution)/shard_map/ppermute | solution.py:42
  64.5 6.9 %collective-permute-start.2 = (f32[1,4,64,128]{3,2,1,0:T(8,128)S(1)}, f32[1,4,64,128]{3,2,1,0:T(8,128)S(1)}, u32[]{:S(2)}, u32[]{:S(2)}) collective-permute-start(f32[1,4,64,128]{3,2,1,0:T(8,128)S(1)} %select_add_fusion.3), channel_id=1, source_target_pairs={{0,16},{8,24},{16,32},{24,40},{32,48},{40,56},{48,64},{56,72},{64,... | collective-permute-start | bytes 393224 | tf_op jit(solution)/shard_map/ppermute | solution.py:42
  68.3 8.1 %collective-permute-start.12 = (f32[1,4,64,128]{3,2,1,0:T(8,128)S(1)}, f32[1,4,64,128]{3,2,1,0:T(8,128)S(1)}, u32[]{:S(2)}, u32[]{:S(2)}) collective-permute-start(f32[1,4,64,128]{3,2,1,0:T(8,128)S(1)} %select_add_fusion.2), channel_id=1, source_target_pairs={{0,16},{8,24},{16,32},{24,40},{32,48},{40,56},{48,64},{56,72},{64,... | collective-permute-start | bytes 393224 | tf_op jit(solution)/shard_map/ppermute | solution.py:42
  71.5 9.2 %collective-permute-start.4 = (f32[1,4,64,128]{3,2,1,0:T(8,128)S(1)}, f32[1,4,64,128]{3,2,1,0:T(8,128)S(1)}, u32[]{:S(2)}, u32[]{:S(2)}) collective-permute-start(f32[1,4,64,128]{3,2,1,0:T(8,128)S(1)} %multiply_add_fusion.19), channel_id=1, source_target_pairs={{0,32},{8,40},{16,48},{24,56},{32,64},{40,72},{48,80},{56,88},{64,... | collective-permute-start | bytes 393224 | tf_op jit(solution)/shard_map/ppermute | solution.py:42
  76.5 8.4 %collective-permute-start.14 = (f32[1,4,64,128]{3,2,1,0:T(8,128)S(1)}, f32[1,4,64,128]{3,2,1,0:T(8,128)S(1)}, u32[]{:S(2)}, u32[]{:S(2)}) collective-permute-start(f32[1,4,64,128]{3,2,1,0:T(8,128)S(1)} %multiply_add_fusion.14), channel_id=1, source_target_pairs={{0,32},{8,40},{16,48},{24,56},{32,64},{40,72},{48,80},{56,88},{64,... | collective-permute-start | bytes 393224 | tf_op jit(solution)/shard_map/ppermute | solution.py:42
  80.8 7.6 %collective-permute-start.6 = (f32[1,4,64,128]{3,2,1,0:T(8,128)S(1)}, f32[1,4,64,128]{3,2,1,0:T(8,128)S(1)}, u32[]{:S(2)}, u32[]{:S(2)}) collective-permute-start(f32[1,4,64,128]{3,2,1,0:T(8,128)S(1)} %multiply_add_fusion.18), channel_id=1, source_target_pairs={{0,64},{8,72},{16,80},{24,88},{32,96},{40,104},{48,112},{56,120},{... | collective-permute-start | bytes 393224 | tf_op jit(solution)/shard_map/ppermute | solution.py:42
  84.9 8.9 %collective-permute-start.16 = (f32[1,4,64,128]{3,2,1,0:T(8,128)S(1)}, f32[1,4,64,128]{3,2,1,0:T(8,128)S(1)}, u32[]{:S(2)}, u32[]{:S(2)}) collective-permute-start(f32[1,4,64,128]{3,2,1,0:T(8,128)S(1)} %multiply_add_fusion.13), channel_id=1, source_target_pairs={{0,64},{8,72},{16,80},{24,88},{32,96},{40,104},{48,112},{56,120},{... | collective-permute-start | bytes 393224 | tf_op jit(solution)/shard_map/ppermute | solution.py:42
  88.5 9.0 %collective-permute-start.8 = (f32[1,4,64,128]{3,2,1,0:T(8,128)S(1)}, f32[1,4,64,128]{3,2,1,0:T(8,128)S(1)}, u32[]{:S(2)}, u32[]{:S(2)}) collective-permute-start(f32[1,4,64,128]{3,2,1,0:T(8,128)S(1)} %multiply_add_fusion.17), channel_id=1, source_target_pairs={{0,128},{8,136},{16,144},{24,152},{32,160},{40,168},{48,176},{56,1... | collective-permute-start | bytes 393224 | tf_op jit(solution)/shard_map/ppermute | solution.py:42
  93.9 6.1 %collective-permute-start.18 = (f32[1,4,64,128]{3,2,1,0:T(8,128)S(1)}, f32[1,4,64,128]{3,2,1,0:T(8,128)S(1)}, u32[]{:S(2)}, u32[]{:S(2)}) collective-permute-start(f32[1,4,64,128]{3,2,1,0:T(8,128)S(1)} %multiply_add_fusion.12), channel_id=1, source_target_pairs={{0,128},{8,136},{16,144},{24,152},{32,160},{40,168},{48,176},{56,1... | collective-permute-start | bytes 393224 | tf_op jit(solution)/shard_map/ppermute | solution.py:42
  97.6 2.9 %collective-permute-start.9 = (f32[1,4,64,128]{3,2,1,0:T(8,128)S(1)}, f32[1,4,64,128]{3,2,1,0:T(8,128)S(1)}, u32[]{:S(2)}, u32[]{:S(2)}) collective-permute-start(f32[1,4,64,128]{3,2,1,0:T(8,128)S(1)} %get-tuple-element.226), channel_id=1, source_target_pairs={{0,8},{8,0},{16,24},{24,16},{32,40},{40,32},{48,56},{56,48},{64,72... | collective-permute-start | bytes 393224 | tf_op jit(solution)/shard_map/ppermute | solution.py:42
  100.1 1.6 collective-permute-start.19
  106.7 11.5 %copy-start.12 = (f32[1,4,64,128]{3,2,1,0:T(8,128)S(1)}, f32[1,4,64,128]{3,2,1,0:T(8,128)}, u32[]{:S(2)}) copy-start(f32[1,4,64,128]{3,2,1,0:T(8,128)} %copy-done.11) | copy-start | bytes 393220
  108.9 16.2 %all-to-all-start = ((f32[8,2,256]{2,1,0:T(2,128)}), f32[8,2,256]{2,1,0:T(2,128)S(1)}, u32[]{:S(2)}, u32[]{:S(2)}) async-start(f32[8,2,256]{2,1,0:T(2,128)} %broadcast_in_dim.97), calls=%async_computation | async-start | bytes 32768 | tf_op jit(solution)/shard_map/all_to_all | solution.py:75
  132.4 13.0 %collective-permute-start.21 = (f32[1,4,64,128]{3,2,1,0:T(8,128)S(1)}, f32[1,4,64,128]{3,2,1,0:T(8,128)S(1)}, u32[]{:S(2)}, u32[]{:S(2)}) collective-permute-start(f32[1,4,64,128]{3,2,1,0:T(8,128)S(1)} %constant_dynamic-slice_fusion.3), channel_id=1, source_target_pairs={{248,240},{240,248},{232,224},{224,232},{216,208},{208,216},{200,1... | collective-permute-start | bytes 393224 | tf_op jit(solution)/shard_map/ppermute | solution.py:42
  133.2 16.1 %collective-permute-start.31 = (f32[1,4,64,128]{3,2,1,0:T(8,128)}, f32[1,4,64,128]{3,2,1,0:T(8,128)S(1)}, u32[]{:S(2)}, u32[]{:S(2)}) collective-permute-start(f32[1,4,64,128]{3,2,1,0:T(8,128)} %constant_dynamic-slice_fusion), channel_id=1, source_target_pairs={{248,240},{240,248},{232,224},{224,232},{216,208},{208,216},{200,1... | collective-permute-start | bytes 393224 | tf_op jit(solution)/shard_map/ppermute | solution.py:42
  145.3 13.7 %copy-start.63 = (f32[1,4]{1,0:T(1,128)S(1)}, f32[1,4]{1,0:T(1,128)}, u32[]{:S(2)}) copy-start(f32[1,4]{1,0:T(1,128)} %copy-done.62) | copy-start | bytes 52
  145.3 19.4 %copy-start.69 = (f32[1,4]{1,0:T(1,128)S(1)}, f32[1,4]{1,0:T(1,128)}, u32[]{:S(2)}) copy-start(f32[1,4]{1,0:T(1,128)} %copy-done.68) | copy-start | bytes 52
  145.3 23.2 %copy-start.67 = (f32[1,4]{1,0:T(1,128)S(1)}, f32[1,4]{1,0:T(1,128)}, u32[]{:S(2)}) copy-start(f32[1,4]{1,0:T(1,128)} %copy-done.66) | copy-start | bytes 52
  145.8 27.4 %copy-start.73 = (f32[1,4]{1,0:T(1,128)S(1)}, f32[1,4]{1,0:T(1,128)}, u32[]{:S(2)}) copy-start(f32[1,4]{1,0:T(1,128)} %copy-done.72) | copy-start | bytes 52
  145.8 9.4 %collective-permute-start.22 = (f32[1,4,64,128]{3,2,1,0:T(8,128)S(1)}, f32[1,4,64,128]{3,2,1,0:T(8,128)S(1)}, u32[]{:S(2)}, u32[]{:S(2)}) collective-permute-start(f32[1,4,64,128]{3,2,1,0:T(8,128)S(1)} %select_add_fusion.1), channel_id=1, source_target_pairs={{248,232},{240,224},{232,216},{224,208},{216,200},{208,192},{200,1... | collective-permute-start | bytes 393224 | tf_op jit(solution)/shard_map/ppermute | solution.py:42
  149.4 26.1 %copy-start.71 = (f32[1,4]{1,0:T(1,128)S(1)}, f32[1,4]{1,0:T(1,128)}, u32[]{:S(2)}) copy-start(f32[1,4]{1,0:T(1,128)} %copy-done.70) | copy-start | bytes 52
  149.4 9.6 %collective-permute-start.32 = (f32[1,4,64,128]{3,2,1,0:T(8,128)S(1)}, f32[1,4,64,128]{3,2,1,0:T(8,128)S(1)}, u32[]{:S(2)}, u32[]{:S(2)}) collective-permute-start(f32[1,4,64,128]{3,2,1,0:T(8,128)S(1)} %select_add_fusion), channel_id=1, source_target_pairs={{248,232},{240,224},{232,216},{224,208},{216,200},{208,192},{200,1... | collective-permute-start | bytes 393224 | tf_op jit(solution)/shard_map/ppermute | solution.py:42
  155.3 27.2 %copy-start.48 = (f32[1,4]{1,0:T(1,128)S(1)}, f32[1,4]{1,0:T(1,128)}, u32[]{:S(2)}) copy-start(f32[1,4]{1,0:T(1,128)} %get-tuple-element.214) | copy-start | bytes 52
  155.3 27.2 %copy-start.53 = (f32[1,4]{1,0:T(1,128)S(1)}, f32[1,4]{1,0:T(1,128)}, u32[]{:S(2)}) copy-start(f32[1,4]{1,0:T(1,128)} %copy-done.52) | copy-start | bytes 52
  155.3 27.2 %copy-start.56 = (f32[4]{0:T(128)S(1)}, f32[4]{0:T(128)}, u32[]{:S(2)}) copy-start(f32[4]{0:T(128)} %get-tuple-element.249) | copy-start | bytes 52
  155.3 27.2 %copy-start.57 = (f32[4]{0:T(128)S(1)}, f32[4]{0:T(128)}, u32[]{:S(2)}) copy-start(f32[4]{0:T(128)} %get-tuple-element.250) | copy-start | bytes 52
  155.3 9.4 %collective-permute-start.24 = (f32[1,4,64,128]{3,2,1,0:T(8,128)S(1)}, f32[1,4,64,128]{3,2,1,0:T(8,128)S(1)}, u32[]{:S(2)}, u32[]{:S(2)}) collective-permute-start(f32[1,4,64,128]{3,2,1,0:T(8,128)S(1)} %multiply_add_fusion.9), channel_id=1, source_target_pairs={{248,216},{240,208},{232,200},{224,192},{216,184},{208,176},{200,1... | collective-permute-start | bytes 393224 | tf_op jit(solution)/shard_map/ppermute | solution.py:42
  159.2 9.4 %collective-permute-start.34 = (f32[1,4,64,128]{3,2,1,0:T(8,128)S(1)}, f32[1,4,64,128]{3,2,1,0:T(8,128)S(1)}, u32[]{:S(2)}, u32[]{:S(2)}) collective-permute-start(f32[1,4,64,128]{3,2,1,0:T(8,128)S(1)} %multiply_add_fusion.4), channel_id=1, source_target_pairs={{248,216},{240,208},{232,200},{224,192},{216,184},{208,176},{200,1... | collective-permute-start | bytes 393224 | tf_op jit(solution)/shard_map/ppermute | solution.py:42
  164.8 8.4 %collective-permute-start.26 = (f32[1,4,64,128]{3,2,1,0:T(8,128)S(1)}, f32[1,4,64,128]{3,2,1,0:T(8,128)S(1)}, u32[]{:S(2)}, u32[]{:S(2)}) collective-permute-start(f32[1,4,64,128]{3,2,1,0:T(8,128)S(1)} %multiply_add_fusion.8), channel_id=1, source_target_pairs={{248,184},{240,176},{232,168},{224,160},{216,152},{208,144},{200,1... | collective-permute-start | bytes 393224 | tf_op jit(solution)/shard_map/ppermute | solution.py:42
  168.5 16.1 %copy-start.49 = (f32[1,4]{1,0:T(1,128)S(1)}, f32[1,4]{1,0:T(1,128)}, u32[]{:S(2)}) copy-start(f32[1,4]{1,0:T(1,128)} %get-tuple-element.219) | copy-start | bytes 52
  168.5 16.1 %copy-start.51 = (f32[1,4]{1,0:T(1,128)S(1)}, f32[1,4]{1,0:T(1,128)}, u32[]{:S(2)}) copy-start(f32[1,4]{1,0:T(1,128)} %copy-done.50) | copy-start | bytes 52
  168.5 16.1 %copy-start.54 = (f32[4]{0:T(128)S(1)}, f32[4]{0:T(128)}, u32[]{:S(2)}) copy-start(f32[4]{0:T(128)} %get-tuple-element.251) | copy-start | bytes 52
  168.5 16.1 %copy-start.55 = (f32[4]{0:T(128)S(1)}, f32[4]{0:T(128)}, u32[]{:S(2)}) copy-start(f32[4]{0:T(128)} %get-tuple-element.252) | copy-start | bytes 52
  168.6 6.9 %collective-permute-start.36 = (f32[1,4,64,128]{3,2,1,0:T(8,128)S(1)}, f32[1,4,64,128]{3,2,1,0:T(8,128)S(1)}, u32[]{:S(2)}, u32[]{:S(2)}) collective-permute-start(f32[1,4,64,128]{3,2,1,0:T(8,128)S(1)} %multiply_add_fusion.3), channel_id=1, source_target_pairs={{248,184},{240,176},{232,168},{224,160},{216,152},{208,144},{200,1... | collective-permute-start | bytes 393224 | tf_op jit(solution)/shard_map/ppermute | solution.py:42
  173.3 9.2 %collective-permute-start.28 = (f32[1,4,64,128]{3,2,1,0:T(8,128)S(1)}, f32[1,4,64,128]{3,2,1,0:T(8,128)S(1)}, u32[]{:S(2)}, u32[]{:S(2)}) collective-permute-start(f32[1,4,64,128]{3,2,1,0:T(8,128)S(1)} %multiply_add_fusion.7), channel_id=1, source_target_pairs={{248,120},{240,112},{232,104},{224,96},{216,88},{208,80},{200,72},... | collective-permute-start | bytes 393224 | tf_op jit(solution)/shard_map/ppermute | solution.py:42
  175.6 9.0 %collective-permute-start.38 = (f32[1,4,64,128]{3,2,1,0:T(8,128)S(1)}, f32[1,4,64,128]{3,2,1,0:T(8,128)S(1)}, u32[]{:S(2)}, u32[]{:S(2)}) collective-permute-start(f32[1,4,64,128]{3,2,1,0:T(8,128)S(1)} %multiply_add_fusion.2), channel_id=1, source_target_pairs={{248,120},{240,112},{232,104},{224,96},{216,88},{208,80},{200,72},... | collective-permute-start | bytes 393224 | tf_op jit(solution)/shard_map/ppermute | solution.py:42
  182.7 2.7 %collective-permute-start.29 = (f32[1,4,64,128]{3,2,1,0:T(8,128)S(1)}, f32[1,4,64,128]{3,2,1,0:T(8,128)S(1)}, u32[]{:S(2)}, u32[]{:S(2)}) collective-permute-start(f32[1,4,64,128]{3,2,1,0:T(8,128)S(1)} %get-tuple-element.211), channel_id=1, source_target_pairs={{248,240},{240,248},{232,224},{224,232},{216,208},{208,216},{200,1... | collective-permute-start | bytes 393224 | tf_op jit(solution)/shard_map/ppermute | solution.py:42
  184.8 1.7 collective-permute-start.39
  (52 other events, 167.6 us)

commit v7 on v4

--- a/solution.py
+++ b/solution.py
@@ -137,7 +137,7 @@
         jnp.einsum("kqgn,kghpn->kqghp", c_spans, full_start, precision=HIGHEST_PRECISION)
         * entry_decay[..., None]
     )
-    mix_block = jax.checkpoint(lambda pieces: span_mix(*pieces))
+    mix_block = lambda pieces: span_mix(*pieces)
     inner_part = lax.map(mix_block, (x_spans, dt_spans, b_spans, c_spans, log_cum, segment))
     return inner_part + carried
 

time: 176 us -> 172 us (0.977)
  blocking collectives: 0 us -> 16 us
  starting transfers between devices: 48.7 us -> 39 us
  waiting for transfers between devices: 56.2 us -> 49.4 us
  matrix products: 29.3 us -> 26.4 us
    all_to_all x0 -> x1, blocking collectives: none -> 16 us  [head_sum(): return jnp.sum(lax.all_to_all(spread, axis, 0, 0), axis=0)]
    all_to_all x1 -> x0, starting transfers between devices: 8.46 us -> none  [head_sum(): return jnp.sum(lax.all_to_all(spread, axis, 0, 0), axis=0)]
    all_to_all x1 -> x0, waiting for transfers between devices: 7.76 us -> none  [head_sum(): return jnp.sum(lax.all_to_all(spread, axis, 0, 0), axis=0)]
    dot_general x4 -> x3, matrix products: 3.56 us -> 2.19 us  [span_mix(): jnp.einsum('tgn,sgn->gts', c_span, b_span, precision=HIGHEST_PRECISION)]
    unnamed x105 -> x107, local copies, waits for them, and re-layouts: 6.25 us -> 7.28 us
  transfers between devices with their start and end apart: 21 -> 20, of which waited for: 12 -> 11; matrix products, arithmetic and copies ran while one was open for 15% -> 11% of each run, Pallas kernels for 0% -> 0%
where the time goes in v7:
time: 172 us; the launch traced here: 169 us
  waiting for transfers between devices  49.4 us (29%)
  starting transfers between devices  39 us (23%)
  matrix products  26.4 us (15%)
  other arithmetic  23.9 us (14%)
  blocking collectives  16 us (9%)
  local copies, waits for them, and re-layouts  11.3 us (7%)
  between operations  2.97 us (2%)
    ppermute x20, waiting for transfers between devices, move(): return lax.ppermute(tree, axis, [(device(a), device(b)) for a, b in pairs])  49.4 us
    ppermute x20, starting transfers between devices, move(): return lax.ppermute(tree, axis, [(device(a), device(b)) for a, b in pairs])  39 us
    all_to_all x1, blocking collectives, head_sum(): return jnp.sum(lax.all_to_all(spread, axis, 0, 0), axis=0)  16 us
    dot_general x3, matrix products, span_mix(): jnp.einsum('ghts,sghp->tghp', weights, x_span, precision=HIGHEST_PRECISION)  14.6 us
    another operation x10, other arithmetic  7.71 us
    unnamed x107, local copies, waits for them, and re-layouts  7.28 us
    dot_general x3, matrix products, local_states(): jnp.einsum('kqgh,kqghp,kqgn->kghpn', tail_decay * dt_spans, x_spans, b_sp...  5.84 us
    dot_general x3, matrix products, output_part(): jnp.einsum('kqgn,kghpn->kqghp', c_spans, full_start, precision=HIGHEST_PR...  3.69 us
  transfers between devices with their start and end apart: 20, of which 11 were waited for; matrix products, arithmetic and copies ran while one was open for 11% of the time, Pallas kernels for 0%

profile of v7, /device:TPU:6, one launch (start us, length us, event | category | flops | bytes accessed | tf_op | source)
XLA Modules:
  0.0 169.0 jit_solution(9878063660400438013)
XLA Ops:
  0.7 0.7 exponential_negate_fusion
  1.3 1.4 multiply_bitcast_fusion.1
  2.8 0.6 reduce-window.26
  3.6 1.0 reduce-window.30
  4.7 0.6 slice.53
  5.6 0.6 slice.54
  7.8 0.6 multiply_bitcast_fusion
  9.6 0.8 fusion.90
  10.4 1.2 copy.122
  11.7 0.7 fusion.40
  12.5 0.7 dynamic-slice_reduce_fusion.1
  13.7 0.8 collective-permute-done
  14.6 3.4 %collective-permute-start.2 = (f32[1,8,64,128]{3,2,1,0:T(8,128)S(1)}, f32[1,8,64,128]{3,2,1,0:T(8,128)S(1)}, u32[]{:S(2)}, u32[]{:S(2)}) collective-permute-start(f32[1,8,64,128]{3,2,1,0:T(8,128)S(1)} %fusion.69), channel_id=1, source_target_pairs={{0,16},{8,24},{16,32},{24,40},{32,48},{40,56},{48,64},{56,72},{64,... | collective-permute-start | bytes 786440 | tf_op jit(solution)/shard_map/ppermute | solution.py:42
  18.0 7.0 %collective-permute-done.2 = f32[1,8,64,128]{3,2,1,0:T(8,128)S(1)} collective-permute-done((f32[1,8,64,128]{3,2,1,0:T(8,128)S(1)}, f32[1,8,64,128]{3,2,1,0:T(8,128)S(1)}, u32[]{:S(2)}, u32[]{:S(2)}) %collective-permute-start.2) | collective-permute-done | bytes 262176 | tf_op jit(solution)/shard_map/ppermute | solution.py:42
  25.2 4.3 %collective-permute-start.4 = (f32[1,8,64,128]{3,2,1,0:T(8,128)S(1)}, f32[1,8,64,128]{3,2,1,0:T(8,128)S(1)}, u32[]{:S(2)}, u32[]{:S(2)}) collective-permute-start(f32[1,8,64,128]{3,2,1,0:T(8,128)S(1)} %multiply_add_fusion.9), channel_id=1, source_target_pairs={{0,32},{8,40},{16,48},{24,56},{32,64},{40,72},{48,80},{56,88},{64,... | collective-permute-start | bytes 786440 | tf_op jit(solution)/shard_map/ppermute | solution.py:42
  29.5 4.0 %collective-permute-start.3 = (f32[1,8]{1,0:T(1,128)S(1)}, f32[1,8]{1,0:T(1,128)S(1)}, u32[]{:S(2)}, u32[]{:S(2)}) collective-permute-start(f32[1,8]{1,0:T(1,128)S(1)} %get-tuple-element.265), channel_id=1, source_target_pairs={{0,16},{8,24},{16,32},{24,40},{32,48},{40,56},{48,64},{56,72},{64,... | collective-permute-start | bytes 104 | tf_op jit(solution)/shard_map/ppermute | solution.py:42
  33.5 3.7 %collective-permute-done.3 = f32[1,8]{1,0:T(1,128)S(1)} collective-permute-done((f32[1,8]{1,0:T(1,128)S(1)}, f32[1,8]{1,0:T(1,128)S(1)}, u32[]{:S(2)}, u32[]{:S(2)}) %collective-permute-start.3) | collective-permute-done | bytes 64 | tf_op jit(solution)/shard_map/ppermute | solution.py:42
  37.3 3.5 %collective-permute-start.6 = (f32[1,8,64,128]{3,2,1,0:T(8,128)S(1)}, f32[1,8,64,128]{3,2,1,0:T(8,128)S(1)}, u32[]{:S(2)}, u32[]{:S(2)}) collective-permute-start(f32[1,8,64,128]{3,2,1,0:T(8,128)S(1)} %multiply_add_fusion.8), channel_id=1, source_target_pairs={{0,64},{8,72},{16,80},{24,88},{32,96},{40,104},{48,112},{56,120},{... | collective-permute-start | bytes 786440 | tf_op jit(solution)/shard_map/ppermute | solution.py:42
  40.8 0.9 fusion.116
  41.7 4.3 %collective-permute-start.5 = (f32[1,8]{1,0:T(1,128)S(1)}, f32[1,8]{1,0:T(1,128)S(1)}, u32[]{:S(2)}, u32[]{:S(2)}) collective-permute-start(f32[1,8]{1,0:T(1,128)S(1)} %mul.705), channel_id=1, source_target_pairs={{0,32},{8,40},{16,48},{24,56},{32,64},{40,72},{48,80},{56,88},{64,... | collective-permute-start | bytes 104 | tf_op jit(solution)/shard_map/ppermute | solution.py:42
  46.0 2.7 %collective-permute-done.5 = f32[1,8]{1,0:T(1,128)S(1)} collective-permute-done((f32[1,8]{1,0:T(1,128)S(1)}, f32[1,8]{1,0:T(1,128)S(1)}, u32[]{:S(2)}, u32[]{:S(2)}) %collective-permute-start.5) | collective-permute-done | bytes 64 | tf_op jit(solution)/shard_map/ppermute | solution.py:42
  48.8 3.9 %collective-permute-start.8 = (f32[1,8,64,128]{3,2,1,0:T(8,128)S(1)}, f32[1,8,64,128]{3,2,1,0:T(8,128)S(1)}, u32[]{:S(2)}, u32[]{:S(2)}) collective-permute-start(f32[1,8,64,128]{3,2,1,0:T(8,128)S(1)} %multiply_add_fusion.7), channel_id=1, source_target_pairs={{0,128},{8,136},{16,144},{24,152},{32,160},{40,168},{48,176},{56,1... | collective-permute-start | bytes 786440 | tf_op jit(solution)/shard_map/ppermute | solution.py:42
  52.6 0.8 fusion.75
  53.4 1.3 collective-permute-start.7
  54.7 1.8 %collective-permute-done.7 = f32[1,8]{1,0:T(1,128)S(1)} collective-permute-done((f32[1,8]{1,0:T(1,128)S(1)}, f32[1,8]{1,0:T(1,128)S(1)}, u32[]{:S(2)}, u32[]{:S(2)}) %collective-permute-start.7) | collective-permute-done | bytes 64 | tf_op jit(solution)/shard_map/ppermute | solution.py:42
  57.3 0.6 fusion.96
  58.0 0.7 mul.729
  58.8 1.2 copy.125
  60.1 0.8 fusion.72
  60.9 0.6 convolution_bitcast_fusion.1
  61.5 1.0 copy-done.2
  62.5 3.2 %fusion.32 = f32[1,256,1,16,64]{1,4,3,2,0:T(8,128)S(1)} fusion(bf16[256,16,64]{0,2,1:T(8,128)(2,1)S(1)} %bitcast.300, f32[16,256]{1,0:T(8,128)S(1)} %copy-done.29, f32[256,256]{1,0:T(8,128)S(1)} %copy-done.11, f32[16,256]{1,0:T(8,128)S(1)} %copy-done.32, f32[256,256]{1,0:T(8,128)S(1)} %copy-done.8, ...), kind=kOutput, calls=%fused_computation.34 | convolution fusion | flops 811073536 | bytes 3194880 | tf_op jit(solution)/shard_map/jvp()/while/body/eval_jaxpr/ghts,sghp->tghp/dot_general | solution.py:88
  65.8 1.6 multiply_reduce_fusion.2
  67.4 16.0 %all_to_all.5 = f32[8,2,256]{2,1,0:T(2,128)S(1)} all-to-all(f32[8,2,256]{2,1,0:T(2,128)S(1)} %broadcast_in_dim.147), channel_id=1, replica_groups=mesh['ctx'=32,'head'=8] {'head'}, dimensions={0} | all-to-all | bytes 32768 | tf_op jit(solution)/shard_map/all_to_all | solution.py:75
  83.5 3.1 %fusion.51 = (bf16[256,1024]{0,1:T(8,128)(2,1)}, f32[256,1024]{0,1:T(8,128)S(1)}) fusion(bf16[256,1024]{0,1:T(8,128)(2,1)S(1)} %copy.124, bf16[256,1024]{0,1:T(8,128)(2,1)S(1)} %copy.122, f32[1,256,1,16,64]{1,4,3,2,0:T(8,128)} %copy-done.1, f32[1024]{0:T(1024)S(1)} %copy-done.21, f32[256]{0:T(256)S(1)} %multiply_multiply_fusion, ...), kind=kLoop, calls=%fused_computation.53 | loop fusion | flops 5767168 | bytes 5253120 | tf_op jit(solution)/shard_map/convert_element_type | solution.py:219
  86.6 0.6 fusion.53
  87.9 1.0 collective-permute-done.10
  89.1 2.9 %collective-permute-start.12 = (f32[1,8,64,128]{3,2,1,0:T(8,128)S(1)}, f32[1,8,64,128]{3,2,1,0:T(8,128)S(1)}, u32[]{:S(2)}, u32[]{:S(2)}) collective-permute-start(f32[1,8,64,128]{3,2,1,0:T(8,128)S(1)} %fusion.68), channel_id=1, source_target_pairs={{248,232},{240,224},{232,216},{224,208},{216,200},{208,192},{200,1... | collective-permute-start | bytes 786440 | tf_op jit(solution)/shard_map/ppermute | solution.py:42
  92.0 12.0 %collective-permute-done.12 = f32[1,8,64,128]{3,2,1,0:T(8,128)S(1)} collective-permute-done((f32[1,8,64,128]{3,2,1,0:T(8,128)S(1)}, f32[1,8,64,128]{3,2,1,0:T(8,128)S(1)}, u32[]{:S(2)}, u32[]{:S(2)}) %collective-permute-start.12) | collective-permute-done | bytes 262176 | tf_op jit(solution)/shard_map/ppermute | solution.py:42
  104.1 1.9 %collective-permute-start.14 = (f32[1,8,64,128]{3,2,1,0:T(8,128)S(1)}, f32[1,8,64,128]{3,2,1,0:T(8,128)S(1)}, u32[]{:S(2)}, u32[]{:S(2)}) collective-permute-start(f32[1,8,64,128]{3,2,1,0:T(8,128)S(1)} %multiply_add_fusion.4), channel_id=1, source_target_pairs={{248,216},{240,208},{232,200},{224,192},{216,184},{208,176},{200,1... | collective-permute-start | bytes 786440 | tf_op jit(solution)/shard_map/ppermute | solution.py:42
  106.1 2.6 %collective-permute-start.13 = (f32[1,8]{1,0:T(1,128)S(1)}, f32[1,8]{1,0:T(1,128)S(1)}, u32[]{:S(2)}, u32[]{:S(2)}) collective-permute-start(f32[1,8]{1,0:T(1,128)S(1)} %get-tuple-element.260), channel_id=1, source_target_pairs={{248,232},{240,224},{232,216},{224,208},{216,200},{208,192},{200,1... | collective-permute-start | bytes 104 | tf_op jit(solution)/shard_map/ppermute | solution.py:42
  108.7 5.0 %collective-permute-done.13 = f32[1,8]{1,0:T(1,128)S(1)} collective-permute-done((f32[1,8]{1,0:T(1,128)S(1)}, f32[1,8]{1,0:T(1,128)S(1)}, u32[]{:S(2)}, u32[]{:S(2)}) %collective-permute-start.13) | collective-permute-done | bytes 64 | tf_op jit(solution)/shard_map/ppermute | solution.py:42
  113.6 1.9 %collective-permute-start.15 = (f32[1,8]{1,0:T(1,128)S(1)}, f32[1,8]{1,0:T(1,128)S(1)}, u32[]{:S(2)}, u32[]{:S(2)}) collective-permute-start(f32[1,8]{1,0:T(1,128)S(1)} %mul.758), channel_id=1, source_target_pairs={{248,216},{240,208},{232,200},{224,192},{216,184},{208,176},{200,1... | collective-permute-start | bytes 104 | tf_op jit(solution)/shard_map/ppermute | solution.py:42
  115.5 5.9 %collective-permute-done.15 = f32[1,8]{1,0:T(1,128)S(1)} collective-permute-done((f32[1,8]{1,0:T(1,128)S(1)}, f32[1,8]{1,0:T(1,128)S(1)}, u32[]{:S(2)}, u32[]{:S(2)}) %collective-permute-start.15) | collective-permute-done | bytes 64 | tf_op jit(solution)/shard_map/ppermute | solution.py:42
  121.5 1.3 collective-permute-start.17
  122.8 4.2 %collective-permute-done.17 = f32[1,8]{1,0:T(1,128)S(1)} collective-permute-done((f32[1,8]{1,0:T(1,128)S(1)}, f32[1,8]{1,0:T(1,128)S(1)}, u32[]{:S(2)}, u32[]{:S(2)}) %collective-permute-start.17) | collective-permute-done | bytes 64 | tf_op jit(solution)/shard_map/ppermute | solution.py:42
  127.1 1.3 collective-permute-start.16
  128.4 6.7 %fusion.67 = (f32[16,256]{1,0:T(8,128)}, f32[16,256]{1,0:T(8,128)}, f32[16,256]{1,0:T(8,128)}, f32[256,256]{1,0:T(8,128)S(1)}) fusion(f32[16,256]{1,0:T(8,128)S(1)} %copy-done.33, f32[256,256]{1,0:T(8,128)S(1)} %copy-done.12, f32[16,256]{1,0:T(8,128)S(1)} %copy-done.30, f32[256,256]{1,0:T(8,128)S(1)} %copy-done.9, f32[16,64,256]{2,1,0:T(8,128)S(1)} %bitcast.295, ...), kind=kOutput, calls=%fused_computation.81 | convolution fusion | flops 825151488 | bytes 2441216 | tf_op jit(solution)/shard_map/transpose(jvp())/while/body/eval_jaxpr/ghts,sghp->tghp/dot_general | solution.py:88
  135.5 1.3 collective-permute-start.18
  136.8 0.8 multiply_reduce_fusion
  137.6 2.5 %fusion.42 = f32[256,128]{1,0:T(8,128)} fusion(f32[256,128]{1,0:T(8,128)S(1)} %fusion.117, f32[1,256,1,16,64]{1,4,3,2,0:T(8,128)S(1)} %bitcast.297, f32[256,16]{0,1:T(8,128)S(1)} %copy-done.15, f32[8,64,128]{2,1,0:T(8,128)S(1)} %bitcast.304, f32[8,64,128]{2,1,0:T(8,128)S(1)} %bitcast.308, pred[]{:T(512)S(6)} %eq.79), kind=kOutput, calls=%fused_computation.44 | convolution fusion | flops 403341312 | bytes 1851393 | tf_op jit(solution)/shard_map/transpose(jvp(kqgn,kghpn->kqghp))/dot_general | solution.py:137
  140.0 5.2 %collective-permute-done.18 = f32[1,8,64,128]{3,2,1,0:T(8,128)S(1)} collective-permute-done((f32[1,8,64,128]{3,2,1,0:T(8,128)S(1)}, f32[1,8,64,128]{3,2,1,0:T(8,128)S(1)}, u32[]{:S(2)}, u32[]{:S(2)}) %collective-permute-start.18) | collective-permute-done | bytes 262176 | tf_op jit(solution)/shard_map/ppermute | solution.py:42
  145.3 1.0 fusion.71
  146.2 1.0 convolution_bitcast_fusion.2
  147.3 1.0 copy.139
  148.3 1.0 fusion.70
  149.3 1.3 multiply_reduce_fusion.3
  150.9 1.7 fusion.45
  153.1 2.5 %reduce-window.36 = f32[1,16,1,2,128]{4,1,2,3,0:T(8,128)S(1)} reduce-window(f32[1,16,1,2,128]{4,1,2,3,0:T(8,128)S(1)} %copy_bitcast_fusion, f32[]{:T(128)} %constant.175.clone.1), window={size=1x1x1x1x128 pad=0_0x0_0x0_0x0_0x0_127}, to_apply=%region_16.17 | reduce-window | flops 520192 | bytes 32772 | tf_op jit(solution)/shard_map/reduce-window.6
  155.7 2.5 %reduce-window.34 = f32[1,16,1,2,128]{4,1,2,3,0:T(8,128)S(1)} reduce-window(f32[1,16,1,2,128]{4,1,2,3,0:T(8,128)S(1)} %bitcast.314, f32[]{:T(128)} %constant.175.clone.1), window={size=1x1x1x1x128 pad=0_0x0_0x0_0x0_0x0_127}, to_apply=%region_11.12 | reduce-window | flops 520192 | bytes 32772 | tf_op jit(solution)/shard_map/reduce-window.4
  158.3 3.5 %fusion.44 = f32[256,128]{1,0:T(8,128)} fusion(f32[1,256,1,128]{3,1,2,0:T(8,128)S(1)} %copy-done.20, bf16[256,16,64]{0,2,1:T(8,128)(2,1)S(1)} %bitcast.302, f32[256,16]{0,1:T(8,128)S(1)} %copy-done.24, f32[8,64,128]{2,1,0:T(8,128)S(1)} %bitcast.306, f32[8,64,128]{2,1,0:T(8,128)} %bitcast.70, pred[]{:T(512)S(6)} %eq.86), kind=kOutput, calls=%fused_computation.46 | convolution fusion | flops 403603456 | bytes 1327105 | tf_op jit(solution)/shard_map/transpose(jvp(kqgh,kqghp,kqgn->kghpn))/dot_general | solution.py:102
  161.8 4.7 %fusion.35 = f32[256,16,64]{0,2,1:T(8,128)S(1)} fusion(f32[16,64,256]{2,1,0:T(8,128)S(1)} %bitcast.298, f32[16,256]{1,0:T(8,128)S(1)} %copy-done.31, f32[256,256]{1,0:T(8,128)} %fusion.75, f32[16,256]{1,0:T(8,128)S(1)} %copy-done.34, f32[256,256]{1,0:T(8,128)S(1)} %copy-done.10, f32[256,16,64]{0,2,1:T(8,128)S(1)} %get-tuple-element.269, ...), kind=kOutput, calls=%fused_computation.35 | convolution fusion | flops 811073536 | bytes 3719168 | tf_op jit(solution)/shard_map/transpose(jvp())/while/body/eval_jaxpr/ghts,sghp->tghp/dot_general | solution.py:88
  166.8 1.0 copy.138
  168.3 0.7 fusion.88
  (181 shorter events, 7.0 us)
Async XLA Ops:
  0.6 11.1 %copy-start = (bf16[256,128]{1,0:T(8,128)(2,1)S(1)}, bf16[256,128]{1,0:T(8,128)(2,1)}, u32[]{:S(2)}) copy-start(bf16[256,128]{1,0:T(8,128)(2,1)} %param.14) | copy-start | bytes 196612
  1.3 1.4 copy-start.46
  3.5 5.1 %copy-start.16 = (f32[1,16,1,2,128]{4,3,2,1,0:T(2,128)}, f32[1,16,1,2,128]{4,3,2,1,0:T(2,128)S(1)}, u32[]{:S(2)}) copy-start(f32[1,16,1,2,128]{4,3,2,1,0:T(2,128)S(1)} %copy.119) | copy-start | bytes 49156
  5.6 3.0 %copy-start.38 = (f32[256]{0:T(256)}, f32[256]{0:T(256)S(1)}, u32[]{:S(2)}) copy-start(f32[256]{0:T(256)S(1)} %get-tuple-element.233) | copy-start | bytes 3076
  10.4 1.9 %copy-start.23 = (f32[256,16]{0,1:T(8,128)}, f32[256,16]{0,1:T(8,128)S(1)}, u32[]{:S(2)}) copy-start(f32[256,16]{0,1:T(8,128)S(1)} %fusion.90) | copy-start | bytes 49156
  12.4 2.1 %collective-permute-start.1 = (f32[1,8,64,128]{3,2,1,0:T(8,128)S(1)}, f32[1,8,64,128]{3,2,1,0:T(8,128)S(1)}, u32[]{:S(2)}, u32[]{:S(2)}) collective-permute-start(f32[1,8,64,128]{3,2,1,0:T(8,128)S(1)} %dynamic-slice_bitcast_fusion.1), channel_id=1, source_target_pairs={{0,8},{8,0},{16,24},{24,16},{32,40},{40,32},{48,56},{56,48},{64,72... | collective-permute-start | bytes 786440 | tf_op jit(solution)/shard_map/ppermute | solution.py:42
  13.2 1.3 collective-permute-start
  14.5 42.0 %copy-start.45 = (f32[8]{0:T(128)}, f32[8]{0:T(128)S(1)}, u32[]{:S(2)}) copy-start(f32[8]{0:T(128)S(1)} %get-tuple-element.266) | copy-start | bytes 100
  14.5 26.3 %copy-start.5 = (bf16[256,128]{1,0:T(8,128)(2,1)S(1)}, bf16[256,128]{1,0:T(8,128)(2,1)}, u32[]{:S(2)}) copy-start(bf16[256,128]{1,0:T(8,128)(2,1)} %param.15) | copy-start | bytes 196612
  14.6 10.4 %collective-permute-start.2 = (f32[1,8,64,128]{3,2,1,0:T(8,128)S(1)}, f32[1,8,64,128]{3,2,1,0:T(8,128)S(1)}, u32[]{:S(2)}, u32[]{:S(2)}) collective-permute-start(f32[1,8,64,128]{3,2,1,0:T(8,128)S(1)} %fusion.69), channel_id=1, source_target_pairs={{0,16},{8,24},{16,32},{24,40},{32,48},{40,56},{48,64},{56,72},{64,... | collective-permute-start | bytes 786440 | tf_op jit(solution)/shard_map/ppermute | solution.py:42
  25.2 12.0 %collective-permute-start.4 = (f32[1,8,64,128]{3,2,1,0:T(8,128)S(1)}, f32[1,8,64,128]{3,2,1,0:T(8,128)S(1)}, u32[]{:S(2)}, u32[]{:S(2)}) collective-permute-start(f32[1,8,64,128]{3,2,1,0:T(8,128)S(1)} %multiply_add_fusion.9), channel_id=1, source_target_pairs={{0,32},{8,40},{16,48},{24,56},{32,64},{40,72},{48,80},{56,88},{64,... | collective-permute-start | bytes 786440 | tf_op jit(solution)/shard_map/ppermute | solution.py:42
  29.5 7.7 %collective-permute-start.3 = (f32[1,8]{1,0:T(1,128)S(1)}, f32[1,8]{1,0:T(1,128)S(1)}, u32[]{:S(2)}, u32[]{:S(2)}) collective-permute-start(f32[1,8]{1,0:T(1,128)S(1)} %get-tuple-element.265), channel_id=1, source_target_pairs={{0,16},{8,24},{16,32},{24,40},{32,48},{40,56},{48,64},{56,72},{64,... | collective-permute-start | bytes 104 | tf_op jit(solution)/shard_map/ppermute | solution.py:42
  37.3 11.4 %collective-permute-start.6 = (f32[1,8,64,128]{3,2,1,0:T(8,128)S(1)}, f32[1,8,64,128]{3,2,1,0:T(8,128)S(1)}, u32[]{:S(2)}, u32[]{:S(2)}) collective-permute-start(f32[1,8,64,128]{3,2,1,0:T(8,128)S(1)} %multiply_add_fusion.8), channel_id=1, source_target_pairs={{0,64},{8,72},{16,80},{24,88},{32,96},{40,104},{48,112},{56,120},{... | collective-permute-start | bytes 786440 | tf_op jit(solution)/shard_map/ppermute | solution.py:42
  41.7 7.0 %collective-permute-start.5 = (f32[1,8]{1,0:T(1,128)S(1)}, f32[1,8]{1,0:T(1,128)S(1)}, u32[]{:S(2)}, u32[]{:S(2)}) collective-permute-start(f32[1,8]{1,0:T(1,128)S(1)} %mul.705), channel_id=1, source_target_pairs={{0,32},{8,40},{16,48},{24,56},{32,64},{40,72},{48,80},{56,88},{64,... | collective-permute-start | bytes 104 | tf_op jit(solution)/shard_map/ppermute | solution.py:42
  48.8 7.8 %collective-permute-start.8 = (f32[1,8,64,128]{3,2,1,0:T(8,128)S(1)}, f32[1,8,64,128]{3,2,1,0:T(8,128)S(1)}, u32[]{:S(2)}, u32[]{:S(2)}) collective-permute-start(f32[1,8,64,128]{3,2,1,0:T(8,128)S(1)} %multiply_add_fusion.7), channel_id=1, source_target_pairs={{0,128},{8,136},{16,144},{24,152},{32,160},{40,168},{48,176},{56,1... | collective-permute-start | bytes 786440 | tf_op jit(solution)/shard_map/ppermute | solution.py:42
  53.4 3.1 %collective-permute-start.7 = (f32[1,8]{1,0:T(1,128)S(1)}, f32[1,8]{1,0:T(1,128)S(1)}, u32[]{:S(2)}, u32[]{:S(2)}) collective-permute-start(f32[1,8]{1,0:T(1,128)S(1)} %mul.713), channel_id=1, source_target_pairs={{0,64},{8,72},{16,80},{24,88},{32,96},{40,104},{48,112},{56,120},{... | collective-permute-start | bytes 104 | tf_op jit(solution)/shard_map/ppermute | solution.py:42
  56.6 1.3 copy-start.49
  56.6 2.0 %copy-start.6 = (bf16[256,1024]{1,0:T(8,128)(2,1)S(1)}, bf16[256,1024]{1,0:T(8,128)(2,1)}, u32[]{:S(2)}) copy-start(bf16[256,1024]{1,0:T(8,128)(2,1)} %param.12) | copy-start | bytes 1572868
  56.8 4.1 %collective-permute-start.9 = (f32[1,8,64,128]{3,2,1,0:T(8,128)S(1)}, f32[1,8,64,128]{3,2,1,0:T(8,128)S(1)}, u32[]{:S(2)}, u32[]{:S(2)}) collective-permute-start(f32[1,8,64,128]{3,2,1,0:T(8,128)S(1)} %get-tuple-element.235), channel_id=1, source_target_pairs={{0,8},{8,0},{16,24},{24,16},{32,40},{40,32},{48,56},{56,48},{64,72... | collective-permute-start | bytes 786440 | tf_op jit(solution)/shard_map/ppermute | solution.py:42
  60.8 1.6 copy-start.8
  60.9 1.6 copy-start.11
  60.9 1.6 copy-start.13
  60.9 1.6 copy-start.29
  60.9 1.6 copy-start.32
  62.5 3.3 %copy-start.21 = (f32[1024]{0:T(1024)S(1)}, f32[1024]{0:T(1024)}, u32[]{:S(2)}) copy-start(f32[1024]{0:T(1024)} %mul.729) | copy-start | bytes 12292
  62.5 3.3 %copy-start.26 = (f32[1024]{0:T(1024)S(1)}, f32[1024]{0:T(1024)}, u32[]{:S(2)}) copy-start(f32[1024]{0:T(1024)} %param.19) | copy-start | bytes 12292
  65.8 1.6 copy-start.1
  83.5 3.1 %copy-start.14 = (f32[256,16]{0,1:T(8,128)S(1)}, f32[256,16]{0,1:T(8,128)}, u32[]{:S(2)}) copy-start(f32[256,16]{0,1:T(8,128)} %get-tuple-element.221) | copy-start | bytes 49156
  86.6 2.3 %copy-start.48 = (f32[8]{0:T(128)S(1)}, f32[8]{0:T(128)}, u32[]{:S(2)}) copy-start(f32[8]{0:T(128)} %get-tuple-element.212) | copy-start | bytes 100
  87.3 1.6 collective-permute-start.11
  87.4 1.5 collective-permute-start.10
  89.0 56.3 %copy-start.43 = (f32[8]{0:T(128)}, f32[8]{0:T(128)S(1)}, u32[]{:S(2)}) copy-start(f32[8]{0:T(128)S(1)} %get-tuple-element.261) | copy-start | bytes 100
  89.0 39.4 %copy-start.9 = (f32[256,256]{1,0:T(8,128)S(1)}, f32[256,256]{1,0:T(8,128)}, u32[]{:S(2)}) copy-start(f32[256,256]{1,0:T(8,128)} %fusion.116) | copy-start | bytes 786436
  89.0 39.4 %copy-start.12 = (f32[256,256]{1,0:T(8,128)S(1)}, f32[256,256]{1,0:T(8,128)}, u32[]{:S(2)}) copy-start(f32[256,256]{1,0:T(8,128)} %fusion.75) | copy-start | bytes 786436
  89.0 39.4 %copy-start.30 = (f32[16,256]{1,0:T(8,128)S(1)}, f32[16,256]{1,0:T(8,128)}, u32[]{:S(2)}) copy-start(f32[16,256]{1,0:T(8,128)} %get-tuple-element.240) | copy-start | bytes 49156
  89.0 39.4 %copy-start.33 = (f32[16,256]{1,0:T(8,128)S(1)}, f32[16,256]{1,0:T(8,128)}, u32[]{:S(2)}) copy-start(f32[16,256]{1,0:T(8,128)} %fusion.96) | copy-start | bytes 49156
  89.1 14.9 %collective-permute-start.12 = (f32[1,8,64,128]{3,2,1,0:T(8,128)S(1)}, f32[1,8,64,128]{3,2,1,0:T(8,128)S(1)}, u32[]{:S(2)}, u32[]{:S(2)}) collective-permute-start(f32[1,8,64,128]{3,2,1,0:T(8,128)S(1)} %fusion.68), channel_id=1, source_target_pairs={{248,232},{240,224},{232,216},{224,208},{216,200},{208,192},{200,1... | collective-permute-start | bytes 786440 | tf_op jit(solution)/shard_map/ppermute | solution.py:42
  104.1 22.8 %collective-permute-start.14 = (f32[1,8,64,128]{3,2,1,0:T(8,128)S(1)}, f32[1,8,64,128]{3,2,1,0:T(8,128)S(1)}, u32[]{:S(2)}, u32[]{:S(2)}) collective-permute-start(f32[1,8,64,128]{3,2,1,0:T(8,128)S(1)} %multiply_add_fusion.4), channel_id=1, source_target_pairs={{248,216},{240,208},{232,200},{224,192},{216,184},{208,176},{200,1... | collective-permute-start | bytes 786440 | tf_op jit(solution)/shard_map/ppermute | solution.py:42
  106.1 7.6 %collective-permute-start.13 = (f32[1,8]{1,0:T(1,128)S(1)}, f32[1,8]{1,0:T(1,128)S(1)}, u32[]{:S(2)}, u32[]{:S(2)}) collective-permute-start(f32[1,8]{1,0:T(1,128)S(1)} %get-tuple-element.260), channel_id=1, source_target_pairs={{248,232},{240,224},{232,216},{224,208},{216,200},{208,192},{200,1... | collective-permute-start | bytes 104 | tf_op jit(solution)/shard_map/ppermute | solution.py:42
  113.6 7.9 %collective-permute-start.15 = (f32[1,8]{1,0:T(1,128)S(1)}, f32[1,8]{1,0:T(1,128)S(1)}, u32[]{:S(2)}, u32[]{:S(2)}) collective-permute-start(f32[1,8]{1,0:T(1,128)S(1)} %mul.758), channel_id=1, source_target_pairs={{248,216},{240,208},{232,200},{224,192},{216,184},{208,176},{200,1... | collective-permute-start | bytes 104 | tf_op jit(solution)/shard_map/ppermute | solution.py:42
  121.5 5.5 %collective-permute-start.17 = (f32[1,8]{1,0:T(1,128)S(1)}, f32[1,8]{1,0:T(1,128)S(1)}, u32[]{:S(2)}, u32[]{:S(2)}) collective-permute-start(f32[1,8]{1,0:T(1,128)S(1)} %mul.766), channel_id=1, source_target_pairs={{248,184},{240,176},{232,168},{224,160},{216,152},{208,144},{200,1... | collective-permute-start | bytes 104 | tf_op jit(solution)/shard_map/ppermute | solution.py:42
  127.1 8.3 %collective-permute-start.16 = (f32[1,8,64,128]{3,2,1,0:T(8,128)S(1)}, f32[1,8,64,128]{3,2,1,0:T(8,128)S(1)}, u32[]{:S(2)}, u32[]{:S(2)}) collective-permute-start(f32[1,8,64,128]{3,2,1,0:T(8,128)S(1)} %multiply_add_fusion.3), channel_id=1, source_target_pairs={{248,184},{240,176},{232,168},{224,160},{216,152},{208,144},{200,1... | collective-permute-start | bytes 786440 | tf_op jit(solution)/shard_map/ppermute | solution.py:42
  135.1 1.7 %copy-start.3 = (f32[1,256,1,16,64]{1,4,3,2,0:T(8,128)S(1)}, f32[1,256,1,16,64]{1,4,3,2,0:T(8,128)}, u32[]{:S(2)}) copy-start(f32[1,256,1,16,64]{1,4,3,2,0:T(8,128)} %copy-done.2) | copy-start | bytes 3145732
  135.5 2.1 %copy-start.15 = (f32[256,16]{0,1:T(8,128)S(1)}, f32[256,16]{0,1:T(8,128)}, u32[]{:S(2)}) copy-start(f32[256,16]{0,1:T(8,128)} %get-tuple-element.221) | copy-start | bytes 49156
  135.5 9.8 %collective-permute-start.18 = (f32[1,8,64,128]{3,2,1,0:T(8,128)S(1)}, f32[1,8,64,128]{3,2,1,0:T(8,128)S(1)}, u32[]{:S(2)}, u32[]{:S(2)}) collective-permute-start(f32[1,8,64,128]{3,2,1,0:T(8,128)S(1)} %multiply_add_fusion.2), channel_id=1, source_target_pairs={{248,120},{240,112},{232,104},{224,96},{216,88},{208,80},{200,72},... | collective-permute-start | bytes 786440 | tf_op jit(solution)/shard_map/ppermute | solution.py:42
  145.3 2.0 %copy-start.4 = (bf16[256,1024]{0,1:T(8,128)(2,1)S(1)}, bf16[256,1024]{0,1:T(8,128)(2,1)}, u32[]{:S(2)}) copy-start(bf16[256,1024]{0,1:T(8,128)(2,1)} %get-tuple-element.237) | copy-start | bytes 1572868
  146.2 3.1 %collective-permute-start.19 = (f32[1,8,64,128]{3,2,1,0:T(8,128)}, f32[1,8,64,128]{3,2,1,0:T(8,128)}, u32[]{:S(2)}, u32[]{:S(2)}) collective-permute-start(f32[1,8,64,128]{3,2,1,0:T(8,128)} %get-tuple-element.218), channel_id=1, source_target_pairs={{248,240},{240,248},{232,224},{224,232},{216,208},{208,216},{200,1... | collective-permute-start | bytes 786440 | tf_op jit(solution)/shard_map/ppermute | solution.py:42
  147.3 1.0 copy-start.44
  150.8 1.8 %copy-start.7 = (f32[256,16]{0,1:T(8,128)S(1)}, f32[256,16]{0,1:T(8,128)}, u32[]{:S(2)}) copy-start(f32[256,16]{0,1:T(8,128)} %param.13) | copy-start | bytes 49156
  150.8 1.8 %copy-start.25 = (f32[256,16]{0,1:T(8,128)S(1)}, f32[256,16]{0,1:T(8,128)}, u32[]{:S(2)}) copy-start(f32[256,16]{0,1:T(8,128)} %multiply_reduce_fusion) | copy-start | bytes 49156
  150.8 1.8 %copy-start.28 = (f32[256]{0:T(256)S(1)}, f32[256]{0:T(256)}, u32[]{:S(2)}) copy-start(f32[256]{0:T(256)} %copy-done.27) | copy-start | bytes 3076
  150.8 1.8 %copy-start.36 = (f32[16,256]{1,0:T(8,128)S(1)}, f32[16,256]{1,0:T(8,128)}, u32[]{:S(2)}) copy-start(f32[16,256]{1,0:T(8,128)} %get-tuple-element.192) | copy-start | bytes 49156
  150.8 1.8 %copy-start.37 = (f32[16,256]{1,0:T(8,128)S(1)}, f32[16,256]{1,0:T(8,128)}, u32[]{:S(2)}) copy-start(f32[16,256]{1,0:T(8,128)} %get-tuple-element.193) | copy-start | bytes 49156
  150.8 1.8 %copy-start.39 = (f32[256]{0:T(256)S(1)}, f32[256]{0:T(256)}, u32[]{:S(2)}) copy-start(f32[256]{0:T(256)} %copy-done.38) | copy-start | bytes 3076
  150.9 1.8 %copy-start.40 = (f32[16]{0:T(128)S(1)}, f32[16]{0:T(128)}, u32[]{:S(2)}) copy-start(f32[16]{0:T(128)} %param.16) | copy-start | bytes 196
  150.9 1.8 %copy-start.42 = (f32[16]{0:T(128)S(1)}, f32[16]{0:T(128)}, u32[]{:S(2)}) copy-start(f32[16]{0:T(128)} %copy-done.41) | copy-start | bytes 196
  150.9 7.4 %copy-start.20 = (f32[1,256,1,128]{3,1,2,0:T(8,128)S(1)}, f32[1,256,1,128]{3,1,2,0:T(8,128)}, u32[]{:S(2)}) copy-start(f32[1,256,1,128]{3,1,2,0:T(8,128)} %convolution_bitcast_fusion.2) | copy-start | bytes 393220
  150.9 7.4 %copy-start.24 = (f32[256,16]{0,1:T(8,128)S(1)}, f32[256,16]{0,1:T(8,128)}, u32[]{:S(2)}) copy-start(f32[256,16]{0,1:T(8,128)} %copy-done.23) | copy-start | bytes 49156
  152.9 8.9 %copy-start.10 = (f32[256,256]{1,0:T(8,128)S(1)}, f32[256,256]{1,0:T(8,128)}, u32[]{:S(2)}) copy-start(f32[256,256]{1,0:T(8,128)} %fusion.116) | copy-start | bytes 786436
  152.9 8.9 %copy-start.31 = (f32[16,256]{1,0:T(8,128)S(1)}, f32[16,256]{1,0:T(8,128)}, u32[]{:S(2)}) copy-start(f32[16,256]{1,0:T(8,128)} %get-tuple-element.240) | copy-start | bytes 49156
  152.9 8.9 %copy-start.34 = (f32[16,256]{1,0:T(8,128)S(1)}, f32[16,256]{1,0:T(8,128)}, u32[]{:S(2)}) copy-start(f32[16,256]{1,0:T(8,128)} %fusion.96) | copy-start | bytes 49156
  161.8 4.7 %copy-start.22 = (f32[1024]{0:T(1024)S(1)}, f32[1024]{0:T(1024)}, u32[]{:S(2)}) copy-start(f32[1024]{0:T(1024)} %mul.729) | copy-start | bytes 12292
  166.8 1.5 copy-start.35
  166.8 1.5 copy-start.47
  (7 other events, 5.1 us)

commit v8 on v7

--- a/solution.py
+++ b/solution.py
@@ -2,6 +2,7 @@
 import jax.numpy as jnp
 from jax import lax
 from jax.sharding import PartitionSpec as P
+
 
 HEAD_DIM = 64
 STATE = 128
@@ -124,7 +125,7 @@
 
 
 def output_part(x_spans, dt_spans, b_spans, c_spans, segment, decay_rate, starts, entry_state):
-    log_cum, closing, through = block_decays(dt_spans, segment, decay_rate)
+    log_cum, _, through = block_decays(dt_spans, segment, decay_rate)
 
     def rolling(product, decay_now):
         return (product * decay_now, product)
@@ -142,7 +143,7 @@
     return inner_part + carried
 
 
-def body(
+def layer_body(
     ssm_input,
     gate_input,
     step_raw,
@@ -203,6 +204,9 @@
     grad_core = grad_gated * gate_act
     grad_gate = grad_gated * core_out * gate_sig * (1.0 + gate_float * (1.0 - gate_sig))
     first_grads = output_back(grad_core.reshape(core_part.shape))
+    first_grads = tuple(
+        lax.optimization_barrier(part) if k < 4 else part for k, part in enumerate(first_grads)
+    )
     exit_adjoint = chip_scan(through_all, first_grads[5], "ctx", False)
     through_grad = jnp.sum(exit_adjoint * entry_state, axis=(2, 3))
     second_grads = states_back((first_grads[4], exit_adjoint, through_grad))
@@ -225,7 +229,7 @@
 
 def solution(mesh):
     return jax.shard_map(
-        body,
+        layer_body,
         mesh=mesh,
         in_specs=(
             P("ctx", "head"),

time: 172 us -> 167 us (0.971)
  waiting for transfers between devices: 49.4 us -> 43.3 us
    ppermute x20, waiting for transfers between devices: 49.4 us -> 43.3 us  [move(): return lax.ppermute(tree, axis, [(device(a), device(b)) for a, b in pairs])]
    unnamed x107 -> x97, local copies, waits for them, and re-layouts: 7.28 us -> 6.4 us
  transfers between devices with their start and end apart: 20 -> 20, of which waited for: 11 -> 12; matrix products, arithmetic and copies ran while one was open for 11% -> 15% of each run, Pallas kernels for 0% -> 0%
where the time goes in v8:
time: 167 us; the launch traced here: 165 us
  waiting for transfers between devices  43.3 us (26%)
  starting transfers between devices  40.6 us (24%)
  matrix products  27.6 us (17%)
  other arithmetic  23.8 us (14%)
  blocking collectives  16 us (10%)
  local copies, waits for them, and re-layouts  10.4 us (6%)
  between operations  2.85 us (2%)
    ppermute x20, waiting for transfers between devices, move(): return lax.ppermute(tree, axis, [(device(a), device(b)) for a, b in pairs])  43.3 us
    ppermute x20, starting transfers between devices, move(): return lax.ppermute(tree, axis, [(device(a), device(b)) for a, b in pairs])  40.6 us
    all_to_all x1, blocking collectives, head_sum(): return jnp.sum(lax.all_to_all(spread, axis, 0, 0), axis=0)  16 us
    dot_general x3, matrix products, span_mix(): jnp.einsum('ghts,sghp->tghp', weights, x_span, precision=HIGHEST_PRECISION)  15.6 us
    another operation x10, other arithmetic  7.72 us
    unnamed x97, local copies, waits for them, and re-layouts  6.4 us
    dot_general x3, matrix products, local_states(): jnp.einsum('kqgh,kqghp,kqgn->kghpn', tail_decay * dt_spans, x_spans, b_sp...  6.14 us
    dot_general x3, matrix products, output_part(): jnp.einsum('kqgn,kghpn->kqghp', c_spans, full_start, precision=HIGHEST_PR...  3.69 us
  transfers between devices with their start and end apart: 20, of which 12 were waited for; matrix products, arithmetic and copies ran while one was open for 15% of the time, Pallas kernels for 0%

profile of v8, /device:TPU:6, one launch (start us, length us, event | category | flops | bytes accessed | tf_op | source)
XLA Modules:
  0.0 164.6 jit_solution(4863584305172916482)
XLA Ops:
  0.7 0.7 exponential_negate_fusion
  1.3 1.4 multiply_bitcast_fusion.1
  2.8 0.6 reduce-window.26
  3.5 1.0 reduce-window.30
  4.7 0.6 slice.53
  5.6 0.6 slice.54
  7.7 0.6 multiply_bitcast_fusion
  8.6 0.8 fusion.86
  9.4 1.2 copy.122
  10.7 0.7 fusion.37
  11.5 0.7 dynamic-slice_reduce_fusion.1
  12.7 0.8 collective-permute-done
  13.6 3.4 %collective-permute-start.2 = (f32[1,8,64,128]{3,2,1,0:T(8,128)S(1)}, f32[1,8,64,128]{3,2,1,0:T(8,128)S(1)}, u32[]{:S(2)}, u32[]{:S(2)}) collective-permute-start(f32[1,8,64,128]{3,2,1,0:T(8,128)S(1)} %fusion.67), channel_id=1, source_target_pairs={{0,16},{8,24},{16,32},{24,40},{32,48},{40,56},{48,64},{56,72},{64,... | collective-permute-start | bytes 786440 | tf_op jit(solution)/shard_map/ppermute | solution.py:43
  17.0 7.0 %collective-permute-done.2 = f32[1,8,64,128]{3,2,1,0:T(8,128)S(1)} collective-permute-done((f32[1,8,64,128]{3,2,1,0:T(8,128)S(1)}, f32[1,8,64,128]{3,2,1,0:T(8,128)S(1)}, u32[]{:S(2)}, u32[]{:S(2)}) %collective-permute-start.2) | collective-permute-done | bytes 262176 | tf_op jit(solution)/shard_map/ppermute | solution.py:43
  24.2 4.3 %collective-permute-start.4 = (f32[1,8,64,128]{3,2,1,0:T(8,128)S(1)}, f32[1,8,64,128]{3,2,1,0:T(8,128)S(1)}, u32[]{:S(2)}, u32[]{:S(2)}) collective-permute-start(f32[1,8,64,128]{3,2,1,0:T(8,128)S(1)} %multiply_add_fusion.9), channel_id=1, source_target_pairs={{0,32},{8,40},{16,48},{24,56},{32,64},{40,72},{48,80},{56,88},{64,... | collective-permute-start | bytes 786440 | tf_op jit(solution)/shard_map/ppermute | solution.py:43
  28.5 4.0 %collective-permute-start.3 = (f32[1,8]{1,0:T(1,128)S(1)}, f32[1,8]{1,0:T(1,128)S(1)}, u32[]{:S(2)}, u32[]{:S(2)}) collective-permute-start(f32[1,8]{1,0:T(1,128)S(1)} %get-tuple-element.265), channel_id=1, source_target_pairs={{0,16},{8,24},{16,32},{24,40},{32,48},{40,56},{48,64},{56,72},{64,... | collective-permute-start | bytes 104 | tf_op jit(solution)/shard_map/ppermute | solution.py:43
  32.5 3.7 %collective-permute-done.3 = f32[1,8]{1,0:T(1,128)S(1)} collective-permute-done((f32[1,8]{1,0:T(1,128)S(1)}, f32[1,8]{1,0:T(1,128)S(1)}, u32[]{:S(2)}, u32[]{:S(2)}) %collective-permute-start.3) | collective-permute-done | bytes 64 | tf_op jit(solution)/shard_map/ppermute | solution.py:43
  36.3 3.5 %collective-permute-start.6 = (f32[1,8,64,128]{3,2,1,0:T(8,128)S(1)}, f32[1,8,64,128]{3,2,1,0:T(8,128)S(1)}, u32[]{:S(2)}, u32[]{:S(2)}) collective-permute-start(f32[1,8,64,128]{3,2,1,0:T(8,128)S(1)} %multiply_add_fusion.8), channel_id=1, source_target_pairs={{0,64},{8,72},{16,80},{24,88},{32,96},{40,104},{48,112},{56,120},{... | collective-permute-start | bytes 786440 | tf_op jit(solution)/shard_map/ppermute | solution.py:43
  39.8 0.9 fusion.112
  40.7 4.3 %collective-permute-start.5 = (f32[1,8]{1,0:T(1,128)S(1)}, f32[1,8]{1,0:T(1,128)S(1)}, u32[]{:S(2)}, u32[]{:S(2)}) collective-permute-start(f32[1,8]{1,0:T(1,128)S(1)} %mul.705), channel_id=1, source_target_pairs={{0,32},{8,40},{16,48},{24,56},{32,64},{40,72},{48,80},{56,88},{64,... | collective-permute-start | bytes 104 | tf_op jit(solution)/shard_map/ppermute | solution.py:43
  45.0 2.7 %collective-permute-done.5 = f32[1,8]{1,0:T(1,128)S(1)} collective-permute-done((f32[1,8]{1,0:T(1,128)S(1)}, f32[1,8]{1,0:T(1,128)S(1)}, u32[]{:S(2)}, u32[]{:S(2)}) %collective-permute-start.5) | collective-permute-done | bytes 64 | tf_op jit(solution)/shard_map/ppermute | solution.py:43
  47.8 3.9 %collective-permute-start.8 = (f32[1,8,64,128]{3,2,1,0:T(8,128)S(1)}, f32[1,8,64,128]{3,2,1,0:T(8,128)S(1)}, u32[]{:S(2)}, u32[]{:S(2)}) collective-permute-start(f32[1,8,64,128]{3,2,1,0:T(8,128)S(1)} %multiply_add_fusion.7), channel_id=1, source_target_pairs={{0,128},{8,136},{16,144},{24,152},{32,160},{40,168},{48,176},{56,1... | collective-permute-start | bytes 786440 | tf_op jit(solution)/shard_map/ppermute | solution.py:43
  51.6 0.8 fusion.73
  52.5 1.3 collective-permute-start.7
  53.7 1.8 %collective-permute-done.7 = f32[1,8]{1,0:T(1,128)S(1)} collective-permute-done((f32[1,8]{1,0:T(1,128)S(1)}, f32[1,8]{1,0:T(1,128)S(1)}, u32[]{:S(2)}, u32[]{:S(2)}) %collective-permute-start.7) | collective-permute-done | bytes 64 | tf_op jit(solution)/shard_map/ppermute | solution.py:43
  55.6 0.9 fusion.71
  56.5 0.6 fusion.92
  57.1 0.7 mul.729
  58.2 0.8 fusion.70
  59.1 0.6 convolution_bitcast_fusion.1
  59.7 1.0 copy-done.2
  60.7 3.2 %fusion.32 = f32[1,256,1,16,64]{1,4,3,2,0:T(8,128)S(1)} fusion(bf16[256,16,64]{0,2,1:T(8,128)(2,1)S(1)} %bitcast.299, f32[16,256]{1,0:T(8,128)S(1)} %copy-done.26, f32[256,256]{1,0:T(8,128)S(1)} %copy-done.10, f32[16,256]{1,0:T(8,128)S(1)} %copy-done.28, f32[256,256]{1,0:T(8,128)S(1)} %copy-done.8, ...), kind=kOutput, calls=%fused_computation.34 | convolution fusion | flops 811073536 | bytes 3194880 | tf_op jit(solution)/shard_map/jvp()/while/body/eval_jaxpr/ghts,sghp->tghp/dot_general | solution.py:89
  64.0 1.6 multiply_reduce_fusion.2
  65.6 16.0 %all_to_all.5 = f32[8,2,256]{2,1,0:T(2,128)S(1)} all-to-all(f32[8,2,256]{2,1,0:T(2,128)S(1)} %broadcast_in_dim.147), channel_id=1, replica_groups=mesh['ctx'=32,'head'=8] {'head'}, dimensions={0} | all-to-all | bytes 32768 | tf_op jit(solution)/shard_map/all_to_all | solution.py:76
  81.7 3.1 %fusion.49 = (bf16[256,1024]{0,1:T(8,128)(2,1)}, f32[256,1024]{0,1:T(8,128)S(1)}) fusion(bf16[256,1024]{0,1:T(8,128)(2,1)S(1)} %copy.124, bf16[256,1024]{0,1:T(8,128)(2,1)S(1)} %copy.122, f32[1,256,1,16,64]{1,4,3,2,0:T(8,128)} %copy-done.1, f32[1024]{0:T(1024)S(1)} %copy-done.19, f32[256]{0:T(256)S(1)} %multiply_multiply_fusion, ...), kind=kLoop, calls=%fused_computation.53 | loop fusion | flops 5767168 | bytes 5253120 | tf_op jit(solution)/shard_map/convert_element_type | solution.py:223
  84.9 0.6 fusion.51
  86.1 1.0 collective-permute-done.10
  87.3 2.7 %collective-permute-start.12 = (f32[1,8,64,128]{3,2,1,0:T(8,128)S(1)}, f32[1,8,64,128]{3,2,1,0:T(8,128)S(1)}, u32[]{:S(2)}, u32[]{:S(2)}) collective-permute-start(f32[1,8,64,128]{3,2,1,0:T(8,128)S(1)} %fusion.66), channel_id=1, source_target_pairs={{248,232},{240,224},{232,216},{224,208},{216,200},{208,192},{200,1... | collective-permute-start | bytes 786440 | tf_op jit(solution)/shard_map/ppermute | solution.py:43
  90.0 4.2 %collective-permute-start.13 = (f32[1,8]{1,0:T(1,128)S(1)}, f32[1,8]{1,0:T(1,128)S(1)}, u32[]{:S(2)}, u32[]{:S(2)}) collective-permute-start(f32[1,8]{1,0:T(1,128)S(1)} %get-tuple-element.260), channel_id=1, source_target_pairs={{248,232},{240,224},{232,216},{224,208},{216,200},{208,192},{200,1... | collective-permute-start | bytes 104 | tf_op jit(solution)/shard_map/ppermute | solution.py:43
  94.3 7.9 %collective-permute-done.13 = f32[1,8]{1,0:T(1,128)S(1)} collective-permute-done((f32[1,8]{1,0:T(1,128)S(1)}, f32[1,8]{1,0:T(1,128)S(1)}, u32[]{:S(2)}, u32[]{:S(2)}) %collective-permute-start.13) | collective-permute-done | bytes 64 | tf_op jit(solution)/shard_map/ppermute | solution.py:43
  102.2 1.9 %collective-permute-start.15 = (f32[1,8]{1,0:T(1,128)S(1)}, f32[1,8]{1,0:T(1,128)S(1)}, u32[]{:S(2)}, u32[]{:S(2)}) collective-permute-start(f32[1,8]{1,0:T(1,128)S(1)} %mul.758), channel_id=1, source_target_pairs={{248,216},{240,208},{232,200},{224,192},{216,184},{208,176},{200,1... | collective-permute-start | bytes 104 | tf_op jit(solution)/shard_map/ppermute | solution.py:43
  104.1 5.9 %collective-permute-done.15 = f32[1,8]{1,0:T(1,128)S(1)} collective-permute-done((f32[1,8]{1,0:T(1,128)S(1)}, f32[1,8]{1,0:T(1,128)S(1)}, u32[]{:S(2)}, u32[]{:S(2)}) %collective-permute-start.15) | collective-permute-done | bytes 64 | tf_op jit(solution)/shard_map/ppermute | solution.py:43
  110.0 1.3 collective-permute-start.17
  111.3 4.2 %collective-permute-done.17 = f32[1,8]{1,0:T(1,128)S(1)} collective-permute-done((f32[1,8]{1,0:T(1,128)S(1)}, f32[1,8]{1,0:T(1,128)S(1)}, u32[]{:S(2)}, u32[]{:S(2)}) %collective-permute-start.17) | collective-permute-done | bytes 64 | tf_op jit(solution)/shard_map/ppermute | solution.py:43
  115.6 1.9 %collective-permute-start.14 = (f32[1,8,64,128]{3,2,1,0:T(8,128)S(1)}, f32[1,8,64,128]{3,2,1,0:T(8,128)S(1)}, u32[]{:S(2)}, u32[]{:S(2)}) collective-permute-start(f32[1,8,64,128]{3,2,1,0:T(8,128)S(1)} %multiply_add_fusion.4), channel_id=1, source_target_pairs={{248,216},{240,208},{232,200},{224,192},{216,184},{208,176},{200,1... | collective-permute-start | bytes 786440 | tf_op jit(solution)/shard_map/ppermute | solution.py:43
  117.5 7.6 %fusion.65 = (f32[16,256]{1,0:T(8,128)}, f32[16,256]{1,0:T(8,128)}, f32[16,256]{1,0:T(8,128)}, f32[256,256]{1,0:T(8,128)S(1)}) fusion(f32[16,256]{1,0:T(8,128)} %fusion.92, f32[256,256]{1,0:T(8,128)} %fusion.73, f32[16,256]{1,0:T(8,128)} %get-tuple-element.240, f32[256,256]{1,0:T(8,128)} %fusion.112, f32[16,64,256]{2,1,0:T(8,128)S(1)} %bitcast.294, ...), kind=kOutput, calls=%fused_computation.82 | convolution fusion | flops 825151488 | bytes 2441216 | tf_op jit(solution)/shard_map/transpose(jvp())/while/body/eval_jaxpr/ghts,sghp->tghp/dot_general | solution.py:89
  125.4 0.9 collective-permute-done.14
  126.4 1.4 collective-permute-start.16
  127.8 2.5 %fusion.40 = f32[1,256,1,128]{3,1,2,0:T(8,128)} fusion(f32[256,128]{1,0:T(8,128)S(1)} %fusion.113, f32[1,256,1,16,64]{1,4,3,2,0:T(8,128)S(1)} %bitcast.295, f32[256,16]{0,1:T(8,128)S(1)} %copy-done.16, f32[8,64,128]{2,1,0:T(8,128)S(1)} %bitcast.303, f32[8,64,128]{2,1,0:T(8,128)S(1)} %bitcast.307, pred[]{:T(512)S(6)} %eq.79), kind=kOutput, calls=%fused_computation.44 | convolution fusion | flops 403341312 | bytes 1851393 | tf_op jit(solution)/shard_map/transpose(jvp(kqgn,kghpn->kqghp))/dot_general | solution.py:138
  130.3 0.7 multiply_reduce_fusion
  131.1 3.7 %collective-permute-done.16 = f32[1,8,64,128]{3,2,1,0:T(8,128)S(1)} collective-permute-done((f32[1,8,64,128]{3,2,1,0:T(8,128)S(1)}, f32[1,8,64,128]{3,2,1,0:T(8,128)S(1)}, u32[]{:S(2)}, u32[]{:S(2)}) %collective-permute-start.16) | collective-permute-done | bytes 262176 | tf_op jit(solution)/shard_map/ppermute | solution.py:43
  134.9 1.3 collective-permute-start.18
  136.2 4.7 %fusion.26 = f32[1,256,1,16,64]{1,4,3,2,0:T(8,128)} fusion(f32[16,64,256]{2,1,0:T(8,128)S(1)} %bitcast.297, f32[16,256]{1,0:T(8,128)S(1)} %copy-done.27, f32[256,256]{1,0:T(8,128)S(1)} %copy-done.11, f32[16,256]{1,0:T(8,128)S(1)} %copy-done.29, f32[256,256]{1,0:T(8,128)S(1)} %copy-done.9), kind=kOutput, calls=%fused_computation.30 | convolution fusion | flops 810549248 | bytes 2654208 | tf_op jit(solution)/shard_map/transpose(jvp())/while/body/eval_jaxpr/ghts,sghp->tghp/dot_general | solution.py:89
  141.0 3.7 %collective-permute-done.18 = f32[1,8,64,128]{3,2,1,0:T(8,128)S(1)} collective-permute-done((f32[1,8,64,128]{3,2,1,0:T(8,128)S(1)}, f32[1,8,64,128]{3,2,1,0:T(8,128)S(1)}, u32[]{:S(2)}, u32[]{:S(2)}) %collective-permute-start.18) | collective-permute-done | bytes 262176 | tf_op jit(solution)/shard_map/ppermute | solution.py:43
  144.6 0.9 fusion.69
  145.5 1.0 convolution_bitcast_fusion.2
  146.6 2.0 %copy.139 = bf16[256,1024]{1,0:T(8,128)(2,1)} copy(bf16[256,1024]{0,1:T(8,128)(2,1)} %get-tuple-element.237) | data formatting | bytes 1048576
  148.7 1.3 multiply_reduce_fusion.3
  150.2 2.0 %bitcast_add_fusion.1 = (f32[1,256,1,16,64]{1,4,3,2,0:T(8,128)S(1)}, f32[256,16,64]{0,2,1:T(8,128)S(1)}) fusion(f32[1,256,1,16,64]{1,4,3,2,0:T(8,128)} %fusion.26, f32[256,16]{0,1:T(8,128)S(1)} %copy-done.13, bf16[256,128]{1,0:T(8,128)(2,1)S(1)} %copy-done, f32[8,64,128]{2,1,0:T(8,128)S(1)} %bitcast.304, f32[8,64,128]{2,1,0:T(8,128)} %bitcast.70, pred[]{:T(512)S(6)} %eq.86), kind=kOutput, calls=%fused_computation.59 | convolution fusion | flops 403570688 | bytes 3751937 | tf_op jit(solution)/shard_map/transpose(jvp(kqgh,kqghp,kqgn->kghpn))/dot_general | solution.py:103
  153.4 2.5 %reduce-window.36 = f32[1,16,1,2,128]{4,1,2,3,0:T(8,128)S(1)} reduce-window(f32[1,16,1,2,128]{4,1,2,3,0:T(8,128)S(1)} %copy_bitcast_fusion, f32[]{:T(128)} %constant.175.clone.1), window={size=1x1x1x1x128 pad=0_0x0_0x0_0x0_0x0_127}, to_apply=%region_16.17 | reduce-window | flops 520192 | bytes 32772 | tf_op jit(solution)/shard_map/reduce-window.6
  156.0 2.5 %reduce-window.34 = f32[1,16,1,2,128]{4,1,2,3,0:T(8,128)S(1)} reduce-window(f32[1,16,1,2,128]{4,1,2,3,0:T(8,128)S(1)} %bitcast.313, f32[]{:T(128)} %constant.175.clone.1), window={size=1x1x1x1x128 pad=0_0x0_0x0_0x0_0x0_127}, to_apply=%region_11.12 | reduce-window | flops 520192 | bytes 32772 | tf_op jit(solution)/shard_map/reduce-window.4
  158.6 3.5 %fusion.42 = f32[256,128]{1,0:T(8,128)} fusion(f32[1,256,1,128]{3,1,2,0:T(8,128)S(1)} %copy-done.17, bf16[256,16,64]{0,2,1:T(8,128)(2,1)S(1)} %bitcast.301, f32[256,16]{0,1:T(8,128)S(1)} %copy-done.13, f32[8,64,128]{2,1,0:T(8,128)S(1)} %bitcast.305, f32[8,64,128]{2,1,0:T(8,128)} %bitcast.70, pred[]{:T(512)S(6)} %eq.86), kind=kOutput, calls=%fused_computation.46 | convolution fusion | flops 403603456 | bytes 1327105 | tf_op jit(solution)/shard_map/transpose(jvp(kqgh,kqghp,kqgn->kghpn))/dot_general | solution.py:103
  162.3 1.0 copy.138
  163.9 0.7 bitcast_multiply_fusion
  (173 shorter events, 6.3 us)
Async XLA Ops:
  0.6 10.0 %copy-start = (bf16[256,128]{1,0:T(8,128)(2,1)S(1)}, bf16[256,128]{1,0:T(8,128)(2,1)}, u32[]{:S(2)}) copy-start(bf16[256,128]{1,0:T(8,128)(2,1)} %param.14) | copy-start | bytes 196612
  1.3 1.4 copy-start.38
  5.6 5.8 %copy-start.33 = (f32[256]{0:T(256)}, f32[256]{0:T(256)S(1)}, u32[]{:S(2)}) copy-start(f32[256]{0:T(256)S(1)} %get-tuple-element.233) | copy-start | bytes 3076
  8.5 2.8 %copy-start.36 = (f32[16]{0:T(128)}, f32[16]{0:T(128)S(1)}, u32[]{:S(2)}) copy-start(f32[16]{0:T(128)S(1)} %get-tuple-element.254) | copy-start | bytes 196
  8.6 2.8 %copy-start.24 = (f32[256]{0:T(256)}, f32[256]{0:T(256)S(1)}, u32[]{:S(2)}) copy-start(f32[256]{0:T(256)S(1)} %compare_convert_fusion.1) | copy-start | bytes 3076
  9.4 2.0 %copy-start.12 = (f32[256,16]{0,1:T(8,128)}, f32[256,16]{0,1:T(8,128)S(1)}, u32[]{:S(2)}) copy-start(f32[256,16]{0,1:T(8,128)S(1)} %fusion.86) | copy-start | bytes 49156
  11.4 2.1 %collective-permute-start.1 = (f32[1,8,64,128]{3,2,1,0:T(8,128)S(1)}, f32[1,8,64,128]{3,2,1,0:T(8,128)S(1)}, u32[]{:S(2)}, u32[]{:S(2)}) collective-permute-start(f32[1,8,64,128]{3,2,1,0:T(8,128)S(1)} %dynamic-slice_bitcast_fusion.1), channel_id=1, source_target_pairs={{0,8},{8,0},{16,24},{24,16},{32,40},{40,32},{48,56},{56,48},{64,72... | collective-permute-start | bytes 786440 | tf_op jit(solution)/shard_map/ppermute | solution.py:43
  12.2 1.3 collective-permute-start
  13.5 42.1 %copy-start.42 = (f32[8]{0:T(128)}, f32[8]{0:T(128)S(1)}, u32[]{:S(2)}) copy-start(f32[8]{0:T(128)S(1)} %get-tuple-element.266) | copy-start | bytes 100
  13.5 26.3 %copy-start.4 = (bf16[256,128]{1,0:T(8,128)(2,1)S(1)}, bf16[256,128]{1,0:T(8,128)(2,1)}, u32[]{:S(2)}) copy-start(bf16[256,128]{1,0:T(8,128)(2,1)} %param.15) | copy-start | bytes 196612
  13.6 10.4 %collective-permute-start.2 = (f32[1,8,64,128]{3,2,1,0:T(8,128)S(1)}, f32[1,8,64,128]{3,2,1,0:T(8,128)S(1)}, u32[]{:S(2)}, u32[]{:S(2)}) collective-permute-start(f32[1,8,64,128]{3,2,1,0:T(8,128)S(1)} %fusion.67), channel_id=1, source_target_pairs={{0,16},{8,24},{16,32},{24,40},{32,48},{40,56},{48,64},{56,72},{64,... | collective-permute-start | bytes 786440 | tf_op jit(solution)/shard_map/ppermute | solution.py:43
  24.2 12.0 %collective-permute-start.4 = (f32[1,8,64,128]{3,2,1,0:T(8,128)S(1)}, f32[1,8,64,128]{3,2,1,0:T(8,128)S(1)}, u32[]{:S(2)}, u32[]{:S(2)}) collective-permute-start(f32[1,8,64,128]{3,2,1,0:T(8,128)S(1)} %multiply_add_fusion.9), channel_id=1, source_target_pairs={{0,32},{8,40},{16,48},{24,56},{32,64},{40,72},{48,80},{56,88},{64,... | collective-permute-start | bytes 786440 | tf_op jit(solution)/shard_map/ppermute | solution.py:43
  28.5 7.7 %collective-permute-start.3 = (f32[1,8]{1,0:T(1,128)S(1)}, f32[1,8]{1,0:T(1,128)S(1)}, u32[]{:S(2)}, u32[]{:S(2)}) collective-permute-start(f32[1,8]{1,0:T(1,128)S(1)} %get-tuple-element.265), channel_id=1, source_target_pairs={{0,16},{8,24},{16,32},{24,40},{32,48},{40,56},{48,64},{56,72},{64,... | collective-permute-start | bytes 104 | tf_op jit(solution)/shard_map/ppermute | solution.py:43
  36.3 11.4 %collective-permute-start.6 = (f32[1,8,64,128]{3,2,1,0:T(8,128)S(1)}, f32[1,8,64,128]{3,2,1,0:T(8,128)S(1)}, u32[]{:S(2)}, u32[]{:S(2)}) collective-permute-start(f32[1,8,64,128]{3,2,1,0:T(8,128)S(1)} %multiply_add_fusion.8), channel_id=1, source_target_pairs={{0,64},{8,72},{16,80},{24,88},{32,96},{40,104},{48,112},{56,120},{... | collective-permute-start | bytes 786440 | tf_op jit(solution)/shard_map/ppermute | solution.py:43
  40.7 7.0 %collective-permute-start.5 = (f32[1,8]{1,0:T(1,128)S(1)}, f32[1,8]{1,0:T(1,128)S(1)}, u32[]{:S(2)}, u32[]{:S(2)}) collective-permute-start(f32[1,8]{1,0:T(1,128)S(1)} %mul.705), channel_id=1, source_target_pairs={{0,32},{8,40},{16,48},{24,56},{32,64},{40,72},{48,80},{56,88},{64,... | collective-permute-start | bytes 104 | tf_op jit(solution)/shard_map/ppermute | solution.py:43
  47.8 7.8 %collective-permute-start.8 = (f32[1,8,64,128]{3,2,1,0:T(8,128)S(1)}, f32[1,8,64,128]{3,2,1,0:T(8,128)S(1)}, u32[]{:S(2)}, u32[]{:S(2)}) collective-permute-start(f32[1,8,64,128]{3,2,1,0:T(8,128)S(1)} %multiply_add_fusion.7), channel_id=1, source_target_pairs={{0,128},{8,136},{16,144},{24,152},{32,160},{40,168},{48,176},{56,1... | collective-permute-start | bytes 786440 | tf_op jit(solution)/shard_map/ppermute | solution.py:43
  52.5 3.1 %collective-permute-start.7 = (f32[1,8]{1,0:T(1,128)S(1)}, f32[1,8]{1,0:T(1,128)S(1)}, u32[]{:S(2)}, u32[]{:S(2)}) collective-permute-start(f32[1,8]{1,0:T(1,128)S(1)} %mul.713), channel_id=1, source_target_pairs={{0,64},{8,72},{16,80},{24,88},{32,96},{40,104},{48,112},{56,120},{... | collective-permute-start | bytes 104 | tf_op jit(solution)/shard_map/ppermute | solution.py:43
  55.6 1.5 copy-start.44
  55.6 2.2 %copy-start.5 = (bf16[256,1024]{1,0:T(8,128)(2,1)S(1)}, bf16[256,1024]{1,0:T(8,128)(2,1)}, u32[]{:S(2)}) copy-start(bf16[256,1024]{1,0:T(8,128)(2,1)} %param.12) | copy-start | bytes 1572868
  56.5 1.6 copy-start.6
  56.5 2.6 %collective-permute-start.9 = (f32[1,8,64,128]{3,2,1,0:T(8,128)}, f32[1,8,64,128]{3,2,1,0:T(8,128)S(1)}, u32[]{:S(2)}, u32[]{:S(2)}) collective-permute-start(f32[1,8,64,128]{3,2,1,0:T(8,128)} %get-tuple-element.235), channel_id=1, source_target_pairs={{0,8},{8,0},{16,24},{24,16},{32,40},{40,32},{48,56},{56,48},{64,72... | collective-permute-start | bytes 786440 | tf_op jit(solution)/shard_map/ppermute | solution.py:43
  59.0 1.7 %copy-start.8 = (f32[256,256]{1,0:T(8,128)S(1)}, f32[256,256]{1,0:T(8,128)}, u32[]{:S(2)}) copy-start(f32[256,256]{1,0:T(8,128)} %fusion.112) | copy-start | bytes 786436
  59.0 1.6 %copy-start.10 = (f32[256,256]{1,0:T(8,128)S(1)}, f32[256,256]{1,0:T(8,128)}, u32[]{:S(2)}) copy-start(f32[256,256]{1,0:T(8,128)} %fusion.73) | copy-start | bytes 786436
  59.0 1.6 copy-start.14
  59.1 1.6 copy-start.26
  59.1 1.6 copy-start.28
  59.7 1.0 copy-start.2
  60.7 3.3 %copy-start.18 = (f32[1024]{0:T(1024)S(1)}, f32[1024]{0:T(1024)}, u32[]{:S(2)}) copy-start(f32[1024]{0:T(1024)} %mul.729) | copy-start | bytes 12292
  60.7 3.3 %copy-start.22 = (f32[1024]{0:T(1024)S(1)}, f32[1024]{0:T(1024)}, u32[]{:S(2)}) copy-start(f32[1024]{0:T(1024)} %param.19) | copy-start | bytes 12292
  64.0 1.6 copy-start.1
  64.0 17.7 %copy-start.19 = (f32[1024]{0:T(1024)S(1)}, f32[1024]{0:T(1024)}, u32[]{:S(2)}) copy-start(f32[1024]{0:T(1024)} %mul.729) | copy-start | bytes 12292
  64.0 17.7 %copy-start.23 = (f32[1024]{0:T(1024)S(1)}, f32[1024]{0:T(1024)}, u32[]{:S(2)}) copy-start(f32[1024]{0:T(1024)} %param.19) | copy-start | bytes 12292
  81.7 3.1 %copy-start.15 = (f32[256,16]{0,1:T(8,128)S(1)}, f32[256,16]{0,1:T(8,128)}, u32[]{:S(2)}) copy-start(f32[256,16]{0,1:T(8,128)} %get-tuple-element.221) | copy-start | bytes 49156
  84.9 0.8 copy-start.45
  84.9 2.3 %copy-start.43 = (f32[8]{0:T(128)S(1)}, f32[8]{0:T(128)}, u32[]{:S(2)}) copy-start(f32[8]{0:T(128)} %get-tuple-element.212) | copy-start | bytes 100
  85.5 1.6 collective-permute-start.11
  85.7 1.5 collective-permute-start.10
  87.2 57.5 %copy-start.40 = (f32[8]{0:T(128)}, f32[8]{0:T(128)S(1)}, u32[]{:S(2)}) copy-start(f32[8]{0:T(128)S(1)} %get-tuple-element.261) | copy-start | bytes 100
  87.3 28.2 %collective-permute-start.12 = (f32[1,8,64,128]{3,2,1,0:T(8,128)S(1)}, f32[1,8,64,128]{3,2,1,0:T(8,128)S(1)}, u32[]{:S(2)}, u32[]{:S(2)}) collective-permute-start(f32[1,8,64,128]{3,2,1,0:T(8,128)S(1)} %fusion.66), channel_id=1, source_target_pairs={{248,232},{240,224},{232,216},{224,208},{216,200},{208,192},{200,1... | collective-permute-start | bytes 786440 | tf_op jit(solution)/shard_map/ppermute | solution.py:43
  90.0 12.1 %collective-permute-start.13 = (f32[1,8]{1,0:T(1,128)S(1)}, f32[1,8]{1,0:T(1,128)S(1)}, u32[]{:S(2)}, u32[]{:S(2)}) collective-permute-start(f32[1,8]{1,0:T(1,128)S(1)} %get-tuple-element.260), channel_id=1, source_target_pairs={{248,232},{240,224},{232,216},{224,208},{216,200},{208,192},{200,1... | collective-permute-start | bytes 104 | tf_op jit(solution)/shard_map/ppermute | solution.py:43
  102.2 7.9 %collective-permute-start.15 = (f32[1,8]{1,0:T(1,128)S(1)}, f32[1,8]{1,0:T(1,128)S(1)}, u32[]{:S(2)}, u32[]{:S(2)}) collective-permute-start(f32[1,8]{1,0:T(1,128)S(1)} %mul.758), channel_id=1, source_target_pairs={{248,216},{240,208},{232,200},{224,192},{216,184},{208,176},{200,1... | collective-permute-start | bytes 104 | tf_op jit(solution)/shard_map/ppermute | solution.py:43
  110.0 5.5 %collective-permute-start.17 = (f32[1,8]{1,0:T(1,128)S(1)}, f32[1,8]{1,0:T(1,128)S(1)}, u32[]{:S(2)}, u32[]{:S(2)}) collective-permute-start(f32[1,8]{1,0:T(1,128)S(1)} %mul.766), channel_id=1, source_target_pairs={{248,184},{240,176},{232,168},{224,160},{216,152},{208,144},{200,1... | collective-permute-start | bytes 104 | tf_op jit(solution)/shard_map/ppermute | solution.py:43
  115.6 10.7 %collective-permute-start.14 = (f32[1,8,64,128]{3,2,1,0:T(8,128)S(1)}, f32[1,8,64,128]{3,2,1,0:T(8,128)S(1)}, u32[]{:S(2)}, u32[]{:S(2)}) collective-permute-start(f32[1,8,64,128]{3,2,1,0:T(8,128)S(1)} %multiply_add_fusion.4), channel_id=1, source_target_pairs={{248,216},{240,208},{232,200},{224,192},{216,184},{208,176},{200,1... | collective-permute-start | bytes 786440 | tf_op jit(solution)/shard_map/ppermute | solution.py:43
  125.1 2.7 %copy-start.16 = (f32[256,16]{0,1:T(8,128)S(1)}, f32[256,16]{0,1:T(8,128)}, u32[]{:S(2)}) copy-start(f32[256,16]{0,1:T(8,128)} %get-tuple-element.221) | copy-start | bytes 49156
  126.4 3.9 %copy-start.3 = (f32[1,256,1,16,64]{1,4,3,2,0:T(8,128)S(1)}, f32[1,256,1,16,64]{1,4,3,2,0:T(8,128)}, u32[]{:S(2)}) copy-start(f32[1,256,1,16,64]{1,4,3,2,0:T(8,128)} %copy-done.2) | copy-start | bytes 3145732
  126.4 8.4 %collective-permute-start.16 = (f32[1,8,64,128]{3,2,1,0:T(8,128)S(1)}, f32[1,8,64,128]{3,2,1,0:T(8,128)S(1)}, u32[]{:S(2)}, u32[]{:S(2)}) collective-permute-start(f32[1,8,64,128]{3,2,1,0:T(8,128)S(1)} %multiply_add_fusion.3), channel_id=1, source_target_pairs={{248,184},{240,176},{232,168},{224,160},{216,152},{208,144},{200,1... | collective-permute-start | bytes 786440 | tf_op jit(solution)/shard_map/ppermute | solution.py:43
  130.3 5.9 %copy-start.9 = (f32[256,256]{1,0:T(8,128)S(1)}, f32[256,256]{1,0:T(8,128)}, u32[]{:S(2)}) copy-start(f32[256,256]{1,0:T(8,128)} %fusion.112) | copy-start | bytes 786436
  130.3 5.9 %copy-start.11 = (f32[256,256]{1,0:T(8,128)S(1)}, f32[256,256]{1,0:T(8,128)}, u32[]{:S(2)}) copy-start(f32[256,256]{1,0:T(8,128)} %fusion.73) | copy-start | bytes 786436
  130.3 5.9 %copy-start.27 = (f32[16,256]{1,0:T(8,128)S(1)}, f32[16,256]{1,0:T(8,128)}, u32[]{:S(2)}) copy-start(f32[16,256]{1,0:T(8,128)} %get-tuple-element.240) | copy-start | bytes 49156
  130.3 5.9 %copy-start.29 = (f32[16,256]{1,0:T(8,128)S(1)}, f32[16,256]{1,0:T(8,128)}, u32[]{:S(2)}) copy-start(f32[16,256]{1,0:T(8,128)} %fusion.92) | copy-start | bytes 49156
  134.9 9.8 %collective-permute-start.18 = (f32[1,8,64,128]{3,2,1,0:T(8,128)S(1)}, f32[1,8,64,128]{3,2,1,0:T(8,128)S(1)}, u32[]{:S(2)}, u32[]{:S(2)}) collective-permute-start(f32[1,8,64,128]{3,2,1,0:T(8,128)S(1)} %multiply_add_fusion.2), channel_id=1, source_target_pairs={{248,120},{240,112},{232,104},{224,96},{216,88},{208,80},{200,72},... | collective-permute-start | bytes 786440 | tf_op jit(solution)/shard_map/ppermute | solution.py:43
  145.5 3.2 %collective-permute-start.19 = (f32[1,8,64,128]{3,2,1,0:T(8,128)}, f32[1,8,64,128]{3,2,1,0:T(8,128)}, u32[]{:S(2)}, u32[]{:S(2)}) collective-permute-start(f32[1,8,64,128]{3,2,1,0:T(8,128)} %get-tuple-element.218), channel_id=1, source_target_pairs={{248,240},{240,248},{232,224},{224,232},{216,208},{208,216},{200,1... | collective-permute-start | bytes 786440 | tf_op jit(solution)/shard_map/ppermute | solution.py:43
  146.6 2.0 %copy-start.41 = (f32[8]{0:T(128)S(1)}, f32[8]{0:T(128)}, u32[]{:S(2)}) copy-start(f32[8]{0:T(128)} %copy-done.40) | copy-start | bytes 100
  148.6 1.6 copy-start.13
  152.2 0.7 copy-start.7
  152.2 0.7 copy-start.21
  152.2 0.7 copy-start.25
  152.2 0.7 copy-start.30
  152.2 0.7 copy-start.31
  152.3 0.7 copy-start.34
  152.3 6.3 %copy-start.17 = (f32[1,256,1,128]{3,1,2,0:T(8,128)S(1)}, f32[1,256,1,128]{3,1,2,0:T(8,128)}, u32[]{:S(2)}) copy-start(f32[1,256,1,128]{3,1,2,0:T(8,128)} %convolution_bitcast_fusion.2) | copy-start | bytes 393220
  153.2 8.9 %copy-start.20 = (f32[1024]{0:T(1024)S(1)}, f32[1024]{0:T(1024)}, u32[]{:S(2)}) copy-start(f32[1024]{0:T(1024)} %mul.729) | copy-start | bytes 12292
  162.3 1.5 copy-start.32
  162.3 1.5 copy-start.39
  (2 other events, 1.4 us)

commit v9 on v8

--- a/solution.py
+++ b/solution.py
@@ -90,7 +90,12 @@
 
 
 def block_decays(dt_spans, segment, decay_rate):
-    log_cum = jnp.cumsum(dt_spans * decay_rate, axis=1)
+    length = dt_spans.shape[1]
+    places = jnp.arange(length, dtype=jnp.int32)
+    lower = (places[:, None] >= places[None, :]).astype(jnp.float32)
+    log_cum = jnp.einsum(
+        "qs,ksgh->kqgh", lower, dt_spans * decay_rate, precision=HIGHEST_PRECISION
+    )
     closing = segment[:, -1]
     through = jnp.exp(log_cum[:, -1]) * (closing == 0).astype(jnp.float32)[:, None, None]
     return (log_cum, closing, through)
@@ -140,6 +145,7 @@
     )
     mix_block = lambda pieces: span_mix(*pieces)
     inner_part = lax.map(mix_block, (x_spans, dt_spans, b_spans, c_spans, log_cum, segment))
+    inner_part = lax.optimization_barrier(inner_part)
     return inner_part + carried
 
 

time: 167 us -> 160 us (0.958)
  other arithmetic: 23.8 us -> 16.2 us
  waiting for transfers between devices: 43.3 us -> 45.3 us
    another operation x10 -> x2, other arithmetic: 7.72 us -> 1.16 us
    unnamed x97 -> x81, local copies, waits for them, and re-layouts: 6.4 us -> 2.86 us
    dot_general x0 -> x3, matrix products: none -> 2 us  [block_decays(): jnp.einsum('qs,ksgh->kqgh', lower, dt_spans * decay_rate, precision=HIGHE...]
    ppermute x20, waiting for transfers between devices: 43.3 us -> 45.3 us  [move(): return lax.ppermute(tree, axis, [(device(a), device(b)) for a, b in pairs])]
    reshape x0 -> x2, local copies, waits for them, and re-layouts: none -> 1.89 us  [the longest x1 1.56 us: layer_body(): (first_grads[0] + second_grads[0]).reshape(tokens_here, heads_here * HEAD...]
where the time goes in v9:
time: 160 us; the launch traced here: 159 us
  waiting for transfers between devices  45.3 us (28%)
  starting transfers between devices  40.7 us (25%)
  matrix products  28.7 us (18%)
  other arithmetic  16.2 us (10%)
  blocking collectives  16 us (10%)
  local copies, waits for them, and re-layouts  8.83 us (6%)
  between operations  2.81 us (2%)
    ppermute x20, waiting for transfers between devices, move(): return lax.ppermute(tree, axis, [(device(a), device(b)) for a, b in pairs])  45.3 us
    ppermute x20, starting transfers between devices, move(): return lax.ppermute(tree, axis, [(device(a), device(b)) for a, b in pairs])  40.7 us
    all_to_all x1, blocking collectives, head_sum(): return jnp.sum(lax.all_to_all(spread, axis, 0, 0), axis=0)  16 us
    dot_general x3, matrix products, span_mix(): jnp.einsum('ghts,sghp->tghp', weights, x_span, precision=HIGHEST_PRECISION)  14.6 us
    dot_general x3, matrix products, local_states(): jnp.einsum('kqgh,kqghp,kqgn->kghpn', tail_decay * dt_spans, x_spans, b_sp...  5.92 us
    dot_general x3, matrix products, output_part(): jnp.einsum('kqgn,kghpn->kqghp', c_spans, full_start, precision=HIGHEST_PR...  4.69 us
  transfers between devices with their start and end apart: 20, of which 12 were waited for; matrix products, arithmetic and copies ran while one was open for 15% of the time, Pallas kernels for 0%

profile of v9, /device:TPU:6, one launch (start us, length us, event | category | flops | bytes accessed | tf_op | source)
XLA Modules:
  0.0 158.5 jit_solution(5672921231489335094)
XLA Ops:
  0.7 0.7 exponential_negate_fusion
  1.4 1.0 reduce-window.6
  2.6 0.6 slice.28
  3.5 0.6 slice.29
  5.4 0.9 fusion.81
  6.6 1.2 copy.37
  8.0 0.7 fusion.34
  8.9 0.7 dynamic-slice_reduce_fusion.1
  9.5 0.5 collective-permute-start
  10.0 0.8 collective-permute-done
  10.9 3.4 %collective-permute-start.2 = (f32[1,8,64,128]{3,2,1,0:T(8,128)S(1)}, f32[1,8,64,128]{3,2,1,0:T(8,128)S(1)}, u32[]{:S(2)}, u32[]{:S(2)}) collective-permute-start(f32[1,8,64,128]{3,2,1,0:T(8,128)S(1)} %fusion.75), channel_id=1, source_target_pairs={{0,16},{8,24},{16,32},{24,40},{32,48},{40,56},{48,64},{56,72},{64,... | collective-permute-start | bytes 786440 | tf_op jit(solution)/shard_map/ppermute | solution.py:43
  14.3 7.0 %collective-permute-done.2 = f32[1,8,64,128]{3,2,1,0:T(8,128)S(1)} collective-permute-done((f32[1,8,64,128]{3,2,1,0:T(8,128)S(1)}, f32[1,8,64,128]{3,2,1,0:T(8,128)S(1)}, u32[]{:S(2)}, u32[]{:S(2)}) %collective-permute-start.2) | collective-permute-done | bytes 262176 | tf_op jit(solution)/shard_map/ppermute | solution.py:43
  21.5 4.3 %collective-permute-start.4 = (f32[1,8,64,128]{3,2,1,0:T(8,128)S(1)}, f32[1,8,64,128]{3,2,1,0:T(8,128)S(1)}, u32[]{:S(2)}, u32[]{:S(2)}) collective-permute-start(f32[1,8,64,128]{3,2,1,0:T(8,128)S(1)} %multiply_add_fusion.11), channel_id=1, source_target_pairs={{0,32},{8,40},{16,48},{24,56},{32,64},{40,72},{48,80},{56,88},{64,... | collective-permute-start | bytes 786440 | tf_op jit(solution)/shard_map/ppermute | solution.py:43
  25.8 4.0 %collective-permute-start.3 = (f32[1,8]{1,0:T(1,128)S(1)}, f32[1,8]{1,0:T(1,128)S(1)}, u32[]{:S(2)}, u32[]{:S(2)}) collective-permute-start(f32[1,8]{1,0:T(1,128)S(1)} %get-tuple-element.204), channel_id=1, source_target_pairs={{0,16},{8,24},{16,32},{24,40},{32,48},{40,56},{48,64},{56,72},{64,... | collective-permute-start | bytes 104 | tf_op jit(solution)/shard_map/ppermute | solution.py:43
  29.8 3.7 %collective-permute-done.3 = f32[1,8]{1,0:T(1,128)S(1)} collective-permute-done((f32[1,8]{1,0:T(1,128)S(1)}, f32[1,8]{1,0:T(1,128)S(1)}, u32[]{:S(2)}, u32[]{:S(2)}) %collective-permute-start.3) | collective-permute-done | bytes 64 | tf_op jit(solution)/shard_map/ppermute | solution.py:43
  33.6 3.5 %collective-permute-start.6 = (f32[1,8,64,128]{3,2,1,0:T(8,128)S(1)}, f32[1,8,64,128]{3,2,1,0:T(8,128)S(1)}, u32[]{:S(2)}, u32[]{:S(2)}) collective-permute-start(f32[1,8,64,128]{3,2,1,0:T(8,128)S(1)} %multiply_add_fusion.10), channel_id=1, source_target_pairs={{0,64},{8,72},{16,80},{24,88},{32,96},{40,104},{48,112},{56,120},{... | collective-permute-start | bytes 786440 | tf_op jit(solution)/shard_map/ppermute | solution.py:43
  37.4 4.3 %collective-permute-start.5 = (f32[1,8]{1,0:T(1,128)S(1)}, f32[1,8]{1,0:T(1,128)S(1)}, u32[]{:S(2)}, u32[]{:S(2)}) collective-permute-start(f32[1,8]{1,0:T(1,128)S(1)} %mul.702), channel_id=1, source_target_pairs={{0,32},{8,40},{16,48},{24,56},{32,64},{40,72},{48,80},{56,88},{64,... | collective-permute-start | bytes 104 | tf_op jit(solution)/shard_map/ppermute | solution.py:43
  41.7 2.7 %collective-permute-done.5 = f32[1,8]{1,0:T(1,128)S(1)} collective-permute-done((f32[1,8]{1,0:T(1,128)S(1)}, f32[1,8]{1,0:T(1,128)S(1)}, u32[]{:S(2)}, u32[]{:S(2)}) %collective-permute-start.5) | collective-permute-done | bytes 64 | tf_op jit(solution)/shard_map/ppermute | solution.py:43
  44.5 3.9 %collective-permute-start.8 = (f32[1,8,64,128]{3,2,1,0:T(8,128)S(1)}, f32[1,8,64,128]{3,2,1,0:T(8,128)S(1)}, u32[]{:S(2)}, u32[]{:S(2)}) collective-permute-start(f32[1,8,64,128]{3,2,1,0:T(8,128)S(1)} %multiply_add_fusion.9), channel_id=1, source_target_pairs={{0,128},{8,136},{16,144},{24,152},{32,160},{40,168},{48,176},{56,1... | collective-permute-start | bytes 786440 | tf_op jit(solution)/shard_map/ppermute | solution.py:43
  48.5 1.3 collective-permute-start.7
  49.8 2.5 %collective-permute-done.7 = f32[1,8]{1,0:T(1,128)S(1)} collective-permute-done((f32[1,8]{1,0:T(1,128)S(1)}, f32[1,8]{1,0:T(1,128)S(1)}, u32[]{:S(2)}, u32[]{:S(2)}) %collective-permute-start.7) | collective-permute-done | bytes 64 | tf_op jit(solution)/shard_map/ppermute | solution.py:43
  52.6 0.4 copy-done.15
  53.0 3.2 %fusion.29 = f32[1,256,1,16,64]{1,4,3,2,0:T(8,128)S(1)} fusion(bf16[256,16,64]{0,2,1:T(8,128)(2,1)S(1)} %bitcast.318, f32[16,256]{1,0:T(8,128)S(1)} %fusion.134, f32[256,256]{1,0:T(8,128)S(1)} %fusion.82, f32[16,256]{1,0:T(8,128)S(1)} %copy-done.15, f32[256,256]{1,0:T(8,128)S(1)} %fusion.136), kind=kOutput, calls=%fused_computation.33 | convolution fusion | flops 810549248 | bytes 2129920 | tf_op jit(solution)/shard_map/jvp()/while/body/eval_jaxpr/ghts,sghp->tghp/dot_general | solution.py:89
  56.3 0.7 mul.726
  57.0 0.8 fusion.78
  57.7 1.6 multiply_add_fusion.1
  59.3 0.3 copy.38
  59.6 0.7 copy-done.1
  60.3 2.6 %multiply_reduce_fusion.2 = (f32[256]{0:T(256)S(1)}, f32[256]{0:T(256)S(1)}, f32[256,1024]{1,0:T(8,128)}) fusion(bf16[256,1024]{1,0:T(8,128)(2,1)} %param.21, f32[1024]{0:T(1024)} %param.19, bf16[256,1024]{1,0:T(8,128)(2,1)} %param.12, f32[256,1024]{1,0:T(8,128)S(1)} %copy.38, f32[1024]{0:T(1024)} %mul.726, bf16[256,1024]{1,0:T(8,128)(2,1)S(1)} %copy-done.1), kind=kLoop, calls=%fused_computation.76 | loop fusion | flops 3931648 | bytes 3680256 | tf_op jit(solution)/shard_map/reduce_sum | solution.py:203
  63.0 16.0 %all_to_all.5 = f32[8,2,256]{2,1,0:T(2,128)S(1)} all-to-all(f32[8,2,256]{2,1,0:T(2,128)S(1)} %broadcast_in_dim.151), channel_id=1, replica_groups=mesh['ctx'=32,'head'=8] {'head'}, dimensions={0} | all-to-all | bytes 32768 | tf_op jit(solution)/shard_map/all_to_all | solution.py:76
  79.1 3.1 %fusion.55 = (bf16[256,1024]{1,0:T(8,128)(2,1)}, f32[256,1024]{1,0:T(8,128)S(1)}) fusion(bf16[256,1024]{1,0:T(8,128)(2,1)} %param.12, f32[256,1024]{1,0:T(8,128)S(1)} %copy.38, bf16[256,1024]{1,0:T(8,128)(2,1)S(1)} %copy-done.1, f32[256]{0:T(256)S(1)} %multiply_multiply_fusion, f32[256,1024]{1,0:T(8,128)} %get-tuple-element.158, ...), kind=kLoop, calls=%fused_computation.63 | loop fusion | flops 5767168 | bytes 5253120 | tf_op jit(solution)/shard_map/convert_element_type | solution.py:229
  82.2 0.3 copy.40
  82.6 0.6 fusion.57
  83.2 0.7 dynamic-slice_bitcast_fusion
  83.9 0.5 collective-permute-start.10
  84.4 1.4 collective-permute-done.10
  85.8 0.7 fusion.131
  86.5 1.0 fusion.74
  87.5 2.8 %collective-permute-start.12 = (f32[1,8,64,128]{3,2,1,0:T(8,128)S(1)}, f32[1,8,64,128]{3,2,1,0:T(8,128)S(1)}, u32[]{:S(2)}, u32[]{:S(2)}) collective-permute-start(f32[1,8,64,128]{3,2,1,0:T(8,128)S(1)} %fusion.74), channel_id=1, source_target_pairs={{248,232},{240,224},{232,216},{224,208},{216,200},{208,192},{200,1... | collective-permute-start | bytes 786440 | tf_op jit(solution)/shard_map/ppermute | solution.py:43
  90.3 4.2 %collective-permute-start.13 = (f32[1,8]{1,0:T(1,128)S(1)}, f32[1,8]{1,0:T(1,128)S(1)}, u32[]{:S(2)}, u32[]{:S(2)}) collective-permute-start(f32[1,8]{1,0:T(1,128)S(1)} %get-tuple-element.193), channel_id=1, source_target_pairs={{248,232},{240,224},{232,216},{224,208},{216,200},{208,192},{200,1... | collective-permute-start | bytes 104 | tf_op jit(solution)/shard_map/ppermute | solution.py:43
  94.5 7.9 %collective-permute-done.13 = f32[1,8]{1,0:T(1,128)S(1)} collective-permute-done((f32[1,8]{1,0:T(1,128)S(1)}, f32[1,8]{1,0:T(1,128)S(1)}, u32[]{:S(2)}, u32[]{:S(2)}) %collective-permute-start.13) | collective-permute-done | bytes 64 | tf_op jit(solution)/shard_map/ppermute | solution.py:43
  102.4 1.9 %collective-permute-start.15 = (f32[1,8]{1,0:T(1,128)S(1)}, f32[1,8]{1,0:T(1,128)S(1)}, u32[]{:S(2)}, u32[]{:S(2)}) collective-permute-start(f32[1,8]{1,0:T(1,128)S(1)} %mul.755), channel_id=1, source_target_pairs={{248,216},{240,208},{232,200},{224,192},{216,184},{208,176},{200,1... | collective-permute-start | bytes 104 | tf_op jit(solution)/shard_map/ppermute | solution.py:43
  104.3 5.9 %collective-permute-done.15 = f32[1,8]{1,0:T(1,128)S(1)} collective-permute-done((f32[1,8]{1,0:T(1,128)S(1)}, f32[1,8]{1,0:T(1,128)S(1)}, u32[]{:S(2)}, u32[]{:S(2)}) %collective-permute-start.15) | collective-permute-done | bytes 64 | tf_op jit(solution)/shard_map/ppermute | solution.py:43
  110.3 1.3 collective-permute-start.17
  111.5 4.2 %collective-permute-done.17 = f32[1,8]{1,0:T(1,128)S(1)} collective-permute-done((f32[1,8]{1,0:T(1,128)S(1)}, f32[1,8]{1,0:T(1,128)S(1)}, u32[]{:S(2)}, u32[]{:S(2)}) %collective-permute-start.17) | collective-permute-done | bytes 64 | tf_op jit(solution)/shard_map/ppermute | solution.py:43
  115.8 1.9 %collective-permute-start.14 = (f32[1,8,64,128]{3,2,1,0:T(8,128)S(1)}, f32[1,8,64,128]{3,2,1,0:T(8,128)S(1)}, u32[]{:S(2)}, u32[]{:S(2)}) collective-permute-start(f32[1,8,64,128]{3,2,1,0:T(8,128)S(1)} %multiply_add_fusion.6), channel_id=1, source_target_pairs={{248,216},{240,208},{232,200},{224,192},{216,184},{208,176},{200,1... | collective-permute-start | bytes 786440 | tf_op jit(solution)/shard_map/ppermute | solution.py:43
  117.8 6.7 %fusion.73 = (f32[16,256]{1,0:T(8,128)}, f32[16,256]{1,0:T(8,128)}, f32[16,256]{1,0:T(8,128)}, f32[256,256]{1,0:T(8,128)S(1)}) fusion(f32[16,256]{1,0:T(8,128)S(1)} %copy-done.16, f32[256,256]{1,0:T(8,128)S(1)} %copy-done.9, f32[16,256]{1,0:T(8,128)S(1)} %copy-done.23, f32[256,256]{1,0:T(8,128)S(1)} %copy-done.7, bf16[256,16,64]{0,2,1:T(8,128)(2,1)S(1)} %bitcast.319, ...), kind=kOutput, calls=%fused_computation.95 | convolution fusion | flops 825151488 | bytes 2441216 | tf_op jit(solution)/shard_map/transpose(jvp())/while/body/eval_jaxpr/ghts,sghp->tghp/dot_general | solution.py:89
  124.7 1.8 %collective-permute-done.14 = f32[1,8,64,128]{3,2,1,0:T(8,128)S(1)} collective-permute-done((f32[1,8,64,128]{3,2,1,0:T(8,128)S(1)}, f32[1,8,64,128]{3,2,1,0:T(8,128)S(1)}, u32[]{:S(2)}, u32[]{:S(2)}) %collective-permute-start.14) | collective-permute-done | bytes 262176 | tf_op jit(solution)/shard_map/ppermute | solution.py:43
  126.6 1.4 collective-permute-start.16
  128.0 2.5 %fusion.37 = f32[1,256,1,128]{3,1,2,0:T(8,128)} fusion(f32[256,128]{1,0:T(8,128)S(1)} %fusion.137, f32[1,256,1,16,64]{1,4,3,2,0:T(8,128)S(1)} %bitcast.314, f32[256,16]{0,1:T(8,128)S(1)} %get-tuple-element.167, f32[8,64,128]{2,1,0:T(8,128)S(1)} %bitcast.322, f32[8,64,128]{2,1,0:T(8,128)S(1)} %bitcast.328, pred[]{:T(512)S(6)} %eq.79), kind=kOutput, calls=%fused_computation.43 | convolution fusion | flops 403341312 | bytes 1851393 | tf_op jit(solution)/shard_map/transpose(jvp(kqgn,kghpn->kqghp))/dot_general | solution.py:143
  130.5 0.8 multiply_reduce_fusion
  131.3 3.7 %collective-permute-done.16 = f32[1,8,64,128]{3,2,1,0:T(8,128)S(1)} collective-permute-done((f32[1,8,64,128]{3,2,1,0:T(8,128)S(1)}, f32[1,8,64,128]{3,2,1,0:T(8,128)S(1)}, u32[]{:S(2)}, u32[]{:S(2)}) %collective-permute-start.16) | collective-permute-done | bytes 262176 | tf_op jit(solution)/shard_map/ppermute | solution.py:43
  135.1 1.3 collective-permute-start.18
  136.4 4.7 %fusion.26 = f32[1,256,1,16,64]{1,4,3,2,0:T(8,128)} fusion(f32[16,256]{1,0:T(8,128)S(1)} %copy-done.23, f32[256,256]{1,0:T(8,128)S(1)} %copy-done.9, f32[16,256]{1,0:T(8,128)S(1)} %copy-done.16, f32[256,256]{1,0:T(8,128)S(1)} %copy-done.7, f32[1,256,1,16,64]{1,4,3,2,0:T(8,128)S(1)} %bitcast.316), kind=kOutput, calls=%fused_computation.30 | convolution fusion | flops 810549248 | bytes 2654208 | tf_op jit(solution)/shard_map/transpose(jvp())/while/body/eval_jaxpr/ghts,sghp->tghp/dot_general | solution.py:89
  141.1 3.7 %collective-permute-done.18 = f32[1,8,64,128]{3,2,1,0:T(8,128)S(1)} collective-permute-done((f32[1,8,64,128]{3,2,1,0:T(8,128)S(1)}, f32[1,8,64,128]{3,2,1,0:T(8,128)S(1)}, u32[]{:S(2)}, u32[]{:S(2)}) %collective-permute-start.18) | collective-permute-done | bytes 262176 | tf_op jit(solution)/shard_map/ppermute | solution.py:43
  144.9 1.1 fusion.77
  146.1 1.0 convolution_bitcast_fusion.2
  147.1 1.1 fusion.76
  148.3 0.3 multiply_reduce_fusion.3
  149.3 2.5 %fusion.39 = f32[256,128]{1,0:T(8,128)} fusion(f32[1,256,1,128]{3,1,2,0:T(8,128)S(1)} %copy-done.19, bf16[256,16,64]{0,2,1:T(8,128)(2,1)S(1)} %bitcast.320, f32[256,16]{0,1:T(8,128)S(1)} %copy-done.11, f32[8,64,128]{2,1,0:T(8,128)S(1)} %bitcast.325, f32[8,64,128]{2,1,0:T(8,128)S(1)} %bitcast.329, pred[]{:T(512)S(6)} %eq.86), kind=kOutput, calls=%fused_computation.45 | convolution fusion | flops 403603456 | bytes 1327105 | tf_op jit(solution)/shard_map/transpose(jvp(kqgh,kqghp,kqgn->kghpn))/dot_general | solution.py:108
  151.8 2.8 %bitcast_add_fusion = (f32[1,256,1,16,64]{1,4,3,2,0:T(8,128)}, f32[256,16,64]{0,2,1:T(8,128)S(1)}) fusion(f32[1,256,1,16,64]{1,4,3,2,0:T(8,128)} %fusion.26, f32[256,16]{0,1:T(8,128)S(1)} %copy-done.11, bf16[256,128]{1,0:T(8,128)(2,1)S(1)} %copy-done.5, f32[8,64,128]{2,1,0:T(8,128)S(1)} %bitcast.326, f32[8,64,128]{2,1,0:T(8,128)S(1)} %bitcast.330, pred[]{:T(512)S(6)} %eq.86), kind=kOutput, calls=%fused_computation.70 | convolution fusion | flops 403570688 | bytes 3751937 | tf_op jit(solution)/shard_map/transpose(jvp(kqgh,kqghp,kqgn->kghpn))/dot_general | solution.py:108
  154.7 1.6 copy.41
  156.4 1.0 add_convert_fusion
  157.7 0.9 fusion.45
  (132 shorter events, 4.1 us)
Async XLA Ops:
  0.6 36.6 %copy-start = (bf16[256,128]{1,0:T(8,128)(2,1)S(1)}, bf16[256,128]{1,0:T(8,128)(2,1)}, u32[]{:S(2)}) copy-start(bf16[256,128]{1,0:T(8,128)(2,1)} %param.15) | copy-start | bytes 196612
  0.6 7.2 %copy-start.26 = (f32[16]{0:T(128)S(1)}, f32[16]{0:T(128)}, u32[]{:S(2)}) copy-start(f32[16]{0:T(128)} %param.16) | copy-start | bytes 196
  0.7 7.2 %copy-start.12 = (f32[256,16]{0,1:T(8,128)S(1)}, f32[256,16]{0,1:T(8,128)}, u32[]{:S(2)}) copy-start(f32[256,16]{0,1:T(8,128)} %param.13) | copy-start | bytes 49156
  0.7 7.3 %copy-start.5 = (bf16[256,128]{1,0:T(8,128)(2,1)S(1)}, bf16[256,128]{1,0:T(8,128)(2,1)}, u32[]{:S(2)}) copy-start(bf16[256,128]{1,0:T(8,128)(2,1)} %param.14) | copy-start | bytes 196612
  1.4 5.0 %copy-start.34 = (f32[16]{0:T(128)}, f32[16]{0:T(128)S(1)}, u32[]{:S(2)}) copy-start(f32[16]{0:T(128)S(1)} %exponential_negate_fusion) | copy-start | bytes 196
  3.4 5.2 %copy-start.31 = (f32[256]{0:T(256)}, f32[256]{0:T(256)S(1)}, u32[]{:S(2)}) copy-start(f32[256]{0:T(256)S(1)} %get-tuple-element.159) | copy-start | bytes 3076
  6.3 2.4 %copy-start.14 = (f32[16,256]{1,0:T(8,128)}, f32[16,256]{1,0:T(8,128)S(1)}, u32[]{:S(2)}) copy-start(f32[16,256]{1,0:T(8,128)S(1)} %fusion.81) | copy-start | bytes 49156
  6.6 2.1 %copy-start.28 = (f32[16]{0:T(128)}, f32[16]{0:T(128)S(1)}, u32[]{:S(2)}) copy-start(f32[16]{0:T(128)S(1)} %get-tuple-element.169) | copy-start | bytes 196
  7.9 3.1 %copy-start.24 = (f32[256]{0:T(256)}, f32[256]{0:T(256)S(1)}, u32[]{:S(2)}) copy-start(f32[256]{0:T(256)S(1)} %compare_convert_fusion.1) | copy-start | bytes 3076
  8.0 0.7 copy-start.10
  8.7 2.1 %collective-permute-start.1 = (f32[1,8,64,128]{3,2,1,0:T(8,128)S(1)}, f32[1,8,64,128]{3,2,1,0:T(8,128)S(1)}, u32[]{:S(2)}, u32[]{:S(2)}) collective-permute-start(f32[1,8,64,128]{3,2,1,0:T(8,128)S(1)} %dynamic-slice_bitcast_fusion.1), channel_id=1, source_target_pairs={{0,8},{8,0},{16,24},{24,16},{32,40},{40,32},{48,56},{56,48},{64,72... | collective-permute-start | bytes 786440 | tf_op jit(solution)/shard_map/ppermute | solution.py:43
  9.5 1.3 collective-permute-start
  10.8 41.5 %copy-start.30 = (f32[8]{0:T(128)}, f32[8]{0:T(128)S(1)}, u32[]{:S(2)}) copy-start(f32[8]{0:T(128)S(1)} %get-tuple-element.205) | copy-start | bytes 100
  10.9 10.4 %collective-permute-start.2 = (f32[1,8,64,128]{3,2,1,0:T(8,128)S(1)}, f32[1,8,64,128]{3,2,1,0:T(8,128)S(1)}, u32[]{:S(2)}, u32[]{:S(2)}) collective-permute-start(f32[1,8,64,128]{3,2,1,0:T(8,128)S(1)} %fusion.75), channel_id=1, source_target_pairs={{0,16},{8,24},{16,32},{24,40},{32,48},{40,56},{48,64},{56,72},{64,... | collective-permute-start | bytes 786440 | tf_op jit(solution)/shard_map/ppermute | solution.py:43
  21.5 12.0 %collective-permute-start.4 = (f32[1,8,64,128]{3,2,1,0:T(8,128)S(1)}, f32[1,8,64,128]{3,2,1,0:T(8,128)S(1)}, u32[]{:S(2)}, u32[]{:S(2)}) collective-permute-start(f32[1,8,64,128]{3,2,1,0:T(8,128)S(1)} %multiply_add_fusion.11), channel_id=1, source_target_pairs={{0,32},{8,40},{16,48},{24,56},{32,64},{40,72},{48,80},{56,88},{64,... | collective-permute-start | bytes 786440 | tf_op jit(solution)/shard_map/ppermute | solution.py:43
  25.8 7.7 %collective-permute-start.3 = (f32[1,8]{1,0:T(1,128)S(1)}, f32[1,8]{1,0:T(1,128)S(1)}, u32[]{:S(2)}, u32[]{:S(2)}) collective-permute-start(f32[1,8]{1,0:T(1,128)S(1)} %get-tuple-element.204), channel_id=1, source_target_pairs={{0,16},{8,24},{16,32},{24,40},{32,48},{40,56},{48,64},{56,72},{64,... | collective-permute-start | bytes 104 | tf_op jit(solution)/shard_map/ppermute | solution.py:43
  33.6 10.8 %collective-permute-start.6 = (f32[1,8,64,128]{3,2,1,0:T(8,128)S(1)}, f32[1,8,64,128]{3,2,1,0:T(8,128)S(1)}, u32[]{:S(2)}, u32[]{:S(2)}) collective-permute-start(f32[1,8,64,128]{3,2,1,0:T(8,128)S(1)} %multiply_add_fusion.10), channel_id=1, source_target_pairs={{0,64},{8,72},{16,80},{24,88},{32,96},{40,104},{48,112},{56,120},{... | collective-permute-start | bytes 786440 | tf_op jit(solution)/shard_map/ppermute | solution.py:43
  37.2 15.4 %copy-start.8 = (f32[256,256]{1,0:T(8,128)}, f32[256,256]{1,0:T(8,128)S(1)}, u32[]{:S(2)}) copy-start(f32[256,256]{1,0:T(8,128)S(1)} %fusion.82) | copy-start | bytes 786436
  37.4 15.2 %copy-start.6 = (f32[256,256]{1,0:T(8,128)}, f32[256,256]{1,0:T(8,128)S(1)}, u32[]{:S(2)}) copy-start(f32[256,256]{1,0:T(8,128)S(1)} %fusion.136) | copy-start | bytes 786436
  37.4 7.0 %collective-permute-start.5 = (f32[1,8]{1,0:T(1,128)S(1)}, f32[1,8]{1,0:T(1,128)S(1)}, u32[]{:S(2)}, u32[]{:S(2)}) collective-permute-start(f32[1,8]{1,0:T(1,128)S(1)} %mul.702), channel_id=1, source_target_pairs={{0,32},{8,40},{16,48},{24,56},{32,64},{40,72},{48,80},{56,88},{64,... | collective-permute-start | bytes 104 | tf_op jit(solution)/shard_map/ppermute | solution.py:43
  44.5 7.8 %collective-permute-start.8 = (f32[1,8,64,128]{3,2,1,0:T(8,128)S(1)}, f32[1,8,64,128]{3,2,1,0:T(8,128)S(1)}, u32[]{:S(2)}, u32[]{:S(2)}) collective-permute-start(f32[1,8,64,128]{3,2,1,0:T(8,128)S(1)} %multiply_add_fusion.9), channel_id=1, source_target_pairs={{0,128},{8,136},{16,144},{24,152},{32,160},{40,168},{48,176},{56,1... | collective-permute-start | bytes 786440 | tf_op jit(solution)/shard_map/ppermute | solution.py:43
  48.5 4.1 %copy-start.22 = (f32[16,256]{1,0:T(8,128)}, f32[16,256]{1,0:T(8,128)S(1)}, u32[]{:S(2)}) copy-start(f32[16,256]{1,0:T(8,128)S(1)} %fusion.134) | copy-start | bytes 49156
  48.5 3.8 %collective-permute-start.7 = (f32[1,8]{1,0:T(1,128)S(1)}, f32[1,8]{1,0:T(1,128)S(1)}, u32[]{:S(2)}, u32[]{:S(2)}) collective-permute-start(f32[1,8]{1,0:T(1,128)S(1)} %mul.710), channel_id=1, source_target_pairs={{0,64},{8,72},{16,80},{24,88},{32,96},{40,104},{48,112},{56,120},{... | collective-permute-start | bytes 104 | tf_op jit(solution)/shard_map/ppermute | solution.py:43
  52.3 0.7 copy-start.15
  52.5 3.7 %copy-start.33 = (f32[16]{0:T(128)S(1)}, f32[16]{0:T(128)}, u32[]{:S(2)}) copy-start(f32[16]{0:T(128)} %param.18) | copy-start | bytes 196
  52.5 5.2 %collective-permute-start.9 = (f32[1,8,64,128]{3,2,1,0:T(8,128)S(1)}, f32[1,8,64,128]{3,2,1,0:T(8,128)S(1)}, u32[]{:S(2)}, u32[]{:S(2)}) collective-permute-start(f32[1,8,64,128]{3,2,1,0:T(8,128)S(1)} %get-tuple-element.161), channel_id=1, source_target_pairs={{0,8},{8,0},{16,24},{24,16},{32,40},{40,32},{48,56},{56,48},{64,72... | collective-permute-start | bytes 786440 | tf_op jit(solution)/shard_map/ppermute | solution.py:43
  57.7 1.6 %copy-start.3 = (f32[1,8,64,128]{3,2,1,0:T(8,128)}, f32[1,8,64,128]{3,2,1,0:T(8,128)S(1)}, u32[]{:S(2)}) copy-start(f32[1,8,64,128]{3,2,1,0:T(8,128)S(1)} %collective-permute-done.9) | copy-start | bytes 786436
  59.3 1.0 copy-start.1
  83.9 2.5 %collective-permute-start.11 = (f32[1,8,64,128]{3,2,1,0:T(8,128)}, f32[1,8,64,128]{3,2,1,0:T(8,128)}, u32[]{:S(2)}, u32[]{:S(2)}) collective-permute-start(f32[1,8,64,128]{3,2,1,0:T(8,128)} %dynamic-slice_bitcast_fusion), channel_id=1, source_target_pairs={{248,240},{240,248},{232,224},{224,232},{216,208},{208,216},{200,1... | collective-permute-start | bytes 786440 | tf_op jit(solution)/shard_map/ppermute | solution.py:43
  83.9 1.9 %collective-permute-start.10 = (f32[1,8]{1,0:T(1,128)}, f32[1,8]{1,0:T(1,128)}, u32[]{:S(2)}, u32[]{:S(2)}) collective-permute-start(f32[1,8]{1,0:T(1,128)} %bitcast.128), channel_id=1, source_target_pairs={{248,240},{240,248},{232,224},{224,232},{216,208},{208,216},{200,1... | collective-permute-start | bytes 104 | tf_op jit(solution)/shard_map/ppermute | solution.py:43
  84.4 33.3 %copy-start.7 = (f32[256,256]{1,0:T(8,128)S(1)}, f32[256,256]{1,0:T(8,128)}, u32[]{:S(2)}) copy-start(f32[256,256]{1,0:T(8,128)} %copy-done.6) | copy-start | bytes 786436
  84.4 33.3 %copy-start.9 = (f32[256,256]{1,0:T(8,128)S(1)}, f32[256,256]{1,0:T(8,128)}, u32[]{:S(2)}) copy-start(f32[256,256]{1,0:T(8,128)} %copy-done.8) | copy-start | bytes 786436
  84.4 33.3 %copy-start.16 = (f32[16,256]{1,0:T(8,128)S(1)}, f32[16,256]{1,0:T(8,128)}, u32[]{:S(2)}) copy-start(f32[16,256]{1,0:T(8,128)} %copy-done.14) | copy-start | bytes 49156
  84.4 33.3 %copy-start.23 = (f32[16,256]{1,0:T(8,128)S(1)}, f32[16,256]{1,0:T(8,128)}, u32[]{:S(2)}) copy-start(f32[16,256]{1,0:T(8,128)} %copy-done.22) | copy-start | bytes 49156
  87.5 28.2 %collective-permute-start.12 = (f32[1,8,64,128]{3,2,1,0:T(8,128)S(1)}, f32[1,8,64,128]{3,2,1,0:T(8,128)S(1)}, u32[]{:S(2)}, u32[]{:S(2)}) collective-permute-start(f32[1,8,64,128]{3,2,1,0:T(8,128)S(1)} %fusion.74), channel_id=1, source_target_pairs={{248,232},{240,224},{232,216},{224,208},{216,200},{208,192},{200,1... | collective-permute-start | bytes 786440 | tf_op jit(solution)/shard_map/ppermute | solution.py:43
  90.3 12.1 %collective-permute-start.13 = (f32[1,8]{1,0:T(1,128)S(1)}, f32[1,8]{1,0:T(1,128)S(1)}, u32[]{:S(2)}, u32[]{:S(2)}) collective-permute-start(f32[1,8]{1,0:T(1,128)S(1)} %get-tuple-element.193), channel_id=1, source_target_pairs={{248,232},{240,224},{232,216},{224,208},{216,200},{208,192},{200,1... | collective-permute-start | bytes 104 | tf_op jit(solution)/shard_map/ppermute | solution.py:43
  102.4 7.9 %collective-permute-start.15 = (f32[1,8]{1,0:T(1,128)S(1)}, f32[1,8]{1,0:T(1,128)S(1)}, u32[]{:S(2)}, u32[]{:S(2)}) collective-permute-start(f32[1,8]{1,0:T(1,128)S(1)} %mul.755), channel_id=1, source_target_pairs={{248,216},{240,208},{232,200},{224,192},{216,184},{208,176},{200,1... | collective-permute-start | bytes 104 | tf_op jit(solution)/shard_map/ppermute | solution.py:43
  110.3 5.5 %collective-permute-start.17 = (f32[1,8]{1,0:T(1,128)S(1)}, f32[1,8]{1,0:T(1,128)S(1)}, u32[]{:S(2)}, u32[]{:S(2)}) collective-permute-start(f32[1,8]{1,0:T(1,128)S(1)} %mul.763), channel_id=1, source_target_pairs={{248,184},{240,176},{232,168},{224,160},{216,152},{208,144},{200,1... | collective-permute-start | bytes 104 | tf_op jit(solution)/shard_map/ppermute | solution.py:43
  115.8 10.7 %collective-permute-start.14 = (f32[1,8,64,128]{3,2,1,0:T(8,128)S(1)}, f32[1,8,64,128]{3,2,1,0:T(8,128)S(1)}, u32[]{:S(2)}, u32[]{:S(2)}) collective-permute-start(f32[1,8,64,128]{3,2,1,0:T(8,128)S(1)} %multiply_add_fusion.6), channel_id=1, source_target_pairs={{248,216},{240,208},{232,200},{224,192},{216,184},{208,176},{200,1... | collective-permute-start | bytes 786440 | tf_op jit(solution)/shard_map/ppermute | solution.py:43
  124.4 3.6 %copy-start.4 = (f32[1,8,64,128]{3,2,1,0:T(8,128)S(1)}, f32[1,8,64,128]{3,2,1,0:T(8,128)}, u32[]{:S(2)}) copy-start(f32[1,8,64,128]{3,2,1,0:T(8,128)} %copy-done.3) | copy-start | bytes 786436
  126.6 3.9 %copy-start.2 = (f32[1,256,1,16,64]{1,4,3,2,0:T(8,128)S(1)}, f32[1,256,1,16,64]{1,4,3,2,0:T(8,128)}, u32[]{:S(2)}) copy-start(f32[1,256,1,16,64]{1,4,3,2,0:T(8,128)} %get-tuple-element.214) | copy-start | bytes 3145732
  126.6 8.4 %collective-permute-start.16 = (f32[1,8,64,128]{3,2,1,0:T(8,128)S(1)}, f32[1,8,64,128]{3,2,1,0:T(8,128)S(1)}, u32[]{:S(2)}, u32[]{:S(2)}) collective-permute-start(f32[1,8,64,128]{3,2,1,0:T(8,128)S(1)} %multiply_add_fusion.5), channel_id=1, source_target_pairs={{248,184},{240,176},{232,168},{224,160},{216,152},{208,144},{200,1... | collective-permute-start | bytes 786440 | tf_op jit(solution)/shard_map/ppermute | solution.py:43
  135.1 9.8 %collective-permute-start.18 = (f32[1,8,64,128]{3,2,1,0:T(8,128)S(1)}, f32[1,8,64,128]{3,2,1,0:T(8,128)S(1)}, u32[]{:S(2)}, u32[]{:S(2)}) collective-permute-start(f32[1,8,64,128]{3,2,1,0:T(8,128)S(1)} %multiply_add_fusion.4), channel_id=1, source_target_pairs={{248,120},{240,112},{232,104},{224,96},{216,88},{208,80},{200,72},... | collective-permute-start | bytes 786440 | tf_op jit(solution)/shard_map/ppermute | solution.py:43
  146.0 2.3 %collective-permute-start.19 = (f32[1,8,64,128]{3,2,1,0:T(8,128)S(1)}, f32[1,8,64,128]{3,2,1,0:T(8,128)S(1)}, u32[]{:S(2)}, u32[]{:S(2)}) collective-permute-start(f32[1,8,64,128]{3,2,1,0:T(8,128)S(1)} %get-tuple-element.156), channel_id=1, source_target_pairs={{248,240},{240,248},{232,224},{224,232},{216,208},{208,216},{200,1... | collective-permute-start | bytes 786440 | tf_op jit(solution)/shard_map/ppermute | solution.py:43
  147.1 2.1 %copy-start.11 = (f32[256,16]{0,1:T(8,128)S(1)}, f32[256,16]{0,1:T(8,128)}, u32[]{:S(2)}) copy-start(f32[256,16]{0,1:T(8,128)} %copy-done.10) | copy-start | bytes 49156
  148.2 0.7 copy-start.17
  148.2 0.8 copy-start.21
  148.2 0.8 copy-start.32
  148.2 0.8 copy-start.35
  148.2 0.8 copy-start.37
  148.3 0.8 copy-start.38
  148.3 0.8 copy-start.39
  148.3 1.0 copy-start.19
  154.7 1.6 copy-start.20
  156.3 1.1 copy-start.13
  156.3 1.1 copy-start.18
  156.3 1.0 copy-start.25
  156.3 1.0 copy-start.27
  156.3 1.0 copy-start.29
  156.4 1.3 copy-start.36

commit v10 on v9

--- a/solution.py
+++ b/solution.py
@@ -10,6 +10,7 @@
 
 
 HIGHEST_PRECISION = lax.Precision.HIGHEST
+MIX_PRECISION = lax.Precision.HIGH
 EPSILON = 1e-05
 
 
@@ -84,9 +85,9 @@
         (places[:, None] >= places[None, :]) & (segment[:, None] == segment[None, :])
     ).astype(jnp.float32)
     masked = jnp.exp(jnp.minimum(spread, 0.0)) * keep_mask
-    scores = jnp.einsum("tgn,sgn->gts", c_span, b_span, precision=HIGHEST_PRECISION)
+    scores = jnp.einsum("tgn,sgn->gts", c_span, b_span, precision=MIX_PRECISION)
     weights = scores[:, None] * masked * jnp.moveaxis(dt_span, 0, -1)[..., None, :]
-    return jnp.einsum("ghts,sghp->tghp", weights, x_span, precision=HIGHEST_PRECISION)
+    return jnp.einsum("ghts,sghp->tghp", weights, x_span, precision=MIX_PRECISION)
 
 
 def block_decays(dt_spans, segment, decay_rate):
@@ -110,7 +111,7 @@
         tail_decay * dt_spans,
         x_spans,
         b_spans,
-        precision=HIGHEST_PRECISION,
+        precision=MIX_PRECISION,
     )
 
     def advance(carried_pair, item_pair):
@@ -140,7 +141,7 @@
     opened = (segment == 0).astype(jnp.float32)
     entry_decay = jnp.exp(log_cum) * opened[:, :, None, None]
     carried = (
-        jnp.einsum("kqgn,kghpn->kqghp", c_spans, full_start, precision=HIGHEST_PRECISION)
+        jnp.einsum("kqgn,kghpn->kqghp", c_spans, full_start, precision=MIX_PRECISION)
         * entry_decay[..., None]
     )
     mix_block = lambda pieces: span_mix(*pieces)

time: 160 us -> 157 us (0.981)
  matrix products: 28.7 us -> 23.3 us
  waiting for transfers between devices: 45.3 us -> 47.9 us
    dot_general x9, matrix products: 20.8 us -> 16.6 us  [the longest x3 11.6 us: span_mix(): jnp.einsum('ghts,sghp->tghp', weights, x_span, precision=MIX_PRECISION)]
    ppermute x20, waiting for transfers between devices: 45.3 us -> 47.9 us  [move(): return lax.ppermute(tree, axis, [(device(a), device(b)) for a, b in pairs])]
  transfers between devices with their start and end apart: 20 -> 20, of which waited for: 12 -> 12; matrix products, arithmetic and copies ran while one was open for 15% -> 12% of each run, Pallas kernels for 0% -> 0%
where the time goes in v10:
time: 157 us; the launch traced here: 156 us
  waiting for transfers between devices  47.9 us (31%)
  starting transfers between devices  40.9 us (26%)
  matrix products  23.3 us (15%)
  other arithmetic  16.2 us (10%)
  blocking collectives  16 us (10%)
  local copies, waits for them, and re-layouts  8.91 us (6%)
  between operations  2.79 us (2%)
    ppermute x20, waiting for transfers between devices, move(): return lax.ppermute(tree, axis, [(device(a), device(b)) for a, b in pairs])  47.9 us
    ppermute x20, starting transfers between devices, move(): return lax.ppermute(tree, axis, [(device(a), device(b)) for a, b in pairs])  40.9 us
    all_to_all x1, blocking collectives, head_sum(): return jnp.sum(lax.all_to_all(spread, axis, 0, 0), axis=0)  16 us
    dot_general x3, matrix products, span_mix(): jnp.einsum('ghts,sghp->tghp', weights, x_span, precision=MIX_PRECISION)  11.6 us
    dot_general x3, matrix products, local_states(): jnp.einsum('kqgh,kqghp,kqgn->kghpn', tail_decay * dt_spans, x_spans, b_sp...  4.77 us
    dot_general x3, matrix products, output_part(): jnp.einsum('kqgn,kghpn->kqghp', c_spans, full_start, precision=MIX_PRECIS...  3.55 us
  transfers between devices with their start and end apart: 20, of which 12 were waited for; matrix products, arithmetic and copies ran while one was open for 12% of the time, Pallas kernels for 0%

profile of v10, /device:TPU:6, one launch (start us, length us, event | category | flops | bytes accessed | tf_op | source)
XLA Modules:
  0.0 156.1 jit_solution(6832108625878021647)
XLA Ops:
  0.7 0.7 exponential_negate_fusion
  1.4 1.0 reduce-window.6
  2.6 0.6 slice.28
  3.5 0.6 slice.29
  5.4 0.9 fusion.81
  6.6 1.2 copy.37
  8.0 0.4 fusion.34
  8.7 0.7 dynamic-slice_reduce_fusion.1
  9.4 0.5 collective-permute-start
  9.9 0.8 collective-permute-done
  10.8 3.4 %collective-permute-start.2 = (f32[1,8,64,128]{3,2,1,0:T(8,128)S(1)}, f32[1,8,64,128]{3,2,1,0:T(8,128)S(1)}, u32[]{:S(2)}, u32[]{:S(2)}) collective-permute-start(f32[1,8,64,128]{3,2,1,0:T(8,128)S(1)} %fusion.75), channel_id=1, source_target_pairs={{0,16},{8,24},{16,32},{24,40},{32,48},{40,56},{48,64},{56,72},{64,... | collective-permute-start | bytes 786440 | tf_op jit(solution)/shard_map/ppermute | solution.py:44
  14.2 7.0 %collective-permute-done.2 = f32[1,8,64,128]{3,2,1,0:T(8,128)S(1)} collective-permute-done((f32[1,8,64,128]{3,2,1,0:T(8,128)S(1)}, f32[1,8,64,128]{3,2,1,0:T(8,128)S(1)}, u32[]{:S(2)}, u32[]{:S(2)}) %collective-permute-start.2) | collective-permute-done | bytes 262176 | tf_op jit(solution)/shard_map/ppermute | solution.py:44
  21.3 4.3 %collective-permute-start.4 = (f32[1,8,64,128]{3,2,1,0:T(8,128)S(1)}, f32[1,8,64,128]{3,2,1,0:T(8,128)S(1)}, u32[]{:S(2)}, u32[]{:S(2)}) collective-permute-start(f32[1,8,64,128]{3,2,1,0:T(8,128)S(1)} %multiply_add_fusion.11), channel_id=1, source_target_pairs={{0,32},{8,40},{16,48},{24,56},{32,64},{40,72},{48,80},{56,88},{64,... | collective-permute-start | bytes 786440 | tf_op jit(solution)/shard_map/ppermute | solution.py:44
  25.7 4.0 %collective-permute-start.3 = (f32[1,8]{1,0:T(1,128)S(1)}, f32[1,8]{1,0:T(1,128)S(1)}, u32[]{:S(2)}, u32[]{:S(2)}) collective-permute-start(f32[1,8]{1,0:T(1,128)S(1)} %get-tuple-element.204), channel_id=1, source_target_pairs={{0,16},{8,24},{16,32},{24,40},{32,48},{40,56},{48,64},{56,72},{64,... | collective-permute-start | bytes 104 | tf_op jit(solution)/shard_map/ppermute | solution.py:44
  29.7 3.7 %collective-permute-done.3 = f32[1,8]{1,0:T(1,128)S(1)} collective-permute-done((f32[1,8]{1,0:T(1,128)S(1)}, f32[1,8]{1,0:T(1,128)S(1)}, u32[]{:S(2)}, u32[]{:S(2)}) %collective-permute-start.3) | collective-permute-done | bytes 64 | tf_op jit(solution)/shard_map/ppermute | solution.py:44
  33.5 3.5 %collective-permute-start.6 = (f32[1,8,64,128]{3,2,1,0:T(8,128)S(1)}, f32[1,8,64,128]{3,2,1,0:T(8,128)S(1)}, u32[]{:S(2)}, u32[]{:S(2)}) collective-permute-start(f32[1,8,64,128]{3,2,1,0:T(8,128)S(1)} %multiply_add_fusion.10), channel_id=1, source_target_pairs={{0,64},{8,72},{16,80},{24,88},{32,96},{40,104},{48,112},{56,120},{... | collective-permute-start | bytes 786440 | tf_op jit(solution)/shard_map/ppermute | solution.py:44
  37.3 4.3 %collective-permute-start.5 = (f32[1,8]{1,0:T(1,128)S(1)}, f32[1,8]{1,0:T(1,128)S(1)}, u32[]{:S(2)}, u32[]{:S(2)}) collective-permute-start(f32[1,8]{1,0:T(1,128)S(1)} %mul.702), channel_id=1, source_target_pairs={{0,32},{8,40},{16,48},{24,56},{32,64},{40,72},{48,80},{56,88},{64,... | collective-permute-start | bytes 104 | tf_op jit(solution)/shard_map/ppermute | solution.py:44
  41.6 2.7 %collective-permute-done.5 = f32[1,8]{1,0:T(1,128)S(1)} collective-permute-done((f32[1,8]{1,0:T(1,128)S(1)}, f32[1,8]{1,0:T(1,128)S(1)}, u32[]{:S(2)}, u32[]{:S(2)}) %collective-permute-start.5) | collective-permute-done | bytes 64 | tf_op jit(solution)/shard_map/ppermute | solution.py:44
  44.4 3.9 %collective-permute-start.8 = (f32[1,8,64,128]{3,2,1,0:T(8,128)S(1)}, f32[1,8,64,128]{3,2,1,0:T(8,128)S(1)}, u32[]{:S(2)}, u32[]{:S(2)}) collective-permute-start(f32[1,8,64,128]{3,2,1,0:T(8,128)S(1)} %multiply_add_fusion.9), channel_id=1, source_target_pairs={{0,128},{8,136},{16,144},{24,152},{32,160},{40,168},{48,176},{56,1... | collective-permute-start | bytes 786440 | tf_op jit(solution)/shard_map/ppermute | solution.py:44
  48.4 1.3 collective-permute-start.7
  49.7 2.5 %collective-permute-done.7 = f32[1,8]{1,0:T(1,128)S(1)} collective-permute-done((f32[1,8]{1,0:T(1,128)S(1)}, f32[1,8]{1,0:T(1,128)S(1)}, u32[]{:S(2)}, u32[]{:S(2)}) %collective-permute-start.7) | collective-permute-done | bytes 64 | tf_op jit(solution)/shard_map/ppermute | solution.py:44
  52.5 0.4 copy-done.15
  52.9 2.2 %fusion.29 = f32[1,256,1,16,64]{1,4,3,2,0:T(8,128)S(1)} fusion(bf16[256,16,64]{0,2,1:T(8,128)(2,1)S(1)} %bitcast.318, f32[16,256]{1,0:T(8,128)S(1)} %fusion.134, f32[256,256]{1,0:T(8,128)S(1)} %fusion.82, f32[16,256]{1,0:T(8,128)S(1)} %copy-done.15, f32[256,256]{1,0:T(8,128)S(1)} %fusion.136), kind=kOutput, calls=%fused_computation.33 | convolution fusion | flops 407896064 | bytes 2129920 | tf_op jit(solution)/shard_map/jvp()/while/body/eval_jaxpr/ghts,sghp->tghp/dot_general | solution.py:90
  55.1 0.7 mul.726
  55.8 0.8 fusion.78
  56.6 1.4 multiply_add_fusion.1
  58.0 0.3 copy.38
  58.3 0.7 copy-done.1
  59.0 2.6 %multiply_reduce_fusion.2 = (f32[256]{0:T(256)S(1)}, f32[256]{0:T(256)S(1)}, f32[256,1024]{1,0:T(8,128)}) fusion(bf16[256,1024]{1,0:T(8,128)(2,1)} %param.21, f32[1024]{0:T(1024)} %param.19, bf16[256,1024]{1,0:T(8,128)(2,1)} %param.12, f32[256,1024]{1,0:T(8,128)S(1)} %copy.38, f32[1024]{0:T(1024)} %mul.726, bf16[256,1024]{1,0:T(8,128)(2,1)S(1)} %copy-done.1), kind=kLoop, calls=%fused_computation.76 | loop fusion | flops 3931648 | bytes 3680256 | tf_op jit(solution)/shard_map/reduce_sum | solution.py:204
  61.7 16.0 %all_to_all.5 = f32[8,2,256]{2,1,0:T(2,128)S(1)} all-to-all(f32[8,2,256]{2,1,0:T(2,128)S(1)} %broadcast_in_dim.151), channel_id=1, replica_groups=mesh['ctx'=32,'head'=8] {'head'}, dimensions={0} | all-to-all | bytes 32768 | tf_op jit(solution)/shard_map/all_to_all | solution.py:77
  77.8 3.1 %fusion.55 = (bf16[256,1024]{1,0:T(8,128)(2,1)}, f32[256,1024]{1,0:T(8,128)S(1)}) fusion(bf16[256,1024]{1,0:T(8,128)(2,1)} %param.12, f32[256,1024]{1,0:T(8,128)S(1)} %copy.38, bf16[256,1024]{1,0:T(8,128)(2,1)S(1)} %copy-done.1, f32[256]{0:T(256)S(1)} %multiply_multiply_fusion, f32[256,1024]{1,0:T(8,128)} %get-tuple-element.158, ...), kind=kLoop, calls=%fused_computation.63 | loop fusion | flops 5767168 | bytes 5253120 | tf_op jit(solution)/shard_map/convert_element_type | solution.py:230
  80.9 0.3 copy.40
  81.3 0.4 fusion.57
  81.7 0.7 dynamic-slice_bitcast_fusion
  82.4 0.5 collective-permute-start.10
  83.0 1.4 collective-permute-done.10
  84.3 0.7 fusion.131
  85.0 1.0 fusion.74
  86.0 2.7 %collective-permute-start.12 = (f32[1,8,64,128]{3,2,1,0:T(8,128)S(1)}, f32[1,8,64,128]{3,2,1,0:T(8,128)S(1)}, u32[]{:S(2)}, u32[]{:S(2)}) collective-permute-start(f32[1,8,64,128]{3,2,1,0:T(8,128)S(1)} %fusion.74), channel_id=1, source_target_pairs={{248,232},{240,224},{232,216},{224,208},{216,200},{208,192},{200,1... | collective-permute-start | bytes 786440 | tf_op jit(solution)/shard_map/ppermute | solution.py:44
  88.8 4.2 %collective-permute-start.13 = (f32[1,8]{1,0:T(1,128)S(1)}, f32[1,8]{1,0:T(1,128)S(1)}, u32[]{:S(2)}, u32[]{:S(2)}) collective-permute-start(f32[1,8]{1,0:T(1,128)S(1)} %get-tuple-element.193), channel_id=1, source_target_pairs={{248,232},{240,224},{232,216},{224,208},{216,200},{208,192},{200,1... | collective-permute-start | bytes 104 | tf_op jit(solution)/shard_map/ppermute | solution.py:44
  93.0 7.9 %collective-permute-done.13 = f32[1,8]{1,0:T(1,128)S(1)} collective-permute-done((f32[1,8]{1,0:T(1,128)S(1)}, f32[1,8]{1,0:T(1,128)S(1)}, u32[]{:S(2)}, u32[]{:S(2)}) %collective-permute-start.13) | collective-permute-done | bytes 64 | tf_op jit(solution)/shard_map/ppermute | solution.py:44
  100.9 1.9 %collective-permute-start.15 = (f32[1,8]{1,0:T(1,128)S(1)}, f32[1,8]{1,0:T(1,128)S(1)}, u32[]{:S(2)}, u32[]{:S(2)}) collective-permute-start(f32[1,8]{1,0:T(1,128)S(1)} %mul.755), channel_id=1, source_target_pairs={{248,216},{240,208},{232,200},{224,192},{216,184},{208,176},{200,1... | collective-permute-start | bytes 104 | tf_op jit(solution)/shard_map/ppermute | solution.py:44
  102.8 5.9 %collective-permute-done.15 = f32[1,8]{1,0:T(1,128)S(1)} collective-permute-done((f32[1,8]{1,0:T(1,128)S(1)}, f32[1,8]{1,0:T(1,128)S(1)}, u32[]{:S(2)}, u32[]{:S(2)}) %collective-permute-start.15) | collective-permute-done | bytes 64 | tf_op jit(solution)/shard_map/ppermute | solution.py:44
  108.8 1.3 collective-permute-start.17
  110.1 4.2 %collective-permute-done.17 = f32[1,8]{1,0:T(1,128)S(1)} collective-permute-done((f32[1,8]{1,0:T(1,128)S(1)}, f32[1,8]{1,0:T(1,128)S(1)}, u32[]{:S(2)}, u32[]{:S(2)}) %collective-permute-start.17) | collective-permute-done | bytes 64 | tf_op jit(solution)/shard_map/ppermute | solution.py:44
  114.3 2.1 %collective-permute-start.14 = (f32[1,8,64,128]{3,2,1,0:T(8,128)S(1)}, f32[1,8,64,128]{3,2,1,0:T(8,128)S(1)}, u32[]{:S(2)}, u32[]{:S(2)}) collective-permute-start(f32[1,8,64,128]{3,2,1,0:T(8,128)S(1)} %multiply_add_fusion.6), channel_id=1, source_target_pairs={{248,216},{240,208},{232,200},{224,192},{216,184},{208,176},{200,1... | collective-permute-start | bytes 786440 | tf_op jit(solution)/shard_map/ppermute | solution.py:44
  116.5 6.2 %fusion.73 = (f32[16,256]{1,0:T(8,128)}, f32[16,256]{1,0:T(8,128)}, f32[16,256]{1,0:T(8,128)}, f32[256,256]{1,0:T(8,128)S(1)}) fusion(f32[16,256]{1,0:T(8,128)S(1)} %copy-done.16, f32[256,256]{1,0:T(8,128)S(1)} %copy-done.9, f32[16,256]{1,0:T(8,128)S(1)} %copy-done.23, f32[256,256]{1,0:T(8,128)S(1)} %copy-done.7, bf16[256,16,64]{0,2,1:T(8,128)(2,1)S(1)} %bitcast.319, ...), kind=kOutput, calls=%fused_computation.95 | convolution fusion | flops 422498304 | bytes 2441216 | tf_op jit(solution)/shard_map/transpose(jvp())/while/body/eval_jaxpr/ghts,sghp->tghp/dot_general | solution.py:90
  122.9 2.1 %collective-permute-done.14 = f32[1,8,64,128]{3,2,1,0:T(8,128)S(1)} collective-permute-done((f32[1,8,64,128]{3,2,1,0:T(8,128)S(1)}, f32[1,8,64,128]{3,2,1,0:T(8,128)S(1)}, u32[]{:S(2)}, u32[]{:S(2)}) %collective-permute-start.14) | collective-permute-done | bytes 262176 | tf_op jit(solution)/shard_map/ppermute | solution.py:44
  125.1 1.4 collective-permute-start.16
  126.6 1.7 %fusion.37 = f32[1,256,1,128]{3,1,2,0:T(8,128)} fusion(f32[256,128]{1,0:T(8,128)S(1)} %fusion.137, f32[1,256,1,16,64]{1,4,3,2,0:T(8,128)S(1)} %bitcast.314, f32[256,16]{0,1:T(8,128)S(1)} %get-tuple-element.167, f32[8,64,128]{2,1,0:T(8,128)S(1)} %bitcast.322, f32[8,64,128]{2,1,0:T(8,128)S(1)} %bitcast.328, pred[]{:T(512)S(6)} %eq.79), kind=kOutput, calls=%fused_computation.43 | convolution fusion | flops 202014720 | bytes 1851393 | tf_op jit(solution)/shard_map/transpose(jvp(kqgn,kghpn->kqghp))/dot_general | solution.py:144
  128.2 0.8 multiply_reduce_fusion
  129.0 4.5 %collective-permute-done.16 = f32[1,8,64,128]{3,2,1,0:T(8,128)S(1)} collective-permute-done((f32[1,8,64,128]{3,2,1,0:T(8,128)S(1)}, f32[1,8,64,128]{3,2,1,0:T(8,128)S(1)}, u32[]{:S(2)}, u32[]{:S(2)}) %collective-permute-start.16) | collective-permute-done | bytes 262176 | tf_op jit(solution)/shard_map/ppermute | solution.py:44
  133.6 1.3 collective-permute-start.18
  134.9 3.2 %fusion.26 = f32[1,256,1,16,64]{1,4,3,2,0:T(8,128)} fusion(f32[16,256]{1,0:T(8,128)S(1)} %copy-done.23, f32[256,256]{1,0:T(8,128)S(1)} %copy-done.9, f32[16,256]{1,0:T(8,128)S(1)} %copy-done.16, f32[256,256]{1,0:T(8,128)S(1)} %copy-done.7, f32[1,256,1,16,64]{1,4,3,2,0:T(8,128)S(1)} %bitcast.316), kind=kOutput, calls=%fused_computation.30 | convolution fusion | flops 407896064 | bytes 2654208 | tf_op jit(solution)/shard_map/transpose(jvp())/while/body/eval_jaxpr/ghts,sghp->tghp/dot_general | solution.py:90
  138.2 5.2 %collective-permute-done.18 = f32[1,8,64,128]{3,2,1,0:T(8,128)S(1)} collective-permute-done((f32[1,8,64,128]{3,2,1,0:T(8,128)S(1)}, f32[1,8,64,128]{3,2,1,0:T(8,128)S(1)}, u32[]{:S(2)}, u32[]{:S(2)}) %collective-permute-start.18) | collective-permute-done | bytes 262176 | tf_op jit(solution)/shard_map/ppermute | solution.py:44
  143.4 1.1 fusion.77
  144.6 1.0 convolution_bitcast_fusion.2
  145.6 1.1 fusion.76
  146.8 0.3 multiply_reduce_fusion.3
  147.8 1.7 %fusion.39 = f32[256,128]{1,0:T(8,128)} fusion(f32[1,256,1,128]{3,1,2,0:T(8,128)S(1)} %copy-done.19, bf16[256,16,64]{0,2,1:T(8,128)(2,1)S(1)} %bitcast.320, f32[256,16]{0,1:T(8,128)S(1)} %copy-done.11, f32[8,64,128]{2,1,0:T(8,128)S(1)} %bitcast.325, f32[8,64,128]{2,1,0:T(8,128)S(1)} %bitcast.329, pred[]{:T(512)S(6)} %eq.86), kind=kOutput, calls=%fused_computation.45 | convolution fusion | flops 202276864 | bytes 1327105 | tf_op jit(solution)/shard_map/transpose(jvp(kqgh,kqghp,kqgn->kghpn))/dot_general | solution.py:109
  149.4 2.7 %bitcast_add_fusion = (f32[1,256,1,16,64]{1,4,3,2,0:T(8,128)}, f32[256,16,64]{0,2,1:T(8,128)S(1)}) fusion(f32[1,256,1,16,64]{1,4,3,2,0:T(8,128)} %fusion.26, f32[256,16]{0,1:T(8,128)S(1)} %copy-done.11, bf16[256,128]{1,0:T(8,128)(2,1)S(1)} %copy-done.5, f32[8,64,128]{2,1,0:T(8,128)S(1)} %bitcast.326, f32[8,64,128]{2,1,0:T(8,128)S(1)} %bitcast.330, pred[]{:T(512)S(6)} %eq.86), kind=kOutput, calls=%fused_computation.70 | convolution fusion | flops 202244096 | bytes 3751937 | tf_op jit(solution)/shard_map/transpose(jvp(kqgh,kqghp,kqgn->kghpn))/dot_general | solution.py:109
  152.2 1.6 copy.41
  153.9 1.0 add_convert_fusion
  155.2 0.9 fusion.45
  (132 shorter events, 4.1 us)
Async XLA Ops:
  0.6 36.5 %copy-start = (bf16[256,128]{1,0:T(8,128)(2,1)S(1)}, bf16[256,128]{1,0:T(8,128)(2,1)}, u32[]{:S(2)}) copy-start(bf16[256,128]{1,0:T(8,128)(2,1)} %param.15) | copy-start | bytes 196612
  0.6 7.2 %copy-start.26 = (f32[16]{0:T(128)S(1)}, f32[16]{0:T(128)}, u32[]{:S(2)}) copy-start(f32[16]{0:T(128)} %param.16) | copy-start | bytes 196
  0.7 7.2 %copy-start.12 = (f32[256,16]{0,1:T(8,128)S(1)}, f32[256,16]{0,1:T(8,128)}, u32[]{:S(2)}) copy-start(f32[256,16]{0,1:T(8,128)} %param.13) | copy-start | bytes 49156
  0.7 7.3 %copy-start.5 = (bf16[256,128]{1,0:T(8,128)(2,1)S(1)}, bf16[256,128]{1,0:T(8,128)(2,1)}, u32[]{:S(2)}) copy-start(bf16[256,128]{1,0:T(8,128)(2,1)} %param.14) | copy-start | bytes 196612
  1.4 5.0 %copy-start.34 = (f32[16]{0:T(128)}, f32[16]{0:T(128)S(1)}, u32[]{:S(2)}) copy-start(f32[16]{0:T(128)S(1)} %exponential_negate_fusion) | copy-start | bytes 196
  3.4 5.0 %copy-start.31 = (f32[256]{0:T(256)}, f32[256]{0:T(256)S(1)}, u32[]{:S(2)}) copy-start(f32[256]{0:T(256)S(1)} %get-tuple-element.159) | copy-start | bytes 3076
  6.3 2.2 %copy-start.14 = (f32[16,256]{1,0:T(8,128)}, f32[16,256]{1,0:T(8,128)S(1)}, u32[]{:S(2)}) copy-start(f32[16,256]{1,0:T(8,128)S(1)} %fusion.81) | copy-start | bytes 49156
  6.6 1.9 %copy-start.28 = (f32[16]{0:T(128)}, f32[16]{0:T(128)S(1)}, u32[]{:S(2)}) copy-start(f32[16]{0:T(128)S(1)} %get-tuple-element.169) | copy-start | bytes 196
  7.9 2.9 %copy-start.24 = (f32[256]{0:T(256)}, f32[256]{0:T(256)S(1)}, u32[]{:S(2)}) copy-start(f32[256]{0:T(256)S(1)} %compare_convert_fusion.1) | copy-start | bytes 3076
  8.0 0.6 copy-start.10
  8.6 2.1 %collective-permute-start.1 = (f32[1,8,64,128]{3,2,1,0:T(8,128)S(1)}, f32[1,8,64,128]{3,2,1,0:T(8,128)S(1)}, u32[]{:S(2)}, u32[]{:S(2)}) collective-permute-start(f32[1,8,64,128]{3,2,1,0:T(8,128)S(1)} %dynamic-slice_bitcast_fusion.1), channel_id=1, source_target_pairs={{0,8},{8,0},{16,24},{24,16},{32,40},{40,32},{48,56},{56,48},{64,72... | collective-permute-start | bytes 786440 | tf_op jit(solution)/shard_map/ppermute | solution.py:44
  9.4 1.3 collective-permute-start
  10.7 41.5 %copy-start.30 = (f32[8]{0:T(128)}, f32[8]{0:T(128)S(1)}, u32[]{:S(2)}) copy-start(f32[8]{0:T(128)S(1)} %get-tuple-element.205) | copy-start | bytes 100
  10.8 10.4 %collective-permute-start.2 = (f32[1,8,64,128]{3,2,1,0:T(8,128)S(1)}, f32[1,8,64,128]{3,2,1,0:T(8,128)S(1)}, u32[]{:S(2)}, u32[]{:S(2)}) collective-permute-start(f32[1,8,64,128]{3,2,1,0:T(8,128)S(1)} %fusion.75), channel_id=1, source_target_pairs={{0,16},{8,24},{16,32},{24,40},{32,48},{40,56},{48,64},{56,72},{64,... | collective-permute-start | bytes 786440 | tf_op jit(solution)/shard_map/ppermute | solution.py:44
  21.3 12.0 %collective-permute-start.4 = (f32[1,8,64,128]{3,2,1,0:T(8,128)S(1)}, f32[1,8,64,128]{3,2,1,0:T(8,128)S(1)}, u32[]{:S(2)}, u32[]{:S(2)}) collective-permute-start(f32[1,8,64,128]{3,2,1,0:T(8,128)S(1)} %multiply_add_fusion.11), channel_id=1, source_target_pairs={{0,32},{8,40},{16,48},{24,56},{32,64},{40,72},{48,80},{56,88},{64,... | collective-permute-start | bytes 786440 | tf_op jit(solution)/shard_map/ppermute | solution.py:44
  25.7 7.7 %collective-permute-start.3 = (f32[1,8]{1,0:T(1,128)S(1)}, f32[1,8]{1,0:T(1,128)S(1)}, u32[]{:S(2)}, u32[]{:S(2)}) collective-permute-start(f32[1,8]{1,0:T(1,128)S(1)} %get-tuple-element.204), channel_id=1, source_target_pairs={{0,16},{8,24},{16,32},{24,40},{32,48},{40,56},{48,64},{56,72},{64,... | collective-permute-start | bytes 104 | tf_op jit(solution)/shard_map/ppermute | solution.py:44
  33.5 10.8 %collective-permute-start.6 = (f32[1,8,64,128]{3,2,1,0:T(8,128)S(1)}, f32[1,8,64,128]{3,2,1,0:T(8,128)S(1)}, u32[]{:S(2)}, u32[]{:S(2)}) collective-permute-start(f32[1,8,64,128]{3,2,1,0:T(8,128)S(1)} %multiply_add_fusion.10), channel_id=1, source_target_pairs={{0,64},{8,72},{16,80},{24,88},{32,96},{40,104},{48,112},{56,120},{... | collective-permute-start | bytes 786440 | tf_op jit(solution)/shard_map/ppermute | solution.py:44
  37.1 15.4 %copy-start.8 = (f32[256,256]{1,0:T(8,128)}, f32[256,256]{1,0:T(8,128)S(1)}, u32[]{:S(2)}) copy-start(f32[256,256]{1,0:T(8,128)S(1)} %fusion.82) | copy-start | bytes 786436
  37.3 15.2 %copy-start.6 = (f32[256,256]{1,0:T(8,128)}, f32[256,256]{1,0:T(8,128)S(1)}, u32[]{:S(2)}) copy-start(f32[256,256]{1,0:T(8,128)S(1)} %fusion.136) | copy-start | bytes 786436
  37.3 7.0 %collective-permute-start.5 = (f32[1,8]{1,0:T(1,128)S(1)}, f32[1,8]{1,0:T(1,128)S(1)}, u32[]{:S(2)}, u32[]{:S(2)}) collective-permute-start(f32[1,8]{1,0:T(1,128)S(1)} %mul.702), channel_id=1, source_target_pairs={{0,32},{8,40},{16,48},{24,56},{32,64},{40,72},{48,80},{56,88},{64,... | collective-permute-start | bytes 104 | tf_op jit(solution)/shard_map/ppermute | solution.py:44
  44.4 7.8 %collective-permute-start.8 = (f32[1,8,64,128]{3,2,1,0:T(8,128)S(1)}, f32[1,8,64,128]{3,2,1,0:T(8,128)S(1)}, u32[]{:S(2)}, u32[]{:S(2)}) collective-permute-start(f32[1,8,64,128]{3,2,1,0:T(8,128)S(1)} %multiply_add_fusion.9), channel_id=1, source_target_pairs={{0,128},{8,136},{16,144},{24,152},{32,160},{40,168},{48,176},{56,1... | collective-permute-start | bytes 786440 | tf_op jit(solution)/shard_map/ppermute | solution.py:44
  48.3 4.1 %copy-start.22 = (f32[16,256]{1,0:T(8,128)}, f32[16,256]{1,0:T(8,128)S(1)}, u32[]{:S(2)}) copy-start(f32[16,256]{1,0:T(8,128)S(1)} %fusion.134) | copy-start | bytes 49156
  48.4 3.8 %collective-permute-start.7 = (f32[1,8]{1,0:T(1,128)S(1)}, f32[1,8]{1,0:T(1,128)S(1)}, u32[]{:S(2)}, u32[]{:S(2)}) collective-permute-start(f32[1,8]{1,0:T(1,128)S(1)} %mul.710), channel_id=1, source_target_pairs={{0,64},{8,72},{16,80},{24,88},{32,96},{40,104},{48,112},{56,120},{... | collective-permute-start | bytes 104 | tf_op jit(solution)/shard_map/ppermute | solution.py:44
  52.2 0.7 copy-start.15
  52.3 2.7 %copy-start.33 = (f32[16]{0:T(128)S(1)}, f32[16]{0:T(128)}, u32[]{:S(2)}) copy-start(f32[16]{0:T(128)} %param.18) | copy-start | bytes 196
  52.4 4.2 %collective-permute-start.9 = (f32[1,8,64,128]{3,2,1,0:T(8,128)S(1)}, f32[1,8,64,128]{3,2,1,0:T(8,128)S(1)}, u32[]{:S(2)}, u32[]{:S(2)}) collective-permute-start(f32[1,8,64,128]{3,2,1,0:T(8,128)S(1)} %get-tuple-element.161), channel_id=1, source_target_pairs={{0,8},{8,0},{16,24},{24,16},{32,40},{40,32},{48,56},{56,48},{64,72... | collective-permute-start | bytes 786440 | tf_op jit(solution)/shard_map/ppermute | solution.py:44
  56.6 1.4 copy-start.3
  58.0 1.0 copy-start.1
  82.4 2.5 %collective-permute-start.11 = (f32[1,8,64,128]{3,2,1,0:T(8,128)}, f32[1,8,64,128]{3,2,1,0:T(8,128)}, u32[]{:S(2)}, u32[]{:S(2)}) collective-permute-start(f32[1,8,64,128]{3,2,1,0:T(8,128)} %dynamic-slice_bitcast_fusion), channel_id=1, source_target_pairs={{248,240},{240,248},{232,224},{224,232},{216,208},{208,216},{200,1... | collective-permute-start | bytes 786440 | tf_op jit(solution)/shard_map/ppermute | solution.py:44
  82.4 1.9 %collective-permute-start.10 = (f32[1,8]{1,0:T(1,128)}, f32[1,8]{1,0:T(1,128)}, u32[]{:S(2)}, u32[]{:S(2)}) collective-permute-start(f32[1,8]{1,0:T(1,128)} %bitcast.128), channel_id=1, source_target_pairs={{248,240},{240,248},{232,224},{224,232},{216,208},{208,216},{200,1... | collective-permute-start | bytes 104 | tf_op jit(solution)/shard_map/ppermute | solution.py:44
  83.0 33.5 %copy-start.7 = (f32[256,256]{1,0:T(8,128)S(1)}, f32[256,256]{1,0:T(8,128)}, u32[]{:S(2)}) copy-start(f32[256,256]{1,0:T(8,128)} %copy-done.6) | copy-start | bytes 786436
  83.0 33.5 %copy-start.9 = (f32[256,256]{1,0:T(8,128)S(1)}, f32[256,256]{1,0:T(8,128)}, u32[]{:S(2)}) copy-start(f32[256,256]{1,0:T(8,128)} %copy-done.8) | copy-start | bytes 786436
  83.0 33.5 %copy-start.16 = (f32[16,256]{1,0:T(8,128)S(1)}, f32[16,256]{1,0:T(8,128)}, u32[]{:S(2)}) copy-start(f32[16,256]{1,0:T(8,128)} %copy-done.14) | copy-start | bytes 49156
  83.0 33.5 %copy-start.23 = (f32[16,256]{1,0:T(8,128)S(1)}, f32[16,256]{1,0:T(8,128)}, u32[]{:S(2)}) copy-start(f32[16,256]{1,0:T(8,128)} %copy-done.22) | copy-start | bytes 49156
  86.0 28.2 %collective-permute-start.12 = (f32[1,8,64,128]{3,2,1,0:T(8,128)S(1)}, f32[1,8,64,128]{3,2,1,0:T(8,128)S(1)}, u32[]{:S(2)}, u32[]{:S(2)}) collective-permute-start(f32[1,8,64,128]{3,2,1,0:T(8,128)S(1)} %fusion.74), channel_id=1, source_target_pairs={{248,232},{240,224},{232,216},{224,208},{216,200},{208,192},{200,1... | collective-permute-start | bytes 786440 | tf_op jit(solution)/shard_map/ppermute | solution.py:44
  88.8 12.1 %collective-permute-start.13 = (f32[1,8]{1,0:T(1,128)S(1)}, f32[1,8]{1,0:T(1,128)S(1)}, u32[]{:S(2)}, u32[]{:S(2)}) collective-permute-start(f32[1,8]{1,0:T(1,128)S(1)} %get-tuple-element.193), channel_id=1, source_target_pairs={{248,232},{240,224},{232,216},{224,208},{216,200},{208,192},{200,1... | collective-permute-start | bytes 104 | tf_op jit(solution)/shard_map/ppermute | solution.py:44
  100.9 7.9 %collective-permute-start.15 = (f32[1,8]{1,0:T(1,128)S(1)}, f32[1,8]{1,0:T(1,128)S(1)}, u32[]{:S(2)}, u32[]{:S(2)}) collective-permute-start(f32[1,8]{1,0:T(1,128)S(1)} %mul.755), channel_id=1, source_target_pairs={{248,216},{240,208},{232,200},{224,192},{216,184},{208,176},{200,1... | collective-permute-start | bytes 104 | tf_op jit(solution)/shard_map/ppermute | solution.py:44
  108.8 5.5 %collective-permute-start.17 = (f32[1,8]{1,0:T(1,128)S(1)}, f32[1,8]{1,0:T(1,128)S(1)}, u32[]{:S(2)}, u32[]{:S(2)}) collective-permute-start(f32[1,8]{1,0:T(1,128)S(1)} %mul.763), channel_id=1, source_target_pairs={{248,184},{240,176},{232,168},{224,160},{216,152},{208,144},{200,1... | collective-permute-start | bytes 104 | tf_op jit(solution)/shard_map/ppermute | solution.py:44
  114.3 10.7 %collective-permute-start.14 = (f32[1,8,64,128]{3,2,1,0:T(8,128)S(1)}, f32[1,8,64,128]{3,2,1,0:T(8,128)S(1)}, u32[]{:S(2)}, u32[]{:S(2)}) collective-permute-start(f32[1,8,64,128]{3,2,1,0:T(8,128)S(1)} %multiply_add_fusion.6), channel_id=1, source_target_pairs={{248,216},{240,208},{232,200},{224,192},{216,184},{208,176},{200,1... | collective-permute-start | bytes 786440 | tf_op jit(solution)/shard_map/ppermute | solution.py:44
  122.7 3.9 %copy-start.4 = (f32[1,8,64,128]{3,2,1,0:T(8,128)S(1)}, f32[1,8,64,128]{3,2,1,0:T(8,128)}, u32[]{:S(2)}) copy-start(f32[1,8,64,128]{3,2,1,0:T(8,128)} %copy-done.3) | copy-start | bytes 786436
  125.1 3.1 %copy-start.2 = (f32[1,256,1,16,64]{1,4,3,2,0:T(8,128)S(1)}, f32[1,256,1,16,64]{1,4,3,2,0:T(8,128)}, u32[]{:S(2)}) copy-start(f32[1,256,1,16,64]{1,4,3,2,0:T(8,128)} %get-tuple-element.214) | copy-start | bytes 3145732
  125.1 8.4 %collective-permute-start.16 = (f32[1,8,64,128]{3,2,1,0:T(8,128)S(1)}, f32[1,8,64,128]{3,2,1,0:T(8,128)S(1)}, u32[]{:S(2)}, u32[]{:S(2)}) collective-permute-start(f32[1,8,64,128]{3,2,1,0:T(8,128)S(1)} %multiply_add_fusion.5), channel_id=1, source_target_pairs={{248,184},{240,176},{232,168},{224,160},{216,152},{208,144},{200,1... | collective-permute-start | bytes 786440 | tf_op jit(solution)/shard_map/ppermute | solution.py:44
  133.6 9.8 %collective-permute-start.18 = (f32[1,8,64,128]{3,2,1,0:T(8,128)S(1)}, f32[1,8,64,128]{3,2,1,0:T(8,128)S(1)}, u32[]{:S(2)}, u32[]{:S(2)}) collective-permute-start(f32[1,8,64,128]{3,2,1,0:T(8,128)S(1)} %multiply_add_fusion.4), channel_id=1, source_target_pairs={{248,120},{240,112},{232,104},{224,96},{216,88},{208,80},{200,72},... | collective-permute-start | bytes 786440 | tf_op jit(solution)/shard_map/ppermute | solution.py:44
  144.5 2.2 %collective-permute-start.19 = (f32[1,8,64,128]{3,2,1,0:T(8,128)S(1)}, f32[1,8,64,128]{3,2,1,0:T(8,128)S(1)}, u32[]{:S(2)}, u32[]{:S(2)}) collective-permute-start(f32[1,8,64,128]{3,2,1,0:T(8,128)S(1)} %get-tuple-element.156), channel_id=1, source_target_pairs={{248,240},{240,248},{232,224},{224,232},{216,208},{208,216},{200,1... | collective-permute-start | bytes 786440 | tf_op jit(solution)/shard_map/ppermute | solution.py:44
  145.6 2.1 %copy-start.11 = (f32[256,16]{0,1:T(8,128)S(1)}, f32[256,16]{0,1:T(8,128)}, u32[]{:S(2)}) copy-start(f32[256,16]{0,1:T(8,128)} %copy-done.10) | copy-start | bytes 49156
  146.7 0.7 copy-start.17
  146.7 0.8 copy-start.21
  146.7 0.8 copy-start.32
  146.7 0.8 copy-start.35
  146.7 0.8 copy-start.37
  146.7 0.8 copy-start.38
  146.7 0.8 copy-start.39
  146.7 1.0 copy-start.19
  152.2 1.6 %copy-start.20 = (f32[1024]{0:T(1024)S(1)}, f32[1024]{0:T(1024)}, u32[]{:S(2)}) copy-start(f32[1024]{0:T(1024)} %mul.726) | copy-start | bytes 12292
  153.8 1.1 copy-start.13
  153.8 1.1 copy-start.18
  153.8 1.0 copy-start.25
  153.8 1.0 copy-start.27
  153.9 1.0 copy-start.29
  153.9 1.3 copy-start.36

commit v11 on v10

--- a/solution.py
+++ b/solution.py
@@ -77,6 +77,25 @@
     return jnp.sum(lax.all_to_all(spread, axis, 0, 0), axis=0)
 
 
+@jax.custom_vjp
+def mix_apply(weights, x_span):
+    return jnp.einsum("ghts,sghp->tghp", weights, x_span, precision=MIX_PRECISION)
+
+
+def mix_apply_fwd(weights, x_span):
+    return mix_apply(weights, x_span), (weights, x_span)
+
+
+def mix_apply_bwd(saved, grad):
+    weights, x_span = saved
+    grad_weights = jnp.einsum("tghp,sghp->ghts", grad, x_span, precision=MIX_PRECISION)
+    grad_x = jnp.einsum("ghts,tghp->sghp", weights, grad, precision=MIX_PRECISION)
+    return grad_weights, grad_x
+
+
+mix_apply.defvjp(mix_apply_fwd, mix_apply_bwd)
+
+
 def span_mix(x_span, dt_span, b_span, c_span, log_cum, segment):
     log_rows = jnp.moveaxis(log_cum, 0, -1)
     spread = log_rows[..., :, None] - log_rows[..., None, :]
@@ -87,7 +106,7 @@
     masked = jnp.exp(jnp.minimum(spread, 0.0)) * keep_mask
     scores = jnp.einsum("tgn,sgn->gts", c_span, b_span, precision=MIX_PRECISION)
     weights = scores[:, None] * masked * jnp.moveaxis(dt_span, 0, -1)[..., None, :]
-    return jnp.einsum("ghts,sghp->tghp", weights, x_span, precision=MIX_PRECISION)
+    return mix_apply(weights, x_span)
 
 
 def block_decays(dt_spans, segment, decay_rate):

time: 157 us -> 157 us (level)
  no operation moved by 1% of the time
where the time goes in v11:
time: 157 us; the launch traced here: 156 us
  waiting for transfers between devices  47.9 us (31%)
  starting transfers between devices  40.9 us (26%)
  matrix products  23.3 us (15%)
  other arithmetic  16.2 us (10%)
  blocking collectives  16 us (10%)
  local copies, waits for them, and re-layouts  8.91 us (6%)
  between operations  2.79 us (2%)
    ppermute x20, waiting for transfers between devices, move(): return lax.ppermute(tree, axis, [(device(a), device(b)) for a, b in pairs])  47.9 us
    ppermute x20, starting transfers between devices, move(): return lax.ppermute(tree, axis, [(device(a), device(b)) for a, b in pairs])  40.9 us
    all_to_all x1, blocking collectives, head_sum(): return jnp.sum(lax.all_to_all(spread, axis, 0, 0), axis=0)  16 us
    dot_general x3, matrix products, span_mix(): return mix_apply(weights, x_span)  11.6 us
    dot_general x3, matrix products, local_states(): jnp.einsum('kqgh,kqghp,kqgn->kghpn', tail_decay * dt_spans, x_spans, b_sp...  4.77 us
    dot_general x3, matrix products, output_part(): jnp.einsum('kqgn,kghpn->kqghp', c_spans, full_start, precision=MIX_PRECIS...  3.55 us
  transfers between devices with their start and end apart: 20, of which 12 were waited for; matrix products, arithmetic and copies ran while one was open for 12% of the time, Pallas kernels for 0%

profile of v11, /device:TPU:6, one launch (start us, length us, event | category | flops | bytes accessed | tf_op | source)
XLA Modules:
  0.0 156.1 jit_solution(6832108625878021647)
XLA Ops:
  0.7 0.7 exponential_negate_fusion
  1.4 1.0 reduce-window.6
  2.6 0.6 slice.28
  3.5 0.6 slice.29
  5.4 0.9 fusion.81
  6.6 1.2 copy.37
  8.0 0.4 fusion.34
  8.7 0.7 dynamic-slice_reduce_fusion.1
  9.4 0.5 collective-permute-start
  9.9 0.8 collective-permute-done
  10.8 3.4 %collective-permute-start.2 = (f32[1,8,64,128]{3,2,1,0:T(8,128)S(1)}, f32[1,8,64,128]{3,2,1,0:T(8,128)S(1)}, u32[]{:S(2)}, u32[]{:S(2)}) collective-permute-start(f32[1,8,64,128]{3,2,1,0:T(8,128)S(1)} %fusion.75), channel_id=1, source_target_pairs={{0,16},{8,24},{16,32},{24,40},{32,48},{40,56},{48,64},{56,72},{64,... | collective-permute-start | bytes 786440 | tf_op jit(solution)/shard_map/ppermute | solution.py:44
  14.2 7.0 %collective-permute-done.2 = f32[1,8,64,128]{3,2,1,0:T(8,128)S(1)} collective-permute-done((f32[1,8,64,128]{3,2,1,0:T(8,128)S(1)}, f32[1,8,64,128]{3,2,1,0:T(8,128)S(1)}, u32[]{:S(2)}, u32[]{:S(2)}) %collective-permute-start.2) | collective-permute-done | bytes 262176 | tf_op jit(solution)/shard_map/ppermute | solution.py:44
  21.3 4.3 %collective-permute-start.4 = (f32[1,8,64,128]{3,2,1,0:T(8,128)S(1)}, f32[1,8,64,128]{3,2,1,0:T(8,128)S(1)}, u32[]{:S(2)}, u32[]{:S(2)}) collective-permute-start(f32[1,8,64,128]{3,2,1,0:T(8,128)S(1)} %multiply_add_fusion.11), channel_id=1, source_target_pairs={{0,32},{8,40},{16,48},{24,56},{32,64},{40,72},{48,80},{56,88},{64,... | collective-permute-start | bytes 786440 | tf_op jit(solution)/shard_map/ppermute | solution.py:44
  25.7 4.0 %collective-permute-start.3 = (f32[1,8]{1,0:T(1,128)S(1)}, f32[1,8]{1,0:T(1,128)S(1)}, u32[]{:S(2)}, u32[]{:S(2)}) collective-permute-start(f32[1,8]{1,0:T(1,128)S(1)} %get-tuple-element.204), channel_id=1, source_target_pairs={{0,16},{8,24},{16,32},{24,40},{32,48},{40,56},{48,64},{56,72},{64,... | collective-permute-start | bytes 104 | tf_op jit(solution)/shard_map/ppermute | solution.py:44
  29.7 3.7 %collective-permute-done.3 = f32[1,8]{1,0:T(1,128)S(1)} collective-permute-done((f32[1,8]{1,0:T(1,128)S(1)}, f32[1,8]{1,0:T(1,128)S(1)}, u32[]{:S(2)}, u32[]{:S(2)}) %collective-permute-start.3) | collective-permute-done | bytes 64 | tf_op jit(solution)/shard_map/ppermute | solution.py:44
  33.5 3.5 %collective-permute-start.6 = (f32[1,8,64,128]{3,2,1,0:T(8,128)S(1)}, f32[1,8,64,128]{3,2,1,0:T(8,128)S(1)}, u32[]{:S(2)}, u32[]{:S(2)}) collective-permute-start(f32[1,8,64,128]{3,2,1,0:T(8,128)S(1)} %multiply_add_fusion.10), channel_id=1, source_target_pairs={{0,64},{8,72},{16,80},{24,88},{32,96},{40,104},{48,112},{56,120},{... | collective-permute-start | bytes 786440 | tf_op jit(solution)/shard_map/ppermute | solution.py:44
  37.3 4.3 %collective-permute-start.5 = (f32[1,8]{1,0:T(1,128)S(1)}, f32[1,8]{1,0:T(1,128)S(1)}, u32[]{:S(2)}, u32[]{:S(2)}) collective-permute-start(f32[1,8]{1,0:T(1,128)S(1)} %mul.702), channel_id=1, source_target_pairs={{0,32},{8,40},{16,48},{24,56},{32,64},{40,72},{48,80},{56,88},{64,... | collective-permute-start | bytes 104 | tf_op jit(solution)/shard_map/ppermute | solution.py:44
  41.6 2.7 %collective-permute-done.5 = f32[1,8]{1,0:T(1,128)S(1)} collective-permute-done((f32[1,8]{1,0:T(1,128)S(1)}, f32[1,8]{1,0:T(1,128)S(1)}, u32[]{:S(2)}, u32[]{:S(2)}) %collective-permute-start.5) | collective-permute-done | bytes 64 | tf_op jit(solution)/shard_map/ppermute | solution.py:44
  44.4 3.9 %collective-permute-start.8 = (f32[1,8,64,128]{3,2,1,0:T(8,128)S(1)}, f32[1,8,64,128]{3,2,1,0:T(8,128)S(1)}, u32[]{:S(2)}, u32[]{:S(2)}) collective-permute-start(f32[1,8,64,128]{3,2,1,0:T(8,128)S(1)} %multiply_add_fusion.9), channel_id=1, source_target_pairs={{0,128},{8,136},{16,144},{24,152},{32,160},{40,168},{48,176},{56,1... | collective-permute-start | bytes 786440 | tf_op jit(solution)/shard_map/ppermute | solution.py:44
  48.4 1.3 collective-permute-start.7
  49.7 2.5 %collective-permute-done.7 = f32[1,8]{1,0:T(1,128)S(1)} collective-permute-done((f32[1,8]{1,0:T(1,128)S(1)}, f32[1,8]{1,0:T(1,128)S(1)}, u32[]{:S(2)}, u32[]{:S(2)}) %collective-permute-start.7) | collective-permute-done | bytes 64 | tf_op jit(solution)/shard_map/ppermute | solution.py:44
  52.5 0.4 copy-done.15
  52.9 2.2 %fusion.29 = f32[1,256,1,16,64]{1,4,3,2,0:T(8,128)S(1)} fusion(bf16[256,16,64]{0,2,1:T(8,128)(2,1)S(1)} %bitcast.314, f32[16,256]{1,0:T(8,128)S(1)} %fusion.134, f32[256,256]{1,0:T(8,128)S(1)} %fusion.82, f32[16,256]{1,0:T(8,128)S(1)} %copy-done.15, f32[256,256]{1,0:T(8,128)S(1)} %fusion.136), kind=kOutput, calls=%fused_computation.33 | convolution fusion | flops 407896064 | bytes 2129920 | tf_op jit(solution)/shard_map/jvp()/while/body/eval_jaxpr/ghts,sghp->tghp/dot_general | solution.py:109
  55.1 0.7 mul.726
  55.8 0.8 fusion.78
  56.6 1.4 multiply_add_fusion.1
  58.0 0.3 copy.38
  58.3 0.7 copy-done.1
  59.0 2.6 %multiply_reduce_fusion.2 = (f32[256]{0:T(256)S(1)}, f32[256]{0:T(256)S(1)}, f32[256,1024]{1,0:T(8,128)}) fusion(bf16[256,1024]{1,0:T(8,128)(2,1)} %param.21, f32[1024]{0:T(1024)} %param.19, bf16[256,1024]{1,0:T(8,128)(2,1)} %param.12, f32[256,1024]{1,0:T(8,128)S(1)} %copy.38, f32[1024]{0:T(1024)} %mul.726, bf16[256,1024]{1,0:T(8,128)(2,1)S(1)} %copy-done.1), kind=kLoop, calls=%fused_computation.76 | loop fusion | flops 3931648 | bytes 3680256 | tf_op jit(solution)/shard_map/reduce_sum | solution.py:223
  61.7 16.0 %all_to_all.5 = f32[8,2,256]{2,1,0:T(2,128)S(1)} all-to-all(f32[8,2,256]{2,1,0:T(2,128)S(1)} %broadcast_in_dim.151), channel_id=1, replica_groups=mesh['ctx'=32,'head'=8] {'head'}, dimensions={0} | all-to-all | bytes 32768 | tf_op jit(solution)/shard_map/all_to_all | solution.py:77
  77.8 3.1 %fusion.55 = (bf16[256,1024]{1,0:T(8,128)(2,1)}, f32[256,1024]{1,0:T(8,128)S(1)}) fusion(bf16[256,1024]{1,0:T(8,128)(2,1)} %param.12, f32[256,1024]{1,0:T(8,128)S(1)} %copy.38, bf16[256,1024]{1,0:T(8,128)(2,1)S(1)} %copy-done.1, f32[256]{0:T(256)S(1)} %multiply_multiply_fusion, f32[256,1024]{1,0:T(8,128)} %get-tuple-element.158, ...), kind=kLoop, calls=%fused_computation.63 | loop fusion | flops 5767168 | bytes 5253120 | tf_op jit(solution)/shard_map/convert_element_type | solution.py:249
  80.9 0.3 copy.40
  81.3 0.4 fusion.57
  81.7 0.7 dynamic-slice_bitcast_fusion
  82.4 0.5 collective-permute-start.10
  83.0 1.4 collective-permute-done.10
  84.3 0.7 fusion.131
  85.0 1.0 fusion.74
  86.0 2.7 %collective-permute-start.12 = (f32[1,8,64,128]{3,2,1,0:T(8,128)S(1)}, f32[1,8,64,128]{3,2,1,0:T(8,128)S(1)}, u32[]{:S(2)}, u32[]{:S(2)}) collective-permute-start(f32[1,8,64,128]{3,2,1,0:T(8,128)S(1)} %fusion.74), channel_id=1, source_target_pairs={{248,232},{240,224},{232,216},{224,208},{216,200},{208,192},{200,1... | collective-permute-start | bytes 786440 | tf_op jit(solution)/shard_map/ppermute | solution.py:44
  88.8 4.2 %collective-permute-start.13 = (f32[1,8]{1,0:T(1,128)S(1)}, f32[1,8]{1,0:T(1,128)S(1)}, u32[]{:S(2)}, u32[]{:S(2)}) collective-permute-start(f32[1,8]{1,0:T(1,128)S(1)} %get-tuple-element.193), channel_id=1, source_target_pairs={{248,232},{240,224},{232,216},{224,208},{216,200},{208,192},{200,1... | collective-permute-start | bytes 104 | tf_op jit(solution)/shard_map/ppermute | solution.py:44
  93.0 7.9 %collective-permute-done.13 = f32[1,8]{1,0:T(1,128)S(1)} collective-permute-done((f32[1,8]{1,0:T(1,128)S(1)}, f32[1,8]{1,0:T(1,128)S(1)}, u32[]{:S(2)}, u32[]{:S(2)}) %collective-permute-start.13) | collective-permute-done | bytes 64 | tf_op jit(solution)/shard_map/ppermute | solution.py:44
  100.9 1.9 %collective-permute-start.15 = (f32[1,8]{1,0:T(1,128)S(1)}, f32[1,8]{1,0:T(1,128)S(1)}, u32[]{:S(2)}, u32[]{:S(2)}) collective-permute-start(f32[1,8]{1,0:T(1,128)S(1)} %mul.755), channel_id=1, source_target_pairs={{248,216},{240,208},{232,200},{224,192},{216,184},{208,176},{200,1... | collective-permute-start | bytes 104 | tf_op jit(solution)/shard_map/ppermute | solution.py:44
  102.8 5.9 %collective-permute-done.15 = f32[1,8]{1,0:T(1,128)S(1)} collective-permute-done((f32[1,8]{1,0:T(1,128)S(1)}, f32[1,8]{1,0:T(1,128)S(1)}, u32[]{:S(2)}, u32[]{:S(2)}) %collective-permute-start.15) | collective-permute-done | bytes 64 | tf_op jit(solution)/shard_map/ppermute | solution.py:44
  108.8 1.3 collective-permute-start.17
  110.1 4.2 %collective-permute-done.17 = f32[1,8]{1,0:T(1,128)S(1)} collective-permute-done((f32[1,8]{1,0:T(1,128)S(1)}, f32[1,8]{1,0:T(1,128)S(1)}, u32[]{:S(2)}, u32[]{:S(2)}) %collective-permute-start.17) | collective-permute-done | bytes 64 | tf_op jit(solution)/shard_map/ppermute | solution.py:44
  114.3 2.1 %collective-permute-start.14 = (f32[1,8,64,128]{3,2,1,0:T(8,128)S(1)}, f32[1,8,64,128]{3,2,1,0:T(8,128)S(1)}, u32[]{:S(2)}, u32[]{:S(2)}) collective-permute-start(f32[1,8,64,128]{3,2,1,0:T(8,128)S(1)} %multiply_add_fusion.6), channel_id=1, source_target_pairs={{248,216},{240,208},{232,200},{224,192},{216,184},{208,176},{200,1... | collective-permute-start | bytes 786440 | tf_op jit(solution)/shard_map/ppermute | solution.py:44
  116.5 6.2 %fusion.73 = (f32[16,256]{1,0:T(8,128)}, f32[16,256]{1,0:T(8,128)}, f32[16,256]{1,0:T(8,128)}, f32[256,256]{1,0:T(8,128)S(1)}) fusion(f32[16,256]{1,0:T(8,128)S(1)} %copy-done.16, f32[256,256]{1,0:T(8,128)S(1)} %copy-done.9, f32[16,256]{1,0:T(8,128)S(1)} %copy-done.23, f32[256,256]{1,0:T(8,128)S(1)} %copy-done.7, bf16[256,16,64]{0,2,1:T(8,128)(2,1)S(1)} %bitcast.315, ...), kind=kOutput, calls=%fused_computation.95 | convolution fusion | flops 422498304 | bytes 2441216 | tf_op jit(solution)/shard_map/transpose(jvp())/while/body/eval_jaxpr/tghp,sghp->ghts/dot_general | solution.py:109
  122.9 2.1 %collective-permute-done.14 = f32[1,8,64,128]{3,2,1,0:T(8,128)S(1)} collective-permute-done((f32[1,8,64,128]{3,2,1,0:T(8,128)S(1)}, f32[1,8,64,128]{3,2,1,0:T(8,128)S(1)}, u32[]{:S(2)}, u32[]{:S(2)}) %collective-permute-start.14) | collective-permute-done | bytes 262176 | tf_op jit(solution)/shard_map/ppermute | solution.py:44
  125.1 1.4 collective-permute-start.16
  126.6 1.7 %fusion.37 = f32[1,256,1,128]{3,1,2,0:T(8,128)} fusion(f32[256,128]{1,0:T(8,128)S(1)} %fusion.137, f32[1,256,1,16,64]{1,4,3,2,0:T(8,128)S(1)} %bitcast.310, f32[256,16]{0,1:T(8,128)S(1)} %get-tuple-element.167, f32[8,64,128]{2,1,0:T(8,128)S(1)} %bitcast.318, f32[8,64,128]{2,1,0:T(8,128)S(1)} %bitcast.324, pred[]{:T(512)S(6)} %eq.79), kind=kOutput, calls=%fused_computation.43 | convolution fusion | flops 202014720 | bytes 1851393 | tf_op jit(solution)/shard_map/transpose(jvp(kqgn,kghpn->kqghp))/dot_general | solution.py:163
  128.2 0.8 multiply_reduce_fusion
  129.0 4.5 %collective-permute-done.16 = f32[1,8,64,128]{3,2,1,0:T(8,128)S(1)} collective-permute-done((f32[1,8,64,128]{3,2,1,0:T(8,128)S(1)}, f32[1,8,64,128]{3,2,1,0:T(8,128)S(1)}, u32[]{:S(2)}, u32[]{:S(2)}) %collective-permute-start.16) | collective-permute-done | bytes 262176 | tf_op jit(solution)/shard_map/ppermute | solution.py:44
  133.6 1.3 collective-permute-start.18
  134.9 3.2 %fusion.26 = f32[1,256,1,16,64]{1,4,3,2,0:T(8,128)} fusion(f32[16,256]{1,0:T(8,128)S(1)} %copy-done.23, f32[256,256]{1,0:T(8,128)S(1)} %copy-done.9, f32[16,256]{1,0:T(8,128)S(1)} %copy-done.16, f32[256,256]{1,0:T(8,128)S(1)} %copy-done.7, f32[1,256,1,16,64]{1,4,3,2,0:T(8,128)S(1)} %bitcast.312), kind=kOutput, calls=%fused_computation.30 | convolution fusion | flops 407896064 | bytes 2654208 | tf_op jit(solution)/shard_map/transpose(jvp())/while/body/eval_jaxpr/ghts,tghp->sghp/dot_general | solution.py:109
  138.2 5.2 %collective-permute-done.18 = f32[1,8,64,128]{3,2,1,0:T(8,128)S(1)} collective-permute-done((f32[1,8,64,128]{3,2,1,0:T(8,128)S(1)}, f32[1,8,64,128]{3,2,1,0:T(8,128)S(1)}, u32[]{:S(2)}, u32[]{:S(2)}) %collective-permute-start.18) | collective-permute-done | bytes 262176 | tf_op jit(solution)/shard_map/ppermute | solution.py:44
  143.4 1.1 fusion.77
  144.6 1.0 convolution_bitcast_fusion.2
  145.6 1.1 fusion.76
  146.8 0.3 multiply_reduce_fusion.3
  147.8 1.7 %fusion.39 = f32[256,128]{1,0:T(8,128)} fusion(f32[1,256,1,128]{3,1,2,0:T(8,128)S(1)} %copy-done.19, bf16[256,16,64]{0,2,1:T(8,128)(2,1)S(1)} %bitcast.316, f32[256,16]{0,1:T(8,128)S(1)} %copy-done.11, f32[8,64,128]{2,1,0:T(8,128)S(1)} %bitcast.321, f32[8,64,128]{2,1,0:T(8,128)S(1)} %bitcast.325, pred[]{:T(512)S(6)} %eq.86), kind=kOutput, calls=%fused_computation.45 | convolution fusion | flops 202276864 | bytes 1327105 | tf_op jit(solution)/shard_map/transpose(jvp(kqgh,kqghp,kqgn->kghpn))/dot_general | solution.py:128
  149.4 2.7 %bitcast_add_fusion = (f32[1,256,1,16,64]{1,4,3,2,0:T(8,128)}, f32[256,16,64]{0,2,1:T(8,128)S(1)}) fusion(f32[1,256,1,16,64]{1,4,3,2,0:T(8,128)} %fusion.26, f32[256,16]{0,1:T(8,128)S(1)} %copy-done.11, bf16[256,128]{1,0:T(8,128)(2,1)S(1)} %copy-done.5, f32[8,64,128]{2,1,0:T(8,128)S(1)} %bitcast.322, f32[8,64,128]{2,1,0:T(8,128)S(1)} %bitcast.326, pred[]{:T(512)S(6)} %eq.86), kind=kOutput, calls=%fused_computation.67 | convolution fusion | flops 202244096 | bytes 3751937 | tf_op jit(solution)/shard_map/transpose(jvp(kqgh,kqghp,kqgn->kghpn))/dot_general | solution.py:128
  152.2 1.6 copy.41
  153.9 1.0 add_convert_fusion
  155.2 0.9 fusion.45
  (132 shorter events, 4.1 us)
Async XLA Ops:
  0.6 36.5 %copy-start = (bf16[256,128]{1,0:T(8,128)(2,1)S(1)}, bf16[256,128]{1,0:T(8,128)(2,1)}, u32[]{:S(2)}) copy-start(bf16[256,128]{1,0:T(8,128)(2,1)} %param.15) | copy-start | bytes 196612
  0.6 7.2 %copy-start.26 = (f32[16]{0:T(128)S(1)}, f32[16]{0:T(128)}, u32[]{:S(2)}) copy-start(f32[16]{0:T(128)} %param.16) | copy-start | bytes 196
  0.7 7.2 %copy-start.12 = (f32[256,16]{0,1:T(8,128)S(1)}, f32[256,16]{0,1:T(8,128)}, u32[]{:S(2)}) copy-start(f32[256,16]{0,1:T(8,128)} %param.13) | copy-start | bytes 49156
  0.7 7.3 %copy-start.5 = (bf16[256,128]{1,0:T(8,128)(2,1)S(1)}, bf16[256,128]{1,0:T(8,128)(2,1)}, u32[]{:S(2)}) copy-start(bf16[256,128]{1,0:T(8,128)(2,1)} %param.14) | copy-start | bytes 196612
  1.4 5.0 %copy-start.34 = (f32[16]{0:T(128)}, f32[16]{0:T(128)S(1)}, u32[]{:S(2)}) copy-start(f32[16]{0:T(128)S(1)} %exponential_negate_fusion) | copy-start | bytes 196
  3.4 5.0 %copy-start.31 = (f32[256]{0:T(256)}, f32[256]{0:T(256)S(1)}, u32[]{:S(2)}) copy-start(f32[256]{0:T(256)S(1)} %get-tuple-element.159) | copy-start | bytes 3076
  6.3 2.2 %copy-start.14 = (f32[16,256]{1,0:T(8,128)}, f32[16,256]{1,0:T(8,128)S(1)}, u32[]{:S(2)}) copy-start(f32[16,256]{1,0:T(8,128)S(1)} %fusion.81) | copy-start | bytes 49156
  6.6 1.9 %copy-start.28 = (f32[16]{0:T(128)}, f32[16]{0:T(128)S(1)}, u32[]{:S(2)}) copy-start(f32[16]{0:T(128)S(1)} %get-tuple-element.169) | copy-start | bytes 196
  7.9 2.9 %copy-start.24 = (f32[256]{0:T(256)}, f32[256]{0:T(256)S(1)}, u32[]{:S(2)}) copy-start(f32[256]{0:T(256)S(1)} %compare_convert_fusion.1) | copy-start | bytes 3076
  8.0 0.6 copy-start.10
  8.6 2.1 %collective-permute-start.1 = (f32[1,8,64,128]{3,2,1,0:T(8,128)S(1)}, f32[1,8,64,128]{3,2,1,0:T(8,128)S(1)}, u32[]{:S(2)}, u32[]{:S(2)}) collective-permute-start(f32[1,8,64,128]{3,2,1,0:T(8,128)S(1)} %dynamic-slice_bitcast_fusion.1), channel_id=1, source_target_pairs={{0,8},{8,0},{16,24},{24,16},{32,40},{40,32},{48,56},{56,48},{64,72... | collective-permute-start | bytes 786440 | tf_op jit(solution)/shard_map/ppermute | solution.py:44
  9.4 1.3 collective-permute-start
  10.7 41.5 %copy-start.30 = (f32[8]{0:T(128)}, f32[8]{0:T(128)S(1)}, u32[]{:S(2)}) copy-start(f32[8]{0:T(128)S(1)} %get-tuple-element.205) | copy-start | bytes 100
  10.8 10.4 %collective-permute-start.2 = (f32[1,8,64,128]{3,2,1,0:T(8,128)S(1)}, f32[1,8,64,128]{3,2,1,0:T(8,128)S(1)}, u32[]{:S(2)}, u32[]{:S(2)}) collective-permute-start(f32[1,8,64,128]{3,2,1,0:T(8,128)S(1)} %fusion.75), channel_id=1, source_target_pairs={{0,16},{8,24},{16,32},{24,40},{32,48},{40,56},{48,64},{56,72},{64,... | collective-permute-start | bytes 786440 | tf_op jit(solution)/shard_map/ppermute | solution.py:44
  21.3 12.0 %collective-permute-start.4 = (f32[1,8,64,128]{3,2,1,0:T(8,128)S(1)}, f32[1,8,64,128]{3,2,1,0:T(8,128)S(1)}, u32[]{:S(2)}, u32[]{:S(2)}) collective-permute-start(f32[1,8,64,128]{3,2,1,0:T(8,128)S(1)} %multiply_add_fusion.11), channel_id=1, source_target_pairs={{0,32},{8,40},{16,48},{24,56},{32,64},{40,72},{48,80},{56,88},{64,... | collective-permute-start | bytes 786440 | tf_op jit(solution)/shard_map/ppermute | solution.py:44
  25.7 7.7 %collective-permute-start.3 = (f32[1,8]{1,0:T(1,128)S(1)}, f32[1,8]{1,0:T(1,128)S(1)}, u32[]{:S(2)}, u32[]{:S(2)}) collective-permute-start(f32[1,8]{1,0:T(1,128)S(1)} %get-tuple-element.204), channel_id=1, source_target_pairs={{0,16},{8,24},{16,32},{24,40},{32,48},{40,56},{48,64},{56,72},{64,... | collective-permute-start | bytes 104 | tf_op jit(solution)/shard_map/ppermute | solution.py:44
  33.5 10.8 %collective-permute-start.6 = (f32[1,8,64,128]{3,2,1,0:T(8,128)S(1)}, f32[1,8,64,128]{3,2,1,0:T(8,128)S(1)}, u32[]{:S(2)}, u32[]{:S(2)}) collective-permute-start(f32[1,8,64,128]{3,2,1,0:T(8,128)S(1)} %multiply_add_fusion.10), channel_id=1, source_target_pairs={{0,64},{8,72},{16,80},{24,88},{32,96},{40,104},{48,112},{56,120},{... | collective-permute-start | bytes 786440 | tf_op jit(solution)/shard_map/ppermute | solution.py:44
  37.1 15.4 %copy-start.8 = (f32[256,256]{1,0:T(8,128)}, f32[256,256]{1,0:T(8,128)S(1)}, u32[]{:S(2)}) copy-start(f32[256,256]{1,0:T(8,128)S(1)} %fusion.82) | copy-start | bytes 786436
  37.3 15.2 %copy-start.6 = (f32[256,256]{1,0:T(8,128)}, f32[256,256]{1,0:T(8,128)S(1)}, u32[]{:S(2)}) copy-start(f32[256,256]{1,0:T(8,128)S(1)} %fusion.136) | copy-start | bytes 786436
  37.3 7.0 %collective-permute-start.5 = (f32[1,8]{1,0:T(1,128)S(1)}, f32[1,8]{1,0:T(1,128)S(1)}, u32[]{:S(2)}, u32[]{:S(2)}) collective-permute-start(f32[1,8]{1,0:T(1,128)S(1)} %mul.702), channel_id=1, source_target_pairs={{0,32},{8,40},{16,48},{24,56},{32,64},{40,72},{48,80},{56,88},{64,... | collective-permute-start | bytes 104 | tf_op jit(solution)/shard_map/ppermute | solution.py:44
  44.4 7.8 %collective-permute-start.8 = (f32[1,8,64,128]{3,2,1,0:T(8,128)S(1)}, f32[1,8,64,128]{3,2,1,0:T(8,128)S(1)}, u32[]{:S(2)}, u32[]{:S(2)}) collective-permute-start(f32[1,8,64,128]{3,2,1,0:T(8,128)S(1)} %multiply_add_fusion.9), channel_id=1, source_target_pairs={{0,128},{8,136},{16,144},{24,152},{32,160},{40,168},{48,176},{56,1... | collective-permute-start | bytes 786440 | tf_op jit(solution)/shard_map/ppermute | solution.py:44
  48.3 4.1 %copy-start.22 = (f32[16,256]{1,0:T(8,128)}, f32[16,256]{1,0:T(8,128)S(1)}, u32[]{:S(2)}) copy-start(f32[16,256]{1,0:T(8,128)S(1)} %fusion.134) | copy-start | bytes 49156
  48.4 3.8 %collective-permute-start.7 = (f32[1,8]{1,0:T(1,128)S(1)}, f32[1,8]{1,0:T(1,128)S(1)}, u32[]{:S(2)}, u32[]{:S(2)}) collective-permute-start(f32[1,8]{1,0:T(1,128)S(1)} %mul.710), channel_id=1, source_target_pairs={{0,64},{8,72},{16,80},{24,88},{32,96},{40,104},{48,112},{56,120},{... | collective-permute-start | bytes 104 | tf_op jit(solution)/shard_map/ppermute | solution.py:44
  52.2 0.7 copy-start.15
  52.3 2.7 %copy-start.33 = (f32[16]{0:T(128)S(1)}, f32[16]{0:T(128)}, u32[]{:S(2)}) copy-start(f32[16]{0:T(128)} %param.18) | copy-start | bytes 196
  52.4 4.2 %collective-permute-start.9 = (f32[1,8,64,128]{3,2,1,0:T(8,128)S(1)}, f32[1,8,64,128]{3,2,1,0:T(8,128)S(1)}, u32[]{:S(2)}, u32[]{:S(2)}) collective-permute-start(f32[1,8,64,128]{3,2,1,0:T(8,128)S(1)} %get-tuple-element.161), channel_id=1, source_target_pairs={{0,8},{8,0},{16,24},{24,16},{32,40},{40,32},{48,56},{56,48},{64,72... | collective-permute-start | bytes 786440 | tf_op jit(solution)/shard_map/ppermute | solution.py:44
  56.6 1.4 copy-start.3
  58.0 1.0 copy-start.1
  82.4 2.5 %collective-permute-start.11 = (f32[1,8,64,128]{3,2,1,0:T(8,128)}, f32[1,8,64,128]{3,2,1,0:T(8,128)}, u32[]{:S(2)}, u32[]{:S(2)}) collective-permute-start(f32[1,8,64,128]{3,2,1,0:T(8,128)} %dynamic-slice_bitcast_fusion), channel_id=1, source_target_pairs={{248,240},{240,248},{232,224},{224,232},{216,208},{208,216},{200,1... | collective-permute-start | bytes 786440 | tf_op jit(solution)/shard_map/ppermute | solution.py:44
  82.4 1.9 %collective-permute-start.10 = (f32[1,8]{1,0:T(1,128)}, f32[1,8]{1,0:T(1,128)}, u32[]{:S(2)}, u32[]{:S(2)}) collective-permute-start(f32[1,8]{1,0:T(1,128)} %bitcast.124), channel_id=1, source_target_pairs={{248,240},{240,248},{232,224},{224,232},{216,208},{208,216},{200,1... | collective-permute-start | bytes 104 | tf_op jit(solution)/shard_map/ppermute | solution.py:44
  83.0 33.5 %copy-start.7 = (f32[256,256]{1,0:T(8,128)S(1)}, f32[256,256]{1,0:T(8,128)}, u32[]{:S(2)}) copy-start(f32[256,256]{1,0:T(8,128)} %copy-done.6) | copy-start | bytes 786436
  83.0 33.5 %copy-start.9 = (f32[256,256]{1,0:T(8,128)S(1)}, f32[256,256]{1,0:T(8,128)}, u32[]{:S(2)}) copy-start(f32[256,256]{1,0:T(8,128)} %copy-done.8) | copy-start | bytes 786436
  83.0 33.5 %copy-start.16 = (f32[16,256]{1,0:T(8,128)S(1)}, f32[16,256]{1,0:T(8,128)}, u32[]{:S(2)}) copy-start(f32[16,256]{1,0:T(8,128)} %copy-done.14) | copy-start | bytes 49156
  83.0 33.5 %copy-start.23 = (f32[16,256]{1,0:T(8,128)S(1)}, f32[16,256]{1,0:T(8,128)}, u32[]{:S(2)}) copy-start(f32[16,256]{1,0:T(8,128)} %copy-done.22) | copy-start | bytes 49156
  86.0 28.2 %collective-permute-start.12 = (f32[1,8,64,128]{3,2,1,0:T(8,128)S(1)}, f32[1,8,64,128]{3,2,1,0:T(8,128)S(1)}, u32[]{:S(2)}, u32[]{:S(2)}) collective-permute-start(f32[1,8,64,128]{3,2,1,0:T(8,128)S(1)} %fusion.74), channel_id=1, source_target_pairs={{248,232},{240,224},{232,216},{224,208},{216,200},{208,192},{200,1... | collective-permute-start | bytes 786440 | tf_op jit(solution)/shard_map/ppermute | solution.py:44
  88.8 12.1 %collective-permute-start.13 = (f32[1,8]{1,0:T(1,128)S(1)}, f32[1,8]{1,0:T(1,128)S(1)}, u32[]{:S(2)}, u32[]{:S(2)}) collective-permute-start(f32[1,8]{1,0:T(1,128)S(1)} %get-tuple-element.193), channel_id=1, source_target_pairs={{248,232},{240,224},{232,216},{224,208},{216,200},{208,192},{200,1... | collective-permute-start | bytes 104 | tf_op jit(solution)/shard_map/ppermute | solution.py:44
  100.9 7.9 %collective-permute-start.15 = (f32[1,8]{1,0:T(1,128)S(1)}, f32[1,8]{1,0:T(1,128)S(1)}, u32[]{:S(2)}, u32[]{:S(2)}) collective-permute-start(f32[1,8]{1,0:T(1,128)S(1)} %mul.755), channel_id=1, source_target_pairs={{248,216},{240,208},{232,200},{224,192},{216,184},{208,176},{200,1... | collective-permute-start | bytes 104 | tf_op jit(solution)/shard_map/ppermute | solution.py:44
  108.8 5.5 %collective-permute-start.17 = (f32[1,8]{1,0:T(1,128)S(1)}, f32[1,8]{1,0:T(1,128)S(1)}, u32[]{:S(2)}, u32[]{:S(2)}) collective-permute-start(f32[1,8]{1,0:T(1,128)S(1)} %mul.763), channel_id=1, source_target_pairs={{248,184},{240,176},{232,168},{224,160},{216,152},{208,144},{200,1... | collective-permute-start | bytes 104 | tf_op jit(solution)/shard_map/ppermute | solution.py:44
  114.3 10.7 %collective-permute-start.14 = (f32[1,8,64,128]{3,2,1,0:T(8,128)S(1)}, f32[1,8,64,128]{3,2,1,0:T(8,128)S(1)}, u32[]{:S(2)}, u32[]{:S(2)}) collective-permute-start(f32[1,8,64,128]{3,2,1,0:T(8,128)S(1)} %multiply_add_fusion.6), channel_id=1, source_target_pairs={{248,216},{240,208},{232,200},{224,192},{216,184},{208,176},{200,1... | collective-permute-start | bytes 786440 | tf_op jit(solution)/shard_map/ppermute | solution.py:44
  122.7 3.9 %copy-start.4 = (f32[1,8,64,128]{3,2,1,0:T(8,128)S(1)}, f32[1,8,64,128]{3,2,1,0:T(8,128)}, u32[]{:S(2)}) copy-start(f32[1,8,64,128]{3,2,1,0:T(8,128)} %copy-done.3) | copy-start | bytes 786436
  125.1 3.1 %copy-start.2 = (f32[1,256,1,16,64]{1,4,3,2,0:T(8,128)S(1)}, f32[1,256,1,16,64]{1,4,3,2,0:T(8,128)}, u32[]{:S(2)}) copy-start(f32[1,256,1,16,64]{1,4,3,2,0:T(8,128)} %get-tuple-element.214) | copy-start | bytes 3145732
  125.1 8.4 %collective-permute-start.16 = (f32[1,8,64,128]{3,2,1,0:T(8,128)S(1)}, f32[1,8,64,128]{3,2,1,0:T(8,128)S(1)}, u32[]{:S(2)}, u32[]{:S(2)}) collective-permute-start(f32[1,8,64,128]{3,2,1,0:T(8,128)S(1)} %multiply_add_fusion.5), channel_id=1, source_target_pairs={{248,184},{240,176},{232,168},{224,160},{216,152},{208,144},{200,1... | collective-permute-start | bytes 786440 | tf_op jit(solution)/shard_map/ppermute | solution.py:44
  133.6 9.8 %collective-permute-start.18 = (f32[1,8,64,128]{3,2,1,0:T(8,128)S(1)}, f32[1,8,64,128]{3,2,1,0:T(8,128)S(1)}, u32[]{:S(2)}, u32[]{:S(2)}) collective-permute-start(f32[1,8,64,128]{3,2,1,0:T(8,128)S(1)} %multiply_add_fusion.4), channel_id=1, source_target_pairs={{248,120},{240,112},{232,104},{224,96},{216,88},{208,80},{200,72},... | collective-permute-start | bytes 786440 | tf_op jit(solution)/shard_map/ppermute | solution.py:44
  144.5 2.2 %collective-permute-start.19 = (f32[1,8,64,128]{3,2,1,0:T(8,128)S(1)}, f32[1,8,64,128]{3,2,1,0:T(8,128)S(1)}, u32[]{:S(2)}, u32[]{:S(2)}) collective-permute-start(f32[1,8,64,128]{3,2,1,0:T(8,128)S(1)} %get-tuple-element.156), channel_id=1, source_target_pairs={{248,240},{240,248},{232,224},{224,232},{216,208},{208,216},{200,1... | collective-permute-start | bytes 786440 | tf_op jit(solution)/shard_map/ppermute | solution.py:44
  145.6 2.1 %copy-start.11 = (f32[256,16]{0,1:T(8,128)S(1)}, f32[256,16]{0,1:T(8,128)}, u32[]{:S(2)}) copy-start(f32[256,16]{0,1:T(8,128)} %copy-done.10) | copy-start | bytes 49156
  146.7 0.7 copy-start.17
  146.7 0.8 copy-start.21
  146.7 0.8 copy-start.32
  146.7 0.8 copy-start.35
  146.7 0.8 copy-start.37
  146.7 0.8 copy-start.38
  146.7 0.8 copy-start.39
  146.7 1.0 copy-start.19
  152.2 1.6 %copy-start.20 = (f32[1024]{0:T(1024)S(1)}, f32[1024]{0:T(1024)}, u32[]{:S(2)}) copy-start(f32[1024]{0:T(1024)} %mul.726) | copy-start | bytes 12292
  153.8 1.1 copy-start.13
  153.8 1.1 copy-start.18
  153.8 1.0 copy-start.25
  153.8 1.0 copy-start.27
  153.9 1.0 copy-start.29
  153.9 1.3 copy-start.36

commit v12 on v11

--- a/solution.py
+++ b/solution.py
@@ -196,7 +196,14 @@
     dt_spans = step_size.reshape(spans, SPAN, groups_here, per_group)
     b_spans = b_matrix.astype(jnp.float32).reshape(spans, SPAN, groups_here, STATE)
     c_spans = c_matrix.astype(jnp.float32).reshape(spans, SPAN, groups_here, STATE)
-    segment = jnp.cumsum(doc_resets.reshape(spans, SPAN), axis=1, dtype=jnp.int32)
+    places = jnp.arange(SPAN, dtype=jnp.int32)
+    lower = (places[:, None] >= places[None, :]).astype(jnp.float32)
+    segment = jnp.einsum(
+        "qs,ks->kq",
+        lower,
+        doc_resets.reshape(spans, SPAN).astype(jnp.float32),
+        precision=HIGHEST_PRECISION,
+    ).astype(jnp.int32)
 
     def states_call(x_value, dt_value, b_value):
         return local_states(x_value, dt_value, b_value, segment, decay_rate)

time: 157 us -> 156 us (level)
  transfers between devices with their start and end apart: 20 -> 20, of which waited for: 12 -> 12; matrix products, arithmetic and copies ran while one was open for 12% -> 13% of each run, Pallas kernels for 0% -> 0%
where the time goes in v12:
time: 156 us; the launch traced here: 155 us
  waiting for transfers between devices  47.9 us (31%)
  starting transfers between devices  40.9 us (26%)
  matrix products  23.6 us (15%)
  other arithmetic  16.2 us (10%)
  blocking collectives  16 us (10%)
  local copies, waits for them, and re-layouts  8.15 us (5%)
  between operations  2.15 us (1%)
    ppermute x20, waiting for transfers between devices, move(): return lax.ppermute(tree, axis, [(device(a), device(b)) for a, b in pairs])  47.9 us
    ppermute x20, starting transfers between devices, move(): return lax.ppermute(tree, axis, [(device(a), device(b)) for a, b in pairs])  40.9 us
    all_to_all x1, blocking collectives, head_sum(): return jnp.sum(lax.all_to_all(spread, axis, 0, 0), axis=0)  16 us
    dot_general x3, matrix products, span_mix(): return mix_apply(weights, x_span)  11.6 us
    dot_general x3, matrix products, local_states(): jnp.einsum('kqgh,kqghp,kqgn->kghpn', tail_decay * dt_spans, x_spans, b_sp...  4.8 us
    dot_general x3, matrix products, output_part(): jnp.einsum('kqgn,kghpn->kqghp', c_spans, full_start, precision=MIX_PRECIS...  3.58 us
    convert_element_type x1, other arithmetic, layer_body(): grad_gate.astype(jnp.bfloat16)  3.14 us
  transfers between devices with their start and end apart: 20, of which 12 were waited for; matrix products, arithmetic and copies ran while one was open for 13% of the time, Pallas kernels for 0%

profile of v12, /device:TPU:6, one launch (start us, length us, event | category | flops | bytes accessed | tf_op | source)
XLA Modules:
  0.0 154.9 jit_solution(6751228682699399303)
XLA Ops:
  0.7 0.7 exponential_negate_fusion
  1.4 0.7 convert_element_type.50
  2.3 0.7 slice.20
  3.6 0.7 compare_convert_fusion
  4.3 0.9 fusion.82
  5.5 1.2 copy.37
  6.9 0.4 fusion.34
  7.6 0.7 dynamic-slice_reduce_fusion.1
  8.3 0.5 collective-permute-start
  8.7 0.8 collective-permute-done
  9.7 3.4 %collective-permute-start.2 = (f32[1,8,64,128]{3,2,1,0:T(8,128)S(1)}, f32[1,8,64,128]{3,2,1,0:T(8,128)S(1)}, u32[]{:S(2)}, u32[]{:S(2)}) collective-permute-start(f32[1,8,64,128]{3,2,1,0:T(8,128)S(1)} %fusion.75), channel_id=1, source_target_pairs={{0,16},{8,24},{16,32},{24,40},{32,48},{40,56},{48,64},{56,72},{64,... | collective-permute-start | bytes 786440 | tf_op jit(solution)/shard_map/ppermute | solution.py:44
  13.1 7.0 %collective-permute-done.2 = f32[1,8,64,128]{3,2,1,0:T(8,128)S(1)} collective-permute-done((f32[1,8,64,128]{3,2,1,0:T(8,128)S(1)}, f32[1,8,64,128]{3,2,1,0:T(8,128)S(1)}, u32[]{:S(2)}, u32[]{:S(2)}) %collective-permute-start.2) | collective-permute-done | bytes 262176 | tf_op jit(solution)/shard_map/ppermute | solution.py:44
  20.2 4.3 %collective-permute-start.4 = (f32[1,8,64,128]{3,2,1,0:T(8,128)S(1)}, f32[1,8,64,128]{3,2,1,0:T(8,128)S(1)}, u32[]{:S(2)}, u32[]{:S(2)}) collective-permute-start(f32[1,8,64,128]{3,2,1,0:T(8,128)S(1)} %multiply_add_fusion.11), channel_id=1, source_target_pairs={{0,32},{8,40},{16,48},{24,56},{32,64},{40,72},{48,80},{56,88},{64,... | collective-permute-start | bytes 786440 | tf_op jit(solution)/shard_map/ppermute | solution.py:44
  24.5 4.0 %collective-permute-start.3 = (f32[1,8]{1,0:T(1,128)S(1)}, f32[1,8]{1,0:T(1,128)S(1)}, u32[]{:S(2)}, u32[]{:S(2)}) collective-permute-start(f32[1,8]{1,0:T(1,128)S(1)} %get-tuple-element.204), channel_id=1, source_target_pairs={{0,16},{8,24},{16,32},{24,40},{32,48},{40,56},{48,64},{56,72},{64,... | collective-permute-start | bytes 104 | tf_op jit(solution)/shard_map/ppermute | solution.py:44
  28.6 3.7 %collective-permute-done.3 = f32[1,8]{1,0:T(1,128)S(1)} collective-permute-done((f32[1,8]{1,0:T(1,128)S(1)}, f32[1,8]{1,0:T(1,128)S(1)}, u32[]{:S(2)}, u32[]{:S(2)}) %collective-permute-start.3) | collective-permute-done | bytes 64 | tf_op jit(solution)/shard_map/ppermute | solution.py:44
  32.3 3.5 %collective-permute-start.6 = (f32[1,8,64,128]{3,2,1,0:T(8,128)S(1)}, f32[1,8,64,128]{3,2,1,0:T(8,128)S(1)}, u32[]{:S(2)}, u32[]{:S(2)}) collective-permute-start(f32[1,8,64,128]{3,2,1,0:T(8,128)S(1)} %multiply_add_fusion.10), channel_id=1, source_target_pairs={{0,64},{8,72},{16,80},{24,88},{32,96},{40,104},{48,112},{56,120},{... | collective-permute-start | bytes 786440 | tf_op jit(solution)/shard_map/ppermute | solution.py:44
  36.2 4.3 %collective-permute-start.5 = (f32[1,8]{1,0:T(1,128)S(1)}, f32[1,8]{1,0:T(1,128)S(1)}, u32[]{:S(2)}, u32[]{:S(2)}) collective-permute-start(f32[1,8]{1,0:T(1,128)S(1)} %mul.702), channel_id=1, source_target_pairs={{0,32},{8,40},{16,48},{24,56},{32,64},{40,72},{48,80},{56,88},{64,... | collective-permute-start | bytes 104 | tf_op jit(solution)/shard_map/ppermute | solution.py:44
  40.5 2.7 %collective-permute-done.5 = f32[1,8]{1,0:T(1,128)S(1)} collective-permute-done((f32[1,8]{1,0:T(1,128)S(1)}, f32[1,8]{1,0:T(1,128)S(1)}, u32[]{:S(2)}, u32[]{:S(2)}) %collective-permute-start.5) | collective-permute-done | bytes 64 | tf_op jit(solution)/shard_map/ppermute | solution.py:44
  43.2 3.9 %collective-permute-start.8 = (f32[1,8,64,128]{3,2,1,0:T(8,128)S(1)}, f32[1,8,64,128]{3,2,1,0:T(8,128)S(1)}, u32[]{:S(2)}, u32[]{:S(2)}) collective-permute-start(f32[1,8,64,128]{3,2,1,0:T(8,128)S(1)} %multiply_add_fusion.9), channel_id=1, source_target_pairs={{0,128},{8,136},{16,144},{24,152},{32,160},{40,168},{48,176},{56,1... | collective-permute-start | bytes 786440 | tf_op jit(solution)/shard_map/ppermute | solution.py:44
  47.2 1.3 collective-permute-start.7
  48.5 2.5 %collective-permute-done.7 = f32[1,8]{1,0:T(1,128)S(1)} collective-permute-done((f32[1,8]{1,0:T(1,128)S(1)}, f32[1,8]{1,0:T(1,128)S(1)}, u32[]{:S(2)}, u32[]{:S(2)}) %collective-permute-start.7) | collective-permute-done | bytes 64 | tf_op jit(solution)/shard_map/ppermute | solution.py:44
  51.4 0.4 copy-done.15
  51.7 2.2 %fusion.29 = f32[1,256,1,16,64]{1,4,3,2,0:T(8,128)S(1)} fusion(bf16[256,16,64]{0,2,1:T(8,128)(2,1)S(1)} %bitcast.306, f32[16,256]{1,0:T(8,128)S(1)} %fusion.135, f32[256,256]{1,0:T(8,128)S(1)} %fusion.83, f32[16,256]{1,0:T(8,128)S(1)} %copy-done.15, f32[256,256]{1,0:T(8,128)S(1)} %fusion.137), kind=kOutput, calls=%fused_computation.33 | convolution fusion | flops 407896064 | bytes 2129920 | tf_op jit(solution)/shard_map/jvp()/while/body/eval_jaxpr/ghts,sghp->tghp/dot_general | solution.py:109
  54.0 0.7 mul.726
  54.7 0.8 fusion.78
  55.5 1.5 multiply_add_fusion.1
  56.9 0.3 copy.38
  57.3 0.7 copy-done.1
  58.0 2.6 %multiply_reduce_fusion.2 = (f32[256]{0:T(256)S(1)}, f32[256]{0:T(256)S(1)}, f32[256,1024]{1,0:T(8,128)}) fusion(bf16[256,1024]{1,0:T(8,128)(2,1)} %param.21, f32[1024]{0:T(1024)} %param.19, bf16[256,1024]{1,0:T(8,128)(2,1)} %param.12, f32[256,1024]{1,0:T(8,128)S(1)} %copy.38, f32[1024]{0:T(1024)} %mul.726, bf16[256,1024]{1,0:T(8,128)(2,1)S(1)} %copy-done.1), kind=kLoop, calls=%fused_computation.76 | loop fusion | flops 3931648 | bytes 3680256 | tf_op jit(solution)/shard_map/reduce_sum | solution.py:230
  60.6 16.0 %all_to_all.5 = f32[8,2,256]{2,1,0:T(2,128)S(1)} all-to-all(f32[8,2,256]{2,1,0:T(2,128)S(1)} %broadcast_in_dim.153), channel_id=1, replica_groups=mesh['ctx'=32,'head'=8] {'head'}, dimensions={0} | all-to-all | bytes 32768 | tf_op jit(solution)/shard_map/all_to_all | solution.py:77
  76.6 3.1 %fusion.55 = (bf16[256,1024]{1,0:T(8,128)(2,1)}, f32[256,1024]{1,0:T(8,128)S(1)}) fusion(bf16[256,1024]{1,0:T(8,128)(2,1)} %param.12, f32[256,1024]{1,0:T(8,128)S(1)} %copy.38, bf16[256,1024]{1,0:T(8,128)(2,1)S(1)} %copy-done.1, f32[256]{0:T(256)S(1)} %multiply_multiply_fusion, f32[256,1024]{1,0:T(8,128)} %get-tuple-element.158, ...), kind=kLoop, calls=%fused_computation.63 | loop fusion | flops 5767168 | bytes 5253120 | tf_op jit(solution)/shard_map/convert_element_type | solution.py:256
  79.8 0.3 copy.40
  80.1 0.4 fusion.57
  80.6 0.7 dynamic-slice_bitcast_fusion
  81.3 0.5 collective-permute-start.10
  81.8 1.4 collective-permute-done.10
  83.2 0.7 fusion.132
  83.9 1.0 fusion.74
  84.9 2.7 %collective-permute-start.12 = (f32[1,8,64,128]{3,2,1,0:T(8,128)S(1)}, f32[1,8,64,128]{3,2,1,0:T(8,128)S(1)}, u32[]{:S(2)}, u32[]{:S(2)}) collective-permute-start(f32[1,8,64,128]{3,2,1,0:T(8,128)S(1)} %fusion.74), channel_id=1, source_target_pairs={{248,232},{240,224},{232,216},{224,208},{216,200},{208,192},{200,1... | collective-permute-start | bytes 786440 | tf_op jit(solution)/shard_map/ppermute | solution.py:44
  87.7 4.2 %collective-permute-start.13 = (f32[1,8]{1,0:T(1,128)S(1)}, f32[1,8]{1,0:T(1,128)S(1)}, u32[]{:S(2)}, u32[]{:S(2)}) collective-permute-start(f32[1,8]{1,0:T(1,128)S(1)} %get-tuple-element.191), channel_id=1, source_target_pairs={{248,232},{240,224},{232,216},{224,208},{216,200},{208,192},{200,1... | collective-permute-start | bytes 104 | tf_op jit(solution)/shard_map/ppermute | solution.py:44
  91.9 7.9 %collective-permute-done.13 = f32[1,8]{1,0:T(1,128)S(1)} collective-permute-done((f32[1,8]{1,0:T(1,128)S(1)}, f32[1,8]{1,0:T(1,128)S(1)}, u32[]{:S(2)}, u32[]{:S(2)}) %collective-permute-start.13) | collective-permute-done | bytes 64 | tf_op jit(solution)/shard_map/ppermute | solution.py:44
  99.8 1.9 %collective-permute-start.15 = (f32[1,8]{1,0:T(1,128)S(1)}, f32[1,8]{1,0:T(1,128)S(1)}, u32[]{:S(2)}, u32[]{:S(2)}) collective-permute-start(f32[1,8]{1,0:T(1,128)S(1)} %mul.755), channel_id=1, source_target_pairs={{248,216},{240,208},{232,200},{224,192},{216,184},{208,176},{200,1... | collective-permute-start | bytes 104 | tf_op jit(solution)/shard_map/ppermute | solution.py:44
  101.7 5.9 %collective-permute-done.15 = f32[1,8]{1,0:T(1,128)S(1)} collective-permute-done((f32[1,8]{1,0:T(1,128)S(1)}, f32[1,8]{1,0:T(1,128)S(1)}, u32[]{:S(2)}, u32[]{:S(2)}) %collective-permute-start.15) | collective-permute-done | bytes 64 | tf_op jit(solution)/shard_map/ppermute | solution.py:44
  107.6 1.3 collective-permute-start.17
  108.9 4.2 %collective-permute-done.17 = f32[1,8]{1,0:T(1,128)S(1)} collective-permute-done((f32[1,8]{1,0:T(1,128)S(1)}, f32[1,8]{1,0:T(1,128)S(1)}, u32[]{:S(2)}, u32[]{:S(2)}) %collective-permute-start.17) | collective-permute-done | bytes 64 | tf_op jit(solution)/shard_map/ppermute | solution.py:44
  113.2 2.1 %collective-permute-start.14 = (f32[1,8,64,128]{3,2,1,0:T(8,128)S(1)}, f32[1,8,64,128]{3,2,1,0:T(8,128)S(1)}, u32[]{:S(2)}, u32[]{:S(2)}) collective-permute-start(f32[1,8,64,128]{3,2,1,0:T(8,128)S(1)} %multiply_add_fusion.6), channel_id=1, source_target_pairs={{248,216},{240,208},{232,200},{224,192},{216,184},{208,176},{200,1... | collective-permute-start | bytes 786440 | tf_op jit(solution)/shard_map/ppermute | solution.py:44
  115.3 6.2 %fusion.73 = (f32[16,256]{1,0:T(8,128)}, f32[16,256]{1,0:T(8,128)}, f32[16,256]{1,0:T(8,128)}, f32[256,256]{1,0:T(8,128)S(1)}) fusion(f32[16,256]{1,0:T(8,128)S(1)} %copy-done.16, f32[256,256]{1,0:T(8,128)S(1)} %copy-done.9, f32[16,256]{1,0:T(8,128)S(1)} %copy-done.23, f32[256,256]{1,0:T(8,128)S(1)} %copy-done.7, bf16[256,16,64]{0,2,1:T(8,128)(2,1)S(1)} %bitcast.307, ...), kind=kOutput, calls=%fused_computation.95 | convolution fusion | flops 422498304 | bytes 2441216 | tf_op jit(solution)/shard_map/transpose(jvp())/while/body/eval_jaxpr/tghp,sghp->ghts/dot_general | solution.py:109
  121.8 2.1 %collective-permute-done.14 = f32[1,8,64,128]{3,2,1,0:T(8,128)S(1)} collective-permute-done((f32[1,8,64,128]{3,2,1,0:T(8,128)S(1)}, f32[1,8,64,128]{3,2,1,0:T(8,128)S(1)}, u32[]{:S(2)}, u32[]{:S(2)}) %collective-permute-start.14) | collective-permute-done | bytes 262176 | tf_op jit(solution)/shard_map/ppermute | solution.py:44
  124.0 1.4 collective-permute-start.16
  125.4 1.7 %fusion.37 = f32[1,256,1,128]{3,1,2,0:T(8,128)} fusion(f32[256,128]{1,0:T(8,128)S(1)} %fusion.138, f32[1,256,1,16,64]{1,4,3,2,0:T(8,128)S(1)} %bitcast.302, f32[256,16]{0,1:T(8,128)S(1)} %get-tuple-element.165, f32[8,64,128]{2,1,0:T(8,128)S(1)} %bitcast.310, f32[8,64,128]{2,1,0:T(8,128)S(1)} %bitcast.316, pred[]{:T(512)S(6)} %eq.69), kind=kOutput, calls=%fused_computation.43 | convolution fusion | flops 202014720 | bytes 1851393 | tf_op jit(solution)/shard_map/transpose(jvp(kqgn,kghpn->kqghp))/dot_general | solution.py:163
  127.1 0.7 multiply_reduce_fusion
  127.8 4.5 %collective-permute-done.16 = f32[1,8,64,128]{3,2,1,0:T(8,128)S(1)} collective-permute-done((f32[1,8,64,128]{3,2,1,0:T(8,128)S(1)}, f32[1,8,64,128]{3,2,1,0:T(8,128)S(1)}, u32[]{:S(2)}, u32[]{:S(2)}) %collective-permute-start.16) | collective-permute-done | bytes 262176 | tf_op jit(solution)/shard_map/ppermute | solution.py:44
  132.5 1.3 collective-permute-start.18
  133.8 3.2 %fusion.26 = f32[1,256,1,16,64]{1,4,3,2,0:T(8,128)} fusion(f32[16,256]{1,0:T(8,128)S(1)} %copy-done.23, f32[256,256]{1,0:T(8,128)S(1)} %copy-done.9, f32[16,256]{1,0:T(8,128)S(1)} %copy-done.16, f32[256,256]{1,0:T(8,128)S(1)} %copy-done.7, f32[1,256,1,16,64]{1,4,3,2,0:T(8,128)S(1)} %bitcast.304), kind=kOutput, calls=%fused_computation.30 | convolution fusion | flops 407896064 | bytes 2654208 | tf_op jit(solution)/shard_map/transpose(jvp())/while/body/eval_jaxpr/ghts,tghp->sghp/dot_general | solution.py:109
  137.0 5.2 %collective-permute-done.18 = f32[1,8,64,128]{3,2,1,0:T(8,128)S(1)} collective-permute-done((f32[1,8,64,128]{3,2,1,0:T(8,128)S(1)}, f32[1,8,64,128]{3,2,1,0:T(8,128)S(1)}, u32[]{:S(2)}, u32[]{:S(2)}) %collective-permute-start.18) | collective-permute-done | bytes 262176 | tf_op jit(solution)/shard_map/ppermute | solution.py:44
  142.2 1.1 fusion.77
  143.5 1.0 convolution_bitcast_fusion.2
  144.4 1.1 fusion.76
  145.6 0.3 multiply_reduce_fusion.3
  146.6 1.7 %fusion.39 = f32[256,128]{1,0:T(8,128)} fusion(f32[1,256,1,128]{3,1,2,0:T(8,128)S(1)} %copy-done.19, bf16[256,16,64]{0,2,1:T(8,128)(2,1)S(1)} %bitcast.308, f32[256,16]{0,1:T(8,128)S(1)} %copy-done.11, f32[8,64,128]{2,1,0:T(8,128)S(1)} %bitcast.313, f32[8,64,128]{2,1,0:T(8,128)S(1)} %bitcast.317, pred[]{:T(512)S(6)} %eq.76), kind=kOutput, calls=%fused_computation.45 | convolution fusion | flops 202276864 | bytes 1327105 | tf_op jit(solution)/shard_map/transpose(jvp(kqgh,kqghp,kqgn->kghpn))/dot_general | solution.py:128
  148.3 2.7 %bitcast_add_fusion = (f32[1,256,1,16,64]{1,4,3,2,0:T(8,128)}, f32[256,16,64]{0,2,1:T(8,128)S(1)}) fusion(f32[1,256,1,16,64]{1,4,3,2,0:T(8,128)} %fusion.26, f32[256,16]{0,1:T(8,128)S(1)} %copy-done.11, bf16[256,128]{1,0:T(8,128)(2,1)S(1)} %copy-done.5, f32[8,64,128]{2,1,0:T(8,128)S(1)} %bitcast.314, f32[8,64,128]{2,1,0:T(8,128)S(1)} %bitcast.318, pred[]{:T(512)S(6)} %eq.76), kind=kOutput, calls=%fused_computation.67 | convolution fusion | flops 202244096 | bytes 3751937 | tf_op jit(solution)/shard_map/transpose(jvp(kqgh,kqghp,kqgn->kghpn))/dot_general | solution.py:128
  151.1 1.6 %copy.41 = f32[256,1024]{1,0:T(8,128)S(1)} copy(f32[256,1024]{0,1:T(8,128)} %bitcast.311) | data formatting | bytes 2097152 | tf_op jit(solution)/shard_map/reshape | solution.py:246
  152.8 1.0 add_convert_fusion
  154.1 0.9 fusion.45
  (128 shorter events, 3.8 us)
Async XLA Ops:
  0.6 35.3 %copy-start = (bf16[256,128]{1,0:T(8,128)(2,1)S(1)}, bf16[256,128]{1,0:T(8,128)(2,1)}, u32[]{:S(2)}) copy-start(bf16[256,128]{1,0:T(8,128)(2,1)} %param.15) | copy-start | bytes 196612
  0.6 6.1 %copy-start.26 = (f32[16]{0:T(128)S(1)}, f32[16]{0:T(128)}, u32[]{:S(2)}) copy-start(f32[16]{0:T(128)} %param.16) | copy-start | bytes 196
  0.7 6.1 %copy-start.12 = (f32[256,16]{0,1:T(8,128)S(1)}, f32[256,16]{0,1:T(8,128)}, u32[]{:S(2)}) copy-start(f32[256,16]{0,1:T(8,128)} %param.13) | copy-start | bytes 49156
  0.7 6.2 %copy-start.5 = (bf16[256,128]{1,0:T(8,128)(2,1)S(1)}, bf16[256,128]{1,0:T(8,128)(2,1)}, u32[]{:S(2)}) copy-start(bf16[256,128]{1,0:T(8,128)(2,1)} %param.14) | copy-start | bytes 196612
  1.4 3.9 %copy-start.34 = (f32[16]{0:T(128)}, f32[16]{0:T(128)S(1)}, u32[]{:S(2)}) copy-start(f32[16]{0:T(128)S(1)} %exponential_negate_fusion) | copy-start | bytes 196
  4.3 3.1 %copy-start.24 = (f32[256]{0:T(256)}, f32[256]{0:T(256)S(1)}, u32[]{:S(2)}) copy-start(f32[256]{0:T(256)S(1)} %get-tuple-element.201) | copy-start | bytes 3076
  4.3 3.1 %copy-start.31 = (f32[256]{0:T(256)}, f32[256]{0:T(256)S(1)}, u32[]{:S(2)}) copy-start(f32[256]{0:T(256)S(1)} %get-tuple-element.200) | copy-start | bytes 3076
  5.2 2.1 %copy-start.14 = (f32[16,256]{1,0:T(8,128)}, f32[16,256]{1,0:T(8,128)S(1)}, u32[]{:S(2)}) copy-start(f32[16,256]{1,0:T(8,128)S(1)} %fusion.82) | copy-start | bytes 49156
  5.5 1.9 %copy-start.28 = (f32[16]{0:T(128)}, f32[16]{0:T(128)S(1)}, u32[]{:S(2)}) copy-start(f32[16]{0:T(128)S(1)} %get-tuple-element.167) | copy-start | bytes 196
  6.9 0.6 copy-start.10
  7.5 2.1 %collective-permute-start.1 = (f32[1,8,64,128]{3,2,1,0:T(8,128)S(1)}, f32[1,8,64,128]{3,2,1,0:T(8,128)S(1)}, u32[]{:S(2)}, u32[]{:S(2)}) collective-permute-start(f32[1,8,64,128]{3,2,1,0:T(8,128)S(1)} %dynamic-slice_bitcast_fusion.1), channel_id=1, source_target_pairs={{0,8},{8,0},{16,24},{24,16},{32,40},{40,32},{48,56},{56,48},{64,72... | collective-permute-start | bytes 786440 | tf_op jit(solution)/shard_map/ppermute | solution.py:44
  8.3 1.3 collective-permute-start
  9.6 41.5 %copy-start.30 = (f32[8]{0:T(128)}, f32[8]{0:T(128)S(1)}, u32[]{:S(2)}) copy-start(f32[8]{0:T(128)S(1)} %get-tuple-element.205) | copy-start | bytes 100
  9.7 10.4 %collective-permute-start.2 = (f32[1,8,64,128]{3,2,1,0:T(8,128)S(1)}, f32[1,8,64,128]{3,2,1,0:T(8,128)S(1)}, u32[]{:S(2)}, u32[]{:S(2)}) collective-permute-start(f32[1,8,64,128]{3,2,1,0:T(8,128)S(1)} %fusion.75), channel_id=1, source_target_pairs={{0,16},{8,24},{16,32},{24,40},{32,48},{40,56},{48,64},{56,72},{64,... | collective-permute-start | bytes 786440 | tf_op jit(solution)/shard_map/ppermute | solution.py:44
  20.2 12.0 %collective-permute-start.4 = (f32[1,8,64,128]{3,2,1,0:T(8,128)S(1)}, f32[1,8,64,128]{3,2,1,0:T(8,128)S(1)}, u32[]{:S(2)}, u32[]{:S(2)}) collective-permute-start(f32[1,8,64,128]{3,2,1,0:T(8,128)S(1)} %multiply_add_fusion.11), channel_id=1, source_target_pairs={{0,32},{8,40},{16,48},{24,56},{32,64},{40,72},{48,80},{56,88},{64,... | collective-permute-start | bytes 786440 | tf_op jit(solution)/shard_map/ppermute | solution.py:44
  24.5 7.7 %collective-permute-start.3 = (f32[1,8]{1,0:T(1,128)S(1)}, f32[1,8]{1,0:T(1,128)S(1)}, u32[]{:S(2)}, u32[]{:S(2)}) collective-permute-start(f32[1,8]{1,0:T(1,128)S(1)} %get-tuple-element.204), channel_id=1, source_target_pairs={{0,16},{8,24},{16,32},{24,40},{32,48},{40,56},{48,64},{56,72},{64,... | collective-permute-start | bytes 104 | tf_op jit(solution)/shard_map/ppermute | solution.py:44
  32.3 10.8 %collective-permute-start.6 = (f32[1,8,64,128]{3,2,1,0:T(8,128)S(1)}, f32[1,8,64,128]{3,2,1,0:T(8,128)S(1)}, u32[]{:S(2)}, u32[]{:S(2)}) collective-permute-start(f32[1,8,64,128]{3,2,1,0:T(8,128)S(1)} %multiply_add_fusion.10), channel_id=1, source_target_pairs={{0,64},{8,72},{16,80},{24,88},{32,96},{40,104},{48,112},{56,120},{... | collective-permute-start | bytes 786440 | tf_op jit(solution)/shard_map/ppermute | solution.py:44
  36.0 15.4 %copy-start.8 = (f32[256,256]{1,0:T(8,128)}, f32[256,256]{1,0:T(8,128)S(1)}, u32[]{:S(2)}) copy-start(f32[256,256]{1,0:T(8,128)S(1)} %fusion.83) | copy-start | bytes 786436
  36.2 15.2 %copy-start.6 = (f32[256,256]{1,0:T(8,128)}, f32[256,256]{1,0:T(8,128)S(1)}, u32[]{:S(2)}) copy-start(f32[256,256]{1,0:T(8,128)S(1)} %fusion.137) | copy-start | bytes 786436
  36.2 7.0 %collective-permute-start.5 = (f32[1,8]{1,0:T(1,128)S(1)}, f32[1,8]{1,0:T(1,128)S(1)}, u32[]{:S(2)}, u32[]{:S(2)}) collective-permute-start(f32[1,8]{1,0:T(1,128)S(1)} %mul.702), channel_id=1, source_target_pairs={{0,32},{8,40},{16,48},{24,56},{32,64},{40,72},{48,80},{56,88},{64,... | collective-permute-start | bytes 104 | tf_op jit(solution)/shard_map/ppermute | solution.py:44
  43.2 7.8 %collective-permute-start.8 = (f32[1,8,64,128]{3,2,1,0:T(8,128)S(1)}, f32[1,8,64,128]{3,2,1,0:T(8,128)S(1)}, u32[]{:S(2)}, u32[]{:S(2)}) collective-permute-start(f32[1,8,64,128]{3,2,1,0:T(8,128)S(1)} %multiply_add_fusion.9), channel_id=1, source_target_pairs={{0,128},{8,136},{16,144},{24,152},{32,160},{40,168},{48,176},{56,1... | collective-permute-start | bytes 786440 | tf_op jit(solution)/shard_map/ppermute | solution.py:44
  47.2 4.1 %copy-start.22 = (f32[16,256]{1,0:T(8,128)}, f32[16,256]{1,0:T(8,128)S(1)}, u32[]{:S(2)}) copy-start(f32[16,256]{1,0:T(8,128)S(1)} %fusion.135) | copy-start | bytes 49156
  47.2 3.8 %collective-permute-start.7 = (f32[1,8]{1,0:T(1,128)S(1)}, f32[1,8]{1,0:T(1,128)S(1)}, u32[]{:S(2)}, u32[]{:S(2)}) collective-permute-start(f32[1,8]{1,0:T(1,128)S(1)} %mul.710), channel_id=1, source_target_pairs={{0,64},{8,72},{16,80},{24,88},{32,96},{40,104},{48,112},{56,120},{... | collective-permute-start | bytes 104 | tf_op jit(solution)/shard_map/ppermute | solution.py:44
  51.0 0.7 copy-start.15
  51.2 2.7 %copy-start.33 = (f32[16]{0:T(128)S(1)}, f32[16]{0:T(128)}, u32[]{:S(2)}) copy-start(f32[16]{0:T(128)} %param.18) | copy-start | bytes 196
  51.2 4.2 %collective-permute-start.9 = (f32[1,8,64,128]{3,2,1,0:T(8,128)S(1)}, f32[1,8,64,128]{3,2,1,0:T(8,128)S(1)}, u32[]{:S(2)}, u32[]{:S(2)}) collective-permute-start(f32[1,8,64,128]{3,2,1,0:T(8,128)S(1)} %get-tuple-element.159), channel_id=1, source_target_pairs={{0,8},{8,0},{16,24},{24,16},{32,40},{40,32},{48,56},{56,48},{64,72... | collective-permute-start | bytes 786440 | tf_op jit(solution)/shard_map/ppermute | solution.py:44
  55.4 1.5 copy-start.3
  56.9 1.0 copy-start.1
  81.3 2.5 %collective-permute-start.11 = (f32[1,8,64,128]{3,2,1,0:T(8,128)}, f32[1,8,64,128]{3,2,1,0:T(8,128)}, u32[]{:S(2)}, u32[]{:S(2)}) collective-permute-start(f32[1,8,64,128]{3,2,1,0:T(8,128)} %dynamic-slice_bitcast_fusion), channel_id=1, source_target_pairs={{248,240},{240,248},{232,224},{224,232},{216,208},{208,216},{200,1... | collective-permute-start | bytes 786440 | tf_op jit(solution)/shard_map/ppermute | solution.py:44
  81.3 1.9 %collective-permute-start.10 = (f32[1,8]{1,0:T(1,128)}, f32[1,8]{1,0:T(1,128)}, u32[]{:S(2)}, u32[]{:S(2)}) collective-permute-start(f32[1,8]{1,0:T(1,128)} %bitcast.120), channel_id=1, source_target_pairs={{248,240},{240,248},{232,224},{224,232},{216,208},{208,216},{200,1... | collective-permute-start | bytes 104 | tf_op jit(solution)/shard_map/ppermute | solution.py:44
  81.8 33.5 %copy-start.7 = (f32[256,256]{1,0:T(8,128)S(1)}, f32[256,256]{1,0:T(8,128)}, u32[]{:S(2)}) copy-start(f32[256,256]{1,0:T(8,128)} %copy-done.6) | copy-start | bytes 786436
  81.8 33.5 %copy-start.9 = (f32[256,256]{1,0:T(8,128)S(1)}, f32[256,256]{1,0:T(8,128)}, u32[]{:S(2)}) copy-start(f32[256,256]{1,0:T(8,128)} %copy-done.8) | copy-start | bytes 786436
  81.8 33.5 %copy-start.16 = (f32[16,256]{1,0:T(8,128)S(1)}, f32[16,256]{1,0:T(8,128)}, u32[]{:S(2)}) copy-start(f32[16,256]{1,0:T(8,128)} %copy-done.14) | copy-start | bytes 49156
  81.8 33.5 %copy-start.23 = (f32[16,256]{1,0:T(8,128)S(1)}, f32[16,256]{1,0:T(8,128)}, u32[]{:S(2)}) copy-start(f32[16,256]{1,0:T(8,128)} %copy-done.22) | copy-start | bytes 49156
  84.9 28.2 %collective-permute-start.12 = (f32[1,8,64,128]{3,2,1,0:T(8,128)S(1)}, f32[1,8,64,128]{3,2,1,0:T(8,128)S(1)}, u32[]{:S(2)}, u32[]{:S(2)}) collective-permute-start(f32[1,8,64,128]{3,2,1,0:T(8,128)S(1)} %fusion.74), channel_id=1, source_target_pairs={{248,232},{240,224},{232,216},{224,208},{216,200},{208,192},{200,1... | collective-permute-start | bytes 786440 | tf_op jit(solution)/shard_map/ppermute | solution.py:44
  87.7 12.1 %collective-permute-start.13 = (f32[1,8]{1,0:T(1,128)S(1)}, f32[1,8]{1,0:T(1,128)S(1)}, u32[]{:S(2)}, u32[]{:S(2)}) collective-permute-start(f32[1,8]{1,0:T(1,128)S(1)} %get-tuple-element.191), channel_id=1, source_target_pairs={{248,232},{240,224},{232,216},{224,208},{216,200},{208,192},{200,1... | collective-permute-start | bytes 104 | tf_op jit(solution)/shard_map/ppermute | solution.py:44
  99.8 7.9 %collective-permute-start.15 = (f32[1,8]{1,0:T(1,128)S(1)}, f32[1,8]{1,0:T(1,128)S(1)}, u32[]{:S(2)}, u32[]{:S(2)}) collective-permute-start(f32[1,8]{1,0:T(1,128)S(1)} %mul.755), channel_id=1, source_target_pairs={{248,216},{240,208},{232,200},{224,192},{216,184},{208,176},{200,1... | collective-permute-start | bytes 104 | tf_op jit(solution)/shard_map/ppermute | solution.py:44
  107.6 5.5 %collective-permute-start.17 = (f32[1,8]{1,0:T(1,128)S(1)}, f32[1,8]{1,0:T(1,128)S(1)}, u32[]{:S(2)}, u32[]{:S(2)}) collective-permute-start(f32[1,8]{1,0:T(1,128)S(1)} %mul.763), channel_id=1, source_target_pairs={{248,184},{240,176},{232,168},{224,160},{216,152},{208,144},{200,1... | collective-permute-start | bytes 104 | tf_op jit(solution)/shard_map/ppermute | solution.py:44
  113.2 10.7 %collective-permute-start.14 = (f32[1,8,64,128]{3,2,1,0:T(8,128)S(1)}, f32[1,8,64,128]{3,2,1,0:T(8,128)S(1)}, u32[]{:S(2)}, u32[]{:S(2)}) collective-permute-start(f32[1,8,64,128]{3,2,1,0:T(8,128)S(1)} %multiply_add_fusion.6), channel_id=1, source_target_pairs={{248,216},{240,208},{232,200},{224,192},{216,184},{208,176},{200,1... | collective-permute-start | bytes 786440 | tf_op jit(solution)/shard_map/ppermute | solution.py:44
  121.5 3.9 %copy-start.4 = (f32[1,8,64,128]{3,2,1,0:T(8,128)S(1)}, f32[1,8,64,128]{3,2,1,0:T(8,128)}, u32[]{:S(2)}) copy-start(f32[1,8,64,128]{3,2,1,0:T(8,128)} %copy-done.3) | copy-start | bytes 786436
  124.0 3.1 %copy-start.2 = (f32[1,256,1,16,64]{1,4,3,2,0:T(8,128)S(1)}, f32[1,256,1,16,64]{1,4,3,2,0:T(8,128)}, u32[]{:S(2)}) copy-start(f32[1,256,1,16,64]{1,4,3,2,0:T(8,128)} %get-tuple-element.214) | copy-start | bytes 3145732
  124.0 8.4 %collective-permute-start.16 = (f32[1,8,64,128]{3,2,1,0:T(8,128)S(1)}, f32[1,8,64,128]{3,2,1,0:T(8,128)S(1)}, u32[]{:S(2)}, u32[]{:S(2)}) collective-permute-start(f32[1,8,64,128]{3,2,1,0:T(8,128)S(1)} %multiply_add_fusion.5), channel_id=1, source_target_pairs={{248,184},{240,176},{232,168},{224,160},{216,152},{208,144},{200,1... | collective-permute-start | bytes 786440 | tf_op jit(solution)/shard_map/ppermute | solution.py:44
  132.5 9.8 %collective-permute-start.18 = (f32[1,8,64,128]{3,2,1,0:T(8,128)S(1)}, f32[1,8,64,128]{3,2,1,0:T(8,128)S(1)}, u32[]{:S(2)}, u32[]{:S(2)}) collective-permute-start(f32[1,8,64,128]{3,2,1,0:T(8,128)S(1)} %multiply_add_fusion.4), channel_id=1, source_target_pairs={{248,120},{240,112},{232,104},{224,96},{216,88},{208,80},{200,72},... | collective-permute-start | bytes 786440 | tf_op jit(solution)/shard_map/ppermute | solution.py:44
  143.4 2.2 %collective-permute-start.19 = (f32[1,8,64,128]{3,2,1,0:T(8,128)S(1)}, f32[1,8,64,128]{3,2,1,0:T(8,128)S(1)}, u32[]{:S(2)}, u32[]{:S(2)}) collective-permute-start(f32[1,8,64,128]{3,2,1,0:T(8,128)S(1)} %get-tuple-element.156), channel_id=1, source_target_pairs={{248,240},{240,248},{232,224},{224,232},{216,208},{208,216},{200,1... | collective-permute-start | bytes 786440 | tf_op jit(solution)/shard_map/ppermute | solution.py:44
  144.4 2.1 %copy-start.11 = (f32[256,16]{0,1:T(8,128)S(1)}, f32[256,16]{0,1:T(8,128)}, u32[]{:S(2)}) copy-start(f32[256,16]{0,1:T(8,128)} %copy-done.10) | copy-start | bytes 49156
  145.5 0.7 copy-start.17
  145.5 0.8 copy-start.21
  145.5 0.8 copy-start.32
  145.5 0.8 copy-start.35
  145.6 0.8 copy-start.37
  145.6 0.8 copy-start.38
  145.6 0.8 copy-start.39
  145.6 1.0 copy-start.19
  151.1 1.6 %copy-start.20 = (f32[1024]{0:T(1024)S(1)}, f32[1024]{0:T(1024)}, u32[]{:S(2)}) copy-start(f32[1024]{0:T(1024)} %mul.726) | copy-start | bytes 12292
  152.7 1.1 copy-start.13
  152.7 1.1 copy-start.18
  152.7 1.0 copy-start.25
  152.7 1.0 copy-start.27
  152.7 1.0 copy-start.29
  152.7 1.3 copy-start.36
